TPU v7x, 32 devices: a whole 2x2x4 slice. The times are simulated.
32 devices in a mesh: img: 4 (over y, core), slab: 8 (over z, x).
Axes of the slice: x: 2, y: 2, z: 4, core: 2. Of those that a mesh axis runs over, the one named last changes fastest.
Arguments:
- images: bfloat16 [32, 400, 400], P(('img', 'slab')), may hold values from -1500 to 1500, as said below
- micrograph: int32 [32], P(('img', 'slab')), may hold values from 0 to 63
- defocus: float32 [64], replicated, may hold values from 30 to 90
- target_slab: int32 [32, 8, 1], P(('img', 'slab')), may hold values from 0 to 7; in each aligned block of 8 rows (0 to 7, 8 to 15, ..., all dimensions but the last counted through in order) at most 2 rows name the same one
- target_plane: int32 [32, 8], P(('img', 'slab')), may hold values from 0 to 1
- target_rows: int32 [32, 8], P(('img', 'slab')), may hold values from 0 to 7
- shift_index: int32 [32, 8], P(('img', 'slab')), may hold values from 0 to 7
- volume: bfloat16 [16, 128, 800], P('slab'), may hold values from -6 to 6
Outputs:
- residual: bfloat16 [32, 400, 400], P(('img', 'slab'))
- reconstruction: float32 [16, 128, 800], P('slab', 'img')
Inputs may be any that keep to these rules, and one draw needn't show every extreme that they name: `target_slab`: in the 8 routed blocks of one device (aligned blocks of rows, particle by particle), no slab is named more than 2 times, a bound that some block reaches. `images`: real pixel values.
All inputs are finite; a program needn't handle non-finite values.
Results may differ from a plain program's by a relative error of at most 0.013.
Values may be sent and summed in bfloat16 or wider, within the bound.
No kernel may reach another device: no remote copies, remote signals or barrier semaphores. Data moves between devices by JAX's collectives and lax.ppermute only.
A program may use at most 128 MiB of HBM per device.

v0:
```python
import math

import jax
import jax.numpy as jnp
from jax import lax
from jax.sharding import PartitionSpec as P

RB = 16
LOW = 4
WL = 8


def dft_tables(box_size):
    positions = jnp.arange(box_size, dtype=jnp.int32)
    phase_steps = positions[:, None] * positions[None, :] % box_size
    angles = phase_steps.astype(jnp.float32) * (2.0 * math.pi / box_size)
    return (jnp.cos(angles).astype(jnp.bfloat16), jnp.sin(angles).astype(jnp.bfloat16))


def forward_tables(cosine_table, sine_table):
    right_table = jnp.concatenate([cosine_table, -sine_table], axis=1)
    left_table = jnp.stack(
        [jnp.stack([cosine_table, sine_table]), jnp.stack([-sine_table, cosine_table])]
    )
    return (right_table, left_table)


def inverse_tables(cosine_table, sine_table):
    upper_half = jnp.concatenate([cosine_table, sine_table], axis=1)
    lower_half = jnp.concatenate([-sine_table, cosine_table], axis=1)
    back_table = jnp.concatenate([upper_half, lower_half], axis=0)
    final_table = jnp.stack([cosine_table, -sine_table])
    return (back_table, final_table)


def transform(image_block, right_table, left_table):
    batch_size, box_size = (image_block.shape[0], image_block.shape[1])
    rowwise = jnp.einsum(
        "nyx,xm->nym", image_block, right_table, preferred_element_type=jnp.float32
    ).astype(jnp.bfloat16)
    quarters = rowwise.reshape(batch_size, box_size, 2, box_size)
    spectrum = jnp.einsum(
        "ahky,nyhm->nkam", left_table, quarters, preferred_element_type=jnp.float32
    )
    return spectrum.reshape(batch_size, box_size, 2 * box_size)


def invert(difference, back_table, final_table):
    batch_size, box_size = (difference.shape[0], difference.shape[1])
    rowwise = jnp.einsum(
        "nyj,jk->nyk", difference, back_table, preferred_element_type=jnp.float32
    ).astype(jnp.bfloat16)
    quarters = rowwise.reshape(batch_size, box_size, 2, box_size)
    picture = (
        jnp.einsum("cxk,nkcm->nxm", final_table, quarters, preferred_element_type=jnp.float32)
        / box_size
    )
    return picture.astype(jnp.bfloat16)


def radius_sq(row_ids, box_size):
    half_size = box_size // 2
    columns = jnp.arange(box_size, dtype=jnp.int32)
    freq_rows = jnp.where(row_ids < half_size, row_ids, row_ids - box_size)
    freq_cols = jnp.where(columns < half_size, columns, columns - box_size)
    total = freq_rows[..., None] * freq_rows[..., None] + freq_cols * freq_cols
    return total.astype(jnp.float32) / float(half_size * half_size)


def contrast_curve(defocus_of, row_ids, box_size):
    radius = radius_sq(row_ids, box_size)
    return (-jnp.sin(defocus_of[:, None, None] * radius + 0.1)).astype(jnp.bfloat16)


def lookup_defocus(mic_ids, defocus):
    labels = jnp.arange(defocus.shape[0], dtype=jnp.int32)
    return jnp.sum(jnp.where(mic_ids[:, None] == labels[None, :], defocus[None, :], 0.0), axis=1)


def shift_halves(values, steps, box_size):
    split_shape = values.shape[:-1] + (2, box_size)
    return jnp.roll(values.reshape(split_shape), steps, axis=-1).reshape(values.shape)


def body(images, micrograph, defocus, target_slab, target_plane, target_rows, shift_index, volume):
    particles, box_size = (images.shape[0], images.shape[1])
    slab_count = lax.axis_size("slab")
    device_count = lax.axis_size("img") * slab_count
    low_rows = LOW * RB
    routed = particles * 2 * LOW
    cosine_table, sine_table = dft_tables(box_size)
    right_table, left_table = forward_tables(cosine_table, sine_table)
    back_table, final_table = inverse_tables(cosine_table, sine_table)
    spectrum = transform(images, right_table, left_table)
    real_part = spectrum[..., :box_size]
    imag_part = spectrum[..., box_size:]
    power_sum = jnp.sum(real_part * real_part + imag_part * imag_part, axis=0)
    power_all = lax.psum(power_sum, ("img", "slab"))
    noise_level = jnp.sqrt(power_all / (particles * device_count) + 1e-06)
    whitened = spectrum / jnp.concatenate([noise_level, noise_level], axis=1)
    row_all = jnp.arange(box_size, dtype=jnp.int32)[None, :]
    contrast = contrast_curve(lookup_defocus(micrograph, defocus), row_all, box_size)
    contrast_both = jnp.concatenate([contrast, contrast], axis=-1).astype(jnp.float32)
    weighted = (contrast_both * whitened).astype(jnp.bfloat16)
    low_blocks = jnp.concatenate(
        [weighted[:, :low_rows], weighted[:, box_size - low_rows :]], axis=1
    )
    low_blocks = low_blocks.reshape(routed, RB, 2 * box_size)
    destination = target_slab.reshape(routed)
    capacity = max(2, (2 * routed + slab_count - 1) // slab_count)
    member = (destination[:, None] == jnp.arange(slab_count, dtype=jnp.int32)[None, :]).astype(
        jnp.int32
    )
    before = jnp.cumsum(member, axis=0) - member
    slot_rank = jnp.sum(member * before, axis=1)
    seat_index = destination * capacity + slot_rank
    seat_count = slab_count * capacity
    live_flag = jnp.ones((routed,), jnp.int32)
    source_block = jnp.tile(jnp.arange(2 * LOW, dtype=jnp.int32), particles)
    block_info = jnp.stack(
        [
            live_flag,
            target_plane.reshape(routed),
            target_rows.reshape(routed),
            shift_index.reshape(routed),
            source_block,
            jnp.repeat(micrograph, 2 * LOW),
        ],
        axis=1,
    )
    send_blocks = (
        jnp.zeros((seat_count, RB, 2 * box_size), jnp.bfloat16).at[seat_index].set(low_blocks)
    )
    send_info = jnp.zeros((seat_count, 6), jnp.int32).at[seat_index].set(block_info)
    low_contrast = jnp.concatenate(
        [contrast[:, :low_rows], contrast[:, box_size - low_rows :]], axis=1
    )
    low_contrast = low_contrast.reshape(routed, RB, box_size)
    send_contrast = (
        jnp.zeros((seat_count, RB, box_size), jnp.bfloat16).at[seat_index].set(low_contrast)
    )
    got_blocks, got_contrast, got_info = (
        lax.all_to_all(send_blocks, "slab", split_axis=0, concat_axis=0, tiled=True),
        lax.all_to_all(send_contrast, "slab", split_axis=0, concat_axis=0, tiled=True),
        lax.all_to_all(send_info, "slab", split_axis=0, concat_axis=0, tiled=True),
    )
    live_mask = got_info[:, 0].astype(jnp.float32)[:, None, None]
    row_index = got_info[:, 2][:, None] * RB + jnp.arange(RB, dtype=jnp.int32)
    plane_index = jnp.broadcast_to(got_info[:, 1][:, None], row_index.shape)
    blend_weight = ((got_info[:, 3].astype(jnp.float32) + 0.5) / WL)[:, None, None]
    nearby = volume[plane_index, row_index].astype(jnp.float32)
    projected = (
        ((1.0 - blend_weight) * nearby + blend_weight * shift_halves(nearby, -1, box_size))
        * live_mask
    ).astype(jnp.bfloat16)
    returned_rows = lax.all_to_all(projected, "slab", split_axis=0, concat_axis=0, tiled=True)
    received = got_blocks.astype(jnp.float32)
    inserted = (1.0 - blend_weight) * received + blend_weight * shift_halves(received, 1, box_size)
    contrast_rows = got_contrast.astype(jnp.float32)
    squared = contrast_rows * contrast_rows
    weights = (1.0 - blend_weight) * squared + blend_weight * jnp.roll(squared, 1, axis=-1)
    numerator = jnp.zeros((volume.shape[0], volume.shape[1], 3 * box_size), jnp.float32)
    numerator = numerator.at[plane_index, row_index].add(
        jnp.concatenate([inserted, weights], axis=-1) * live_mask
    )
    volume_part = lax.psum_scatter(
        numerator.astype(jnp.bfloat16), "img", scatter_dimension=1, tiled=True
    ).astype(jnp.float32)
    weight_sum = volume_part[..., 2 * box_size :]
    reconstruction = volume_part[..., : 2 * box_size] / (
        jnp.concatenate([weight_sum, weight_sum], axis=-1) + 1.0
    )
    own_rows = returned_rows[seat_index].reshape(particles, 2 * low_rows, 2 * box_size)
    middle = jnp.zeros((particles, box_size - 2 * low_rows, 2 * box_size), jnp.bfloat16)
    full_projection = jnp.concatenate(
        [own_rows[:, :low_rows], middle, own_rows[:, low_rows:]], axis=1
    )
    difference = (whitened - contrast_both * full_projection.astype(jnp.float32)).astype(
        jnp.bfloat16
    )
    residual = invert(difference, back_table, final_table)
    return (residual, reconstruction)


def solution(mesh):
    in_specs = (
        P(("img", "slab"), None, None),
        P(("img", "slab")),
        P(),
        P(("img", "slab"), None, None),
        P(("img", "slab"), None),
        P(("img", "slab"), None),
        P(("img", "slab"), None),
        P("slab", None, None),
    )
    out_specs = (P(("img", "slab"), None, None), P("slab", "img", None))
    return jax.shard_map(body, mesh=mesh, in_specs=in_specs, out_specs=out_specs, check_vma=False)
```

profile of v0, /device:TPU:0, one launch (start us, length us, event | category | flops | bytes accessed | tf_op | source)
XLA Modules:
  0.0 247.4 jit_solution(15363540202320379219)
XLA Ops:
  7.2 3.5 %sine_convert_fusion = (bf16[1,400,400]{2,1,0:T(8,128)(2,1)S(1)}, bf16[1,400,400]{2,1,0:T(8,128)(2,1)S(1)}) fusion(), kind=kLoop, calls=%fused_computation.54 | loop fusion | flops 1760000 | bytes 640000 | tf_op jit(solution)/shard_map/convert_element_type | solution.py:17
  10.7 3.2 %fusion.52 = bf16[1,400,400]{2,1,0:T(8,128)(2,1)S(1)} fusion(), kind=kLoop, calls=%fused_computation.85 | loop fusion | flops 2080000 | bytes 320000 | tf_op jit(solution)/shard_map/neg | solution.py:21
  13.9 3.2 %cosine_convert_fusion.1 = bf16[400,400]{1,0:T(8,128)(2,1)S(1)} fusion(), kind=kLoop, calls=%fused_computation.60 | loop fusion | flops 1600000 | bytes 320000 | tf_op jit(solution)/shard_map/convert_element_type | solution.py:17
  17.1 3.2 %fusion.51 = bf16[400,400]{1,0:T(8,128)(2,1)S(1)} fusion(), kind=kLoop, calls=%fused_computation.84 | loop fusion | flops 2080000 | bytes 320000 | tf_op jit(solution)/shard_map/neg | solution.py:21
  21.7 1.2 copy.35
  26.3 1.2 fusion.29
  28.7 1.2 scatter_custom_fusion
  29.9 7.3 %all-to-all-start = ((s32[8,2,6]{2,1,0:T(2,128)}), s32[8,2,6]{2,1,0:T(2,128)S(1)}, u32[]{:S(2)}, u32[]{:S(2)}) async-start(s32[8,2,6]{2,1,0:T(2,128)} %bitcast.23), calls=%async_computation | async-start | bytes 16384 | tf_op jit(solution)/shard_map/all_to_all | solution.py:145
  38.3 3.8 %fusion.53 = (bf16[1,400,400]{2,1,0:T(8,128)(2,1)}, bf16[400,400]{1,0:T(8,128)(2,1)}) fusion(f32[]{:T(128)S(6)} %mul.305, s32[400]{0:T(512)S(1)} %fusion.65), kind=kLoop, calls=%fused_computation.89 | loop fusion | flops 960000 | bytes 641604 | tf_op jit(solution)/shard_map/concatenate | solution.py:103
  42.1 3.0 %negate_convert_fusion = bf16[1,400,400]{2,1,0:T(8,128)(2,1)S(1)} fusion(f32[]{:T(128)S(6)} %mul.305, s32[400]{0:T(512)S(1)} %fusion.65), kind=kLoop, calls=%fused_computation.51 | loop fusion | flops 960000 | bytes 321604 | tf_op jit(solution)/shard_map/convert_element_type | solution.py:72
  45.5 3.1 %copy.28 = f32[400,800]{1,0:T(8,128)} copy(f32[400,800]{0,1:T(8,128)} %bitcast.75) | data formatting | bytes 2560000 | tf_op jit(solution)/shard_map/reshape | solution.py:45
  49.3 2.1 scatter_fusion.1
  51.4 6.0 %all-to-all-start.3 = ((bf16[16,16,400]{2,1,0:T(8,128)(2,1)}), bf16[16,16,400]{2,1,0:T(8,128)(2,1)}, u32[]{:S(2)}, u32[]{:S(2)}) async-start(bf16[16,16,400]{2,1,0:T(8,128)(2,1)} %scatter_fusion.1), calls=%async_computation.3 | async-start | bytes 524288 | tf_op jit(solution)/shard_map/all_to_all | solution.py:144
  57.8 2.7 %gather_fusion = bf16[256,800]{1,0:T(8,128)(2,1)S(1)} fusion(bf16[2,128,800]{2,1,0:T(8,128)(2,1)S(1)} %copy.30, s32[256]{0:T(256)S(1)} %reshape.583), kind=kCustom, calls=%fused_computation | custom fusion | bytes 821248 | tf_op jit(solution)/shard_map/gather | solution.py:151
  60.5 1.3 reshape.582
  63.7 94.8 %all-reduce.2.cloned.1.call-done = f32[400,400]{1,0:T(8,128)} async-done(((f32[400,400]{1,0:T(8,128)}), f32[400,400]{1,0:T(8,128)}) %all-reduce.2.cloned.1.call-update) | async-done | bytes 640016 | tf_op jit(solution)/shard_map/psum | solution.py:98
  158.5 2.4 fusion.73
  162.3 2.2 scatter_fusion
  164.4 5.8 %all-to-all-start.2 = ((bf16[16,16,800]{2,1,0:T(8,128)(2,1)}), bf16[16,16,800]{2,1,0:T(8,128)(2,1)}, u32[]{:S(2)}, u32[]{:S(2)}) async-start(bf16[16,16,800]{2,1,0:T(8,128)(2,1)} %scatter_fusion), calls=%async_computation.2 | async-start | bytes 917504 | tf_op jit(solution)/shard_map/all_to_all | solution.py:143
  171.4 1.9 reshape.575
  174.5 2.0 fusion.48
  176.5 5.9 %all-to-all-done.2 = bf16[16,16,800]{2,1,0:T(8,128)(2,1)} async-done(((bf16[16,16,800]{2,1,0:T(8,128)(2,1)}), bf16[16,16,800]{2,1,0:T(8,128)(2,1)}, u32[]{:S(2)}, u32[]{:S(2)}) %all-to-all-start.2) | async-done | bytes 409632 | tf_op jit(solution)/shard_map/all_to_all | solution.py:143
  182.4 2.3 reshape.579
  186.2 1.9 reshape.580
  188.1 2.6 %multiply_add_fusion = (f32[16,16,800]{2,1,0:T(8,128)}, bf16[16,16,800]{2,1,0:T(8,128)(2,1)}) fusion(f32[16,16,800]{2,1,0:T(8,128)} %reshape.580, f32[16]{0:T(128)S(1)} %get-tuple-element.8, f32[16]{0:T(128)S(1)} %broadcast_subtract_fusion, bf16[16,16,800]{2,1,0:T(8,128)(2,1)} %all-to-all-done.2, f32[16]{0:T(128)S(1)} %get-tuple-element.9, ...), kind=kLoop, calls=%fused_computation.38 | loop fusion | flops 1843200 | bytes 4096192 | tf_op jit(solution)/shard_map/add | solution.py:158
  190.7 3.8 %all-to-all-start.1 = ((bf16[16,16,800]{2,1,0:T(8,128)(2,1)}), bf16[16,16,800]{2,1,0:T(8,128)(2,1)S(1)}, u32[]{:S(2)}, u32[]{:S(2)}) async-start(bf16[16,16,800]{2,1,0:T(8,128)(2,1)} %get-tuple-element.27), calls=%async_computation.1 | async-start | bytes 917504 | tf_op jit(solution)/shard_map/all_to_all | solution.py:156
  194.6 1.3 maximum_multiply_fusion
  196.0 17.0 %scatter_fusion.2 = f32[2,128,1200]{2,1,0:T(8,128)S(1)} fusion(f32[2,128,1200]{2,1,0:T(8,128)S(1)} %broadcast_in_dim.29, s32[256]{0:T(256)S(1)} %reshape.621, f32[256,1200]{1,0:T(8,128)S(1)} %bitcast.77), kind=kCustom, calls=%fused_computation.5 | custom fusion | flops 307200 | bytes 3688448 | tf_op jit(solution)/shard_map/scatter-add | solution.py:163
  214.0 3.9 %sine_convert_fusion.1 = bf16[400,400]{1,0:T(8,128)(2,1)} fusion(), kind=kLoop, calls=%fused_computation.59 | loop fusion | flops 1600000 | bytes 320000 | tf_op jit(solution)/shard_map/convert_element_type | solution.py:17
  218.5 3.8 %fusion.16 = bf16[400,800]{1,0:T(8,128)(2,1)} fusion(bf16[400,400]{1,0:T(8,128)(2,1)} %copy-done.13, bf16[400,400]{1,0:T(8,128)(2,1)} %copy-done.14, bf16[400,400]{1,0:T(8,128)(2,1)} %sine_convert_fusion.1, f32[400,800]{1,0:T(8,128)S(1)} %copy-done.10, f32[400,400]{1,0:T(8,128)S(1)} %copy-done.11, bf16[400,400]{1,0:T(8,128)(2,1)} %get-tuple-element.23, ...), kind=kOutput, calls=%fused_computation.24 | convolution fusion | flops 522240000 | bytes 4045600 | tf_op jit(solution)/shard_map/nyj,jk->nyk/dot_general | solution.py:50
  222.3 1.5 copy.36
  225.4 12.5 %reduce-scatter.2.cloned.1.call-done = bf16[2,32,1200]{2,1,0:T(8,128)(2,1)} async-done(((bf16[2,128,1200]{2,1,0:T(8,128)(2,1)}), bf16[2,32,1200]{2,1,0:T(8,128)(2,1)}) %reduce-scatter.2.cloned.1.call-update) | async-done | bytes 153616 | tf_op jit(solution)/shard_map/reduce_scatter | solution.py:166
  (100 shorter events, 20.4 us)
Async XLA Ops:
  7.2 13.9 %copy-start = (bf16[1,400,400]{2,1,0:T(8,128)(2,1)S(1)}, bf16[1,400,400]{2,1,0:T(8,128)(2,1)}, u32[]{:S(2)}) copy-start(bf16[1,400,400]{2,1,0:T(8,128)(2,1)} %param.8) | copy-start | bytes 960004
  7.2 151.4 %all-reduce.2.cloned.1.call-start = ((), (), s32[]{:S(2)}) async-start(), calls=%async_computation.5 | async-start | bytes 1638400 | tf_op jit(solution)/shard_map/psum | solution.py:98
  10.7 12.3 %copy-start.6 = (bf16[1,400,400]{2,1,0:T(8,128)(2,1)}, bf16[1,400,400]{2,1,0:T(8,128)(2,1)S(1)}, u32[]{:S(2)}) copy-start(bf16[1,400,400]{2,1,0:T(8,128)(2,1)S(1)} %get-tuple-element.29) | copy-start | bytes 960004
  13.9 9.0 %copy-start.8 = (bf16[1,400,400]{2,1,0:T(8,128)(2,1)}, bf16[1,400,400]{2,1,0:T(8,128)(2,1)S(1)}, u32[]{:S(2)}) copy-start(bf16[1,400,400]{2,1,0:T(8,128)(2,1)S(1)} %fusion.52) | copy-start | bytes 960004
  17.1 3.2 %copy-start.13 = (bf16[400,400]{1,0:T(8,128)(2,1)}, bf16[400,400]{1,0:T(8,128)(2,1)S(1)}, u32[]{:S(2)}) copy-start(bf16[400,400]{1,0:T(8,128)(2,1)S(1)} %cosine_convert_fusion.1) | copy-start | bytes 960004
  20.3 0.8 copy-start.14
  22.9 1.1 copy-start.12
  25.1 1.2 copy-start.1
  26.3 1.9 copy-start.16
  26.3 2.3 copy-start.17
  26.3 2.3 copy-start.18
  26.3 2.3 copy-start.19
  26.3 10.8 %copy-start.20 = (f32[64]{0:T(128)S(1)}, f32[64]{0:T(128)}, u32[]{:S(2)}) copy-start(f32[64]{0:T(128)} %param.10) | copy-start | bytes 772
  27.5 17.7 %copy-start.15 = (bf16[2,128,800]{1,2,0:T(8,128)(2,1)S(1)}, bf16[2,128,800]{1,2,0:T(8,128)(2,1)}, u32[]{:S(2)}) copy-start(bf16[2,128,800]{1,2,0:T(8,128)(2,1)} %param.15) | copy-start | bytes 1228804
  29.9 21.5 %all-to-all-start = ((s32[8,2,6]{2,1,0:T(2,128)}), s32[8,2,6]{2,1,0:T(2,128)S(1)}, u32[]{:S(2)}, u32[]{:S(2)}) async-start(s32[8,2,6]{2,1,0:T(2,128)} %bitcast.23), calls=%async_computation | async-start | bytes 16384 | tf_op jit(solution)/shard_map/all_to_all | solution.py:145
  51.4 113.0 %all-to-all-start.3 = ((bf16[16,16,400]{2,1,0:T(8,128)(2,1)}), bf16[16,16,400]{2,1,0:T(8,128)(2,1)}, u32[]{:S(2)}, u32[]{:S(2)}) async-start(bf16[16,16,400]{2,1,0:T(8,128)(2,1)} %scatter_fusion.1), calls=%async_computation.3 | async-start | bytes 524288 | tf_op jit(solution)/shard_map/all_to_all | solution.py:144
  158.5 2.4 copy-start.5
  164.4 17.9 %all-to-all-start.2 = ((bf16[16,16,800]{2,1,0:T(8,128)(2,1)}), bf16[16,16,800]{2,1,0:T(8,128)(2,1)}, u32[]{:S(2)}, u32[]{:S(2)}) async-start(bf16[16,16,800]{2,1,0:T(8,128)(2,1)} %scatter_fusion), calls=%async_computation.2 | async-start | bytes 917504 | tf_op jit(solution)/shard_map/all_to_all | solution.py:143
  186.2 2.0 copy-start.2
  186.2 1.9 copy-start.3
  190.7 3.9 %copy-start.4 = (f32[16,16,800]{2,1,0:T(8,128)S(1)}, f32[16,16,800]{2,1,0:T(8,128)}, u32[]{:S(2)}) copy-start(f32[16,16,800]{2,1,0:T(8,128)} %get-tuple-element.26) | copy-start | bytes 2457604
  190.7 27.1 %all-to-all-start.1 = ((bf16[16,16,800]{2,1,0:T(8,128)(2,1)}), bf16[16,16,800]{2,1,0:T(8,128)(2,1)S(1)}, u32[]{:S(2)}, u32[]{:S(2)}) async-start(bf16[16,16,800]{2,1,0:T(8,128)(2,1)} %get-tuple-element.27), calls=%async_computation.1 | async-start | bytes 917504 | tf_op jit(solution)/shard_map/all_to_all | solution.py:156
  194.5 43.3 %reduce-scatter.2.cloned.1.call-start = ((), (), s32[]{:S(2)}) async-start(), calls=%async_computation.6 | async-start | bytes 819200 | tf_op jit(solution)/shard_map/reduce_scatter | solution.py:166
  213.0 5.5 %copy-start.11 = (f32[400,400]{1,0:T(8,128)S(1)}, f32[400,400]{1,0:T(8,128)}, u32[]{:S(2)}) copy-start(f32[400,400]{1,0:T(8,128)} %get-tuple-element.13) | copy-start | bytes 1920004
  213.9 4.5 %copy-start.10 = (f32[400,800]{1,0:T(8,128)S(1)}, f32[400,800]{1,0:T(8,128)}, u32[]{:S(2)}) copy-start(f32[400,800]{1,0:T(8,128)} %copy.28) | copy-start | bytes 3840004
  222.3 1.5 copy-start.7
  222.3 1.5 copy-start.9
Sparse Core Ops, SparseCore 0:
  27.7 130.8 all-reduce.1
  214.1 23.7 reduce-scatter.1
where the time goes:
time: 248 us; the launch traced here: 247 us
  waiting for transfers between devices  113 us (46%)
  other arithmetic  58.7 us (24%)
  local copies, waits for them, and re-layouts  30.7 us (12%)
  starting transfers between devices  22.9 us (9%)
  between operations  15.8 us (6%)
  matrix products  6.11 us (2%)
    psum x1, waiting for transfers between devices, body(): power_all = lax.psum(power_sum, ('img', 'slab'))  94.8 us
    scatter-add x1, other arithmetic, body(): numerator.at[plane_index, row_index]  17 us
    reduce_scatter x1, waiting for transfers between devices, body(): lax.psum_scatter(numerator.astype(jnp.bfloat16), 'img', scatter_dimension...  12.5 us
    convert_element_type x2, other arithmetic, dft_tables(): jnp.sin(angles).astype(jnp.bfloat16)  7.32 us
    all_to_all x1, starting transfers between devices, body(): lax.all_to_all(send_info, 'slab', split_axis=0, concat_axis=0, tiled=True)  7.25 us
    neg x2, other arithmetic, forward_tables(): right_table = jnp.concatenate([cosine_table, -sine_table], axis=1)  6.42 us
    all_to_all x1, starting transfers between devices, body(): lax.all_to_all(send_contrast, 'slab', split_axis=0, concat_axis=0, tiled=...  6 us
    all_to_all x1, waiting for transfers between devices, body(): lax.all_to_all(send_blocks, 'slab', split_axis=0, concat_axis=0, tiled=True)  5.85 us
  transfers between devices with their start and end apart: 6, of which 3 were waited for; matrix products, arithmetic and copies ran while one was open for 26% of the time, Pallas kernels for 0%

commit v1 on v0

--- a/solution.py
+++ b/solution.py
@@ -8,6 +8,7 @@
 RB = 16
 LOW = 4
 WL = 8
+HI = lax.Precision.HIGHEST
 
 
 def dft_tables(box_size):
@@ -82,30 +83,46 @@
     return jnp.roll(values.reshape(split_shape), steps, axis=-1).reshape(values.shape)
 
 
+def low_row_ids(block_ids, box_size):
+    base = block_ids * RB + jnp.where(block_ids < LOW, 0, box_size - 2 * LOW * RB)
+    return base[..., None] + jnp.arange(RB, dtype=jnp.int32)
+
+
+def power_all(power_half, device_count, box_size):
+    rows = power_half.shape[0]
+    chunk = rows * box_size // device_count
+    pieces = power_half.reshape(device_count, chunk)
+    gathered = lax.all_to_all(pieces, ("img", "slab"), 0, 0, tiled=True)
+    total = jnp.sum(gathered, axis=0, keepdims=True)
+    spread = jnp.broadcast_to(total, (device_count, chunk))
+    back = lax.all_to_all(spread, ("img", "slab"), 0, 0, tiled=True)
+    half = back.reshape(rows, box_size)[: box_size // 2 + 1]
+    mirrored = jnp.roll(half[1 : box_size // 2][::-1, ::-1], 1, axis=1)
+    return jnp.concatenate([half, mirrored], axis=0)
+
+
+def half_rows(box_size, device_count):
+    rows = box_size // 2 + 1
+    while (rows * box_size) % device_count:
+        rows += 1
+    return rows
+
+
 def body(images, micrograph, defocus, target_slab, target_plane, target_rows, shift_index, volume):
     particles, box_size = (images.shape[0], images.shape[1])
     slab_count = lax.axis_size("slab")
-    device_count = lax.axis_size("img") * slab_count
+    img_count = lax.axis_size("img")
+    device_count = img_count * slab_count
     low_rows = LOW * RB
-    routed = particles * 2 * LOW
+    blocks_per = 2 * LOW
+    routed = particles * blocks_per
+    planes, vrows = volume.shape[0], volume.shape[1]
+    row_blocks = vrows // RB
+    slots = planes * row_blocks
     cosine_table, sine_table = dft_tables(box_size)
     right_table, left_table = forward_tables(cosine_table, sine_table)
     back_table, final_table = inverse_tables(cosine_table, sine_table)
-    spectrum = transform(images, right_table, left_table)
-    real_part = spectrum[..., :box_size]
-    imag_part = spectrum[..., box_size:]
-    power_sum = jnp.sum(real_part * real_part + imag_part * imag_part, axis=0)
-    power_all = lax.psum(power_sum, ("img", "slab"))
-    noise_level = jnp.sqrt(power_all / (particles * device_count) + 1e-06)
-    whitened = spectrum / jnp.concatenate([noise_level, noise_level], axis=1)
-    row_all = jnp.arange(box_size, dtype=jnp.int32)[None, :]
-    contrast = contrast_curve(lookup_defocus(micrograph, defocus), row_all, box_size)
-    contrast_both = jnp.concatenate([contrast, contrast], axis=-1).astype(jnp.float32)
-    weighted = (contrast_both * whitened).astype(jnp.bfloat16)
-    low_blocks = jnp.concatenate(
-        [weighted[:, :low_rows], weighted[:, box_size - low_rows :]], axis=1
-    )
-    low_blocks = low_blocks.reshape(routed, RB, 2 * box_size)
+
     destination = target_slab.reshape(routed)
     capacity = max(2, (2 * routed + slab_count - 1) // slab_count)
     member = (destination[:, None] == jnp.arange(slab_count, dtype=jnp.int32)[None, :]).astype(
@@ -115,62 +132,94 @@
     slot_rank = jnp.sum(member * before, axis=1)
     seat_index = destination * capacity + slot_rank
     seat_count = slab_count * capacity
-    live_flag = jnp.ones((routed,), jnp.int32)
-    source_block = jnp.tile(jnp.arange(2 * LOW, dtype=jnp.int32), particles)
+    seat_pick = (seat_index[:, None] == jnp.arange(seat_count, dtype=jnp.int32)[None, :]).astype(
+        jnp.bfloat16
+    )
+    source_block = jnp.tile(jnp.arange(blocks_per, dtype=jnp.int32), particles)
     block_info = jnp.stack(
         [
-            live_flag,
+            jnp.ones((routed,), jnp.int32),
             target_plane.reshape(routed),
             target_rows.reshape(routed),
             shift_index.reshape(routed),
             source_block,
-            jnp.repeat(micrograph, 2 * LOW),
+            jnp.repeat(micrograph, blocks_per),
         ],
         axis=1,
     )
-    send_blocks = (
-        jnp.zeros((seat_count, RB, 2 * box_size), jnp.bfloat16).at[seat_index].set(low_blocks)
-    )
-    send_info = jnp.zeros((seat_count, 6), jnp.int32).at[seat_index].set(block_info)
-    low_contrast = jnp.concatenate(
-        [contrast[:, :low_rows], contrast[:, box_size - low_rows :]], axis=1
-    )
-    low_contrast = low_contrast.reshape(routed, RB, box_size)
-    send_contrast = (
-        jnp.zeros((seat_count, RB, box_size), jnp.bfloat16).at[seat_index].set(low_contrast)
-    )
-    got_blocks, got_contrast, got_info = (
-        lax.all_to_all(send_blocks, "slab", split_axis=0, concat_axis=0, tiled=True),
-        lax.all_to_all(send_contrast, "slab", split_axis=0, concat_axis=0, tiled=True),
-        lax.all_to_all(send_info, "slab", split_axis=0, concat_axis=0, tiled=True),
-    )
-    live_mask = got_info[:, 0].astype(jnp.float32)[:, None, None]
-    row_index = got_info[:, 2][:, None] * RB + jnp.arange(RB, dtype=jnp.int32)
-    plane_index = jnp.broadcast_to(got_info[:, 1][:, None], row_index.shape)
+    send_info = jnp.einsum(
+        "rs,rc->sc", seat_pick.astype(jnp.int32), block_info, preferred_element_type=jnp.int32
+    )
+    got_info = lax.all_to_all(send_info, "slab", 0, 0, tiled=True)
+
+    live = got_info[:, 0].astype(jnp.float32)[:, None, None]
+    slot_of = got_info[:, 1] * row_blocks + got_info[:, 2]
+    slot_pick = (slot_of[:, None] == jnp.arange(slots, dtype=jnp.int32)[None, :]).astype(
+        jnp.bfloat16
+    )
     blend_weight = ((got_info[:, 3].astype(jnp.float32) + 0.5) / WL)[:, None, None]
-    nearby = volume[plane_index, row_index].astype(jnp.float32)
+    volume_slots = volume.reshape(slots, RB, 2 * box_size)
+    nearby = jnp.einsum(
+        "sq,qrx->srx", slot_pick, volume_slots, preferred_element_type=jnp.float32
+    )
     projected = (
-        ((1.0 - blend_weight) * nearby + blend_weight * shift_halves(nearby, -1, box_size))
-        * live_mask
-    ).astype(jnp.bfloat16)
-    returned_rows = lax.all_to_all(projected, "slab", split_axis=0, concat_axis=0, tiled=True)
-    received = got_blocks.astype(jnp.float32)
+        ((1.0 - blend_weight) * nearby + blend_weight * shift_halves(nearby, -1, box_size)) * live
+    ).astype(jnp.bfloat16)
+    returned_rows = lax.all_to_all(projected, "slab", 0, 0, tiled=True)
+
+    spectrum = transform(images, right_table, left_table)
+    low_spectrum = jnp.concatenate(
+        [spectrum[:, :low_rows], spectrum[:, box_size - low_rows :]], axis=1
+    ).astype(jnp.bfloat16)
+    low_spectrum = low_spectrum.reshape(routed, RB * 2 * box_size)
+    send_blocks = jnp.einsum(
+        "rs,rx->sx", seat_pick, low_spectrum, preferred_element_type=jnp.float32
+    ).astype(jnp.bfloat16)
+    got_blocks = lax.all_to_all(
+        send_blocks.reshape(seat_count, RB, 2 * box_size), "slab", 0, 0, tiled=True
+    )
+
+    rows_half = half_rows(box_size, device_count)
+    real_part = spectrum[:, :rows_half, :box_size]
+    imag_part = spectrum[:, :rows_half, box_size:]
+    power_half = jnp.sum(real_part * real_part + imag_part * imag_part, axis=0)
+    power = power_all(power_half, device_count, box_size)
+    noise_level = jnp.sqrt(power / (particles * device_count) + 1e-06)
+    level_both = jnp.concatenate([noise_level, noise_level], axis=1)
+
+    got_rows = low_row_ids(got_info[:, 4], box_size)
+    got_contrast = contrast_curve(lookup_defocus(got_info[:, 5], defocus), got_rows, box_size)
+    got_level = level_both[got_rows]
+    got_contrast_both = jnp.concatenate([got_contrast, got_contrast], axis=-1).astype(jnp.float32)
+    received = got_contrast_both * got_blocks.astype(jnp.float32) / got_level
     inserted = (1.0 - blend_weight) * received + blend_weight * shift_halves(received, 1, box_size)
     contrast_rows = got_contrast.astype(jnp.float32)
     squared = contrast_rows * contrast_rows
     weights = (1.0 - blend_weight) * squared + blend_weight * jnp.roll(squared, 1, axis=-1)
-    numerator = jnp.zeros((volume.shape[0], volume.shape[1], 3 * box_size), jnp.float32)
-    numerator = numerator.at[plane_index, row_index].add(
-        jnp.concatenate([inserted, weights], axis=-1) * live_mask
-    )
-    volume_part = lax.psum_scatter(
-        numerator.astype(jnp.bfloat16), "img", scatter_dimension=1, tiled=True
-    ).astype(jnp.float32)
+    seat_data = jnp.concatenate([inserted, weights], axis=-1) * live
+    numerator = jnp.einsum(
+        "sq,srx->qrx", slot_pick.astype(jnp.float32), seat_data, precision=HI,
+        preferred_element_type=jnp.float32,
+    )
+    share = vrows // img_count
+    numerator = numerator.reshape(planes, img_count, share, 3 * box_size).astype(jnp.bfloat16)
+    numerator = jnp.swapaxes(numerator, 0, 1)
+    parts = lax.all_to_all(numerator, "img", 0, 0, tiled=True)
+    volume_part = jnp.sum(parts.astype(jnp.float32), axis=0)
     weight_sum = volume_part[..., 2 * box_size :]
     reconstruction = volume_part[..., : 2 * box_size] / (
         jnp.concatenate([weight_sum, weight_sum], axis=-1) + 1.0
     )
-    own_rows = returned_rows[seat_index].reshape(particles, 2 * low_rows, 2 * box_size)
+
+    whitened = spectrum / level_both
+    row_all = jnp.arange(box_size, dtype=jnp.int32)[None, :]
+    contrast = contrast_curve(lookup_defocus(micrograph, defocus), row_all, box_size)
+    contrast_both = jnp.concatenate([contrast, contrast], axis=-1).astype(jnp.float32)
+    own_rows = jnp.einsum(
+        "rs,sx->rx", seat_pick, returned_rows.reshape(seat_count, RB * 2 * box_size),
+        preferred_element_type=jnp.float32,
+    ).astype(jnp.bfloat16)
+    own_rows = own_rows.reshape(particles, 2 * low_rows, 2 * box_size)
     middle = jnp.zeros((particles, box_size - 2 * low_rows, 2 * box_size), jnp.bfloat16)
     full_projection = jnp.concatenate(
         [own_rows[:, :low_rows], middle, own_rows[:, low_rows:]], axis=1

time: 248 us -> 149 us (0.60)
  waiting for transfers between devices: 113 us -> 28.6 us
  other arithmetic: 58.7 us -> 42.3 us
  between operations: 15.8 us -> 2.56 us
  starting transfers between devices: 22.9 us -> 30.4 us
  local copies, waits for them, and re-layouts: 30.7 us -> 35.2 us
  matrix products: 6.11 us -> 8.76 us
    psum x1 -> x0, waiting for transfers between devices: 94.8 us -> none  [body(): power_all = lax.psum(power_sum, ('img', 'slab'))]
    all_to_all x4 -> x6, waiting for transfers between devices: 5.86 us -> 28.6 us  [the longest x1 10.2 us: power_all(): back = lax.all_to_all(spread, ('img', 'slab'), 0, 0, tiled=True)]
    scatter-add x1 -> x0, other arithmetic: 17 us -> none  [body(): numerator.at[plane_index, row_index]]
    reduce_scatter x1 -> x0, waiting for transfers between devices: 12.5 us -> none  [body(): lax.psum_scatter(numerator.astype(jnp.bfloat16), 'img', scatter_dimension...]
    all_to_all x4 -> x6, starting transfers between devices: 22.8 us -> 30.4 us  [the longest x1 7.25 us: body(): got_info = lax.all_to_all(send_info, 'slab', 0, 0, tiled=True)]
    concatenate x5 -> x2, other arithmetic: 6.27 us -> 0.3 us  [the longest x1 0.28 us: body(): level_both = jnp.concatenate([noise_level, noise_level], axis=1)]
    convert_element_type x1 -> x2, other arithmetic: 3.01 us -> 8.88 us  [contrast_curve(): (-jnp.sin(defocus_of[:, None, None] * radius + 0.1)).astype(jnp.bfloat16)]
    scatter x3 -> x0, local copies, waits for them, and re-layouts: 5.43 us -> none  [the longest x1 2.19 us: body(): jnp.zeros((seat_count, RB, 2 * box_size), jnp.bfloat16).at[seat_index]]
  transfers between devices with their start and end apart: 6 -> 6, of which waited for: 3 -> 4; matrix products, arithmetic and copies ran while one was open for 26% -> 36% of each run, Pallas kernels for 0% -> 0%
where the time goes in v1:
time: 149 us; the launch traced here: 148 us
  other arithmetic  42.3 us (28%)
  local copies, waits for them, and re-layouts  35.2 us (24%)
  starting transfers between devices  30.4 us (20%)
  waiting for transfers between devices  28.6 us (19%)
  matrix products  8.76 us (6%)
  between operations  2.56 us (2%)
    all_to_all x1, waiting for transfers between devices, power_all(): back = lax.all_to_all(spread, ('img', 'slab'), 0, 0, tiled=True)  10.2 us
    convert_element_type x2, other arithmetic, contrast_curve(): (-jnp.sin(defocus_of[:, None, None] * radius + 0.1)).astype(jnp.bfloat16)  8.88 us
    all_to_all x1, waiting for transfers between devices, body(): parts = lax.all_to_all(numerator, 'img', 0, 0, tiled=True)  7.74 us
    all_to_all x1, starting transfers between devices, body(): got_info = lax.all_to_all(send_info, 'slab', 0, 0, tiled=True)  7.25 us
    all_to_all x1, waiting for transfers between devices, power_all(): gathered = lax.all_to_all(pieces, ('img', 'slab'), 0, 0, tiled=True)  7.04 us
    neg x2, other arithmetic, forward_tables(): right_table = jnp.concatenate([cosine_table, -sine_table], axis=1)  6.42 us
    unnamed x62, local copies, waits for them, and re-layouts  6.35 us
    reshape x2, local copies, waits for them, and re-layouts, shift_halves(): jnp.roll(values.reshape(split_shape), steps, axis=-1).reshape(values.shape)  6.3 us
  transfers between devices with their start and end apart: 6, of which 4 were waited for; matrix products, arithmetic and copies ran while one was open for 36% of the time, Pallas kernels for 0%

profile of v1, /device:TPU:0, one launch (start us, length us, event | category | flops | bytes accessed | tf_op | source)
XLA Modules:
  0.0 147.7 jit_solution(3072011065229474511)
XLA Ops:
  5.2 7.3 %all-to-all-start.2 = ((s32[8,2,6]{2,1,0:T(2,128)}), s32[8,2,6]{2,1,0:T(2,128)S(1)}, u32[]{:S(2)}, u32[]{:S(2)}) async-start(s32[8,2,6]{2,1,0:T(2,128)} %bitcast.19), calls=%async_computation.2 | async-start | bytes 16384 | tf_op jit(solution)/shard_map/all_to_all | solution.py:153
  12.5 3.4 %sine_convert_fusion = (bf16[1,400,400]{2,1,0:T(8,128)(2,1)S(1)}, bf16[1,400,400]{2,1,0:T(8,128)(2,1)S(1)}) fusion(), kind=kLoop, calls=%fused_computation.49 | loop fusion | flops 1760000 | bytes 640000 | tf_op jit(solution)/shard_map/convert_element_type | solution.py:18
  15.9 3.2 %fusion.53 = bf16[1,400,400]{2,1,0:T(8,128)(2,1)S(1)} fusion(), kind=kLoop, calls=%fused_computation.87 | loop fusion | flops 2080000 | bytes 320000 | tf_op jit(solution)/shard_map/neg | solution.py:22
  19.2 3.2 %cosine_convert_fusion.1 = bf16[400,400]{1,0:T(8,128)(2,1)S(1)} fusion(), kind=kLoop, calls=%fused_computation.55 | loop fusion | flops 1600000 | bytes 320000 | tf_op jit(solution)/shard_map/convert_element_type | solution.py:18
  22.3 3.2 %fusion.52 = bf16[400,400]{1,0:T(8,128)(2,1)S(1)} fusion(), kind=kLoop, calls=%fused_computation.86 | loop fusion | flops 2080000 | bytes 320000 | tf_op jit(solution)/shard_map/neg | solution.py:22
  33.6 1.4 all_to_all.36
  35.0 1.5 reshape.371
  36.8 6.2 %all-to-all-start = ((f32[32,1,2525]{2,1,0:T(1,128)}), f32[32,1,2525]{2,1,0:T(1,128)S(1)}, u32[]{:S(2)}, u32[]{:S(2)}) async-start(f32[32,1,2525]{2,1,0:T(1,128)} %all_to_all.36), calls=%async_computation | async-start | bytes 655360 | tf_op jit(solution)/shard_map/all_to_all | solution.py:95
  44.8 2.1 %slice.124 = f32[16,16,2,399]{3,2,0,1:T(2,128)} slice(f32[16,16,2,400]{3,2,0,1:T(2,128)S(1)} %reshape.366), slice={[0:16], [0:16], [0:2], [1:400]} | slice | bytes 1634304 | tf_op jit(solution)/shard_map/jit(_roll_static)/slice | solution.py:83
  47.9 7.0 %all-to-all-done = f32[32,1,2525]{2,1,0:T(1,128)S(1)} async-done(((f32[32,1,2525]{2,1,0:T(1,128)}), f32[32,1,2525]{2,1,0:T(1,128)S(1)}, u32[]{:S(2)}, u32[]{:S(2)}) %all-to-all-start) | async-done | bytes 323232 | tf_op jit(solution)/shard_map/all_to_all | solution.py:95
  56.1 3.4 %all-to-all-start.1 = ((f32[32,1,2525]{2,1,0:T(1,128)}), f32[32,1,2525]{2,1,0:T(1,128)}, u32[]{:S(2)}, u32[]{:S(2)}) async-start(f32[32,1,2525]{2,1,0:T(1,128)} %broadcast_in_dim.23), calls=%async_computation.1 | async-start | bytes 655360 | tf_op jit(solution)/shard_map/all_to_all | solution.py:98
  59.5 1.9 %negate_convert_fusion.1 = (bf16[16,16,400]{2,0,1:T(8,128)(2,1)S(1)}, f32[16,16,400]{2,0,1:T(8,128)S(1)}) fusion(f32[16]{0:T(128)S(1)} %get-tuple-element.29, s32[400]{0:T(512)S(1)} %fusion.70, s32[16,16]{0,1:T(8,128)S(1)} %fusion.54), kind=kLoop, calls=%fused_computation.75 | loop fusion | flops 819200 | bytes 617088 | tf_op jit(solution)/shard_map/convert_element_type | solution.py:73
  61.5 10.2 %all-to-all-done.1 = f32[32,1,2525]{2,1,0:T(1,128)} async-done(((f32[32,1,2525]{2,1,0:T(1,128)}), f32[32,1,2525]{2,1,0:T(1,128)}, u32[]{:S(2)}, u32[]{:S(2)}) %all-to-all-start.1) | async-done | bytes 323232 | tf_op jit(solution)/shard_map/all_to_all | solution.py:98
  71.6 4.1 %all-to-all-start.4 = ((bf16[16,16,800]{2,1,0:T(8,128)(2,1)}), bf16[16,16,800]{2,1,0:T(8,128)(2,1)}, u32[]{:S(2)}, u32[]{:S(2)}) async-start(bf16[16,16,800]{2,1,0:T(8,128)(2,1)} %reshape.371), calls=%async_computation.4 | async-start | bytes 917504 | tf_op jit(solution)/shard_map/all_to_all | solution.py:178
  75.8 1.8 %pad_maximum_fusion.1 = f32[16,16,2,400]{3,2,0,1:T(2,128)} fusion(f32[16,16,2,1]{3,2,0,1:T(2,128)S(1)} %slice-done, f32[16,16,2,399]{3,2,0,1:T(2,128)S(1)} %copy-done.4), kind=kLoop, calls=%fused_computation.31 | loop fusion | flops 204800 | bytes 1638400 | tf_op jit(solution)/shard_map/jit(_roll_static)/concatenate | solution.py:83
  77.6 3.1 %reshape.367 = f32[16,16,800]{2,0,1:T(8,128)} reshape(f32[16,16,2,400]{3,2,0,1:T(2,128)} %pad_maximum_fusion.1) | data formatting | bytes 1638400 | tf_op jit(solution)/shard_map/reshape | solution.py:83
  80.8 2.9 %fusion.46 = f32[16,16,400]{2,0,1:T(8,128)} fusion(f32[16,16,399]{2,0,1:T(8,128)S(1)} %bitcast.82, f32[16,16,1]{2,0,1:T(8,128)S(1)} %slice.135, f32[16]{0:T(128)S(1)} %get-tuple-element.13, f32[16]{0:T(128)S(1)} %get-tuple-element.30, f32[16]{0:T(128)S(1)} %get-tuple-element.29, s32[400]{0:T(512)S(1)} %fusion.70, s32[16,16]{0,1:T(8,128)S(1)} %fusion.54), kind=kLoop, calls=%fused_computation.73 | loop fusion | flops 1228800 | bytes 822016 | tf_op jit(solution)/shard_map/add | solution.py:198
  83.7 1.8 %reduce.3 = f32[32,2525]{1,0:T(8,128)S(1)} reduce(f32[32,1,2525]{2,1,0:T(1,128)} %all-to-all-done.1, f32[]{:T(128)} %constant.78), dimensions={1}, to_apply=%all_to_all.29.reduce_sub_computation | reduce | bytes 646404 | tf_op jit(solution)/shard_map/all_to_all | solution.py:98
  89.6 2.0 %gather_fusion = f32[256,800]{1,0:T(8,128)} fusion(f32[400,800]{1,0:T(8,128)S(1)} %pad_maximum_fusion, s32[1024]{0:T(1024)S(1)} %pad_clamp_fusion), kind=kCustom, calls=%fused_computation | custom fusion | bytes 1639424 | tf_op jit(solution)/shard_map/gather | solution.py:192
  91.6 1.7 %copy_divide_fusion = f32[16,16,800]{2,0,1:T(8,128)S(1)} fusion(f32[16,16,800]{2,1,0:T(8,128)} %bitcast.81, bf16[16,16,400]{2,0,1:T(8,128)(2,1)S(1)} %get-tuple-element.21, bf16[16,16,800]{2,1,0:T(8,128)(2,1)} %all-to-all-done.4), kind=kLoop, calls=%fused_computation.35 | loop fusion | flops 1433600 | bytes 2252800 | tf_op jit(solution)/shard_map/div | solution.py:194
  93.3 2.2 %reshape.372 = f32[16,16,2,400]{3,2,0,1:T(2,128)} reshape(f32[16,16,800]{2,0,1:T(8,128)S(1)} %copy_divide_fusion) | data formatting | bytes 1638400 | tf_op jit(solution)/shard_map/reshape | solution.py:83
  96.8 3.4 %pad_maximum_fusion.2 = f32[16,16,2,400]{3,2,0,1:T(2,128)} fusion(f32[16,16,2,399]{3,2,0,1:T(2,128)} %bitcast.79, f32[16,16,2,1]{3,2,0,1:T(2,128)S(1)} %slice.133), kind=kLoop, calls=%fused_computation.32 | loop fusion | flops 204800 | bytes 1638400 | tf_op jit(solution)/shard_map/jit(_roll_static)/concatenate | solution.py:83
  100.2 3.2 %reshape.373 = f32[16,16,800]{2,0,1:T(8,128)} reshape(f32[16,16,2,400]{3,2,0,1:T(2,128)} %pad_maximum_fusion.2) | data formatting | bytes 1638400 | tf_op jit(solution)/shard_map/reshape | solution.py:83
  103.4 1.9 %multiply_add_fusion = (f32[16,16,800]{2,0,1:T(8,128)S(1)}, bf16[16,16,800]{2,0,1:T(8,128)(2,1)S(1)}) fusion(f32[16,16,800]{2,0,1:T(8,128)} %reshape.373, f32[16,16,800]{2,0,1:T(8,128)S(1)} %copy_divide_fusion, f32[16]{0:T(128)S(1)} %copy-done.19, f32[16]{0:T(128)S(1)} %copy-done.21, f32[16]{0:T(128)S(1)} %copy-done.24, f32[16,16,800]{2,0,1:T(8,128)} %reshape.367, ...), kind=kLoop, calls=%fused_computation.36 | loop fusion | flops 1638400 | bytes 4505792 | tf_op jit(solution)/shard_map/add | solution.py:195
  107.2 3.5 %all-to-all-start.5 = ((bf16[4,2,32,1200]{3,2,1,0:T(8,128)(2,1)}), bf16[4,2,32,1200]{3,2,1,0:T(8,128)(2,1)S(1)}, u32[]{:S(2)}, u32[]{:S(2)}) async-start(bf16[4,2,32,1200]{3,2,1,0:T(8,128)(2,1)} %copy.63), calls=%async_computation.5 | async-start | bytes 1310720 | tf_op jit(solution)/shard_map/all_to_all | solution.py:207
  110.7 1.6 %copy.52 = f32[400,800]{1,0:T(8,128)} copy(f32[400,800]{0,1:T(8,128)S(1)} %bitcast.78) | data formatting | bytes 2560000 | tf_op jit(solution)/shard_map/reshape | solution.py:46
  113.2 7.7 %all-to-all-done.5 = bf16[4,2,32,1200]{3,2,1,0:T(8,128)(2,1)S(1)} async-done(((bf16[4,2,32,1200]{3,2,1,0:T(8,128)(2,1)}), bf16[4,2,32,1200]{3,2,1,0:T(8,128)(2,1)S(1)}, u32[]{:S(2)}, u32[]{:S(2)}) %all-to-all-start.5) | async-done | bytes 614432 | tf_op jit(solution)/shard_map/all_to_all | solution.py:207
  120.9 5.9 %all-to-all-start.3 = ((bf16[16,16,800]{2,1,0:T(8,128)(2,1)}), bf16[16,16,800]{2,1,0:T(8,128)(2,1)S(1)}, u32[]{:S(2)}, u32[]{:S(2)}) async-start(bf16[16,16,800]{2,1,0:T(8,128)(2,1)} %copy.57), calls=%async_computation.3 | async-start | bytes 917504 | tf_op jit(solution)/shard_map/all_to_all | solution.py:168
  128.2 7.0 %negate_convert_fusion = (bf16[400,400]{1,0:T(8,128)(2,1)}, bf16[400,400]{1,0:T(8,128)(2,1)}) fusion(f32[]{:T(128)S(6)} %mul.297, s32[400]{0:T(512)S(1)} %fusion.70), kind=kLoop, calls=%fused_computation.48 | loop fusion | flops 2560000 | bytes 641604 | tf_op jit(solution)/shard_map/convert_element_type | solution.py:73
  136.2 3.6 %all-to-all-done.3 = bf16[16,16,800]{2,1,0:T(8,128)(2,1)S(1)} async-done(((bf16[16,16,800]{2,1,0:T(8,128)(2,1)}), bf16[16,16,800]{2,1,0:T(8,128)(2,1)S(1)}, u32[]{:S(2)}, u32[]{:S(2)}) %all-to-all-start.3) | async-done | bytes 409632 | tf_op jit(solution)/shard_map/all_to_all | solution.py:168
  140.9 3.8 %fusion.12 = bf16[400,800]{1,0:T(8,128)(2,1)} fusion(bf16[400,400]{1,0:T(8,128)(2,1)} %copy-done.15, bf16[400,400]{1,0:T(8,128)(2,1)} %copy-done.16, bf16[400,400]{1,0:T(8,128)(2,1)} %get-tuple-element.28, f32[400,800]{1,0:T(8,128)S(1)} %copy-done.13, bf16[400,400]{1,0:T(8,128)(2,1)} %get-tuple-element.27, bf16[64,800]{1,0:T(8,128)(2,1)S(1)} %get-tuple-element.20, ...), kind=kOutput, calls=%fused_computation.18 | convolution fusion | flops 522240000 | bytes 4045600 | tf_op jit(solution)/shard_map/nyj,jk->nyk/dot_general | solution.py:51
  144.7 1.5 copy.70
  (122 shorter events, 28.6 us)
Async XLA Ops:
  0.6 25.7 %copy-start = (bf16[1,400,400]{2,1,0:T(8,128)(2,1)S(1)}, bf16[1,400,400]{2,1,0:T(8,128)(2,1)}, u32[]{:S(2)}) copy-start(bf16[1,400,400]{2,1,0:T(8,128)(2,1)} %param.8) | copy-start | bytes 960004
  2.9 30.0 %copy-start.25 = (s32[8]{0:T(128)}, s32[8]{0:T(128)S(1)}, u32[]{:S(2)}) copy-start(s32[8]{0:T(128)S(1)} %multiply_add_fusion.1) | copy-start | bytes 100
  5.2 31.5 %all-to-all-start.2 = ((s32[8,2,6]{2,1,0:T(2,128)}), s32[8,2,6]{2,1,0:T(2,128)S(1)}, u32[]{:S(2)}, u32[]{:S(2)}) async-start(s32[8,2,6]{2,1,0:T(2,128)} %bitcast.19), calls=%async_computation.2 | async-start | bytes 16384 | tf_op jit(solution)/shard_map/all_to_all | solution.py:153
  15.9 12.3 %copy-start.9 = (bf16[1,400,400]{2,1,0:T(8,128)(2,1)}, bf16[1,400,400]{2,1,0:T(8,128)(2,1)S(1)}, u32[]{:S(2)}) copy-start(bf16[1,400,400]{2,1,0:T(8,128)(2,1)S(1)} %get-tuple-element.26) | copy-start | bytes 960004
  19.2 9.1 %copy-start.11 = (bf16[1,400,400]{2,1,0:T(8,128)(2,1)}, bf16[1,400,400]{2,1,0:T(8,128)(2,1)S(1)}, u32[]{:S(2)}) copy-start(bf16[1,400,400]{2,1,0:T(8,128)(2,1)S(1)} %fusion.53) | copy-start | bytes 960004
  22.3 3.2 %copy-start.15 = (bf16[400,400]{1,0:T(8,128)(2,1)}, bf16[400,400]{1,0:T(8,128)(2,1)S(1)}, u32[]{:S(2)}) copy-start(bf16[400,400]{1,0:T(8,128)(2,1)S(1)} %cosine_convert_fusion.1) | copy-start | bytes 960004
  30.4 1.2 copy-start.1
  32.7 3.8 %copy-start.17 = (bf16[2,128,800]{1,2,0:T(8,128)(2,1)S(1)}, bf16[2,128,800]{1,2,0:T(8,128)(2,1)}, u32[]{:S(2)}) copy-start(bf16[2,128,800]{1,2,0:T(8,128)(2,1)} %param.15) | copy-start | bytes 1228804
  36.8 18.2 %all-to-all-start = ((f32[32,1,2525]{2,1,0:T(1,128)}), f32[32,1,2525]{2,1,0:T(1,128)S(1)}, u32[]{:S(2)}, u32[]{:S(2)}) async-start(f32[32,1,2525]{2,1,0:T(1,128)} %all_to_all.36), calls=%async_computation | async-start | bytes 655360 | tf_op jit(solution)/shard_map/all_to_all | solution.py:95
  43.2 1.6 %copy-start.22 = (s32[16]{0:T(128)}, s32[16]{0:T(128)S(1)}, u32[]{:S(2)}) copy-start(s32[16]{0:T(128)S(1)} %get-tuple-element.11) | copy-start | bytes 196
  44.8 10.4 %copy-start.3 = (f32[16,16,2,400]{3,2,0,1:T(2,128)}, f32[16,16,2,400]{3,2,0,1:T(2,128)S(1)}, u32[]{:S(2)}) copy-start(f32[16,16,2,400]{3,2,0,1:T(2,128)S(1)} %reshape.366) | copy-start | bytes 2457604
  44.8 2.9 %copy-start.27 = (f32[64]{0:T(128)S(1)}, f32[64]{0:T(128)}, u32[]{:S(2)}) copy-start(f32[64]{0:T(128)} %param.10) | copy-start | bytes 772
  47.7 33.1 %copy-start.18 = (f32[16]{0:T(128)}, f32[16]{0:T(128)S(1)}, u32[]{:S(2)}) copy-start(f32[16]{0:T(128)S(1)} %get-tuple-element.13) | copy-start | bytes 196
  56.1 19.7 %slice-start = ((f32[16,16,2,400]{3,2,0,1:T(2,128)}), f32[16,16,2,1]{3,2,0,1:T(2,128)S(1)}, s32[]{:S(2)}) async-start(f32[16,16,2,400]{3,2,0,1:T(2,128)} %copy-done.3), calls=%async_computation.6 | async-start | bytes 524288 | tf_op jit(solution)/shard_map/jit(_roll_static)/slice | solution.py:83
  56.1 19.7 %copy-start.4 = (f32[16,16,2,399]{3,2,0,1:T(2,128)S(1)}, f32[16,16,2,399]{3,2,0,1:T(2,128)}, u32[]{:S(2)}) copy-start(f32[16,16,2,399]{3,2,0,1:T(2,128)} %slice.124) | copy-start | bytes 2451460
  56.1 15.6 %all-to-all-start.1 = ((f32[32,1,2525]{2,1,0:T(1,128)}), f32[32,1,2525]{2,1,0:T(1,128)}, u32[]{:S(2)}, u32[]{:S(2)}) async-start(f32[32,1,2525]{2,1,0:T(1,128)} %broadcast_in_dim.23), calls=%async_computation.1 | async-start | bytes 655360 | tf_op jit(solution)/shard_map/all_to_all | solution.py:98
  59.5 21.3 %copy-start.20 = (f32[16]{0:T(128)}, f32[16]{0:T(128)S(1)}, u32[]{:S(2)}) copy-start(f32[16]{0:T(128)S(1)} %get-tuple-element.30) | copy-start | bytes 196
  71.6 19.9 %all-to-all-start.4 = ((bf16[16,16,800]{2,1,0:T(8,128)(2,1)}), bf16[16,16,800]{2,1,0:T(8,128)(2,1)}, u32[]{:S(2)}, u32[]{:S(2)}) async-start(bf16[16,16,800]{2,1,0:T(8,128)(2,1)} %reshape.371), calls=%async_computation.4 | async-start | bytes 917504 | tf_op jit(solution)/shard_map/all_to_all | solution.py:178
  100.2 3.2 %copy-start.19 = (f32[16]{0:T(128)S(1)}, f32[16]{0:T(128)}, u32[]{:S(2)}) copy-start(f32[16]{0:T(128)} %copy-done.18) | copy-start | bytes 196
  100.2 3.2 %copy-start.21 = (f32[16]{0:T(128)S(1)}, f32[16]{0:T(128)}, u32[]{:S(2)}) copy-start(f32[16]{0:T(128)} %copy-done.20) | copy-start | bytes 196
  100.2 3.2 %copy-start.24 = (f32[16]{0:T(128)S(1)}, f32[16]{0:T(128)}, u32[]{:S(2)}) copy-start(f32[16]{0:T(128)} %get-tuple-element.14) | copy-start | bytes 196
  103.3 1.9 %copy-start.7 = (f32[16,16,400]{2,0,1:T(8,128)S(1)}, f32[16,16,400]{2,0,1:T(8,128)}, u32[]{:S(2)}) copy-start(f32[16,16,400]{2,0,1:T(8,128)} %fusion.46) | copy-start | bytes 1228804
  103.4 1.9 %copy-start.23 = (s32[16]{0:T(128)S(1)}, s32[16]{0:T(128)}, u32[]{:S(2)}) copy-start(s32[16]{0:T(128)} %copy-done.22) | copy-start | bytes 196
  106.3 4.4 %copy-start.2 = (f32[400,2,400,1]{2,0,3,1:T(8,128)S(1)}, f32[400,2,400,1]{2,0,3,1:T(8,128)}, u32[]{:S(2)}) copy-start(f32[400,2,400,1]{2,0,3,1:T(8,128)} %copy-done.1) | copy-start | bytes 3840004
  107.2 13.7 %all-to-all-start.5 = ((bf16[4,2,32,1200]{3,2,1,0:T(8,128)(2,1)}), bf16[4,2,32,1200]{3,2,1,0:T(8,128)(2,1)S(1)}, u32[]{:S(2)}, u32[]{:S(2)}) async-start(bf16[4,2,32,1200]{3,2,1,0:T(8,128)(2,1)} %copy.63), calls=%async_computation.5 | async-start | bytes 1310720 | tf_op jit(solution)/shard_map/all_to_all | solution.py:207
  112.3 14.5 %copy-start.28 = (f32[64]{0:T(128)S(1)}, f32[64]{0:T(128)}, u32[]{:S(2)}) copy-start(f32[64]{0:T(128)} %param.10) | copy-start | bytes 772
  120.9 18.8 %all-to-all-start.3 = ((bf16[16,16,800]{2,1,0:T(8,128)(2,1)}), bf16[16,16,800]{2,1,0:T(8,128)(2,1)S(1)}, u32[]{:S(2)}, u32[]{:S(2)}) async-start(bf16[16,16,800]{2,1,0:T(8,128)(2,1)} %copy.57), calls=%async_computation.3 | async-start | bytes 917504 | tf_op jit(solution)/shard_map/all_to_all | solution.py:168
  135.1 5.1 %copy-start.26 = (s32[8]{0:T(128)S(1)}, s32[8]{0:T(128)}, u32[]{:S(2)}) copy-start(s32[8]{0:T(128)} %copy-done.25) | copy-start | bytes 100
  135.3 5.5 %copy-start.6 = (f32[400,400]{1,0:T(8,128)S(1)}, f32[400,400]{1,0:T(8,128)}, u32[]{:S(2)}) copy-start(f32[400,400]{1,0:T(8,128)} %copy-done.5) | copy-start | bytes 1920004
  135.4 5.5 %copy-start.13 = (f32[400,800]{1,0:T(8,128)S(1)}, f32[400,800]{1,0:T(8,128)}, u32[]{:S(2)}) copy-start(f32[400,800]{1,0:T(8,128)} %copy.52) | copy-start | bytes 3840004
  144.7 1.5 copy-start.10
  144.7 1.5 %copy-start.12 = (bf16[1,400,400]{2,1,0:T(8,128)(2,1)S(1)}, bf16[1,400,400]{2,1,0:T(8,128)(2,1)}, u32[]{:S(2)}) copy-start(bf16[1,400,400]{2,1,0:T(8,128)(2,1)} %copy-done.11) | copy-start | bytes 960004
  (4 other events, 3.9 us)

commit v2 on v1

--- a/solution.py
+++ b/solution.py
@@ -1,6 +1,8 @@
 import math
 
 import jax
+import ml_dtypes
+import numpy as np
 import jax.numpy as jnp
 from jax import lax
 from jax.sharding import PartitionSpec as P
@@ -11,52 +13,32 @@
 HI = lax.Precision.HIGHEST
 
 
-def dft_tables(box_size):
-    positions = jnp.arange(box_size, dtype=jnp.int32)
-    phase_steps = positions[:, None] * positions[None, :] % box_size
-    angles = phase_steps.astype(jnp.float32) * (2.0 * math.pi / box_size)
-    return (jnp.cos(angles).astype(jnp.bfloat16), jnp.sin(angles).astype(jnp.bfloat16))
-
-
-def forward_tables(cosine_table, sine_table):
-    right_table = jnp.concatenate([cosine_table, -sine_table], axis=1)
-    left_table = jnp.stack(
-        [jnp.stack([cosine_table, sine_table]), jnp.stack([-sine_table, cosine_table])]
-    )
-    return (right_table, left_table)
-
-
-def inverse_tables(cosine_table, sine_table):
-    upper_half = jnp.concatenate([cosine_table, sine_table], axis=1)
-    lower_half = jnp.concatenate([-sine_table, cosine_table], axis=1)
-    back_table = jnp.concatenate([upper_half, lower_half], axis=0)
-    final_table = jnp.stack([cosine_table, -sine_table])
-    return (back_table, final_table)
-
-
-def transform(image_block, right_table, left_table):
-    batch_size, box_size = (image_block.shape[0], image_block.shape[1])
+def table_stack(box_size):
+    positions = np.arange(box_size)
+    angles = ((positions[:, None] * positions[None, :]) % box_size) * (2.0 * np.pi / box_size)
+    both = np.stack([np.cos(angles), np.sin(angles)]).astype(ml_dtypes.bfloat16)
+    return jnp.asarray(both)
+
+
+def transform(image, tables):
     rowwise = jnp.einsum(
-        "nyx,xm->nym", image_block, right_table, preferred_element_type=jnp.float32
-    ).astype(jnp.bfloat16)
-    quarters = rowwise.reshape(batch_size, box_size, 2, box_size)
-    spectrum = jnp.einsum(
-        "ahky,nyhm->nkam", left_table, quarters, preferred_element_type=jnp.float32
-    )
-    return spectrum.reshape(batch_size, box_size, 2 * box_size)
-
-
-def invert(difference, back_table, final_table):
-    batch_size, box_size = (difference.shape[0], difference.shape[1])
-    rowwise = jnp.einsum(
-        "nyj,jk->nyk", difference, back_table, preferred_element_type=jnp.float32
-    ).astype(jnp.bfloat16)
-    quarters = rowwise.reshape(batch_size, box_size, 2, box_size)
-    picture = (
-        jnp.einsum("cxk,nkcm->nxm", final_table, quarters, preferred_element_type=jnp.float32)
-        / box_size
-    )
-    return picture.astype(jnp.bfloat16)
+        "yx,hmx->hym", image, tables, preferred_element_type=jnp.float32
+    ).astype(jnp.bfloat16)
+    products = jnp.einsum("gky,hym->ghkm", tables, rowwise, preferred_element_type=jnp.float32)
+    real = products[0, 0] - products[1, 1]
+    imag = -(products[0, 1] + products[1, 0])
+    return jnp.stack([real, imag])
+
+
+def invert(difference, tables, box_size):
+    products = jnp.einsum(
+        "hyj,gmj->hgym", difference, tables, preferred_element_type=jnp.float32
+    )
+    back_real = products[0, 0] - products[1, 1]
+    back_imag = products[0, 1] + products[1, 0]
+    back_rows = jnp.stack([back_real, -back_imag]).astype(jnp.bfloat16)
+    picture = jnp.einsum("hxk,hkm->hxm", tables, back_rows, preferred_element_type=jnp.float32)
+    return ((picture[0] + picture[1]) / box_size).astype(jnp.bfloat16)
 
 
 def radius_sq(row_ids, box_size):
@@ -119,9 +101,7 @@
     planes, vrows = volume.shape[0], volume.shape[1]
     row_blocks = vrows // RB
     slots = planes * row_blocks
-    cosine_table, sine_table = dft_tables(box_size)
-    right_table, left_table = forward_tables(cosine_table, sine_table)
-    back_table, final_table = inverse_tables(cosine_table, sine_table)
+    tables = lax.optimization_barrier(table_stack(box_size))
 
     destination = target_slab.reshape(routed)
     capacity = max(2, (2 * routed + slab_count - 1) // slab_count)
@@ -146,11 +126,22 @@
             jnp.repeat(micrograph, blocks_per),
         ],
         axis=1,
-    )
-    send_info = jnp.einsum(
-        "rs,rc->sc", seat_pick.astype(jnp.int32), block_info, preferred_element_type=jnp.int32
-    )
-    got_info = lax.all_to_all(send_info, "slab", 0, 0, tiled=True)
+    ).astype(jnp.bfloat16)
+    info_width = 128
+    block_info = jnp.pad(block_info, ((0, 0), (0, info_width - block_info.shape[1])))
+
+    spectrum = jnp.stack([transform(images[n], tables) for n in range(particles)])
+    low_spectrum = jnp.concatenate(
+        [spectrum[:, :, :low_rows], spectrum[:, :, box_size - low_rows :]], axis=2
+    ).astype(jnp.bfloat16)
+    low_spectrum = jnp.moveaxis(low_spectrum, 1, 2).reshape(routed, RB * 2 * box_size)
+    payload = jnp.concatenate([low_spectrum, block_info], axis=1)
+    send = jnp.einsum(
+        "rs,rx->sx", seat_pick, payload, preferred_element_type=jnp.float32
+    ).astype(jnp.bfloat16)
+    got = lax.all_to_all(send, "slab", 0, 0, tiled=True)
+    got_blocks = got[:, : RB * 2 * box_size].reshape(seat_count, RB, 2 * box_size)
+    got_info = got[:, RB * 2 * box_size : RB * 2 * box_size + 6].astype(jnp.int32)
 
     live = got_info[:, 0].astype(jnp.float32)[:, None, None]
     slot_of = got_info[:, 1] * row_blocks + got_info[:, 2]
@@ -167,22 +158,9 @@
     ).astype(jnp.bfloat16)
     returned_rows = lax.all_to_all(projected, "slab", 0, 0, tiled=True)
 
-    spectrum = transform(images, right_table, left_table)
-    low_spectrum = jnp.concatenate(
-        [spectrum[:, :low_rows], spectrum[:, box_size - low_rows :]], axis=1
-    ).astype(jnp.bfloat16)
-    low_spectrum = low_spectrum.reshape(routed, RB * 2 * box_size)
-    send_blocks = jnp.einsum(
-        "rs,rx->sx", seat_pick, low_spectrum, preferred_element_type=jnp.float32
-    ).astype(jnp.bfloat16)
-    got_blocks = lax.all_to_all(
-        send_blocks.reshape(seat_count, RB, 2 * box_size), "slab", 0, 0, tiled=True
-    )
-
     rows_half = half_rows(box_size, device_count)
-    real_part = spectrum[:, :rows_half, :box_size]
-    imag_part = spectrum[:, :rows_half, box_size:]
-    power_half = jnp.sum(real_part * real_part + imag_part * imag_part, axis=0)
+    low_half = spectrum[:, :, :rows_half]
+    power_half = jnp.sum(low_half * low_half, axis=(0, 1))
     power = power_all(power_half, device_count, box_size)
     noise_level = jnp.sqrt(power / (particles * device_count) + 1e-06)
     level_both = jnp.concatenate([noise_level, noise_level], axis=1)
@@ -211,23 +189,23 @@
         jnp.concatenate([weight_sum, weight_sum], axis=-1) + 1.0
     )
 
-    whitened = spectrum / level_both
+    whitened = spectrum / noise_level
     row_all = jnp.arange(box_size, dtype=jnp.int32)[None, :]
     contrast = contrast_curve(lookup_defocus(micrograph, defocus), row_all, box_size)
-    contrast_both = jnp.concatenate([contrast, contrast], axis=-1).astype(jnp.float32)
     own_rows = jnp.einsum(
         "rs,sx->rx", seat_pick, returned_rows.reshape(seat_count, RB * 2 * box_size),
         preferred_element_type=jnp.float32,
     ).astype(jnp.bfloat16)
-    own_rows = own_rows.reshape(particles, 2 * low_rows, 2 * box_size)
-    middle = jnp.zeros((particles, box_size - 2 * low_rows, 2 * box_size), jnp.bfloat16)
+    own_rows = own_rows.reshape(particles, 2 * low_rows, 2, box_size)
+    own_rows = jnp.moveaxis(own_rows, 2, 1)
+    middle = jnp.zeros((particles, 2, box_size - 2 * low_rows, box_size), jnp.bfloat16)
     full_projection = jnp.concatenate(
-        [own_rows[:, :low_rows], middle, own_rows[:, low_rows:]], axis=1
-    )
-    difference = (whitened - contrast_both * full_projection.astype(jnp.float32)).astype(
-        jnp.bfloat16
-    )
-    residual = invert(difference, back_table, final_table)
+        [own_rows[:, :, :low_rows], middle, own_rows[:, :, low_rows:]], axis=2
+    )
+    difference = (
+        whitened - contrast.astype(jnp.float32)[:, None] * full_projection.astype(jnp.float32)
+    ).astype(jnp.bfloat16)
+    residual = jnp.stack([invert(difference[n], tables, box_size) for n in range(particles)])
     return (residual, reconstruction)
 
 

time: 149 us -> 132 us (0.89)
  other arithmetic: 42.3 us -> 28 us
  waiting for transfers between devices: 28.6 us -> 35.7 us
  starting transfers between devices: 30.4 us -> 23.8 us
  local copies, waits for them, and re-layouts: 35.2 us -> 30.3 us
  matrix products: 8.76 us -> 10.5 us
    all_to_all x2 -> x1, waiting for transfers between devices: 0.01 us -> 11.4 us  [body(): got = lax.all_to_all(send, 'slab', 0, 0, tiled=True)]
    all_to_all x1, waiting for transfers between devices: 10.2 us -> 0.01 us  [power_all(): back = lax.all_to_all(spread, ('img', 'slab'), 0, 0, tiled=True)]
    all_to_all x2 -> x1, starting transfers between devices: 11.4 us -> 3.46 us  [body(): got = lax.all_to_all(send, 'slab', 0, 0, tiled=True)]
    neg x2 -> x1, other arithmetic: 6.42 us -> 1.55 us  [transform(): imag = -(products[0, 1] + products[1, 0])]
    convert_element_type x1 -> x2, local copies, waits for them, and re-layouts: 0.24 us -> 3.92 us  [body(): received = got_contrast_both * got_blocks.astype(jnp.float32) / got_level]
    convert_element_type x2, other arithmetic: 8.88 us -> 5.35 us  [contrast_curve(): (-jnp.sin(defocus_of[:, None, None] * radius + 0.1)).astype(jnp.bfloat16)]
    all_to_all x1, waiting for transfers between devices: 3.61 us -> 6.9 us  [body(): returned_rows = lax.all_to_all(projected, 'slab', 0, 0, tiled=True)]
    reshape x4 -> x3, local copies, waits for them, and re-layouts: 3.94 us -> 0.95 us  [the longest x2 0.61 us: body(): own_rows = own_rows.reshape(particles, 2 * low_rows, 2, box_size)]
  transfers between devices with their start and end apart: 6 -> 5, of which waited for: 4 -> 4; matrix products, arithmetic and copies ran while one was open for 36% -> 23% of each run, Pallas kernels for 0% -> 0%
where the time goes in v2:
time: 132 us; the launch traced here: 131 us
  waiting for transfers between devices  35.7 us (27%)
  local copies, waits for them, and re-layouts  30.3 us (23%)
  other arithmetic  28 us (21%)
  starting transfers between devices  23.8 us (18%)
  matrix products  10.5 us (8%)
  between operations  2.57 us (2%)
    all_to_all x1, waiting for transfers between devices, body(): got = lax.all_to_all(send, 'slab', 0, 0, tiled=True)  11.4 us
    all_to_all x1, waiting for transfers between devices, body(): parts = lax.all_to_all(numerator, 'img', 0, 0, tiled=True)  9.35 us
    all_to_all x1, waiting for transfers between devices, power_all(): gathered = lax.all_to_all(pieces, ('img', 'slab'), 0, 0, tiled=True)  8.1 us
    all_to_all x1, starting transfers between devices, power_all(): gathered = lax.all_to_all(pieces, ('img', 'slab'), 0, 0, tiled=True)  7.3 us
    all_to_all x1, waiting for transfers between devices, body(): returned_rows = lax.all_to_all(projected, 'slab', 0, 0, tiled=True)  6.9 us
    all_to_all x1, starting transfers between devices, body(): returned_rows = lax.all_to_all(projected, 'slab', 0, 0, tiled=True)  5.64 us
    convert_element_type x2, other arithmetic, contrast_curve(): (-jnp.sin(defocus_of[:, None, None] * radius + 0.1)).astype(jnp.bfloat16)  5.35 us
    unnamed x61, local copies, waits for them, and re-layouts  5.3 us
  transfers between devices with their start and end apart: 5, of which 4 were waited for; matrix products, arithmetic and copies ran while one was open for 23% of the time, Pallas kernels for 0%

profile of v2, /device:TPU:0, one launch (start us, length us, event | category | flops | bytes accessed | tf_op | source)
XLA Modules:
  0.0 130.9 jit_solution(12396805244956057730)
XLA Ops:
  1.6 4.7 %convolution_bitcast_fusion.1 = f32[2,2,400,400]{3,2,0,1:T(8,128)} fusion(bf16[2,400,400]{2,1,0:T(8,128)(2,1)} %constant.63.clone, bf16[1,400,400]{2,1,0:T(8,128)(2,1)S(1)} %copy-done), kind=kOutput, calls=%fused_computation.5 | convolution fusion | flops 768320000 | bytes 3520000 | tf_op jit(solution)/shard_map/gky,hym->ghkm/dot_general | solution.py:27
  6.3 1.6 %fusion.13 = f32[1,400,400]{2,1,0:T(8,128)S(1)} fusion(f32[2,2,400,400]{3,2,0,1:T(8,128)} %convolution_bitcast_fusion.1), kind=kLoop, calls=%fused_computation.37 | loop fusion | flops 320000 | bytes 1920000 | tf_op jit(solution)/shard_map/neg | solution.py:29
  7.9 1.8 %fusion.15 = f32[1,400,400]{2,1,0:T(8,128)S(1)} fusion(f32[2,2,400,400]{3,2,0,1:T(8,128)} %convolution_bitcast_fusion.1), kind=kLoop, calls=%fused_computation.40 | loop fusion | flops 160000 | bytes 1920000 | tf_op jit(solution)/shard_map/sub | solution.py:28
  10.0 1.4 %all_to_all.32 = f32[32,1,2525]{2,1,0:T(1,128)} reshape(f32[202,400]{1,0:T(8,128)S(1)} %fusion.6) | data formatting | bytes 646400 | tf_op jit(solution)/shard_map/all_to_all | solution.py:77
  11.3 7.3 %all-to-all-start = ((f32[32,1,2525]{2,1,0:T(1,128)}), f32[32,1,2525]{2,1,0:T(1,128)S(1)}, u32[]{:S(2)}, u32[]{:S(2)}) async-start(f32[32,1,2525]{2,1,0:T(1,128)} %all_to_all.32), calls=%async_computation | async-start | bytes 655360 | tf_op jit(solution)/shard_map/all_to_all | solution.py:77
  22.7 8.1 %all-to-all-done = f32[32,1,2525]{2,1,0:T(1,128)S(1)} async-done(((f32[32,1,2525]{2,1,0:T(1,128)}), f32[32,1,2525]{2,1,0:T(1,128)S(1)}, u32[]{:S(2)}, u32[]{:S(2)}) %all-to-all-start) | async-done | bytes 323232 | tf_op jit(solution)/shard_map/all_to_all | solution.py:77
  30.8 3.5 %all-to-all-start.2 = ((bf16[8,2,12928]{2,1,0:T(2,128)(2,1)}), bf16[8,2,12928]{2,1,0:T(2,128)(2,1)S(1)}, u32[]{:S(2)}, u32[]{:S(2)}) async-start(bf16[8,2,12928]{2,1,0:T(2,128)(2,1)} %all_to_all.27), calls=%async_computation.2 | async-start | bytes 827392 | tf_op jit(solution)/shard_map/all_to_all | solution.py:142
  34.7 11.4 %all-to-all-done.2 = bf16[8,2,12928]{2,1,0:T(2,128)(2,1)S(1)} async-done(((bf16[8,2,12928]{2,1,0:T(2,128)(2,1)}), bf16[8,2,12928]{2,1,0:T(2,128)(2,1)S(1)}, u32[]{:S(2)}, u32[]{:S(2)}) %all-to-all-start.2) | async-done | bytes 413728 | tf_op jit(solution)/shard_map/all_to_all | solution.py:142
  47.0 3.8 %all-to-all-start.1 = ((f32[32,1,2525]{2,1,0:T(1,128)}), f32[32,1,2525]{2,1,0:T(1,128)S(1)}, u32[]{:S(2)}, u32[]{:S(2)}) async-start(f32[32,1,2525]{2,1,0:T(1,128)} %broadcast_in_dim.23), calls=%async_computation.1 | async-start | bytes 655360 | tf_op jit(solution)/shard_map/all_to_all | solution.py:80
  52.7 1.2 reshape.412
  54.0 2.1 %slice.174 = f32[16,16,2,399]{3,2,0,1:T(2,128)} slice(f32[16,16,2,400]{3,2,0,1:T(2,128)S(1)} %reshape.412), slice={[0:16], [0:16], [0:2], [1:400]} | slice | bytes 1634304 | tf_op jit(solution)/shard_map/jit(_roll_static)/slice | solution.py:65
  57.2 2.7 %negate_convert_fusion.2 = (bf16[16,16,400]{2,0,1:T(8,128)(2,1)}, f32[16,16,400]{2,0,1:T(8,128)S(1)}) fusion(f32[16]{0:T(128)S(1)} %get-tuple-element.17, s32[400]{0:T(512)S(1)} %fusion.55, s32[16,16]{0,1:T(8,128)S(1)} %copy.121), kind=kLoop, calls=%fused_computation.59 | loop fusion | flops 819200 | bytes 617088 | tf_op jit(solution)/shard_map/convert_element_type | solution.py:55
  59.9 2.0 %pad_maximum_fusion.2 = f32[16,16,2,400]{3,2,0,1:T(2,128)S(1)} fusion(f32[16,16,2,1]{3,2,0,1:T(2,128)} %slice.175, f32[16,16,2,399]{3,2,0,1:T(2,128)} %slice.174), kind=kLoop, calls=%fused_computation.16 | loop fusion | flops 204800 | bytes 1638400 | tf_op jit(solution)/shard_map/jit(_roll_static)/concatenate | solution.py:65
  61.8 2.4 %reshape.418 = f32[16,16,2,400]{3,2,1,0:T(2,128)} reshape(f32[16,12800]{1,0:T(8,128)S(1)} %slice_convert_fusion) | data formatting | bytes 1638400 | tf_op jit(solution)/shard_map/convert_element_type | solution.py:172
  64.2 1.6 %reshape.417 = f32[16,16,800]{2,1,0:T(8,128)} reshape(f32[16,12800]{1,0:T(8,128)S(1)} %slice_convert_fusion) | data formatting | bytes 1638400 | tf_op jit(solution)/shard_map/convert_element_type | solution.py:172
  65.9 1.9 %reshape.413 = f32[16,16,800]{2,0,1:T(8,128)} reshape(f32[16,16,2,400]{3,2,0,1:T(2,128)S(1)} %pad_maximum_fusion.2) | data formatting | bytes 1638400 | tf_op jit(solution)/shard_map/reshape | solution.py:65
  67.9 2.7 %negate_convert_fusion.1 = bf16[16,16,1,400]{3,1,2,0:T(8,128)(2,1)} fusion(f32[16]{0:T(128)S(1)} %get-tuple-element.17, s32[400]{0:T(512)S(1)} %fusion.55, s32[16,16]{1,0:T(8,128)S(1)} %fusion.43), kind=kLoop, calls=%fused_computation.58 | loop fusion | flops 614400 | bytes 207488 | tf_op jit(solution)/shard_map/convert_element_type | solution.py:55
  70.5 2.9 %fusion.27 = f32[16,16,400]{2,0,1:T(8,128)} fusion(f32[16,16,399]{2,0,1:T(8,128)S(1)} %bitcast.97, f32[16,16,1]{2,0,1:T(8,128)S(1)} %slice.190, f32[16]{0:T(128)S(1)} %get-tuple-element.5, f32[16]{0:T(128)S(1)} %get-tuple-element.18, f32[16]{0:T(128)S(1)} %get-tuple-element.17, s32[400]{0:T(512)S(1)} %fusion.55, s32[16,16]{0,1:T(8,128)S(1)} %copy.121), kind=kLoop, calls=%fused_computation.56 | loop fusion | flops 1228800 | bytes 822016 | tf_op jit(solution)/shard_map/add | solution.py:176
  74.9 1.3 reverse.2
  78.5 1.1 gather_fusion
  79.6 1.2 gather.6
  80.8 1.5 %copy_divide_fusion = f32[16,16,2,400]{3,1,2,0:T(8,128)S(1)} fusion(f32[16,16,2,400]{3,2,1,0:T(2,128)S(1)} %gather.6, f32[16,16,2,400]{3,2,1,0:T(2,128)S(1)} %copy-done.7, bf16[16,16,1,400]{3,1,2,0:T(8,128)(2,1)} %negate_convert_fusion.1), kind=kLoop, calls=%fused_computation.18 | loop fusion | flops 819200 | bytes 2662400 | tf_op jit(solution)/shard_map/div | solution.py:172
  83.7 1.9 %reshape.435 = f32[16,16,800]{2,0,1:T(8,128)} reshape(f32[16,16,2,400]{3,2,0,1:T(2,128)S(1)} %copy.136) | data formatting | bytes 1638400 | tf_op jit(solution)/shard_map/reshape | solution.py:65
  85.6 2.6 %fusion.5 = (f32[16,16,800]{2,0,1:T(8,128)S(1)}, bf16[16,16,800]{2,0,1:T(8,128)(2,1)S(1)}) fusion(f32[16,16,800]{2,1,0:T(8,128)S(1)} %bitcast.94, f32[16,16,800]{2,1,0:T(8,128)} %reshape.417, f32[16,16,800]{2,0,1:T(8,128)} %reshape.435, bf16[16,16,400]{2,0,1:T(8,128)(2,1)S(1)} %copy-done.11, f32[16]{0:T(128)} %copy-done.16, f32[16]{0:T(128)} %copy-done.19, ...), kind=kLoop, calls=%fused_computation.22 | loop fusion | flops 2867200 | bytes 5529792 | tf_op jit(solution)/shard_map/add | solution.py:173
  90.2 3.6 %all-to-all-start.4 = ((bf16[4,2,32,1200]{3,2,1,0:T(8,128)(2,1)}), bf16[4,2,32,1200]{3,2,1,0:T(8,128)(2,1)S(1)}, u32[]{:S(2)}, u32[]{:S(2)}) async-start(bf16[4,2,32,1200]{3,2,1,0:T(8,128)(2,1)} %copy.129), calls=%async_computation.4 | async-start | bytes 1310720 | tf_op jit(solution)/shard_map/all_to_all | solution.py:185
  94.6 9.4 %all-to-all-done.4 = bf16[4,2,32,1200]{3,2,1,0:T(8,128)(2,1)S(1)} async-done(((bf16[4,2,32,1200]{3,2,1,0:T(8,128)(2,1)}), bf16[4,2,32,1200]{3,2,1,0:T(8,128)(2,1)S(1)}, u32[]{:S(2)}, u32[]{:S(2)}) %all-to-all-start.4) | async-done | bytes 614432 | tf_op jit(solution)/shard_map/all_to_all | solution.py:185
  104.0 5.6 %all-to-all-start.3 = ((bf16[16,16,800]{2,1,0:T(8,128)(2,1)}), bf16[16,16,800]{2,1,0:T(8,128)(2,1)S(1)}, u32[]{:S(2)}, u32[]{:S(2)}) async-start(bf16[16,16,800]{2,1,0:T(8,128)(2,1)} %copy.119), calls=%async_computation.3 | async-start | bytes 917504 | tf_op jit(solution)/shard_map/all_to_all | solution.py:159
  111.0 3.7 %fusion.31 = f32[400,400]{1,0:T(8,128)} fusion(f32[]{:T(128)S(6)} %mul.165, s32[400]{0:T(512)S(1)} %copy-done.15), kind=kLoop, calls=%fused_computation.64 | loop fusion | flops 1120000 | bytes 641604 | tf_op jit(solution)/shard_map/convert_element_type | solution.py:206
  115.7 6.9 %all-to-all-done.3 = bf16[16,16,800]{2,1,0:T(8,128)(2,1)S(1)} async-done(((bf16[16,16,800]{2,1,0:T(8,128)(2,1)}), bf16[16,16,800]{2,1,0:T(8,128)(2,1)S(1)}, u32[]{:S(2)}, u32[]{:S(2)}) %all-to-all-start.3) | async-done | bytes 409632 | tf_op jit(solution)/shard_map/all_to_all | solution.py:159
  122.6 1.2 reshape.414
  123.8 1.2 convolution_convert_fusion.1
  125.7 2.5 %convolution_bitcast_fusion = f32[2,2,400,400]{3,2,1,0:T(8,128)S(1)} fusion(bf16[2,400,400]{2,1,0:T(8,128)(2,1)} %constant.63.clone, f32[1,400,400]{2,1,0:T(8,128)S(1)} %copy-done.4, f32[1,400,400]{2,1,0:T(8,128)S(1)} %copy-done.6, bf16[2,64,400]{2,1,0:T(8,128)(2,1)S(1)} %get-tuple-element.12, bf16[2,64,400]{2,1,0:T(8,128)(2,1)S(1)} %get-tuple-element.11, ...), kind=kOutput, calls=%fused_computation.4 | convolution fusion | flops 515520000 | bytes 5965600 | tf_op jit(solution)/shard_map/hyj,gmj->hgym/dot_general | solution.py:34
  (128 shorter events, 21.8 us)
Async XLA Ops:
  0.6 1.0 copy-start
  7.8 10.8 %copy-start.3 = (f32[1,400,400]{2,1,0:T(8,128)}, f32[1,400,400]{2,1,0:T(8,128)S(1)}, u32[]{:S(2)}) copy-start(f32[1,400,400]{2,1,0:T(8,128)S(1)} %fusion.13) | copy-start | bytes 1920004
  9.7 8.9 %copy-start.5 = (f32[1,400,400]{2,1,0:T(8,128)}, f32[1,400,400]{2,1,0:T(8,128)S(1)}, u32[]{:S(2)}) copy-start(f32[1,400,400]{2,1,0:T(8,128)S(1)} %fusion.15) | copy-start | bytes 1920004
  11.3 19.4 %all-to-all-start = ((f32[32,1,2525]{2,1,0:T(1,128)}), f32[32,1,2525]{2,1,0:T(1,128)S(1)}, u32[]{:S(2)}, u32[]{:S(2)}) async-start(f32[32,1,2525]{2,1,0:T(1,128)} %all_to_all.32), calls=%async_computation | async-start | bytes 655360 | tf_op jit(solution)/shard_map/all_to_all | solution.py:77
  18.7 0.7 copy-start.24
  18.7 0.7 copy-start.25
  18.7 0.7 copy-start.26
  19.5 14.8 %copy-start.13 = (bf16[2,128,800]{1,2,0:T(8,128)(2,1)S(1)}, bf16[2,128,800]{1,2,0:T(8,128)(2,1)}, u32[]{:S(2)}) copy-start(bf16[2,128,800]{1,2,0:T(8,128)(2,1)} %param.16) | copy-start | bytes 1228804
  21.4 13.4 %copy-start.22 = (s32[8]{0:T(128)}, s32[8]{0:T(128)S(1)}, u32[]{:S(2)}) copy-start(s32[8]{0:T(128)S(1)} %multiply_add_fusion) | copy-start | bytes 100
  30.8 15.4 %all-to-all-start.2 = ((bf16[8,2,12928]{2,1,0:T(2,128)(2,1)}), bf16[8,2,12928]{2,1,0:T(2,128)(2,1)S(1)}, u32[]{:S(2)}, u32[]{:S(2)}) async-start(bf16[8,2,12928]{2,1,0:T(2,128)(2,1)} %all_to_all.27), calls=%async_computation.2 | async-start | bytes 827392 | tf_op jit(solution)/shard_map/all_to_all | solution.py:142
  34.5 36.0 %copy-start.14 = (s32[400]{0:T(512)}, s32[400]{0:T(512)S(1)}, u32[]{:S(2)}) copy-start(s32[400]{0:T(512)S(1)} %fusion.55) | copy-start | bytes 4804
  47.0 26.4 %all-to-all-start.1 = ((f32[32,1,2525]{2,1,0:T(1,128)}), f32[32,1,2525]{2,1,0:T(1,128)S(1)}, u32[]{:S(2)}, u32[]{:S(2)}) async-start(f32[32,1,2525]{2,1,0:T(1,128)} %broadcast_in_dim.23), calls=%async_computation.1 | async-start | bytes 655360 | tf_op jit(solution)/shard_map/all_to_all | solution.py:80
  51.6 18.9 %copy-start.16 = (f32[16]{0:T(128)}, f32[16]{0:T(128)S(1)}, u32[]{:S(2)}) copy-start(f32[16]{0:T(128)S(1)} %get-tuple-element.5) | copy-start | bytes 196
  52.7 3.4 %copy-start.1 = (f32[16,16,800]{2,0,1:T(8,128)}, f32[16,16,800]{2,0,1:T(8,128)S(1)}, u32[]{:S(2)}) copy-start(f32[16,16,800]{2,0,1:T(8,128)S(1)} %fusion.28) | copy-start | bytes 2457604
  54.0 3.0 %copy-start.27 = (f32[64]{0:T(128)S(1)}, f32[64]{0:T(128)}, u32[]{:S(2)}) copy-start(f32[64]{0:T(128)} %param.11) | copy-start | bytes 772
  57.2 13.4 %copy-start.19 = (f32[16]{0:T(128)}, f32[16]{0:T(128)S(1)}, u32[]{:S(2)}) copy-start(f32[16]{0:T(128)S(1)} %get-tuple-element.18) | copy-start | bytes 196
  77.3 0.9 copy-start.8
  79.6 1.2 copy-start.7
  82.8 2.8 %copy-start.2 = (f32[16,16,800]{2,0,1:T(8,128)S(1)}, f32[16,16,800]{2,0,1:T(8,128)}, u32[]{:S(2)}) copy-start(f32[16,16,800]{2,0,1:T(8,128)} %copy-done.1) | copy-start | bytes 2457604
  82.8 2.8 %copy-start.11 = (bf16[16,16,400]{2,0,1:T(8,128)(2,1)S(1)}, bf16[16,16,400]{2,0,1:T(8,128)(2,1)}, u32[]{:S(2)}) copy-start(bf16[16,16,400]{2,0,1:T(8,128)(2,1)} %get-tuple-element.13) | copy-start | bytes 614404
  85.6 2.6 %copy-start.10 = (f32[16,16,400]{2,0,1:T(8,128)S(1)}, f32[16,16,400]{2,0,1:T(8,128)}, u32[]{:S(2)}) copy-start(f32[16,16,400]{2,0,1:T(8,128)} %fusion.27) | copy-start | bytes 1228804
  85.6 2.6 %copy-start.18 = (s32[16]{0:T(128)S(1)}, s32[16]{0:T(128)}, u32[]{:S(2)}) copy-start(s32[16]{0:T(128)} %copy-done.17) | copy-start | bytes 196
  85.6 2.6 %copy-start.20 = (f32[16]{0:T(128)S(1)}, f32[16]{0:T(128)}, u32[]{:S(2)}) copy-start(f32[16]{0:T(128)} %get-tuple-element.6) | copy-start | bytes 196
  90.2 19.5 %copy-start.28 = (f32[64]{0:T(128)S(1)}, f32[64]{0:T(128)}, u32[]{:S(2)}) copy-start(f32[64]{0:T(128)} %param.11) | copy-start | bytes 772
  90.2 20.8 %copy-start.15 = (s32[400]{0:T(512)S(1)}, s32[400]{0:T(512)}, u32[]{:S(2)}) copy-start(s32[400]{0:T(512)} %copy-done.14) | copy-start | bytes 4804
  90.2 13.8 %all-to-all-start.4 = ((bf16[4,2,32,1200]{3,2,1,0:T(8,128)(2,1)}), bf16[4,2,32,1200]{3,2,1,0:T(8,128)(2,1)S(1)}, u32[]{:S(2)}, u32[]{:S(2)}) async-start(bf16[4,2,32,1200]{3,2,1,0:T(8,128)(2,1)} %copy.129), calls=%async_computation.4 | async-start | bytes 1310720 | tf_op jit(solution)/shard_map/all_to_all | solution.py:185
  104.0 18.6 %all-to-all-start.3 = ((bf16[16,16,800]{2,1,0:T(8,128)(2,1)}), bf16[16,16,800]{2,1,0:T(8,128)(2,1)S(1)}, u32[]{:S(2)}, u32[]{:S(2)}) async-start(bf16[16,16,800]{2,1,0:T(8,128)(2,1)} %copy.119), calls=%async_computation.3 | async-start | bytes 917504 | tf_op jit(solution)/shard_map/all_to_all | solution.py:159
  111.0 12.8 %copy-start.23 = (s32[8]{0:T(128)S(1)}, s32[8]{0:T(128)}, u32[]{:S(2)}) copy-start(s32[8]{0:T(128)} %copy-done.22) | copy-start | bytes 100
  115.7 10.0 %copy-start.4 = (f32[1,400,400]{2,1,0:T(8,128)S(1)}, f32[1,400,400]{2,1,0:T(8,128)}, u32[]{:S(2)}) copy-start(f32[1,400,400]{2,1,0:T(8,128)} %copy-done.3) | copy-start | bytes 1920004
  115.7 10.0 %copy-start.6 = (f32[1,400,400]{2,1,0:T(8,128)S(1)}, f32[1,400,400]{2,1,0:T(8,128)}, u32[]{:S(2)}) copy-start(f32[1,400,400]{2,1,0:T(8,128)} %copy-done.5) | copy-start | bytes 1920004
  115.7 10.0 %copy-start.9 = (f32[400,400]{1,0:T(8,128)S(1)}, f32[400,400]{1,0:T(8,128)}, u32[]{:S(2)}) copy-start(f32[400,400]{1,0:T(8,128)} %copy-done.8) | copy-start | bytes 1920004
  128.2 1.1 copy-start.12
  (2 other events, 1.2 us)

commit v3 on v2

--- a/solution.py
+++ b/solution.py
@@ -61,8 +61,15 @@
 
 
 def shift_halves(values, steps, box_size):
-    split_shape = values.shape[:-1] + (2, box_size)
-    return jnp.roll(values.reshape(split_shape), steps, axis=-1).reshape(values.shape)
+    rolled = jnp.roll(values, steps, axis=-1)
+    column = lax.broadcasted_iota(jnp.int32, values.shape, values.ndim - 1)
+    if steps == 1:
+        first, second = values[..., box_size - 1 : box_size], values[..., 2 * box_size - 1 :]
+        rolled = jnp.where(column == 0, first, rolled)
+        return jnp.where(column == box_size, second, rolled)
+    first, second = values[..., 0:1], values[..., box_size : box_size + 1]
+    rolled = jnp.where(column == box_size - 1, first, rolled)
+    return jnp.where(column == 2 * box_size - 1, second, rolled)
 
 
 def low_row_ids(block_ids, box_size):
@@ -70,13 +77,8 @@
     return base[..., None] + jnp.arange(RB, dtype=jnp.int32)
 
 
-def power_all(power_half, device_count, box_size):
-    rows = power_half.shape[0]
-    chunk = rows * box_size // device_count
-    pieces = power_half.reshape(device_count, chunk)
-    gathered = lax.all_to_all(pieces, ("img", "slab"), 0, 0, tiled=True)
-    total = jnp.sum(gathered, axis=0, keepdims=True)
-    spread = jnp.broadcast_to(total, (device_count, chunk))
+def power_gather(total, device_count, rows, box_size):
+    spread = jnp.broadcast_to(total, (device_count, total.shape[1]))
     back = lax.all_to_all(spread, ("img", "slab"), 0, 0, tiled=True)
     half = back.reshape(rows, box_size)[: box_size // 2 + 1]
     mirrored = jnp.roll(half[1 : box_size // 2][::-1, ::-1], 1, axis=1)
@@ -139,6 +141,12 @@
     send = jnp.einsum(
         "rs,rx->sx", seat_pick, payload, preferred_element_type=jnp.float32
     ).astype(jnp.bfloat16)
+    rows_half = half_rows(box_size, device_count)
+    low_half = spectrum[:, :, :rows_half]
+    power_half = jnp.sum(low_half * low_half, axis=(0, 1))
+    pieces = power_half.reshape(device_count, rows_half * box_size // device_count)
+    gathered = lax.all_to_all(pieces, ("img", "slab"), 0, 0, tiled=True)
+    gathered, send = lax.optimization_barrier((gathered, send))
     got = lax.all_to_all(send, "slab", 0, 0, tiled=True)
     got_blocks = got[:, : RB * 2 * box_size].reshape(seat_count, RB, 2 * box_size)
     got_info = got[:, RB * 2 * box_size : RB * 2 * box_size + 6].astype(jnp.int32)
@@ -156,14 +164,15 @@
     projected = (
         ((1.0 - blend_weight) * nearby + blend_weight * shift_halves(nearby, -1, box_size)) * live
     ).astype(jnp.bfloat16)
-    returned_rows = lax.all_to_all(projected, "slab", 0, 0, tiled=True)
-
-    rows_half = half_rows(box_size, device_count)
-    low_half = spectrum[:, :, :rows_half]
-    power_half = jnp.sum(low_half * low_half, axis=(0, 1))
-    power = power_all(power_half, device_count, box_size)
+
+    total = jnp.sum(gathered, axis=0, keepdims=True)
+    total, got = lax.optimization_barrier((total, got))
+    power = power_gather(total, device_count, rows_half, box_size)
     noise_level = jnp.sqrt(power / (particles * device_count) + 1e-06)
     level_both = jnp.concatenate([noise_level, noise_level], axis=1)
+
+    projected, power = lax.optimization_barrier((projected, power))
+    returned_rows = lax.all_to_all(projected, "slab", 0, 0, tiled=True)
 
     got_rows = low_row_ids(got_info[:, 4], box_size)
     got_contrast = contrast_curve(lookup_defocus(got_info[:, 5], defocus), got_rows, box_size)
@@ -182,6 +191,7 @@
     share = vrows // img_count
     numerator = numerator.reshape(planes, img_count, share, 3 * box_size).astype(jnp.bfloat16)
     numerator = jnp.swapaxes(numerator, 0, 1)
+    numerator, returned_rows = lax.optimization_barrier((numerator, returned_rows))
     parts = lax.all_to_all(numerator, "img", 0, 0, tiled=True)
     volume_part = jnp.sum(parts.astype(jnp.float32), axis=0)
     weight_sum = volume_part[..., 2 * box_size :]

time: 132 us -> 115 us (0.87)
  waiting for transfers between devices: 35.7 us -> 26.6 us
  other arithmetic: 28 us -> 24.3 us
  local copies, waits for them, and re-layouts: 30.3 us -> 27.2 us
  starting transfers between devices: 23.8 us -> 21.8 us
    all_to_all x1, waiting for transfers between devices: 9.35 us -> 0.01 us  [body(): parts = lax.all_to_all(numerator, 'img', 0, 0, tiled=True)]
    reshape x5 -> x1, local copies, waits for them, and re-layouts: 6.36 us -> 0.46 us  [power_gather(): half = back.reshape(rows, box_size)[:box_size // 2 + 1]]
    all_to_all x2, waiting for transfers between devices: 8.1 us -> 12.4 us  [the longest x1 8.86 us: body(): gathered = lax.all_to_all(pieces, ('img', 'slab'), 0, 0, tiled=True)]
    broadcast_in_dim x1 -> x6, local copies, waits for them, and re-layouts: 0.89 us -> 3.91 us  [the longest x1 0.89 us: power_gather(): spread = jnp.broadcast_to(total, (device_count, total.shape[1]))]
    convert_element_type x0 -> x2, other arithmetic: none -> 2.93 us  [the longest x1 2.26 us: body(): projected = (((1.0 - blend_weight) * nearby + blend_weight * shift_halves...]
    all_to_all x1, waiting for transfers between devices: 11.4 us -> 8.48 us  [body(): got = lax.all_to_all(send, 'slab', 0, 0, tiled=True)]
    convert_element_type x2 -> x1, other arithmetic: 5.35 us -> 2.75 us  [contrast_curve(): (-jnp.sin(defocus_of[:, None, None] * radius + 0.1)).astype(jnp.bfloat16)]
    reshape x2, local copies, waits for them, and re-layouts: 0.61 us -> 3.2 us  [body(): own_rows = own_rows.reshape(particles, 2 * low_rows, 2, box_size)]
  transfers between devices with their start and end apart: 5 -> 5, of which waited for: 4 -> 4; matrix products, arithmetic and copies ran while one was open for 23% -> 28% of each run, Pallas kernels for 0% -> 0%
where the time goes in v3:
time: 115 us; the launch traced here: 114 us
  local copies, waits for them, and re-layouts  27.2 us (24%)
  waiting for transfers between devices  26.6 us (23%)
  other arithmetic  24.3 us (21%)
  starting transfers between devices  21.8 us (19%)
  matrix products  11.2 us (10%)
  between operations  2.61 us (2%)
    all_to_all x1, waiting for transfers between devices, body(): gathered = lax.all_to_all(pieces, ('img', 'slab'), 0, 0, tiled=True)  8.86 us
    all_to_all x1, waiting for transfers between devices, body(): got = lax.all_to_all(send, 'slab', 0, 0, tiled=True)  8.48 us
    all_to_all x1, starting transfers between devices, body(): gathered = lax.all_to_all(pieces, ('img', 'slab'), 0, 0, tiled=True)  7.3 us
    all_to_all x1, waiting for transfers between devices, body(): returned_rows = lax.all_to_all(projected, 'slab', 0, 0, tiled=True)  5.78 us
    unnamed x70, local copies, waits for them, and re-layouts  5.16 us
    dot_general x1, matrix products, transform(): jnp.einsum('gky,hym->ghkm', tables, rowwise, preferred_element_type=jnp.f...  4.56 us
    all_to_all x1, starting transfers between devices, power_gather(): back = lax.all_to_all(spread, ('img', 'slab'), 0, 0, tiled=True)  3.77 us
    convert_element_type x1, other arithmetic, body(): contrast.astype(jnp.float32)[:, None] * full_projection.astype(jnp.float32)  3.71 us
  transfers between devices with their start and end apart: 5, of which 4 were waited for; matrix products, arithmetic and copies ran while one was open for 28% of the time, Pallas kernels for 0%

profile of v3, /device:TPU:0, one launch (start us, length us, event | category | flops | bytes accessed | tf_op | source)
XLA Modules:
  0.0 113.7 jit_solution(13852627558487927358)
XLA Ops:
  0.6 1.0 copy-done
  1.6 4.6 %convolution_bitcast_fusion.1 = f32[2,2,400,400]{3,2,0,1:T(8,128)} fusion(bf16[2,400,400]{2,1,0:T(8,128)(2,1)} %constant.69.clone, bf16[1,400,400]{2,1,0:T(8,128)(2,1)S(1)} %copy-done), kind=kOutput, calls=%fused_computation.5 | convolution fusion | flops 768320000 | bytes 3520000 | tf_op jit(solution)/shard_map/gky,hym->ghkm/dot_general | solution.py:27
  6.2 1.6 %fusion.19 = f32[1,400,400]{2,1,0:T(8,128)S(1)} fusion(f32[2,2,400,400]{3,2,0,1:T(8,128)} %convolution_bitcast_fusion.1), kind=kLoop, calls=%fused_computation.40 | loop fusion | flops 320000 | bytes 1920000 | tf_op jit(solution)/shard_map/neg | solution.py:29
  7.8 1.8 %fusion.21 = f32[1,400,400]{2,1,0:T(8,128)S(1)} fusion(f32[2,2,400,400]{3,2,0,1:T(8,128)} %convolution_bitcast_fusion.1), kind=kLoop, calls=%fused_computation.43 | loop fusion | flops 160000 | bytes 1920000 | tf_op jit(solution)/shard_map/sub | solution.py:28
  9.9 1.4 %all_to_all.35 = f32[32,1,2525]{2,1,0:T(1,128)} reshape(f32[202,400]{1,0:T(8,128)S(1)} %fusion.12) | data formatting | bytes 646400 | tf_op jit(solution)/shard_map/all_to_all | solution.py:148
  11.2 7.3 %all-to-all-start = ((f32[32,1,2525]{2,1,0:T(1,128)}), f32[32,1,2525]{2,1,0:T(1,128)S(1)}, u32[]{:S(2)}, u32[]{:S(2)}) async-start(f32[32,1,2525]{2,1,0:T(1,128)} %all_to_all.35), calls=%async_computation | async-start | bytes 655360 | tf_op jit(solution)/shard_map/all_to_all | solution.py:148
  21.8 8.9 %all-to-all-done = f32[32,1,2525]{2,1,0:T(1,128)S(1)} async-done(((f32[32,1,2525]{2,1,0:T(1,128)}), f32[32,1,2525]{2,1,0:T(1,128)S(1)}, u32[]{:S(2)}, u32[]{:S(2)}) %all-to-all-start) | async-done | bytes 323232 | tf_op jit(solution)/shard_map/all_to_all | solution.py:148
  30.7 0.9 all_to_all.29
  31.6 3.5 %all-to-all-start.1 = ((bf16[8,2,12928]{2,1,0:T(2,128)(2,1)}), bf16[8,2,12928]{2,1,0:T(2,128)(2,1)S(1)}, u32[]{:S(2)}, u32[]{:S(2)}) async-start(bf16[8,2,12928]{2,1,0:T(2,128)(2,1)} %all_to_all.29), calls=%async_computation.1 | async-start | bytes 827392 | tf_op jit(solution)/shard_map/all_to_all | solution.py:150
  38.5 8.5 %all-to-all-done.1 = bf16[8,2,12928]{2,1,0:T(2,128)(2,1)S(1)} async-done(((bf16[8,2,12928]{2,1,0:T(2,128)(2,1)}), bf16[8,2,12928]{2,1,0:T(2,128)(2,1)S(1)}, u32[]{:S(2)}, u32[]{:S(2)}) %all-to-all-start.1) | async-done | bytes 413728 | tf_op jit(solution)/shard_map/all_to_all | solution.py:150
  49.0 3.8 %all-to-all-start.2 = ((f32[32,1,2525]{2,1,0:T(1,128)}), f32[32,1,2525]{2,1,0:T(1,128)S(1)}, u32[]{:S(2)}, u32[]{:S(2)}) async-start(f32[32,1,2525]{2,1,0:T(1,128)} %broadcast_in_dim.94), calls=%async_computation.2 | async-start | bytes 655360 | tf_op jit(solution)/shard_map/all_to_all | solution.py:82
  54.0 1.2 %slice.195 = f32[16,16,799]{2,0,1:T(8,128)} slice(f32[16,16,800]{2,0,1:T(8,128)S(1)} %fusion.32), slice={[0:16], [0:16], [1:800]} | slice | bytes 1636352 | tf_op jit(solution)/shard_map/jit(_roll_static)/slice | solution.py:64
  55.3 1.6 %reshape.384 = f32[16,16,800]{2,1,0:T(8,128)} reshape(f32[16,12800]{1,0:T(8,128)S(1)} %slice_convert_fusion) | data formatting | bytes 1638400 | tf_op jit(solution)/shard_map/convert_element_type | solution.py:181
  58.5 2.7 %negate_convert_fusion.1 = (bf16[16,16,400]{2,0,1:T(8,128)(2,1)S(1)}, f32[16,16,400]{2,0,1:T(8,128)}) fusion(f32[16]{0:T(128)S(1)} %get-tuple-element.35, s32[400]{0:T(512)S(1)} %fusion.59, s32[16,16]{0,1:T(8,128)S(1)} %fusion.47), kind=kLoop, calls=%fused_computation.60 | loop fusion | flops 819200 | bytes 617088 | tf_op jit(solution)/shard_map/convert_element_type | solution.py:55
  61.2 3.5 %all-to-all-done.2 = f32[32,1,2525]{2,1,0:T(1,128)S(1)} async-done(((f32[32,1,2525]{2,1,0:T(1,128)}), f32[32,1,2525]{2,1,0:T(1,128)S(1)}, u32[]{:S(2)}, u32[]{:S(2)}) %all-to-all-start.2) | async-done | bytes 323232 | tf_op jit(solution)/shard_map/all_to_all | solution.py:82
  66.2 1.3 %reverse.2 = f32[200,512]{1,0:T(8,128)S(1)} reverse(f32[200,512]{1,0:T(8,128)S(1)} %bitcast.105), dimensions={0,1} | reverse | bytes 819200
  68.4 0.9 copy-done.7
  69.6 2.0 %gather_fusion = f32[256,800]{1,0:T(8,128)} fusion(f32[400,800]{1,0:T(8,128)S(1)} %pad_maximum_fusion.1, s32[1024]{0:T(1024)S(1)} %pad_clamp_fusion), kind=kCustom, calls=%fused_computation | custom fusion | bytes 1639424 | tf_op jit(solution)/shard_map/gather | solution.py:179
  71.6 2.2 %copy_divide_fusion = f32[16,16,800]{2,0,1:T(8,128)S(1)} fusion(f32[16,16,800]{2,1,0:T(8,128)} %bitcast.101, f32[16,16,800]{2,1,0:T(8,128)} %reshape.384, bf16[16,16,400]{2,0,1:T(8,128)(2,1)S(1)} %get-tuple-element.31), kind=kLoop, calls=%fused_computation.26 | loop fusion | flops 1228800 | bytes 2662400 | tf_op jit(solution)/shard_map/div | solution.py:181
  75.5 2.3 %fusion.11 = (bf16[16,16,800]{2,0,1:T(8,128)(2,1)S(1)}, f32[16,16,800]{2,0,1:T(8,128)}) fusion(f32[16,16,1]{2,0,1:T(8,128)S(1)} %get-tuple-element.24, f32[16,16,799]{2,0,1:T(8,128)S(1)} %copy-done.5, f32[16,16,800]{2,0,1:T(8,128)S(1)} %fusion.32, f32[16]{0:T(128)} %get-tuple-element.17, f32[16,16]{0,1:T(8,128)} %bitcast.108, f32[16,16]{0,1:T(8,128)} %bitcast.109, ...), kind=kLoop, calls=%fused_computation.25 | loop fusion | flops 2867200 | bytes 4513088 | tf_op jit(solution)/shard_map/convert_element_type | solution.py:166
  78.7 3.6 %all-to-all-start.3 = ((bf16[16,16,800]{2,1,0:T(8,128)(2,1)}), bf16[16,16,800]{2,1,0:T(8,128)(2,1)S(1)}, u32[]{:S(2)}, u32[]{:S(2)}) async-start(bf16[16,16,800]{2,1,0:T(8,128)(2,1)} %copy.108), calls=%async_computation.3 | async-start | bytes 917504 | tf_op jit(solution)/shard_map/all_to_all | solution.py:175
  82.3 3.7 %fusion.35 = f32[400,400]{1,0:T(8,128)} fusion(f32[]{:T(128)S(6)} %mul.153, s32[400]{0:T(512)S(1)} %copy-done.16), kind=kLoop, calls=%fused_computation.65 | loop fusion | flops 1120000 | bytes 641604 | tf_op jit(solution)/shard_map/convert_element_type | solution.py:216
  86.1 2.1 %fusion.31 = f32[16,16,400]{2,0,1:T(8,128)S(1)} fusion(f32[16,16,399]{2,0,1:T(8,128)S(1)} %bitcast.102, f32[16,16,1]{2,0,1:T(8,128)S(1)} %slice.190, f32[16]{0:T(128)S(1)} %copy-done.18, f32[16]{0:T(128)S(1)} %copy-done.23, f32[16]{0:T(128)S(1)} %copy-done.20, s32[400]{0:T(512)S(1)} %copy-done.16, s32[16,16]{0,1:T(8,128)S(1)} %copy-done.14), kind=kLoop, calls=%fused_computation.58 | loop fusion | flops 1228800 | bytes 822016 | tf_op jit(solution)/shard_map/add | solution.py:185
  89.3 5.8 %all-to-all-done.3 = bf16[16,16,800]{2,1,0:T(8,128)(2,1)S(1)} async-done(((bf16[16,16,800]{2,1,0:T(8,128)(2,1)}), bf16[16,16,800]{2,1,0:T(8,128)(2,1)S(1)}, u32[]{:S(2)}, u32[]{:S(2)}) %all-to-all-start.3) | async-done | bytes 409632 | tf_op jit(solution)/shard_map/all_to_all | solution.py:175
  95.1 1.0 copy.110
  96.1 3.7 %all-to-all-start.4 = ((bf16[4,2,32,1200]{3,2,1,0:T(8,128)(2,1)}), bf16[4,2,32,1200]{3,2,1,0:T(8,128)(2,1)S(1)}, u32[]{:S(2)}, u32[]{:S(2)}) async-start(bf16[4,2,32,1200]{3,2,1,0:T(8,128)(2,1)} %copy.110), calls=%async_computation.4 | async-start | bytes 1310720 | tf_op jit(solution)/shard_map/all_to_all | solution.py:195
  99.9 2.4 %reshape.382 = bf16[16,12800]{1,0:T(8,128)(2,1)} reshape(bf16[16,16,800]{2,1,0:T(8,128)(2,1)} %copy-done.10) | data formatting | bytes 819200 | tf_op jit(solution)/shard_map/reshape | solution.py:206
  102.3 1.9 %convolution_convert_fusion.1 = bf16[8,12800]{1,0:T(8,128)(2,1)} fusion(bf16[16,12800]{1,0:T(8,128)(2,1)} %reshape.382, s32[8]{0:T(128)S(1)} %copy-done.27), kind=kOutput, calls=%fused_computation.2 | convolution fusion | flops 3379328 | bytes 614432 | tf_op jit(solution)/shard_map/rs,sx->rx/dot_general | solution.py:205
  104.2 2.2 %reshape.383 = bf16[1,128,2,400]{3,2,1,0:T(2,128)(2,1)} reshape(bf16[8,12800]{1,0:T(8,128)(2,1)} %convolution_convert_fusion.1) | data formatting | bytes 409600 | tf_op jit(solution)/shard_map/reshape | solution.py:209
  106.4 1.0 copy.133
  107.5 2.5 %convolution_bitcast_fusion = f32[2,2,400,400]{3,2,1,0:T(8,128)S(1)} fusion(bf16[2,400,400]{2,1,0:T(8,128)(2,1)} %constant.69.clone, f32[1,400,400]{2,1,0:T(8,128)S(1)} %copy-done.2, f32[1,400,400]{2,1,0:T(8,128)S(1)} %copy-done.4, bf16[2,64,400]{2,1,0:T(8,128)(2,1)S(1)} %get-tuple-element.30, bf16[2,64,400]{2,1,0:T(8,128)(2,1)S(1)} %get-tuple-element.29, ...), kind=kOutput, calls=%fused_computation.4 | convolution fusion | flops 515520000 | bytes 5965600 | tf_op jit(solution)/shard_map/hyj,gmj->hgym/dot_general | solution.py:34
  111.7 0.9 fusion.14
  (135 shorter events, 19.5 us)
Async XLA Ops:
  0.6 1.0 copy-start
  7.8 10.8 %copy-start.1 = (f32[1,400,400]{2,1,0:T(8,128)}, f32[1,400,400]{2,1,0:T(8,128)S(1)}, u32[]{:S(2)}) copy-start(f32[1,400,400]{2,1,0:T(8,128)S(1)} %fusion.19) | copy-start | bytes 1920004
  9.6 8.9 %copy-start.3 = (f32[1,400,400]{2,1,0:T(8,128)}, f32[1,400,400]{2,1,0:T(8,128)S(1)}, u32[]{:S(2)}) copy-start(f32[1,400,400]{2,1,0:T(8,128)S(1)} %fusion.21) | copy-start | bytes 1920004
  11.2 19.4 %all-to-all-start = ((f32[32,1,2525]{2,1,0:T(1,128)}), f32[32,1,2525]{2,1,0:T(1,128)S(1)}, u32[]{:S(2)}, u32[]{:S(2)}) async-start(f32[32,1,2525]{2,1,0:T(1,128)} %all_to_all.35), calls=%async_computation | async-start | bytes 655360 | tf_op jit(solution)/shard_map/all_to_all | solution.py:148
  19.6 15.4 %copy-start.12 = (bf16[2,128,800]{1,2,0:T(8,128)(2,1)S(1)}, bf16[2,128,800]{1,2,0:T(8,128)(2,1)}, u32[]{:S(2)}) copy-start(bf16[2,128,800]{1,2,0:T(8,128)(2,1)} %param.16) | copy-start | bytes 1228804
  21.8 13.5 %copy-start.32 = (f32[64]{0:T(128)S(1)}, f32[64]{0:T(128)}, u32[]{:S(2)}) copy-start(f32[64]{0:T(128)} %param.11) | copy-start | bytes 772
  31.6 15.4 %all-to-all-start.1 = ((bf16[8,2,12928]{2,1,0:T(2,128)(2,1)}), bf16[8,2,12928]{2,1,0:T(2,128)(2,1)S(1)}, u32[]{:S(2)}, u32[]{:S(2)}) async-start(bf16[8,2,12928]{2,1,0:T(2,128)(2,1)} %all_to_all.29), calls=%async_computation.1 | async-start | bytes 827392 | tf_op jit(solution)/shard_map/all_to_all | solution.py:150
  37.2 21.2 %copy-start.15 = (s32[400]{0:T(512)}, s32[400]{0:T(512)S(1)}, u32[]{:S(2)}) copy-start(s32[400]{0:T(512)S(1)} %fusion.59) | copy-start | bytes 4804
  47.4 6.0 %copy-start.21 = (s32[16]{0:T(128)}, s32[16]{0:T(128)S(1)}, u32[]{:S(2)}) copy-start(s32[16]{0:T(128)S(1)} %get-tuple-element.14) | copy-start | bytes 196
  48.0 5.5 %copy-start.17 = (f32[16]{0:T(128)}, f32[16]{0:T(128)S(1)}, u32[]{:S(2)}) copy-start(f32[16]{0:T(128)S(1)} %get-tuple-element.18) | copy-start | bytes 196
  49.0 15.7 %all-to-all-start.2 = ((f32[32,1,2525]{2,1,0:T(1,128)}), f32[32,1,2525]{2,1,0:T(1,128)S(1)}, u32[]{:S(2)}, u32[]{:S(2)}) async-start(f32[32,1,2525]{2,1,0:T(1,128)} %broadcast_in_dim.94), calls=%async_computation.2 | async-start | bytes 655360 | tf_op jit(solution)/shard_map/all_to_all | solution.py:82
  54.0 4.4 %copy-start.19 = (f32[16]{0:T(128)}, f32[16]{0:T(128)S(1)}, u32[]{:S(2)}) copy-start(f32[16]{0:T(128)S(1)} %get-tuple-element.35) | copy-start | bytes 196
  58.4 9.0 %copy-start.13 = (s32[16,16]{0,1:T(8,128)}, s32[16,16]{0,1:T(8,128)S(1)}, u32[]{:S(2)}) copy-start(s32[16,16]{0,1:T(8,128)S(1)} %fusion.47) | copy-start | bytes 3076
  71.6 3.8 %copy-start.5 = (f32[16,16,799]{2,0,1:T(8,128)S(1)}, f32[16,16,799]{2,0,1:T(8,128)}, u32[]{:S(2)}) copy-start(f32[16,16,799]{2,0,1:T(8,128)} %slice.195) | copy-start | bytes 2454532
  77.7 4.5 %copy-start.16 = (s32[400]{0:T(512)S(1)}, s32[400]{0:T(512)}, u32[]{:S(2)}) copy-start(s32[400]{0:T(512)} %copy-done.15) | copy-start | bytes 4804
  77.7 8.3 %copy-start.9 = (f32[16,16,400]{2,0,1:T(8,128)S(1)}, f32[16,16,400]{2,0,1:T(8,128)}, u32[]{:S(2)}) copy-start(f32[16,16,400]{2,0,1:T(8,128)} %get-tuple-element.32) | copy-start | bytes 1228804
  77.7 8.4 %copy-start.14 = (s32[16,16]{0,1:T(8,128)S(1)}, s32[16,16]{0,1:T(8,128)}, u32[]{:S(2)}) copy-start(s32[16,16]{0,1:T(8,128)} %copy-done.13) | copy-start | bytes 3076
  77.7 8.4 %copy-start.18 = (f32[16]{0:T(128)S(1)}, f32[16]{0:T(128)}, u32[]{:S(2)}) copy-start(f32[16]{0:T(128)} %copy-done.17) | copy-start | bytes 196
  77.7 8.4 %copy-start.20 = (f32[16]{0:T(128)S(1)}, f32[16]{0:T(128)}, u32[]{:S(2)}) copy-start(f32[16]{0:T(128)} %copy-done.19) | copy-start | bytes 196
  77.7 8.4 %copy-start.23 = (f32[16]{0:T(128)S(1)}, f32[16]{0:T(128)}, u32[]{:S(2)}) copy-start(f32[16]{0:T(128)} %get-tuple-element.36) | copy-start | bytes 196
  78.6 9.6 %copy-start.6 = (f32[16,16,800]{2,0,1:T(8,128)S(1)}, f32[16,16,800]{2,0,1:T(8,128)}, u32[]{:S(2)}) copy-start(f32[16,16,800]{2,0,1:T(8,128)} %get-tuple-element.34) | copy-start | bytes 2457604
  78.6 9.6 %copy-start.22 = (s32[16]{0:T(128)S(1)}, s32[16]{0:T(128)}, u32[]{:S(2)}) copy-start(s32[16]{0:T(128)} %copy-done.21) | copy-start | bytes 196
  78.6 9.6 %copy-start.24 = (f32[16]{0:T(128)S(1)}, f32[16]{0:T(128)}, u32[]{:S(2)}) copy-start(f32[16]{0:T(128)} %get-tuple-element.17) | copy-start | bytes 196
  78.7 16.5 %all-to-all-start.3 = ((bf16[16,16,800]{2,1,0:T(8,128)(2,1)}), bf16[16,16,800]{2,1,0:T(8,128)(2,1)S(1)}, u32[]{:S(2)}, u32[]{:S(2)}) async-start(bf16[16,16,800]{2,1,0:T(8,128)(2,1)} %copy.108), calls=%async_computation.3 | async-start | bytes 917504 | tf_op jit(solution)/shard_map/all_to_all | solution.py:175
  95.1 1.0 copy-start.10
  95.1 7.1 %copy-start.27 = (s32[8]{0:T(128)S(1)}, s32[8]{0:T(128)}, u32[]{:S(2)}) copy-start(s32[8]{0:T(128)} %copy-done.26) | copy-start | bytes 100
  96.1 16.5 %all-to-all-start.4 = ((bf16[4,2,32,1200]{3,2,1,0:T(8,128)(2,1)}), bf16[4,2,32,1200]{3,2,1,0:T(8,128)(2,1)S(1)}, u32[]{:S(2)}, u32[]{:S(2)}) async-start(bf16[4,2,32,1200]{3,2,1,0:T(8,128)(2,1)} %copy.110), calls=%async_computation.4 | async-start | bytes 1310720 | tf_op jit(solution)/shard_map/all_to_all | solution.py:195
  99.9 7.6 %copy-start.2 = (f32[1,400,400]{2,1,0:T(8,128)S(1)}, f32[1,400,400]{2,1,0:T(8,128)}, u32[]{:S(2)}) copy-start(f32[1,400,400]{2,1,0:T(8,128)} %copy-done.1) | copy-start | bytes 1920004
  99.9 7.6 %copy-start.4 = (f32[1,400,400]{2,1,0:T(8,128)S(1)}, f32[1,400,400]{2,1,0:T(8,128)}, u32[]{:S(2)}) copy-start(f32[1,400,400]{2,1,0:T(8,128)} %copy-done.3) | copy-start | bytes 1920004
  99.9 7.6 %copy-start.8 = (f32[400,400]{1,0:T(8,128)S(1)}, f32[400,400]{1,0:T(8,128)}, u32[]{:S(2)}) copy-start(f32[400,400]{1,0:T(8,128)} %copy-done.7) | copy-start | bytes 1920004
  99.9 7.6 %copy-start.28 = (bf16[400]{0:T(512)(128)(2,1)S(1)}, bf16[400]{0:T(512)(128)(2,1)}, u32[]{:S(2)}) copy-start(bf16[400]{0:T(512)(128)(2,1)} %pad.10.clone) | copy-start | bytes 2404
  110.0 1.1 %copy-start.11 = (bf16[2,400,400]{2,1,0:T(8,128)(2,1)S(1)}, bf16[2,400,400]{2,1,0:T(8,128)(2,1)}, u32[]{:S(2)}) copy-start(bf16[2,400,400]{2,1,0:T(8,128)(2,1)} %constant.69.clone) | copy-start | bytes 1920004
  (6 other events, 4.3 us)

commit v4 on v3

--- a/solution.py
+++ b/solution.py
@@ -80,7 +80,7 @@
 def power_gather(total, device_count, rows, box_size):
     spread = jnp.broadcast_to(total, (device_count, total.shape[1]))
     back = lax.all_to_all(spread, ("img", "slab"), 0, 0, tiled=True)
-    half = back.reshape(rows, box_size)[: box_size // 2 + 1]
+    half = back.reshape(rows, box_size)[: box_size // 2 + 1].astype(jnp.float32)
     mirrored = jnp.roll(half[1 : box_size // 2][::-1, ::-1], 1, axis=1)
     return jnp.concatenate([half, mirrored], axis=0)
 
@@ -145,7 +145,7 @@
     low_half = spectrum[:, :, :rows_half]
     power_half = jnp.sum(low_half * low_half, axis=(0, 1))
     pieces = power_half.reshape(device_count, rows_half * box_size // device_count)
-    gathered = lax.all_to_all(pieces, ("img", "slab"), 0, 0, tiled=True)
+    gathered = lax.all_to_all(pieces.astype(jnp.bfloat16), ("img", "slab"), 0, 0, tiled=True)
     gathered, send = lax.optimization_barrier((gathered, send))
     got = lax.all_to_all(send, "slab", 0, 0, tiled=True)
     got_blocks = got[:, : RB * 2 * box_size].reshape(seat_count, RB, 2 * box_size)
@@ -165,7 +165,7 @@
         ((1.0 - blend_weight) * nearby + blend_weight * shift_halves(nearby, -1, box_size)) * live
     ).astype(jnp.bfloat16)
 
-    total = jnp.sum(gathered, axis=0, keepdims=True)
+    total = jnp.sum(gathered.astype(jnp.float32), axis=0, keepdims=True).astype(jnp.bfloat16)
     total, got = lax.optimization_barrier((total, got))
     power = power_gather(total, device_count, rows_half, box_size)
     noise_level = jnp.sqrt(power / (particles * device_count) + 1e-06)

time: 115 us -> 116 us (level)
  waiting for transfers between devices: 26.6 us -> 29 us
    all_to_all x1, waiting for transfers between devices: 3.53 us -> 5.32 us  [power_gather(): back = lax.all_to_all(spread, ('img', 'slab'), 0, 0, tiled=True)]
    all_to_all x1 -> x0, local copies, waits for them, and re-layouts: 1.36 us -> none  [body(): gathered = lax.all_to_all(pieces, ('img', 'slab'), 0, 0, tiled=True)]
  transfers between devices with their start and end apart: 5 -> 5, of which waited for: 4 -> 4; matrix products, arithmetic and copies ran while one was open for 28% -> 26% of each run, Pallas kernels for 0% -> 0%
where the time goes in v4:
time: 116 us
  waiting for transfers between devices  29 us (25%)
  local copies, waits for them, and re-layouts  26.4 us (23%)
  other arithmetic  24.5 us (21%)
  starting transfers between devices  21.8 us (19%)
  matrix products  11.2 us (10%)
  between operations  2.6 us (2%)
    all_to_all x1, waiting for transfers between devices, body(): lax.all_to_all(pieces.astype(jnp.bfloat16), ('img', 'slab'), 0, 0, tiled=...  9.45 us
    all_to_all x1, waiting for transfers between devices, body(): got = lax.all_to_all(send, 'slab', 0, 0, tiled=True)  8.45 us
    all_to_all x1, starting transfers between devices, body(): lax.all_to_all(pieces.astype(jnp.bfloat16), ('img', 'slab'), 0, 0, tiled=...  7.3 us
    all_to_all x1, waiting for transfers between devices, body(): returned_rows = lax.all_to_all(projected, 'slab', 0, 0, tiled=True)  5.78 us
    all_to_all x1, waiting for transfers between devices, power_gather(): back = lax.all_to_all(spread, ('img', 'slab'), 0, 0, tiled=True)  5.32 us
    unnamed x70, local copies, waits for them, and re-layouts  4.56 us
    dot_general x1, matrix products, transform(): jnp.einsum('gky,hym->ghkm', tables, rowwise, preferred_element_type=jnp.f...  4.56 us
    all_to_all x1, starting transfers between devices, power_gather(): back = lax.all_to_all(spread, ('img', 'slab'), 0, 0, tiled=True)  3.77 us
  transfers between devices with their start and end apart: 5, of which 4 were waited for; matrix products, arithmetic and copies ran while one was open for 26% of the time, Pallas kernels for 0%

profile of v4, /device:TPU:0, one launch (start us, length us, event | category | flops | bytes accessed | tf_op | source)
XLA Modules:
  0.0 115.5 jit_solution(18262730925676193582)
XLA Ops:
  0.6 1.0 copy-done
  1.6 4.6 %convolution_bitcast_fusion.1 = f32[2,2,400,400]{3,2,0,1:T(8,128)} fusion(bf16[2,400,400]{2,1,0:T(8,128)(2,1)} %constant.70.clone, bf16[1,400,400]{2,1,0:T(8,128)(2,1)S(1)} %copy-done), kind=kOutput, calls=%fused_computation.5 | convolution fusion | flops 768320000 | bytes 3520000 | tf_op jit(solution)/shard_map/gky,hym->ghkm/dot_general | solution.py:27
  6.2 1.6 %fusion.19 = f32[1,400,400]{2,1,0:T(8,128)S(1)} fusion(f32[2,2,400,400]{3,2,0,1:T(8,128)} %convolution_bitcast_fusion.1), kind=kLoop, calls=%fused_computation.40 | loop fusion | flops 320000 | bytes 1920000 | tf_op jit(solution)/shard_map/neg | solution.py:29
  7.8 1.8 %fusion.21 = f32[1,400,400]{2,1,0:T(8,128)S(1)} fusion(f32[2,2,400,400]{3,2,0,1:T(8,128)} %convolution_bitcast_fusion.1), kind=kLoop, calls=%fused_computation.43 | loop fusion | flops 160000 | bytes 1920000 | tf_op jit(solution)/shard_map/sub | solution.py:28
  9.9 1.1 convert_element_type.187
  11.0 7.3 %all-to-all-start = ((bf16[32,1,2525]{2,1,0:T(2,128)(2,1)}), bf16[32,1,2525]{2,1,0:T(2,128)(2,1)S(1)}, u32[]{:S(2)}, u32[]{:S(2)}) async-start(bf16[32,1,2525]{2,1,0:T(2,128)(2,1)} %convert_element_type.187), calls=%async_computation | async-start | bytes 655360 | tf_op jit(solution)/shard_map/all_to_all | solution.py:148
  21.0 9.5 %all-to-all-done = bf16[32,1,2525]{2,1,0:T(2,128)(2,1)S(1)} async-done(((bf16[32,1,2525]{2,1,0:T(2,128)(2,1)}), bf16[32,1,2525]{2,1,0:T(2,128)(2,1)S(1)}, u32[]{:S(2)}, u32[]{:S(2)}) %all-to-all-start) | async-done | bytes 161632 | tf_op jit(solution)/shard_map/all_to_all | solution.py:148
  31.4 3.5 %all-to-all-start.1 = ((bf16[8,2,12928]{2,1,0:T(2,128)(2,1)}), bf16[8,2,12928]{2,1,0:T(2,128)(2,1)S(1)}, u32[]{:S(2)}, u32[]{:S(2)}) async-start(bf16[8,2,12928]{2,1,0:T(2,128)(2,1)} %all_to_all.26), calls=%async_computation.1 | async-start | bytes 827392 | tf_op jit(solution)/shard_map/all_to_all | solution.py:150
  38.3 8.5 %all-to-all-done.1 = bf16[8,2,12928]{2,1,0:T(2,128)(2,1)S(1)} async-done(((bf16[8,2,12928]{2,1,0:T(2,128)(2,1)}), bf16[8,2,12928]{2,1,0:T(2,128)(2,1)S(1)}, u32[]{:S(2)}, u32[]{:S(2)}) %all-to-all-start.1) | async-done | bytes 413728 | tf_op jit(solution)/shard_map/all_to_all | solution.py:150
  48.4 1.2 %slice.194 = f32[16,16,799]{2,0,1:T(8,128)} slice(f32[16,16,800]{2,0,1:T(8,128)S(1)} %fusion.32), slice={[0:16], [0:16], [1:800]} | slice | bytes 1636352 | tf_op jit(solution)/shard_map/jit(_roll_static)/slice | solution.py:64
  50.6 3.8 %all-to-all-start.2 = ((bf16[32,1,2525]{2,1,0:T(2,128)(2,1)}), bf16[32,1,2525]{2,1,0:T(2,128)(2,1)S(1)}, u32[]{:S(2)}, u32[]{:S(2)}) async-start(bf16[32,1,2525]{2,1,0:T(2,128)(2,1)} %broadcast_in_dim.91), calls=%async_computation.2 | async-start | bytes 655360 | tf_op jit(solution)/shard_map/all_to_all | solution.py:82
  54.6 1.6 %reshape.403 = f32[16,16,800]{2,1,0:T(8,128)} reshape(f32[16,12800]{1,0:T(8,128)S(1)} %slice_convert_fusion) | data formatting | bytes 1638400 | tf_op jit(solution)/shard_map/convert_element_type | solution.py:181
  58.2 2.7 %negate_convert_fusion.1 = (bf16[16,16,400]{2,0,1:T(8,128)(2,1)S(1)}, f32[16,16,400]{2,0,1:T(8,128)}) fusion(f32[16]{0:T(128)S(1)} %get-tuple-element.35, s32[400]{0:T(512)S(1)} %fusion.59, s32[16,16]{0,1:T(8,128)S(1)} %fusion.47), kind=kLoop, calls=%fused_computation.60 | loop fusion | flops 819200 | bytes 617088 | tf_op jit(solution)/shard_map/convert_element_type | solution.py:55
  61.0 5.3 %all-to-all-done.2 = bf16[32,1,2525]{2,1,0:T(2,128)(2,1)S(1)} async-done(((bf16[32,1,2525]{2,1,0:T(2,128)(2,1)}), bf16[32,1,2525]{2,1,0:T(2,128)(2,1)S(1)}, u32[]{:S(2)}, u32[]{:S(2)}) %all-to-all-start.2) | async-done | bytes 161632 | tf_op jit(solution)/shard_map/all_to_all | solution.py:82
  66.3 1.0 reduce.4
  68.1 1.3 %reverse.2 = f32[200,512]{1,0:T(8,128)S(1)} reverse(f32[200,512]{1,0:T(8,128)S(1)} %bitcast.103), dimensions={0,1} | reverse | bytes 819200
  70.3 0.9 copy-done.7
  71.5 2.0 %gather_fusion = f32[256,800]{1,0:T(8,128)} fusion(f32[400,800]{1,0:T(8,128)S(1)} %pad_maximum_fusion.1, s32[1024]{0:T(1024)S(1)} %pad_clamp_fusion), kind=kCustom, calls=%fused_computation | custom fusion | bytes 1639424 | tf_op jit(solution)/shard_map/gather | solution.py:179
  73.5 2.2 %copy_divide_fusion = f32[16,16,800]{2,0,1:T(8,128)S(1)} fusion(f32[16,16,800]{2,1,0:T(8,128)} %bitcast.99, f32[16,16,800]{2,1,0:T(8,128)} %reshape.403, bf16[16,16,400]{2,0,1:T(8,128)(2,1)S(1)} %get-tuple-element.31), kind=kLoop, calls=%fused_computation.26 | loop fusion | flops 1228800 | bytes 2662400 | tf_op jit(solution)/shard_map/div | solution.py:181
  77.3 2.3 %fusion.11 = (bf16[16,16,800]{2,0,1:T(8,128)(2,1)S(1)}, f32[16,16,800]{2,0,1:T(8,128)}) fusion(f32[16,16,1]{2,0,1:T(8,128)S(1)} %get-tuple-element.24, f32[16,16,799]{2,0,1:T(8,128)S(1)} %copy-done.5, f32[16,16,800]{2,0,1:T(8,128)S(1)} %fusion.32, f32[16]{0:T(128)} %get-tuple-element.17, f32[16,16]{0,1:T(8,128)} %bitcast.106, f32[16,16]{0,1:T(8,128)} %bitcast.107, ...), kind=kLoop, calls=%fused_computation.25 | loop fusion | flops 2867200 | bytes 4513088 | tf_op jit(solution)/shard_map/convert_element_type | solution.py:166
  80.5 3.6 %all-to-all-start.3 = ((bf16[16,16,800]{2,1,0:T(8,128)(2,1)}), bf16[16,16,800]{2,1,0:T(8,128)(2,1)S(1)}, u32[]{:S(2)}, u32[]{:S(2)}) async-start(bf16[16,16,800]{2,1,0:T(8,128)(2,1)} %copy.133), calls=%async_computation.3 | async-start | bytes 917504 | tf_op jit(solution)/shard_map/all_to_all | solution.py:175
  84.2 3.7 %fusion.35 = f32[400,400]{1,0:T(8,128)} fusion(f32[]{:T(128)S(6)} %mul.153, s32[400]{0:T(512)S(1)} %copy-done.16), kind=kLoop, calls=%fused_computation.65 | loop fusion | flops 1120000 | bytes 641604 | tf_op jit(solution)/shard_map/convert_element_type | solution.py:216
  88.0 2.1 %fusion.31 = f32[16,16,400]{2,0,1:T(8,128)S(1)} fusion(f32[16,16,399]{2,0,1:T(8,128)S(1)} %bitcast.100, f32[16,16,1]{2,0,1:T(8,128)S(1)} %slice.189, f32[16]{0:T(128)S(1)} %copy-done.18, f32[16]{0:T(128)S(1)} %copy-done.23, f32[16]{0:T(128)S(1)} %copy-done.20, s32[400]{0:T(512)S(1)} %copy-done.16, s32[16,16]{0,1:T(8,128)S(1)} %copy-done.14), kind=kLoop, calls=%fused_computation.58 | loop fusion | flops 1228800 | bytes 822016 | tf_op jit(solution)/shard_map/add | solution.py:185
  91.2 5.8 %all-to-all-done.3 = bf16[16,16,800]{2,1,0:T(8,128)(2,1)S(1)} async-done(((bf16[16,16,800]{2,1,0:T(8,128)(2,1)}), bf16[16,16,800]{2,1,0:T(8,128)(2,1)S(1)}, u32[]{:S(2)}, u32[]{:S(2)}) %all-to-all-start.3) | async-done | bytes 409632 | tf_op jit(solution)/shard_map/all_to_all | solution.py:175
  97.0 1.0 copy.135
  98.0 3.7 %all-to-all-start.4 = ((bf16[4,2,32,1200]{3,2,1,0:T(8,128)(2,1)}), bf16[4,2,32,1200]{3,2,1,0:T(8,128)(2,1)S(1)}, u32[]{:S(2)}, u32[]{:S(2)}) async-start(bf16[4,2,32,1200]{3,2,1,0:T(8,128)(2,1)} %copy.135), calls=%async_computation.4 | async-start | bytes 1310720 | tf_op jit(solution)/shard_map/all_to_all | solution.py:195
  101.8 2.4 %reshape.401 = bf16[16,12800]{1,0:T(8,128)(2,1)} reshape(bf16[16,16,800]{2,1,0:T(8,128)(2,1)} %copy-done.10) | data formatting | bytes 819200 | tf_op jit(solution)/shard_map/reshape | solution.py:206
  104.1 1.9 %convolution_convert_fusion.1 = bf16[8,12800]{1,0:T(8,128)(2,1)} fusion(bf16[16,12800]{1,0:T(8,128)(2,1)} %reshape.401, s32[8]{0:T(128)S(1)} %copy-done.27), kind=kOutput, calls=%fused_computation.2 | convolution fusion | flops 3379328 | bytes 614432 | tf_op jit(solution)/shard_map/rs,sx->rx/dot_general | solution.py:205
  106.1 2.2 %reshape.402 = bf16[1,128,2,400]{3,2,1,0:T(2,128)(2,1)} reshape(bf16[8,12800]{1,0:T(8,128)(2,1)} %convolution_convert_fusion.1) | data formatting | bytes 409600 | tf_op jit(solution)/shard_map/reshape | solution.py:209
  108.3 1.0 copy.157
  109.4 2.5 %convolution_bitcast_fusion = f32[2,2,400,400]{3,2,1,0:T(8,128)S(1)} fusion(bf16[2,400,400]{2,1,0:T(8,128)(2,1)} %constant.70.clone, f32[1,400,400]{2,1,0:T(8,128)S(1)} %copy-done.2, f32[1,400,400]{2,1,0:T(8,128)S(1)} %copy-done.4, bf16[2,64,400]{2,1,0:T(8,128)(2,1)S(1)} %get-tuple-element.30, bf16[2,64,400]{2,1,0:T(8,128)(2,1)S(1)} %get-tuple-element.29, ...), kind=kOutput, calls=%fused_computation.4 | convolution fusion | flops 515520000 | bytes 5965600 | tf_op jit(solution)/shard_map/hyj,gmj->hgym/dot_general | solution.py:34
  113.6 0.9 fusion.14
  (136 shorter events, 19.1 us)
Async XLA Ops:
  7.8 10.6 %copy-start.1 = (f32[1,400,400]{2,1,0:T(8,128)}, f32[1,400,400]{2,1,0:T(8,128)S(1)}, u32[]{:S(2)}) copy-start(f32[1,400,400]{2,1,0:T(8,128)S(1)} %fusion.19) | copy-start | bytes 1920004
  9.6 8.7 %copy-start.3 = (f32[1,400,400]{2,1,0:T(8,128)}, f32[1,400,400]{2,1,0:T(8,128)S(1)}, u32[]{:S(2)}) copy-start(f32[1,400,400]{2,1,0:T(8,128)S(1)} %fusion.21) | copy-start | bytes 1920004
  11.0 19.4 %all-to-all-start = ((bf16[32,1,2525]{2,1,0:T(2,128)(2,1)}), bf16[32,1,2525]{2,1,0:T(2,128)(2,1)S(1)}, u32[]{:S(2)}, u32[]{:S(2)}) async-start(bf16[32,1,2525]{2,1,0:T(2,128)(2,1)} %convert_element_type.187), calls=%async_computation | async-start | bytes 655360 | tf_op jit(solution)/shard_map/all_to_all | solution.py:148
  18.4 1.7 %copy-start.29 = (s32[1,8]{1,0:T(1,128)S(1)}, s32[1,8]{1,0:T(1,128)}, u32[]{:S(2)}) copy-start(s32[1,8]{1,0:T(1,128)} %param.13) | copy-start | bytes 100
  18.5 1.8 %copy-start.30 = (s32[1,8]{1,0:T(1,128)S(1)}, s32[1,8]{1,0:T(1,128)}, u32[]{:S(2)}) copy-start(s32[1,8]{1,0:T(1,128)} %param.14) | copy-start | bytes 100
  18.5 1.9 %copy-start.31 = (s32[1,8]{1,0:T(1,128)S(1)}, s32[1,8]{1,0:T(1,128)}, u32[]{:S(2)}) copy-start(s32[1,8]{1,0:T(1,128)} %param.15) | copy-start | bytes 100
  18.8 16.0 %copy-start.12 = (bf16[2,128,800]{1,2,0:T(8,128)(2,1)S(1)}, bf16[2,128,800]{1,2,0:T(8,128)(2,1)}, u32[]{:S(2)}) copy-start(bf16[2,128,800]{1,2,0:T(8,128)(2,1)} %param.16) | copy-start | bytes 1228804
  19.5 15.6 %copy-start.26 = (s32[8]{0:T(128)}, s32[8]{0:T(128)S(1)}, u32[]{:S(2)}) copy-start(s32[8]{0:T(128)S(1)} %multiply_add_fusion) | copy-start | bytes 100
  21.0 14.2 %copy-start.32 = (f32[64]{0:T(128)S(1)}, f32[64]{0:T(128)}, u32[]{:S(2)}) copy-start(f32[64]{0:T(128)} %param.11) | copy-start | bytes 772
  31.4 15.4 %all-to-all-start.1 = ((bf16[8,2,12928]{2,1,0:T(2,128)(2,1)}), bf16[8,2,12928]{2,1,0:T(2,128)(2,1)S(1)}, u32[]{:S(2)}, u32[]{:S(2)}) async-start(bf16[8,2,12928]{2,1,0:T(2,128)(2,1)} %all_to_all.26), calls=%async_computation.1 | async-start | bytes 827392 | tf_op jit(solution)/shard_map/all_to_all | solution.py:150
  37.0 21.2 %copy-start.15 = (s32[400]{0:T(512)}, s32[400]{0:T(512)S(1)}, u32[]{:S(2)}) copy-start(s32[400]{0:T(512)S(1)} %fusion.59) | copy-start | bytes 4804
  47.8 9.9 %copy-start.17 = (f32[16]{0:T(128)}, f32[16]{0:T(128)S(1)}, u32[]{:S(2)}) copy-start(f32[16]{0:T(128)S(1)} %get-tuple-element.18) | copy-start | bytes 196
  47.9 10.4 %copy-start.13 = (s32[16,16]{0,1:T(8,128)}, s32[16,16]{0,1:T(8,128)S(1)}, u32[]{:S(2)}) copy-start(s32[16,16]{0,1:T(8,128)S(1)} %fusion.47) | copy-start | bytes 3076
  50.6 15.7 %all-to-all-start.2 = ((bf16[32,1,2525]{2,1,0:T(2,128)(2,1)}), bf16[32,1,2525]{2,1,0:T(2,128)(2,1)S(1)}, u32[]{:S(2)}, u32[]{:S(2)}) async-start(bf16[32,1,2525]{2,1,0:T(2,128)(2,1)} %broadcast_in_dim.91), calls=%async_computation.2 | async-start | bytes 655360 | tf_op jit(solution)/shard_map/all_to_all | solution.py:82
  58.2 9.6 %copy-start.19 = (f32[16]{0:T(128)}, f32[16]{0:T(128)S(1)}, u32[]{:S(2)}) copy-start(f32[16]{0:T(128)S(1)} %get-tuple-element.35) | copy-start | bytes 196
  73.5 3.8 %copy-start.5 = (f32[16,16,799]{2,0,1:T(8,128)S(1)}, f32[16,16,799]{2,0,1:T(8,128)}, u32[]{:S(2)}) copy-start(f32[16,16,799]{2,0,1:T(8,128)} %slice.194) | copy-start | bytes 2454532
  79.6 4.5 %copy-start.16 = (s32[400]{0:T(512)S(1)}, s32[400]{0:T(512)}, u32[]{:S(2)}) copy-start(s32[400]{0:T(512)} %copy-done.15) | copy-start | bytes 4804
  79.6 8.3 %copy-start.9 = (f32[16,16,400]{2,0,1:T(8,128)S(1)}, f32[16,16,400]{2,0,1:T(8,128)}, u32[]{:S(2)}) copy-start(f32[16,16,400]{2,0,1:T(8,128)} %get-tuple-element.32) | copy-start | bytes 1228804
  79.6 8.4 %copy-start.14 = (s32[16,16]{0,1:T(8,128)S(1)}, s32[16,16]{0,1:T(8,128)}, u32[]{:S(2)}) copy-start(s32[16,16]{0,1:T(8,128)} %copy-done.13) | copy-start | bytes 3076
  79.6 8.4 %copy-start.18 = (f32[16]{0:T(128)S(1)}, f32[16]{0:T(128)}, u32[]{:S(2)}) copy-start(f32[16]{0:T(128)} %copy-done.17) | copy-start | bytes 196
  79.6 8.4 %copy-start.20 = (f32[16]{0:T(128)S(1)}, f32[16]{0:T(128)}, u32[]{:S(2)}) copy-start(f32[16]{0:T(128)} %copy-done.19) | copy-start | bytes 196
  79.6 8.4 %copy-start.23 = (f32[16]{0:T(128)S(1)}, f32[16]{0:T(128)}, u32[]{:S(2)}) copy-start(f32[16]{0:T(128)} %get-tuple-element.36) | copy-start | bytes 196
  80.5 9.6 %copy-start.6 = (f32[16,16,800]{2,0,1:T(8,128)S(1)}, f32[16,16,800]{2,0,1:T(8,128)}, u32[]{:S(2)}) copy-start(f32[16,16,800]{2,0,1:T(8,128)} %get-tuple-element.34) | copy-start | bytes 2457604
  80.5 9.6 %copy-start.22 = (s32[16]{0:T(128)S(1)}, s32[16]{0:T(128)}, u32[]{:S(2)}) copy-start(s32[16]{0:T(128)} %copy-done.21) | copy-start | bytes 196
  80.5 9.6 %copy-start.24 = (f32[16]{0:T(128)S(1)}, f32[16]{0:T(128)}, u32[]{:S(2)}) copy-start(f32[16]{0:T(128)} %get-tuple-element.17) | copy-start | bytes 196
  80.5 16.5 %all-to-all-start.3 = ((bf16[16,16,800]{2,1,0:T(8,128)(2,1)}), bf16[16,16,800]{2,1,0:T(8,128)(2,1)S(1)}, u32[]{:S(2)}, u32[]{:S(2)}) async-start(bf16[16,16,800]{2,1,0:T(8,128)(2,1)} %copy.133), calls=%async_computation.3 | async-start | bytes 917504 | tf_op jit(solution)/shard_map/all_to_all | solution.py:175
  97.0 7.1 %copy-start.27 = (s32[8]{0:T(128)S(1)}, s32[8]{0:T(128)}, u32[]{:S(2)}) copy-start(s32[8]{0:T(128)} %copy-done.26) | copy-start | bytes 100
  98.0 16.5 %all-to-all-start.4 = ((bf16[4,2,32,1200]{3,2,1,0:T(8,128)(2,1)}), bf16[4,2,32,1200]{3,2,1,0:T(8,128)(2,1)S(1)}, u32[]{:S(2)}, u32[]{:S(2)}) async-start(bf16[4,2,32,1200]{3,2,1,0:T(8,128)(2,1)} %copy.135), calls=%async_computation.4 | async-start | bytes 1310720 | tf_op jit(solution)/shard_map/all_to_all | solution.py:195
  101.7 7.6 %copy-start.2 = (f32[1,400,400]{2,1,0:T(8,128)S(1)}, f32[1,400,400]{2,1,0:T(8,128)}, u32[]{:S(2)}) copy-start(f32[1,400,400]{2,1,0:T(8,128)} %copy-done.1) | copy-start | bytes 1920004
  101.7 7.6 %copy-start.4 = (f32[1,400,400]{2,1,0:T(8,128)S(1)}, f32[1,400,400]{2,1,0:T(8,128)}, u32[]{:S(2)}) copy-start(f32[1,400,400]{2,1,0:T(8,128)} %copy-done.3) | copy-start | bytes 1920004
  101.8 7.6 %copy-start.8 = (f32[400,400]{1,0:T(8,128)S(1)}, f32[400,400]{1,0:T(8,128)}, u32[]{:S(2)}) copy-start(f32[400,400]{1,0:T(8,128)} %copy-done.7) | copy-start | bytes 1920004
  101.8 7.6 %copy-start.28 = (bf16[400]{0:T(512)(128)(2,1)S(1)}, bf16[400]{0:T(512)(128)(2,1)}, u32[]{:S(2)}) copy-start(bf16[400]{0:T(512)(128)(2,1)} %pad.10.clone) | copy-start | bytes 2404
  (6 other events, 6.1 us)

commit v5 on v3

--- a/solution.py
+++ b/solution.py
@@ -83,6 +83,24 @@
     half = back.reshape(rows, box_size)[: box_size // 2 + 1]
     mirrored = jnp.roll(half[1 : box_size // 2][::-1, ::-1], 1, axis=1)
     return jnp.concatenate([half, mirrored], axis=0)
+
+
+def shift_exchange(values, count, capacity, direction):
+    pieces = [values[:capacity]]
+    for d in range(1, count):
+        pairs = [(i, (i + direction * d) % count) for i in range(count)]
+        pieces.append(lax.ppermute(values[d * capacity : (d + 1) * capacity], "slab", pairs))
+    return jnp.concatenate(pieces, axis=0)
+
+
+def reduce_over_img(numerator, count):
+    me = lax.axis_index("img")
+    total = lax.dynamic_index_in_dim(numerator, me, 0, keepdims=False).astype(jnp.float32)
+    for d in range(1, count):
+        piece = lax.dynamic_index_in_dim(numerator, (me + d) % count, 0, keepdims=False)
+        pairs = [(i, (i + d) % count) for i in range(count)]
+        total = total + lax.ppermute(piece, "img", pairs).astype(jnp.float32)
+    return total
 
 
 def half_rows(box_size, device_count):
@@ -112,7 +130,8 @@
     )
     before = jnp.cumsum(member, axis=0) - member
     slot_rank = jnp.sum(member * before, axis=1)
-    seat_index = destination * capacity + slot_rank
+    me = lax.axis_index("slab")
+    seat_index = ((destination - me) % slab_count) * capacity + slot_rank
     seat_count = slab_count * capacity
     seat_pick = (seat_index[:, None] == jnp.arange(seat_count, dtype=jnp.int32)[None, :]).astype(
         jnp.bfloat16
@@ -146,8 +165,7 @@
     power_half = jnp.sum(low_half * low_half, axis=(0, 1))
     pieces = power_half.reshape(device_count, rows_half * box_size // device_count)
     gathered = lax.all_to_all(pieces, ("img", "slab"), 0, 0, tiled=True)
-    gathered, send = lax.optimization_barrier((gathered, send))
-    got = lax.all_to_all(send, "slab", 0, 0, tiled=True)
+    got = shift_exchange(send, slab_count, capacity, 1)
     got_blocks = got[:, : RB * 2 * box_size].reshape(seat_count, RB, 2 * box_size)
     got_info = got[:, RB * 2 * box_size : RB * 2 * box_size + 6].astype(jnp.int32)
 
@@ -166,13 +184,11 @@
     ).astype(jnp.bfloat16)
 
     total = jnp.sum(gathered, axis=0, keepdims=True)
-    total, got = lax.optimization_barrier((total, got))
     power = power_gather(total, device_count, rows_half, box_size)
     noise_level = jnp.sqrt(power / (particles * device_count) + 1e-06)
     level_both = jnp.concatenate([noise_level, noise_level], axis=1)
 
-    projected, power = lax.optimization_barrier((projected, power))
-    returned_rows = lax.all_to_all(projected, "slab", 0, 0, tiled=True)
+    returned_rows = shift_exchange(projected, slab_count, capacity, -1)
 
     got_rows = low_row_ids(got_info[:, 4], box_size)
     got_contrast = contrast_curve(lookup_defocus(got_info[:, 5], defocus), got_rows, box_size)
@@ -191,9 +207,7 @@
     share = vrows // img_count
     numerator = numerator.reshape(planes, img_count, share, 3 * box_size).astype(jnp.bfloat16)
     numerator = jnp.swapaxes(numerator, 0, 1)
-    numerator, returned_rows = lax.optimization_barrier((numerator, returned_rows))
-    parts = lax.all_to_all(numerator, "img", 0, 0, tiled=True)
-    volume_part = jnp.sum(parts.astype(jnp.float32), axis=0)
+    volume_part = reduce_over_img(numerator, img_count)
     weight_sum = volume_part[..., 2 * box_size :]
     reconstruction = volume_part[..., : 2 * box_size] / (
         jnp.concatenate([weight_sum, weight_sum], axis=-1) + 1.0

time: 115 us -> 116 us (level)
  waiting for transfers between devices: 26.6 us -> 10.4 us
  starting transfers between devices: 21.8 us -> 34.1 us
  local copies, waits for them, and re-layouts: 27.2 us -> 31.6 us
    ppermute x0 -> x17, starting transfers between devices: none -> 25.8 us  [the longest x14 25.2 us: shift_exchange(): lax.ppermute(values[d * capacity:(d + 1) * capacity], 'slab', pairs)]
    all_to_all x3 -> x0, waiting for transfers between devices: 14.3 us -> none  [the longest x1 8.48 us: body(): got = lax.all_to_all(send, 'slab', 0, 0, tiled=True)]
    all_to_all x3 -> x0, starting transfers between devices: 10.8 us -> none  [the longest x1 3.7 us: body(): parts = lax.all_to_all(numerator, 'img', 0, 0, tiled=True)]
    all_to_all x1, waiting for transfers between devices: 8.86 us -> 0.01 us  [body(): gathered = lax.all_to_all(pieces, ('img', 'slab'), 0, 0, tiled=True)]
    ppermute x0 -> x17, waiting for transfers between devices: none -> 4.9 us  [the longest x14 4.9 us: shift_exchange(): lax.ppermute(values[d * capacity:(d + 1) * capacity], 'slab', pairs)]
    concatenate x0 -> x3, local copies, waits for them, and re-layouts: none -> 4.63 us  [shift_exchange(): return jnp.concatenate(pieces, axis=0)]
    all_to_all x1, starting transfers between devices: 7.3 us -> 2.75 us  [body(): gathered = lax.all_to_all(pieces, ('img', 'slab'), 0, 0, tiled=True)]
    convert_element_type x2 -> x0, other arithmetic: 2.93 us -> none  [the longest x1 2.26 us: body(): projected = (((1.0 - blend_weight) * nearby + blend_weight * shift_halves...]
  transfers between devices with their start and end apart: 5 -> 19, of which waited for: 4 -> 5; matrix products, arithmetic and copies ran while one was open for 28% -> 31% of each run, Pallas kernels for 0% -> 0%
where the time goes in v5:
time: 116 us; the launch traced here: 115 us
  starting transfers between devices  34.1 us (29%)
  local copies, waits for them, and re-layouts  31.6 us (27%)
  other arithmetic  24.7 us (21%)
  matrix products  11.2 us (10%)
  waiting for transfers between devices  10.4 us (9%)
  between operations  2.59 us (2%)
    ppermute x14, starting transfers between devices, shift_exchange(): lax.ppermute(values[d * capacity:(d + 1) * capacity], 'slab', pairs)  25.2 us
    all_to_all x1, starting transfers between devices, power_gather(): back = lax.all_to_all(spread, ('img', 'slab'), 0, 0, tiled=True)  5.59 us
    all_to_all x1, waiting for transfers between devices, power_gather(): back = lax.all_to_all(spread, ('img', 'slab'), 0, 0, tiled=True)  5.52 us
    unnamed x59, local copies, waits for them, and re-layouts  4.91 us
    ppermute x14, waiting for transfers between devices, shift_exchange(): lax.ppermute(values[d * capacity:(d + 1) * capacity], 'slab', pairs)  4.9 us
    dot_general x1, matrix products, transform(): jnp.einsum('gky,hym->ghkm', tables, rowwise, preferred_element_type=jnp.f...  4.65 us
    concatenate x3, local copies, waits for them, and re-layouts, shift_exchange(): return jnp.concatenate(pieces, axis=0)  4.63 us
    convert_element_type x1, other arithmetic, body(): contrast.astype(jnp.float32)[:, None] * full_projection.astype(jnp.float32)  3.72 us
  transfers between devices with their start and end apart: 19, of which 5 were waited for; matrix products, arithmetic and copies ran while one was open for 31% of the time, Pallas kernels for 0%

profile of v5, /device:TPU:0, one launch (start us, length us, event | category | flops | bytes accessed | tf_op | source)
XLA Modules:
  0.0 114.7 jit_solution(13703837277708563766)
XLA Ops:
  1.6 4.6 %convolution_bitcast_fusion.1 = f32[2,2,400,400]{3,2,0,1:T(8,128)} fusion(bf16[2,400,400]{2,1,0:T(8,128)(2,1)} %constant.123.clone, bf16[1,400,400]{2,1,0:T(8,128)(2,1)S(1)} %copy-done), kind=kOutput, calls=%fused_computation.5 | convolution fusion | flops 768320000 | bytes 3520000 | tf_op jit(solution)/shard_map/gky,hym->ghkm/dot_general | solution.py:27
  6.3 1.6 %fusion.19 = f32[1,400,400]{2,1,0:T(8,128)S(1)} fusion(f32[2,2,400,400]{3,2,0,1:T(8,128)} %convolution_bitcast_fusion.1), kind=kLoop, calls=%fused_computation.39 | loop fusion | flops 320000 | bytes 1920000 | tf_op jit(solution)/shard_map/neg | solution.py:29
  7.9 1.8 %fusion.21 = f32[1,400,400]{2,1,0:T(8,128)S(1)} fusion(f32[2,2,400,400]{3,2,0,1:T(8,128)} %convolution_bitcast_fusion.1), kind=kLoop, calls=%fused_computation.42 | loop fusion | flops 160000 | bytes 1920000 | tf_op jit(solution)/shard_map/sub | solution.py:28
  13.1 3.0 %collective-permute-start = (bf16[2,12928]{1,0:T(2,128)(2,1)S(1)}, bf16[2,12928]{1,0:T(2,128)(2,1)S(1)}, u32[]{:S(2)}, u32[]{:S(2)}) collective-permute-start(bf16[2,12928]{1,0:T(2,128)(2,1)S(1)} %get-tuple-element.32), channel_id=1, source_target_pairs={{0,1},{1,2},{2,3},{3,4},{4,5},{5,6},{6,7},{7,0},{8,9},{9,10},{10,1... | collective-permute-start | bytes 155144 | tf_op jit(solution)/shard_map/ppermute | solution.py:92
  16.1 1.6 %collective-permute-start.1 = (bf16[2,12928]{1,0:T(2,128)(2,1)S(1)}, bf16[2,12928]{1,0:T(2,128)(2,1)S(1)}, u32[]{:S(2)}, u32[]{:S(2)}) collective-permute-start(bf16[2,12928]{1,0:T(2,128)(2,1)S(1)} %get-tuple-element.31), channel_id=1, source_target_pairs={{0,2},{1,3},{2,4},{3,5},{4,6},{5,7},{6,0},{7,1},{8,10},{9,11},{10,... | collective-permute-start | bytes 155144 | tf_op jit(solution)/shard_map/ppermute | solution.py:92
  17.7 2.6 %collective-permute-start.2 = (bf16[2,12928]{1,0:T(2,128)(2,1)S(1)}, bf16[2,12928]{1,0:T(2,128)(2,1)S(1)}, u32[]{:S(2)}, u32[]{:S(2)}) collective-permute-start(bf16[2,12928]{1,0:T(2,128)(2,1)S(1)} %get-tuple-element.30), channel_id=1, source_target_pairs={{0,3},{1,4},{2,5},{3,6},{4,7},{5,0},{6,1},{7,2},{8,11},{9,12},{10,... | collective-permute-start | bytes 155144 | tf_op jit(solution)/shard_map/ppermute | solution.py:92
  21.5 2.6 %collective-permute-start.4 = (bf16[2,12928]{1,0:T(2,128)(2,1)S(1)}, bf16[2,12928]{1,0:T(2,128)(2,1)S(1)}, u32[]{:S(2)}, u32[]{:S(2)}) collective-permute-start(bf16[2,12928]{1,0:T(2,128)(2,1)S(1)} %get-tuple-element.28), channel_id=1, source_target_pairs={{0,5},{1,6},{2,7},{3,0},{4,1},{5,2},{6,3},{7,4},{8,13},{9,14},{10,... | collective-permute-start | bytes 155144 | tf_op jit(solution)/shard_map/ppermute | solution.py:92
  24.4 1.4 %all_to_all.13 = f32[32,1,2525]{2,1,0:T(1,128)} reshape(f32[202,400]{1,0:T(8,128)S(1)} %fusion.12) | data formatting | bytes 646400 | tf_op jit(solution)/shard_map/all_to_all | solution.py:167
  25.8 2.8 %all-to-all-start = ((f32[32,1,2525]{2,1,0:T(1,128)}), f32[32,1,2525]{2,1,0:T(1,128)S(1)}, u32[]{:S(2)}, u32[]{:S(2)}) async-start(f32[32,1,2525]{2,1,0:T(1,128)} %all_to_all.13), calls=%async_computation | async-start | bytes 655360 | tf_op jit(solution)/shard_map/all_to_all | solution.py:167
  29.9 3.7 %fusion.37 = f32[400,400]{1,0:T(8,128)} fusion(f32[]{:T(128)S(6)} %mul.151, s32[400]{0:T(512)S(1)} %fusion.63), kind=kLoop, calls=%fused_computation.65 | loop fusion | flops 1120000 | bytes 641604 | tf_op jit(solution)/shard_map/convert_element_type | solution.py:230
  34.2 3.6 %collective-permute-start.5 = (bf16[2,12928]{1,0:T(2,128)(2,1)S(1)}, bf16[2,12928]{1,0:T(2,128)(2,1)S(1)}, u32[]{:S(2)}, u32[]{:S(2)}) collective-permute-start(bf16[2,12928]{1,0:T(2,128)(2,1)S(1)} %get-tuple-element.27), channel_id=1, source_target_pairs={{0,6},{1,7},{2,0},{3,1},{4,2},{5,3},{6,4},{7,5},{8,14},{9,15},{10,... | collective-permute-start | bytes 155144 | tf_op jit(solution)/shard_map/ppermute | solution.py:92
  37.9 1.4 %collective-permute-start.6 = (bf16[2,12928]{1,0:T(2,128)(2,1)S(1)}, bf16[2,12928]{1,0:T(2,128)(2,1)S(1)}, u32[]{:S(2)}, u32[]{:S(2)}) collective-permute-start(bf16[2,12928]{1,0:T(2,128)(2,1)S(1)} %get-tuple-element.26), channel_id=1, source_target_pairs={{0,7},{1,0},{2,1},{3,2},{4,3},{5,4},{6,5},{7,6},{8,15},{9,8},{10,9... | collective-permute-start | bytes 155144 | tf_op jit(solution)/shard_map/ppermute | solution.py:92
  42.0 2.9 %concatenate.72 = bf16[16,12928]{1,0:T(8,128)(2,1)S(1)} concatenate(bf16[2,12928]{1,0:T(2,128)(2,1)S(1)} %get-tuple-element.33, bf16[2,12928]{1,0:T(2,128)(2,1)S(1)} %collective-permute-done, bf16[2,12928]{1,0:T(2,128)(2,1)S(1)} %collective-permute-done.1, bf16[2,12928]{1,0:T(2,128)(2,1)} %copy-done.12, bf16[2,12928]{1,0:T(2,128)(2,1)} %copy-done.13, ...), dimensions={0} | concatenate | bytes 827392 | tf_op jit(solution)/shard_map/concatenate | solution.py:93
  45.6 2.7 %negate_convert_fusion.1 = (bf16[16,16,400]{2,0,1:T(8,128)(2,1)}, f32[16,16,400]{2,0,1:T(8,128)S(1)}) fusion(f32[16]{0:T(128)S(1)} %broadcast_multiply_fusion, s32[400]{0:T(512)S(1)} %fusion.63, s32[16,16]{0,1:T(8,128)S(1)} %fusion.51), kind=kLoop, calls=%fused_computation.60 | loop fusion | flops 819200 | bytes 617088 | tf_op jit(solution)/shard_map/convert_element_type | solution.py:55
  49.7 5.6 %all-to-all-start.1 = ((f32[32,1,2525]{2,1,0:T(1,128)}), f32[32,1,2525]{2,1,0:T(1,128)S(1)}, u32[]{:S(2)}, u32[]{:S(2)}) async-start(f32[32,1,2525]{2,1,0:T(1,128)} %broadcast_in_dim.91), calls=%async_computation.1 | async-start | bytes 655360 | tf_op jit(solution)/shard_map/all_to_all | solution.py:82
  55.4 1.6 %reshape.404 = f32[16,16,800]{2,1,0:T(8,128)} reshape(f32[16,12800]{1,0:T(8,128)S(1)} %slice_convert_fusion) | data formatting | bytes 1638400 | tf_op jit(solution)/shard_map/convert_element_type | solution.py:197
  58.9 2.8 %fusion.33 = f32[16,16,400]{2,0,1:T(8,128)} fusion(f32[16,16,399]{2,0,1:T(8,128)S(1)} %bitcast.106, f32[16,16,1]{2,0,1:T(8,128)S(1)} %slice.282, f32[16]{0:T(128)S(1)} %get-tuple-element.5, f32[16]{0:T(128)S(1)} %broadcast_subtract_fusion, f32[16]{0:T(128)S(1)} %broadcast_multiply_fusion, s32[400]{0:T(512)S(1)} %fusion.63, s32[16,16]{0,1:T(8,128)S(1)} %fusion.51), kind=kLoop, calls=%fused_computation.58 | loop fusion | flops 1228800 | bytes 822016 | tf_op jit(solution)/shard_map/add | solution.py:201
  61.7 5.5 %all-to-all-done.1 = f32[32,1,2525]{2,1,0:T(1,128)S(1)} async-done(((f32[32,1,2525]{2,1,0:T(1,128)}), f32[32,1,2525]{2,1,0:T(1,128)S(1)}, u32[]{:S(2)}, u32[]{:S(2)}) %all-to-all-start.1) | async-done | bytes 323232 | tf_op jit(solution)/shard_map/all_to_all | solution.py:82
  72.1 2.0 %gather_fusion = f32[256,800]{1,0:T(8,128)} fusion(f32[400,800]{1,0:T(8,128)S(1)} %pad_maximum_fusion.1, s32[1024]{0:T(1024)S(1)} %pad_clamp_fusion), kind=kCustom, calls=%fused_computation | custom fusion | bytes 1639424 | tf_op jit(solution)/shard_map/gather | solution.py:195
  74.2 2.2 %copy_divide_fusion = f32[16,16,800]{2,0,1:T(8,128)S(1)} fusion(f32[16,16,800]{2,1,0:T(8,128)} %bitcast.105, f32[16,16,800]{2,1,0:T(8,128)} %reshape.404, bf16[16,16,400]{2,0,1:T(8,128)(2,1)S(1)} %copy-done.9), kind=kLoop, calls=%fused_computation.25 | loop fusion | flops 1228800 | bytes 2662400 | tf_op jit(solution)/shard_map/div | solution.py:197
  77.1 1.7 %copy.92 = f32[16,16,1]{0,1,2:T(8,128)} copy(f32[16,16,1]{2,0,1:T(8,128)} %get-tuple-element.45) | data formatting | bytes 2048 | tf_op jit(solution)/shard_map/jit(_where)/broadcast_in_dim | solution.py:72
  81.1 1.4 %fusion.11 = (f32[16,16,800]{2,0,1:T(8,128)S(1)}, bf16[16,16,800]{2,0,1:T(8,128)(2,1)S(1)}) fusion(f32[16,16,799]{2,0,1:T(8,128)S(1)} %bitcast.103, f32[16,16,1]{2,0,1:T(8,128)S(1)} %get-tuple-element.10, f32[16,16,800]{2,0,1:T(8,128)S(1)} %copy_divide_fusion, f32[16,16]{0,1:T(8,128)} %bitcast.115, f32[16,16]{0,1:T(8,128)} %bitcast.114, f32[16]{0:T(128)} %copy-done.20, ...), kind=kLoop, calls=%fused_computation.24 | loop fusion | flops 2867200 | bytes 4513088 | tf_op jit(solution)/shard_map/add | solution.py:198
  82.9 2.3 %collective-permute-start.11 = (bf16[2,16,800]{2,0,1:T(2,128)(2,1)S(1)}, bf16[2,16,800]{2,0,1:T(2,128)(2,1)S(1)}, u32[]{:S(2)}, u32[]{:S(2)}) collective-permute-start(bf16[2,16,800]{2,0,1:T(2,128)(2,1)S(1)} %get-tuple-element.20), channel_id=1, source_target_pairs={{0,3},{1,4},{2,5},{3,6},{4,7},{5,0},{6,1},{7,2},{8,11},{9,12},{10,... | collective-permute-start | bytes 153608 | tf_op jit(solution)/shard_map/ppermute | solution.py:92
  86.3 1.5 %collective-permute-start.12 = (bf16[2,16,800]{2,0,1:T(2,128)(2,1)S(1)}, bf16[2,16,800]{2,0,1:T(2,128)(2,1)S(1)}, u32[]{:S(2)}, u32[]{:S(2)}) collective-permute-start(bf16[2,16,800]{2,0,1:T(2,128)(2,1)S(1)} %get-tuple-element.19), channel_id=1, source_target_pairs={{0,2},{1,3},{2,4},{3,5},{4,6},{5,7},{6,0},{7,1},{8,10},{9,11},{10,... | collective-permute-start | bytes 153608 | tf_op jit(solution)/shard_map/ppermute | solution.py:92
  87.8 1.4 %collective-permute-start.13 = (bf16[2,16,800]{2,0,1:T(2,128)(2,1)S(1)}, bf16[2,16,800]{2,0,1:T(2,128)(2,1)S(1)}, u32[]{:S(2)}, u32[]{:S(2)}) collective-permute-start(bf16[2,16,800]{2,0,1:T(2,128)(2,1)S(1)} %get-tuple-element.18), channel_id=1, source_target_pairs={{0,1},{1,2},{2,3},{3,4},{4,5},{5,6},{6,7},{7,0},{8,9},{9,10},{10,1... | collective-permute-start | bytes 153608 | tf_op jit(solution)/shard_map/ppermute | solution.py:92
  89.2 3.4 %collective-permute-start.7 = (bf16[2,16,800]{2,0,1:T(2,128)(2,1)S(1)}, bf16[2,16,800]{2,0,1:T(2,128)(2,1)S(1)}, u32[]{:S(2)}, u32[]{:S(2)}) collective-permute-start(bf16[2,16,800]{2,0,1:T(2,128)(2,1)S(1)} %get-tuple-element.24), channel_id=1, source_target_pairs={{0,7},{1,0},{2,1},{3,2},{4,3},{5,4},{6,5},{7,6},{8,15},{9,8},{10,9... | collective-permute-start | bytes 153608 | tf_op jit(solution)/shard_map/ppermute | solution.py:92
  93.9 1.5 %collective-permute-done.13 = bf16[2,16,800]{2,0,1:T(2,128)(2,1)S(1)} collective-permute-done((bf16[2,16,800]{2,0,1:T(2,128)(2,1)S(1)}, bf16[2,16,800]{2,0,1:T(2,128)(2,1)S(1)}, u32[]{:S(2)}, u32[]{:S(2)}) %collective-permute-start.13) | collective-permute-done | bytes 51232 | tf_op jit(solution)/shard_map/ppermute | solution.py:92
  96.7 1.4 %collective-permute-done.9 = bf16[2,16,800]{2,0,1:T(2,128)(2,1)S(1)} collective-permute-done((bf16[2,16,800]{2,0,1:T(2,128)(2,1)S(1)}, bf16[2,16,800]{2,0,1:T(2,128)(2,1)S(1)}, u32[]{:S(2)}, u32[]{:S(2)}) %collective-permute-start.9) | collective-permute-done | bytes 51232 | tf_op jit(solution)/shard_map/ppermute | solution.py:92
  99.9 2.4 %reshape.402 = bf16[16,12800]{1,0:T(8,128)(2,1)} reshape(bf16[16,16,800]{2,1,0:T(8,128)(2,1)} %copy.77) | data formatting | bytes 819200 | tf_op jit(solution)/shard_map/reshape | solution.py:220
  102.3 1.9 %convolution_convert_fusion.1 = bf16[8,12800]{1,0:T(8,128)(2,1)} fusion(bf16[16,12800]{1,0:T(8,128)(2,1)} %reshape.402, s32[8]{0:T(128)S(1)} %copy-done.19), kind=kOutput, calls=%fused_computation.2 | convolution fusion | flops 3379328 | bytes 614432 | tf_op jit(solution)/shard_map/rs,sx->rx/dot_general | solution.py:219
  104.2 2.2 %reshape.403 = bf16[1,128,2,400]{3,2,1,0:T(2,128)(2,1)} reshape(bf16[8,12800]{1,0:T(8,128)(2,1)} %convolution_convert_fusion.1) | data formatting | bytes 409600 | tf_op jit(solution)/shard_map/reshape | solution.py:223
  107.5 2.5 %convolution_bitcast_fusion = f32[2,2,400,400]{3,2,1,0:T(8,128)S(1)} fusion(bf16[2,400,400]{2,1,0:T(8,128)(2,1)} %constant.123.clone, f32[1,400,400]{2,1,0:T(8,128)S(1)} %copy-done.2, f32[1,400,400]{2,1,0:T(8,128)S(1)} %copy-done.4, bf16[2,64,400]{2,1,0:T(8,128)(2,1)S(1)} %get-tuple-element.35, bf16[2,64,400]{2,1,0:T(8,128)(2,1)S(1)} %get-tuple-element.34, ...), kind=kOutput, calls=%fused_computation.4 | convolution fusion | flops 515520000 | bytes 5965600 | tf_op jit(solution)/shard_map/hyj,gmj->hgym/dot_general | solution.py:34
  (152 shorter events, 32.5 us)
Async XLA Ops:
  7.8 16.3 %copy-start.1 = (f32[1,400,400]{2,1,0:T(8,128)}, f32[1,400,400]{2,1,0:T(8,128)S(1)}, u32[]{:S(2)}) copy-start(f32[1,400,400]{2,1,0:T(8,128)S(1)} %fusion.19) | copy-start | bytes 1920004
  9.7 14.4 %copy-start.3 = (f32[1,400,400]{2,1,0:T(8,128)}, f32[1,400,400]{2,1,0:T(8,128)S(1)}, u32[]{:S(2)}) copy-start(f32[1,400,400]{2,1,0:T(8,128)S(1)} %fusion.21) | copy-start | bytes 1920004
  13.1 21.1 %collective-permute-start = (bf16[2,12928]{1,0:T(2,128)(2,1)S(1)}, bf16[2,12928]{1,0:T(2,128)(2,1)S(1)}, u32[]{:S(2)}, u32[]{:S(2)}) collective-permute-start(bf16[2,12928]{1,0:T(2,128)(2,1)S(1)} %get-tuple-element.32), channel_id=1, source_target_pairs={{0,1},{1,2},{2,3},{3,4},{4,5},{5,6},{6,7},{7,0},{8,9},{9,10},{10,1... | collective-permute-start | bytes 155144 | tf_op jit(solution)/shard_map/ppermute | solution.py:92
  16.1 21.7 %collective-permute-start.1 = (bf16[2,12928]{1,0:T(2,128)(2,1)S(1)}, bf16[2,12928]{1,0:T(2,128)(2,1)S(1)}, u32[]{:S(2)}, u32[]{:S(2)}) collective-permute-start(bf16[2,12928]{1,0:T(2,128)(2,1)S(1)} %get-tuple-element.31), channel_id=1, source_target_pairs={{0,2},{1,3},{2,4},{3,5},{4,6},{5,7},{6,0},{7,1},{8,10},{9,11},{10,... | collective-permute-start | bytes 155144 | tf_op jit(solution)/shard_map/ppermute | solution.py:92
  17.7 23.0 %collective-permute-start.2 = (bf16[2,12928]{1,0:T(2,128)(2,1)S(1)}, bf16[2,12928]{1,0:T(2,128)(2,1)S(1)}, u32[]{:S(2)}, u32[]{:S(2)}) collective-permute-start(bf16[2,12928]{1,0:T(2,128)(2,1)S(1)} %get-tuple-element.30), channel_id=1, source_target_pairs={{0,3},{1,4},{2,5},{3,6},{4,7},{5,0},{6,1},{7,2},{8,11},{9,12},{10,... | collective-permute-start | bytes 155144 | tf_op jit(solution)/shard_map/ppermute | solution.py:92
  20.3 20.5 %collective-permute-start.3 = (bf16[2,12928]{1,0:T(2,128)(2,1)S(1)}, bf16[2,12928]{1,0:T(2,128)(2,1)S(1)}, u32[]{:S(2)}, u32[]{:S(2)}) collective-permute-start(bf16[2,12928]{1,0:T(2,128)(2,1)S(1)} %get-tuple-element.29), channel_id=1, source_target_pairs={{0,4},{1,5},{2,6},{3,7},{4,0},{5,1},{6,2},{7,3},{8,12},{9,13},{10,... | collective-permute-start | bytes 155144 | tf_op jit(solution)/shard_map/ppermute | solution.py:92
  21.5 19.3 %collective-permute-start.4 = (bf16[2,12928]{1,0:T(2,128)(2,1)S(1)}, bf16[2,12928]{1,0:T(2,128)(2,1)S(1)}, u32[]{:S(2)}, u32[]{:S(2)}) collective-permute-start(bf16[2,12928]{1,0:T(2,128)(2,1)S(1)} %get-tuple-element.28), channel_id=1, source_target_pairs={{0,5},{1,6},{2,7},{3,0},{4,1},{5,2},{6,3},{7,4},{8,13},{9,14},{10,... | collective-permute-start | bytes 155144 | tf_op jit(solution)/shard_map/ppermute | solution.py:92
  24.3 4.3 %copy-start.27 = (f32[64]{0:T(128)S(1)}, f32[64]{0:T(128)}, u32[]{:S(2)}) copy-start(f32[64]{0:T(128)} %param.11) | copy-start | bytes 772
  24.3 15.5 %copy-start.11 = (bf16[2,128,800]{1,2,0:T(8,128)(2,1)S(1)}, bf16[2,128,800]{1,2,0:T(8,128)(2,1)}, u32[]{:S(2)}) copy-start(bf16[2,128,800]{1,2,0:T(8,128)(2,1)} %param.16) | copy-start | bytes 1228804
  25.8 22.8 %all-to-all-start = ((f32[32,1,2525]{2,1,0:T(1,128)}), f32[32,1,2525]{2,1,0:T(1,128)S(1)}, u32[]{:S(2)}, u32[]{:S(2)}) async-start(f32[32,1,2525]{2,1,0:T(1,128)} %all_to_all.13), calls=%async_computation | async-start | bytes 655360 | tf_op jit(solution)/shard_map/all_to_all | solution.py:167
  34.2 6.5 %collective-permute-start.5 = (bf16[2,12928]{1,0:T(2,128)(2,1)S(1)}, bf16[2,12928]{1,0:T(2,128)(2,1)S(1)}, u32[]{:S(2)}, u32[]{:S(2)}) collective-permute-start(bf16[2,12928]{1,0:T(2,128)(2,1)S(1)} %get-tuple-element.27), channel_id=1, source_target_pairs={{0,6},{1,7},{2,0},{3,1},{4,2},{5,3},{6,4},{7,5},{8,14},{9,15},{10,... | collective-permute-start | bytes 155144 | tf_op jit(solution)/shard_map/ppermute | solution.py:92
  37.9 4.1 %collective-permute-start.6 = (bf16[2,12928]{1,0:T(2,128)(2,1)S(1)}, bf16[2,12928]{1,0:T(2,128)(2,1)S(1)}, u32[]{:S(2)}, u32[]{:S(2)}) collective-permute-start(bf16[2,12928]{1,0:T(2,128)(2,1)S(1)} %get-tuple-element.26), channel_id=1, source_target_pairs={{0,7},{1,0},{2,1},{3,2},{4,3},{5,4},{6,5},{7,6},{8,15},{9,8},{10,9... | collective-permute-start | bytes 155144 | tf_op jit(solution)/shard_map/ppermute | solution.py:92
  45.2 4.5 %copy-start.16 = (s32[16]{0:T(128)}, s32[16]{0:T(128)S(1)}, u32[]{:S(2)}) copy-start(s32[16]{0:T(128)S(1)} %get-tuple-element.3) | copy-start | bytes 196
  49.7 17.6 %all-to-all-start.1 = ((f32[32,1,2525]{2,1,0:T(1,128)}), f32[32,1,2525]{2,1,0:T(1,128)S(1)}, u32[]{:S(2)}, u32[]{:S(2)}) async-start(f32[32,1,2525]{2,1,0:T(1,128)} %broadcast_in_dim.91), calls=%async_computation.1 | async-start | bytes 655360 | tf_op jit(solution)/shard_map/all_to_all | solution.py:82
  58.9 9.8 %copy-start.20 = (f32[16]{0:T(128)}, f32[16]{0:T(128)S(1)}, u32[]{:S(2)}) copy-start(f32[16]{0:T(128)S(1)} %get-tuple-element.5) | copy-start | bytes 196
  58.9 9.8 %copy-start.22 = (f32[16]{0:T(128)}, f32[16]{0:T(128)S(1)}, u32[]{:S(2)}) copy-start(f32[16]{0:T(128)S(1)} %broadcast_subtract_fusion) | copy-start | bytes 196
  74.2 6.9 %copy-start.5 = (f32[16,16,799]{2,0,1:T(8,128)S(1)}, f32[16,16,799]{2,0,1:T(8,128)}, u32[]{:S(2)}) copy-start(f32[16,16,799]{2,0,1:T(8,128)} %slice.258) | copy-start | bytes 2454532
  82.8 9.8 %collective-permute-start.10 = (bf16[2,16,800]{2,0,1:T(2,128)(2,1)S(1)}, bf16[2,16,800]{2,0,1:T(2,128)(2,1)S(1)}, u32[]{:S(2)}, u32[]{:S(2)}) collective-permute-start(bf16[2,16,800]{2,0,1:T(2,128)(2,1)S(1)} %get-tuple-element.21), channel_id=1, source_target_pairs={{0,4},{1,5},{2,6},{3,7},{4,0},{5,1},{6,2},{7,3},{8,12},{9,13},{10,... | collective-permute-start | bytes 153608 | tf_op jit(solution)/shard_map/ppermute | solution.py:92
  82.9 10.2 %collective-permute-start.11 = (bf16[2,16,800]{2,0,1:T(2,128)(2,1)S(1)}, bf16[2,16,800]{2,0,1:T(2,128)(2,1)S(1)}, u32[]{:S(2)}, u32[]{:S(2)}) collective-permute-start(bf16[2,16,800]{2,0,1:T(2,128)(2,1)S(1)} %get-tuple-element.20), channel_id=1, source_target_pairs={{0,3},{1,4},{2,5},{3,6},{4,7},{5,0},{6,1},{7,2},{8,11},{9,12},{10,... | collective-permute-start | bytes 153608 | tf_op jit(solution)/shard_map/ppermute | solution.py:92
  86.3 7.6 %collective-permute-start.12 = (bf16[2,16,800]{2,0,1:T(2,128)(2,1)S(1)}, bf16[2,16,800]{2,0,1:T(2,128)(2,1)S(1)}, u32[]{:S(2)}, u32[]{:S(2)}) collective-permute-start(bf16[2,16,800]{2,0,1:T(2,128)(2,1)S(1)} %get-tuple-element.19), channel_id=1, source_target_pairs={{0,2},{1,3},{2,4},{3,5},{4,6},{5,7},{6,0},{7,1},{8,10},{9,11},{10,... | collective-permute-start | bytes 153608 | tf_op jit(solution)/shard_map/ppermute | solution.py:92
  87.8 7.6 %collective-permute-start.13 = (bf16[2,16,800]{2,0,1:T(2,128)(2,1)S(1)}, bf16[2,16,800]{2,0,1:T(2,128)(2,1)S(1)}, u32[]{:S(2)}, u32[]{:S(2)}) collective-permute-start(bf16[2,16,800]{2,0,1:T(2,128)(2,1)S(1)} %get-tuple-element.18), channel_id=1, source_target_pairs={{0,1},{1,2},{2,3},{3,4},{4,5},{5,6},{6,7},{7,0},{8,9},{9,10},{10,1... | collective-permute-start | bytes 153608 | tf_op jit(solution)/shard_map/ppermute | solution.py:92
  89.2 6.8 %collective-permute-start.7 = (bf16[2,16,800]{2,0,1:T(2,128)(2,1)S(1)}, bf16[2,16,800]{2,0,1:T(2,128)(2,1)S(1)}, u32[]{:S(2)}, u32[]{:S(2)}) collective-permute-start(bf16[2,16,800]{2,0,1:T(2,128)(2,1)S(1)} %get-tuple-element.24), channel_id=1, source_target_pairs={{0,7},{1,0},{2,1},{3,2},{4,3},{5,4},{6,5},{7,6},{8,15},{9,8},{10,9... | collective-permute-start | bytes 153608 | tf_op jit(solution)/shard_map/ppermute | solution.py:92
  92.6 4.2 %collective-permute-start.8 = (bf16[2,16,800]{2,0,1:T(2,128)(2,1)S(1)}, bf16[2,16,800]{2,0,1:T(2,128)(2,1)S(1)}, u32[]{:S(2)}, u32[]{:S(2)}) collective-permute-start(bf16[2,16,800]{2,0,1:T(2,128)(2,1)S(1)} %get-tuple-element.23), channel_id=1, source_target_pairs={{0,6},{1,7},{2,0},{3,1},{4,2},{5,3},{6,4},{7,5},{8,14},{9,15},{10,... | collective-permute-start | bytes 153608 | tf_op jit(solution)/shard_map/ppermute | solution.py:92
  93.1 5.1 %collective-permute-start.9 = (bf16[2,16,800]{2,0,1:T(2,128)(2,1)S(1)}, bf16[2,16,800]{2,0,1:T(2,128)(2,1)S(1)}, u32[]{:S(2)}, u32[]{:S(2)}) collective-permute-start(bf16[2,16,800]{2,0,1:T(2,128)(2,1)S(1)} %get-tuple-element.22), channel_id=1, source_target_pairs={{0,5},{1,6},{2,7},{3,0},{4,1},{5,2},{6,3},{7,4},{8,13},{9,14},{10,... | collective-permute-start | bytes 153608 | tf_op jit(solution)/shard_map/ppermute | solution.py:92
  93.1 9.2 %copy-start.19 = (s32[8]{0:T(128)S(1)}, s32[8]{0:T(128)}, u32[]{:S(2)}) copy-start(s32[8]{0:T(128)} %copy-done.18) | copy-start | bytes 100
  93.9 18.7 %collective-permute-start.14 = (bf16[2,32,1200]{2,1,0:T(8,128)(2,1)}, bf16[2,32,1200]{2,1,0:T(8,128)(2,1)}, u32[]{:S(2)}, u32[]{:S(2)}) collective-permute-start(bf16[2,32,1200]{2,1,0:T(8,128)(2,1)} %get-tuple-element.15), channel_id=1, source_target_pairs={{0,8},{8,16},{16,24},{24,0},{1,9},{9,17},{17,25},{25,1},{2,10},{10... | collective-permute-start | bytes 460808 | tf_op jit(solution)/shard_map/ppermute | solution.py:102
  95.5 17.2 %collective-permute-start.15 = (bf16[2,32,1200]{2,1,0:T(8,128)(2,1)}, bf16[2,32,1200]{2,1,0:T(8,128)(2,1)}, u32[]{:S(2)}, u32[]{:S(2)}) collective-permute-start(bf16[2,32,1200]{2,1,0:T(8,128)(2,1)} %get-tuple-element.17), channel_id=1, source_target_pairs={{0,16},{8,24},{16,0},{24,8},{1,17},{9,25},{17,1},{25,9},{2,18},{10... | collective-permute-start | bytes 460808 | tf_op jit(solution)/shard_map/ppermute | solution.py:102
  96.0 16.6 %collective-permute-start.16 = (bf16[2,32,1200]{2,1,0:T(8,128)(2,1)}, bf16[2,32,1200]{2,1,0:T(8,128)(2,1)}, u32[]{:S(2)}, u32[]{:S(2)}) collective-permute-start(bf16[2,32,1200]{2,1,0:T(8,128)(2,1)} %get-tuple-element.16), channel_id=1, source_target_pairs={{0,24},{8,0},{16,8},{24,16},{1,25},{9,1},{17,9},{25,17},{2,26},{10... | collective-permute-start | bytes 460808 | tf_op jit(solution)/shard_map/ppermute | solution.py:102
  99.9 7.6 %copy-start.2 = (f32[1,400,400]{2,1,0:T(8,128)S(1)}, f32[1,400,400]{2,1,0:T(8,128)}, u32[]{:S(2)}) copy-start(f32[1,400,400]{2,1,0:T(8,128)} %copy-done.1) | copy-start | bytes 1920004
  99.9 7.6 %copy-start.4 = (f32[1,400,400]{2,1,0:T(8,128)S(1)}, f32[1,400,400]{2,1,0:T(8,128)}, u32[]{:S(2)}) copy-start(f32[1,400,400]{2,1,0:T(8,128)} %copy-done.3) | copy-start | bytes 1920004
  99.9 7.6 %copy-start.7 = (f32[400,400]{1,0:T(8,128)S(1)}, f32[400,400]{1,0:T(8,128)}, u32[]{:S(2)}) copy-start(f32[400,400]{1,0:T(8,128)} %copy-done.6) | copy-start | bytes 1920004
  99.9 7.6 %copy-start.23 = (bf16[400]{0:T(512)(128)(2,1)S(1)}, bf16[400]{0:T(512)(128)(2,1)}, u32[]{:S(2)}) copy-start(bf16[400]{0:T(512)(128)(2,1)} %pad.20.clone) | copy-start | bytes 2404
  (15 other events, 28.1 us)

commit v6 on v5

--- a/solution.py
+++ b/solution.py
@@ -175,12 +175,14 @@
         jnp.bfloat16
     )
     blend_weight = ((got_info[:, 3].astype(jnp.float32) + 0.5) / WL)[:, None, None]
-    volume_slots = volume.reshape(slots, RB, 2 * box_size)
+    volume_slots = volume.reshape(planes, row_blocks, RB, 2, box_size)
+    volume_slots = jnp.transpose(volume_slots, (0, 1, 3, 2, 4)).reshape(slots, 2, RB, box_size)
     nearby = jnp.einsum(
-        "sq,qrx->srx", slot_pick, volume_slots, preferred_element_type=jnp.float32
-    )
+        "sq,qhix->shix", slot_pick, volume_slots, preferred_element_type=jnp.float32
+    )
+    blend_4 = blend_weight[:, :, :, None]
     projected = (
-        ((1.0 - blend_weight) * nearby + blend_weight * shift_halves(nearby, -1, box_size)) * live
+        ((1.0 - blend_4) * nearby + blend_4 * jnp.roll(nearby, -1, axis=-1)) * live[..., None]
     ).astype(jnp.bfloat16)
 
     total = jnp.sum(gathered, axis=0, keepdims=True)
@@ -192,7 +194,15 @@
 
     got_rows = low_row_ids(got_info[:, 4], box_size)
     got_contrast = contrast_curve(lookup_defocus(got_info[:, 5], defocus), got_rows, box_size)
-    got_level = level_both[got_rows]
+    level_low = jnp.concatenate(
+        [level_both[:low_rows], level_both[box_size - low_rows :]], axis=0
+    ).reshape(blocks_per, RB, 2 * box_size)
+    block_pick = (got_info[:, 4:5] == jnp.arange(blocks_per, dtype=jnp.int32)[None, :]).astype(
+        jnp.float32
+    )
+    got_level = jnp.einsum(
+        "sj,jix->six", block_pick, level_low, precision=HI, preferred_element_type=jnp.float32
+    )
     got_contrast_both = jnp.concatenate([got_contrast, got_contrast], axis=-1).astype(jnp.float32)
     received = got_contrast_both * got_blocks.astype(jnp.float32) / got_level
     inserted = (1.0 - blend_weight) * received + blend_weight * shift_halves(received, 1, box_size)
@@ -217,11 +227,10 @@
     row_all = jnp.arange(box_size, dtype=jnp.int32)[None, :]
     contrast = contrast_curve(lookup_defocus(micrograph, defocus), row_all, box_size)
     own_rows = jnp.einsum(
-        "rs,sx->rx", seat_pick, returned_rows.reshape(seat_count, RB * 2 * box_size),
-        preferred_element_type=jnp.float32,
-    ).astype(jnp.bfloat16)
-    own_rows = own_rows.reshape(particles, 2 * low_rows, 2, box_size)
-    own_rows = jnp.moveaxis(own_rows, 2, 1)
+        "rs,shix->rhix", seat_pick, returned_rows, preferred_element_type=jnp.float32
+    ).astype(jnp.bfloat16)
+    own_rows = own_rows.reshape(particles, blocks_per, 2, RB, box_size)
+    own_rows = jnp.moveaxis(own_rows, 2, 1).reshape(particles, 2, 2 * low_rows, box_size)
     middle = jnp.zeros((particles, 2, box_size - 2 * low_rows, box_size), jnp.bfloat16)
     full_projection = jnp.concatenate(
         [own_rows[:, :, :low_rows], middle, own_rows[:, :, low_rows:]], axis=2

time: 116 us -> 109 us (0.940)
  waiting for transfers between devices: 10.4 us -> 5.15 us
  local copies, waits for them, and re-layouts: 31.6 us -> 27.2 us
  starting transfers between devices: 34.1 us -> 37.8 us
  matrix products: 11.2 us -> 9.21 us
    all_to_all x1, waiting for transfers between devices: 5.52 us -> 0.01 us  [power_gather(): back = lax.all_to_all(spread, ('img', 'slab'), 0, 0, tiled=True)]
    reshape x3 -> x1, local copies, waits for them, and re-layouts: 5.57 us -> 0.51 us  [body(): volume_slots = volume.reshape(planes, row_blocks, RB, 2, box_size)]
    ppermute x14, starting transfers between devices: 25.2 us -> 28.2 us  [shift_exchange(): lax.ppermute(values[d * capacity:(d + 1) * capacity], 'slab', pairs)]
    ppermute x3, waiting for transfers between devices: 0.01 us -> 2.93 us  [reduce_over_img(): total = total + lax.ppermute(piece, 'img', pairs).astype(jnp.float32)]
    ppermute x14, waiting for transfers between devices: 4.9 us -> 2.22 us  [shift_exchange(): lax.ppermute(values[d * capacity:(d + 1) * capacity], 'slab', pairs)]
    ppermute x3, starting transfers between devices: 0.57 us -> 3.01 us  [reduce_over_img(): total = total + lax.ppermute(piece, 'img', pairs).astype(jnp.float32)]
    broadcast_in_dim x2 -> x0, local copies, waits for them, and re-layouts: 2.41 us -> none  [the longest x1 1.65 us: shift_halves(): return jnp.where(column == 2 * box_size - 1, second, rolled)]
    all_to_all x1, starting transfers between devices: 5.59 us -> 3.3 us  [power_gather(): back = lax.all_to_all(spread, ('img', 'slab'), 0, 0, tiled=True)]
  transfers between devices with their start and end apart: 19 -> 19, of which waited for: 5 -> 4; matrix products, arithmetic and copies ran while one was open for 31% -> 29% of each run, Pallas kernels for 0% -> 0%
where the time goes in v6:
time: 109 us; the launch traced here: 107 us
  starting transfers between devices  37.8 us (35%)
  local copies, waits for them, and re-layouts  27.2 us (25%)
  other arithmetic  25.2 us (23%)
  matrix products  9.21 us (8%)
  waiting for transfers between devices  5.15 us (5%)
  between operations  2.62 us (2%)
    ppermute x14, starting transfers between devices, shift_exchange(): lax.ppermute(values[d * capacity:(d + 1) * capacity], 'slab', pairs)  28.2 us
    concatenate x2, local copies, waits for them, and re-layouts, shift_exchange(): return jnp.concatenate(pieces, axis=0)  5.94 us
    unnamed x73, local copies, waits for them, and re-layouts  5.64 us
    dot_general x1, matrix products, transform(): jnp.einsum('gky,hym->ghkm', tables, rowwise, preferred_element_type=jnp.f...  4.52 us
    convert_element_type x1, other arithmetic, body(): contrast.astype(jnp.float32)[:, None] * full_projection.astype(jnp.float32)  3.71 us
    all_to_all x1, starting transfers between devices, power_gather(): back = lax.all_to_all(spread, ('img', 'slab'), 0, 0, tiled=True)  3.3 us
    all_to_all x1, starting transfers between devices, body(): gathered = lax.all_to_all(pieces, ('img', 'slab'), 0, 0, tiled=True)  3.29 us
    ppermute x3, starting transfers between devices, reduce_over_img(): total = total + lax.ppermute(piece, 'img', pairs).astype(jnp.float32)  3.01 us
  transfers between devices with their start and end apart: 19, of which 4 were waited for; matrix products, arithmetic and copies ran while one was open for 29% of the time, Pallas kernels for 0%

profile of v6, /device:TPU:0, one launch (start us, length us, event | category | flops | bytes accessed | tf_op | source)
XLA Modules:
  0.0 107.1 jit_solution(5030308928548019773)
XLA Ops:
  1.6 4.5 %convolution_bitcast_fusion.1 = f32[2,2,400,400]{3,2,0,1:T(8,128)} fusion(bf16[2,400,400]{2,1,0:T(8,128)(2,1)} %constant.119.clone, bf16[1,400,400]{2,1,0:T(8,128)(2,1)S(1)} %copy-done), kind=kOutput, calls=%fused_computation.3 | convolution fusion | flops 768320000 | bytes 3520000 | tf_op jit(solution)/shard_map/gky,hym->ghkm/dot_general | solution.py:27
  6.2 1.6 %fusion.18 = f32[1,400,400]{2,1,0:T(8,128)S(1)} fusion(f32[2,2,400,400]{3,2,0,1:T(8,128)} %convolution_bitcast_fusion.1), kind=kLoop, calls=%fused_computation.36 | loop fusion | flops 320000 | bytes 1920000 | tf_op jit(solution)/shard_map/neg | solution.py:29
  7.7 1.5 %fusion.20 = f32[1,400,400]{2,1,0:T(8,128)S(1)} fusion(f32[2,2,400,400]{3,2,0,1:T(8,128)} %convolution_bitcast_fusion.1), kind=kLoop, calls=%fused_computation.39 | loop fusion | flops 160000 | bytes 1920000 | tf_op jit(solution)/shard_map/sub | solution.py:28
  12.9 2.9 %collective-permute-start = (bf16[2,12928]{1,0:T(2,128)(2,1)S(1)}, bf16[2,12928]{1,0:T(2,128)(2,1)S(1)}, u32[]{:S(2)}, u32[]{:S(2)}) collective-permute-start(bf16[2,12928]{1,0:T(2,128)(2,1)S(1)} %get-tuple-element.31), channel_id=1, source_target_pairs={{0,1},{1,2},{2,3},{3,4},{4,5},{5,6},{6,7},{7,0},{8,9},{9,10},{10,1... | collective-permute-start | bytes 155144 | tf_op jit(solution)/shard_map/ppermute | solution.py:92
  15.8 1.6 %collective-permute-start.1 = (bf16[2,12928]{1,0:T(2,128)(2,1)S(1)}, bf16[2,12928]{1,0:T(2,128)(2,1)S(1)}, u32[]{:S(2)}, u32[]{:S(2)}) collective-permute-start(bf16[2,12928]{1,0:T(2,128)(2,1)S(1)} %get-tuple-element.30), channel_id=1, source_target_pairs={{0,2},{1,3},{2,4},{3,5},{4,6},{5,7},{6,0},{7,1},{8,10},{9,11},{10,... | collective-permute-start | bytes 155144 | tf_op jit(solution)/shard_map/ppermute | solution.py:92
  17.4 2.6 %collective-permute-start.2 = (bf16[2,12928]{1,0:T(2,128)(2,1)}, bf16[2,12928]{1,0:T(2,128)(2,1)}, u32[]{:S(2)}, u32[]{:S(2)}) collective-permute-start(bf16[2,12928]{1,0:T(2,128)(2,1)} %get-tuple-element.29), channel_id=1, source_target_pairs={{0,3},{1,4},{2,5},{3,6},{4,7},{5,0},{6,1},{7,2},{8,11},{9,12},{10,... | collective-permute-start | bytes 155144 | tf_op jit(solution)/shard_map/ppermute | solution.py:92
  20.0 1.2 %collective-permute-start.3 = (bf16[2,12928]{1,0:T(2,128)(2,1)}, bf16[2,12928]{1,0:T(2,128)(2,1)}, u32[]{:S(2)}, u32[]{:S(2)}) collective-permute-start(bf16[2,12928]{1,0:T(2,128)(2,1)} %get-tuple-element.28), channel_id=1, source_target_pairs={{0,4},{1,5},{2,6},{3,7},{4,0},{5,1},{6,2},{7,3},{8,12},{9,13},{10,... | collective-permute-start | bytes 155144 | tf_op jit(solution)/shard_map/ppermute | solution.py:92
  21.2 2.6 %collective-permute-start.4 = (bf16[2,12928]{1,0:T(2,128)(2,1)}, bf16[2,12928]{1,0:T(2,128)(2,1)}, u32[]{:S(2)}, u32[]{:S(2)}) collective-permute-start(bf16[2,12928]{1,0:T(2,128)(2,1)} %get-tuple-element.27), channel_id=1, source_target_pairs={{0,5},{1,6},{2,7},{3,0},{4,1},{5,2},{6,3},{7,4},{8,13},{9,14},{10,... | collective-permute-start | bytes 155144 | tf_op jit(solution)/shard_map/ppermute | solution.py:92
  24.1 1.4 %all_to_all.13 = f32[32,1,2525]{2,1,0:T(1,128)} reshape(f32[202,400]{1,0:T(8,128)S(1)} %fusion.11) | data formatting | bytes 646400 | tf_op jit(solution)/shard_map/all_to_all | solution.py:167
  25.5 3.3 %all-to-all-start = ((f32[32,1,2525]{2,1,0:T(1,128)}), f32[32,1,2525]{2,1,0:T(1,128)}, u32[]{:S(2)}, u32[]{:S(2)}) async-start(f32[32,1,2525]{2,1,0:T(1,128)} %all_to_all.13), calls=%async_computation | async-start | bytes 655360 | tf_op jit(solution)/shard_map/all_to_all | solution.py:167
  30.0 3.7 %fusion.38 = f32[400,400]{1,0:T(8,128)} fusion(f32[]{:T(128)S(6)} %mul.155, s32[400]{0:T(512)S(1)} %fusion.69), kind=kLoop, calls=%fused_computation.68 | loop fusion | flops 1120000 | bytes 641604 | tf_op jit(solution)/shard_map/convert_element_type | solution.py:239
  33.7 3.6 %collective-permute-start.5 = (bf16[2,12928]{1,0:T(2,128)(2,1)}, bf16[2,12928]{1,0:T(2,128)(2,1)}, u32[]{:S(2)}, u32[]{:S(2)}) collective-permute-start(bf16[2,12928]{1,0:T(2,128)(2,1)} %get-tuple-element.26), channel_id=1, source_target_pairs={{0,6},{1,7},{2,0},{3,1},{4,2},{5,3},{6,4},{7,5},{8,14},{9,15},{10,... | collective-permute-start | bytes 155144 | tf_op jit(solution)/shard_map/ppermute | solution.py:92
  37.3 1.4 %collective-permute-start.6 = (bf16[2,12928]{1,0:T(2,128)(2,1)S(1)}, bf16[2,12928]{1,0:T(2,128)(2,1)}, u32[]{:S(2)}, u32[]{:S(2)}) collective-permute-start(bf16[2,12928]{1,0:T(2,128)(2,1)S(1)} %get-tuple-element.25), channel_id=1, source_target_pairs={{0,7},{1,0},{2,1},{3,2},{4,3},{5,4},{6,5},{7,6},{8,15},{9,8},{10,9... | collective-permute-start | bytes 155144 | tf_op jit(solution)/shard_map/ppermute | solution.py:92
  41.5 3.5 %concatenate.75 = bf16[16,12928]{1,0:T(8,128)(2,1)} concatenate(bf16[2,12928]{1,0:T(2,128)(2,1)S(1)} %get-tuple-element.32, bf16[2,12928]{1,0:T(2,128)(2,1)S(1)} %collective-permute-done, bf16[2,12928]{1,0:T(2,128)(2,1)} %copy-done.12, bf16[2,12928]{1,0:T(2,128)(2,1)} %collective-permute-done.2, bf16[2,12928]{1,0:T(2,128)(2,1)} %collective-permute-done.3, ...), dimensions={0} | concatenate | bytes 827392 | tf_op jit(solution)/shard_map/concatenate | solution.py:93
  50.4 4.7 %collective-permute-start.11 = (bf16[2,2,16,400]{3,0,2,1:T(2,128)(2,1)S(1)}, bf16[2,2,16,400]{3,0,2,1:T(2,128)(2,1)S(1)}, u32[]{:S(2)}, u32[]{:S(2)}) collective-permute-start(bf16[2,2,16,400]{3,0,2,1:T(2,128)(2,1)S(1)} %get-tuple-element.19), channel_id=1, source_target_pairs={{0,3},{1,4},{2,5},{3,6},{4,7},{5,0},{6,1},{7,2},{8,11},{9,12},{10,... | collective-permute-start | bytes 153608 | tf_op jit(solution)/shard_map/ppermute | solution.py:92
  57.1 3.3 %all-to-all-start.1 = ((f32[32,1,2525]{2,1,0:T(1,128)}), f32[32,1,2525]{2,1,0:T(1,128)}, u32[]{:S(2)}, u32[]{:S(2)}) async-start(f32[32,1,2525]{2,1,0:T(1,128)} %broadcast_in_dim.44), calls=%async_computation.1 | async-start | bytes 655360 | tf_op jit(solution)/shard_map/all_to_all | solution.py:82
  60.4 2.7 %negate_convert_fusion.1 = (bf16[16,16,400]{2,0,1:T(8,128)(2,1)}, f32[16,16,400]{2,0,1:T(8,128)S(1)}) fusion(f32[16]{0:T(128)S(1)} %get-tuple-element.37, s32[400]{0:T(512)S(1)} %copy-done.14, s32[16,16]{0,1:T(8,128)S(1)} %fusion.52), kind=kLoop, calls=%fused_computation.59 | loop fusion | flops 819200 | bytes 617088 | tf_op jit(solution)/shard_map/convert_element_type | solution.py:55
  63.2 1.7 %collective-permute-start.12 = (bf16[2,2,16,400]{3,0,2,1:T(2,128)(2,1)}, bf16[2,2,16,400]{3,0,2,1:T(2,128)(2,1)}, u32[]{:S(2)}, u32[]{:S(2)}) collective-permute-start(bf16[2,2,16,400]{3,0,2,1:T(2,128)(2,1)} %get-tuple-element.18), channel_id=1, source_target_pairs={{0,2},{1,3},{2,4},{3,5},{4,6},{5,7},{6,0},{7,1},{8,10},{9,11},{10,... | collective-permute-start | bytes 153608 | tf_op jit(solution)/shard_map/ppermute | solution.py:92
  64.9 1.5 %collective-permute-start.13 = (bf16[2,2,16,400]{3,0,2,1:T(2,128)(2,1)}, bf16[2,2,16,400]{3,0,2,1:T(2,128)(2,1)}, u32[]{:S(2)}, u32[]{:S(2)}) collective-permute-start(bf16[2,2,16,400]{3,0,2,1:T(2,128)(2,1)} %get-tuple-element.17), channel_id=1, source_target_pairs={{0,1},{1,2},{2,3},{3,4},{4,5},{5,6},{6,7},{7,0},{8,9},{9,10},{10,1... | collective-permute-start | bytes 153608 | tf_op jit(solution)/shard_map/ppermute | solution.py:92
  66.4 3.2 %collective-permute-start.7 = (bf16[2,2,16,400]{3,0,2,1:T(2,128)(2,1)}, bf16[2,2,16,400]{3,0,2,1:T(2,128)(2,1)}, u32[]{:S(2)}, u32[]{:S(2)}) collective-permute-start(bf16[2,2,16,400]{3,0,2,1:T(2,128)(2,1)} %get-tuple-element.23), channel_id=1, source_target_pairs={{0,7},{1,0},{2,1},{3,2},{4,3},{5,4},{6,5},{7,6},{8,15},{9,8},{10,9... | collective-permute-start | bytes 153608 | tf_op jit(solution)/shard_map/ppermute | solution.py:92
  70.8 2.8 %fusion.32 = f32[16,16,400]{2,0,1:T(8,128)S(1)} fusion(f32[16,16,399]{2,0,1:T(8,128)S(1)} %bitcast.112, f32[16,16,1]{2,0,1:T(8,128)S(1)} %slice.283, f32[16]{0:T(128)} %copy-done.15, f32[16]{0:T(128)} %copy-done.17, f32[16]{0:T(128)} %copy-done.19, s32[400]{0:T(512)} %copy-done.13, s32[16,16]{0,1:T(8,128)S(1)} %fusion.52), kind=kLoop, calls=%fused_computation.55 | loop fusion | flops 1228800 | bytes 822016 | tf_op jit(solution)/shard_map/add | solution.py:211
  73.7 1.6 %reshape.389 = f32[16,16,800]{2,1,0:T(8,128)} reshape(f32[16,12800]{1,0:T(8,128)S(1)} %slice_convert_fusion) | data formatting | bytes 1638400 | tf_op jit(solution)/shard_map/convert_element_type | solution.py:207
  75.2 1.4 %collective-permute-done.9 = bf16[2,2,16,400]{3,0,2,1:T(2,128)(2,1)} collective-permute-done((bf16[2,2,16,400]{3,0,2,1:T(2,128)(2,1)S(1)}, bf16[2,2,16,400]{3,0,2,1:T(2,128)(2,1)}, u32[]{:S(2)}, u32[]{:S(2)}) %collective-permute-start.9) | collective-permute-done | bytes 51232 | tf_op jit(solution)/shard_map/ppermute | solution.py:92
  76.7 2.4 %concatenate.77 = bf16[16,2,16,400]{3,0,2,1:T(8,128)(2,1)S(1)} concatenate(bf16[2,2,16,400]{3,0,2,1:T(2,128)(2,1)S(1)} %get-tuple-element.24, bf16[2,2,16,400]{3,0,2,1:T(2,128)(2,1)} %collective-permute-done.7, bf16[2,2,16,400]{3,0,2,1:T(2,128)(2,1)} %collective-permute-done.8, bf16[2,2,16,400]{3,0,2,1:T(2,128)(2,1)} %collective-permute-done.9, ...), dimensions={0} | concatenate | bytes 819200 | tf_op jit(solution)/shard_map/concatenate | solution.py:93
  80.2 1.8 %reduce.3 = f32[32,2525]{1,0:T(8,128)S(1)} reduce(f32[32,1,2525]{2,1,0:T(1,128)} %all-to-all-done.1, f32[]{:T(128)} %constant.129), dimensions={1}, to_apply=%all_to_all.12.reduce_sub_computation | reduce | bytes 646404 | tf_op jit(solution)/shard_map/all_to_all | solution.py:82
  83.2 3.1 %reverse.2 = f32[200,512]{1,0:T(8,128)} reverse(f32[200,512]{1,0:T(8,128)S(1)} %bitcast.116), dimensions={0,1} | reverse | bytes 819200
  87.5 1.7 %slice.188 = f32[199,1]{1,0:T(8,128)} reverse(f32[199,1]{1,0:T(8,128)} %slice.242), dimensions={0,1} | reverse | bytes 1592 | tf_op jit(solution)/shard_map/jit(_roll_static)/slice | solution.py:84
  89.2 1.3 %fusion.22 = f32[400,400]{1,0:T(8,128)S(1)} fusion(f32[199,399]{1,0:T(8,128)S(1)} %slice.352, f32[199,1]{1,0:T(8,128)} %slice.188, f32[201,400]{1,0:T(8,128)S(1)} %bitcast.111), kind=kLoop, calls=%fused_computation.43 | loop fusion | flops 640000 | bytes 1280000 | tf_op jit(solution)/shard_map/sqrt | solution.py:190
  94.5 1.3 %fusion.10 = f32[16,16,800]{2,0,1:T(8,128)S(1)} fusion(f32[16,16,799]{2,0,1:T(8,128)S(1)} %bitcast.110, f32[16,16,1]{2,0,1:T(8,128)} %get-tuple-element.11, f32[16,16,800]{2,0,1:T(8,128)S(1)} %convolution_divide_fusion, f32[16,16]{0,1:T(8,128)S(1)} %bitcast.120, f32[16,16]{0,1:T(8,128)S(1)} %bitcast.119, f32[16]{0:T(128)S(1)} %copy-done.16, ...), kind=kLoop, calls=%fused_computation.22 | loop fusion | flops 1228800 | bytes 2461376 | tf_op jit(solution)/shard_map/add | solution.py:208
  97.1 1.6 %collective-permute-start.15 = (bf16[2,32,1200]{2,1,0:T(8,128)(2,1)S(1)}, bf16[2,32,1200]{2,1,0:T(8,128)(2,1)S(1)}, u32[]{:S(2)}, u32[]{:S(2)}) collective-permute-start(bf16[2,32,1200]{2,1,0:T(8,128)(2,1)S(1)} %get-tuple-element.16), channel_id=1, source_target_pairs={{0,16},{8,24},{16,0},{24,8},{1,17},{9,25},{17,1},{25,9},{2,18},{10... | collective-permute-start | bytes 460808 | tf_op jit(solution)/shard_map/ppermute | solution.py:102
  98.7 1.4 %collective-permute-start.16 = (bf16[2,32,1200]{2,1,0:T(8,128)(2,1)S(1)}, bf16[2,32,1200]{2,1,0:T(8,128)(2,1)S(1)}, u32[]{:S(2)}, u32[]{:S(2)}) collective-permute-start(bf16[2,32,1200]{2,1,0:T(8,128)(2,1)S(1)} %get-tuple-element.15), channel_id=1, source_target_pairs={{0,24},{8,0},{16,8},{24,16},{1,25},{9,1},{17,9},{25,17},{2,26},{10... | collective-permute-start | bytes 460808 | tf_op jit(solution)/shard_map/ppermute | solution.py:102
  104.2 1.9 %collective-permute-done.16 = bf16[2,32,1200]{2,1,0:T(8,128)(2,1)S(1)} collective-permute-done((bf16[2,32,1200]{2,1,0:T(8,128)(2,1)S(1)}, bf16[2,32,1200]{2,1,0:T(8,128)(2,1)S(1)}, u32[]{:S(2)}, u32[]{:S(2)}) %collective-permute-start.16) | collective-permute-done | bytes 153632 | tf_op jit(solution)/shard_map/ppermute | solution.py:102
  (158 shorter events, 29.8 us)
Async XLA Ops:
  11.4 12.4 %copy-start.21 = (s32[8]{0:T(128)}, s32[8]{0:T(128)S(1)}, u32[]{:S(2)}) copy-start(s32[8]{0:T(128)S(1)} %fusion.75) | copy-start | bytes 100
  12.9 20.8 %collective-permute-start = (bf16[2,12928]{1,0:T(2,128)(2,1)S(1)}, bf16[2,12928]{1,0:T(2,128)(2,1)S(1)}, u32[]{:S(2)}, u32[]{:S(2)}) collective-permute-start(bf16[2,12928]{1,0:T(2,128)(2,1)S(1)} %get-tuple-element.31), channel_id=1, source_target_pairs={{0,1},{1,2},{2,3},{3,4},{4,5},{5,6},{6,7},{7,0},{8,9},{9,10},{10,1... | collective-permute-start | bytes 155144 | tf_op jit(solution)/shard_map/ppermute | solution.py:92
  15.8 21.4 %collective-permute-start.1 = (bf16[2,12928]{1,0:T(2,128)(2,1)S(1)}, bf16[2,12928]{1,0:T(2,128)(2,1)S(1)}, u32[]{:S(2)}, u32[]{:S(2)}) collective-permute-start(bf16[2,12928]{1,0:T(2,128)(2,1)S(1)} %get-tuple-element.30), channel_id=1, source_target_pairs={{0,2},{1,3},{2,4},{3,5},{4,6},{5,7},{6,0},{7,1},{8,10},{9,11},{10,... | collective-permute-start | bytes 155144 | tf_op jit(solution)/shard_map/ppermute | solution.py:92
  17.4 23.3 %collective-permute-start.2 = (bf16[2,12928]{1,0:T(2,128)(2,1)}, bf16[2,12928]{1,0:T(2,128)(2,1)}, u32[]{:S(2)}, u32[]{:S(2)}) collective-permute-start(bf16[2,12928]{1,0:T(2,128)(2,1)} %get-tuple-element.29), channel_id=1, source_target_pairs={{0,3},{1,4},{2,5},{3,6},{4,7},{5,0},{6,1},{7,2},{8,11},{9,12},{10,... | collective-permute-start | bytes 155144 | tf_op jit(solution)/shard_map/ppermute | solution.py:92
  20.0 20.7 %collective-permute-start.3 = (bf16[2,12928]{1,0:T(2,128)(2,1)}, bf16[2,12928]{1,0:T(2,128)(2,1)}, u32[]{:S(2)}, u32[]{:S(2)}) collective-permute-start(bf16[2,12928]{1,0:T(2,128)(2,1)} %get-tuple-element.28), channel_id=1, source_target_pairs={{0,4},{1,5},{2,6},{3,7},{4,0},{5,1},{6,2},{7,3},{8,12},{9,13},{10,... | collective-permute-start | bytes 155144 | tf_op jit(solution)/shard_map/ppermute | solution.py:92
  21.2 19.5 %collective-permute-start.4 = (bf16[2,12928]{1,0:T(2,128)(2,1)}, bf16[2,12928]{1,0:T(2,128)(2,1)}, u32[]{:S(2)}, u32[]{:S(2)}) collective-permute-start(bf16[2,12928]{1,0:T(2,128)(2,1)} %get-tuple-element.27), channel_id=1, source_target_pairs={{0,5},{1,6},{2,7},{3,0},{4,1},{5,2},{6,3},{7,4},{8,13},{9,14},{10,... | collective-permute-start | bytes 155144 | tf_op jit(solution)/shard_map/ppermute | solution.py:92
  24.0 4.8 %copy-start.34 = (f32[64]{0:T(128)S(1)}, f32[64]{0:T(128)}, u32[]{:S(2)}) copy-start(f32[64]{0:T(128)} %param.11) | copy-start | bytes 772
  24.0 15.2 %copy-start.6 = (bf16[2,128,800]{1,2,0:T(8,128)(2,1)S(1)}, bf16[2,128,800]{1,2,0:T(8,128)(2,1)}, u32[]{:S(2)}) copy-start(bf16[2,128,800]{1,2,0:T(8,128)(2,1)} %param.16) | copy-start | bytes 1228804
  25.5 29.6 %all-to-all-start = ((f32[32,1,2525]{2,1,0:T(1,128)}), f32[32,1,2525]{2,1,0:T(1,128)}, u32[]{:S(2)}, u32[]{:S(2)}) async-start(f32[32,1,2525]{2,1,0:T(1,128)} %all_to_all.13), calls=%async_computation | async-start | bytes 655360 | tf_op jit(solution)/shard_map/all_to_all | solution.py:167
  28.8 10.4 %copy-start.13 = (s32[400]{0:T(512)}, s32[400]{0:T(512)S(1)}, u32[]{:S(2)}) copy-start(s32[400]{0:T(512)S(1)} %fusion.69) | copy-start | bytes 4804
  33.7 7.0 %collective-permute-start.5 = (bf16[2,12928]{1,0:T(2,128)(2,1)}, bf16[2,12928]{1,0:T(2,128)(2,1)}, u32[]{:S(2)}, u32[]{:S(2)}) collective-permute-start(bf16[2,12928]{1,0:T(2,128)(2,1)} %get-tuple-element.26), channel_id=1, source_target_pairs={{0,6},{1,7},{2,0},{3,1},{4,2},{5,3},{6,4},{7,5},{8,14},{9,15},{10,... | collective-permute-start | bytes 155144 | tf_op jit(solution)/shard_map/ppermute | solution.py:92
  37.3 4.2 %collective-permute-start.6 = (bf16[2,12928]{1,0:T(2,128)(2,1)S(1)}, bf16[2,12928]{1,0:T(2,128)(2,1)}, u32[]{:S(2)}, u32[]{:S(2)}) collective-permute-start(bf16[2,12928]{1,0:T(2,128)(2,1)S(1)} %get-tuple-element.25), channel_id=1, source_target_pairs={{0,7},{1,0},{2,1},{3,2},{4,3},{5,4},{6,5},{7,6},{8,15},{9,8},{10,9... | collective-permute-start | bytes 155144 | tf_op jit(solution)/shard_map/ppermute | solution.py:92
  48.9 11.5 %copy-start.19 = (f32[16]{0:T(128)}, f32[16]{0:T(128)S(1)}, u32[]{:S(2)}) copy-start(f32[16]{0:T(128)S(1)} %get-tuple-element.37) | copy-start | bytes 196
  49.3 11.2 %copy-start.14 = (s32[400]{0:T(512)S(1)}, s32[400]{0:T(512)}, u32[]{:S(2)}) copy-start(s32[400]{0:T(512)} %copy-done.13) | copy-start | bytes 4804
  50.4 19.3 %collective-permute-start.10 = (bf16[2,2,16,400]{3,0,2,1:T(2,128)(2,1)S(1)}, bf16[2,2,16,400]{3,0,2,1:T(2,128)(2,1)S(1)}, u32[]{:S(2)}, u32[]{:S(2)}) collective-permute-start(bf16[2,2,16,400]{3,0,2,1:T(2,128)(2,1)S(1)} %get-tuple-element.20), channel_id=1, source_target_pairs={{0,4},{1,5},{2,6},{3,7},{4,0},{5,1},{6,2},{7,3},{8,12},{9,13},{10,... | collective-permute-start | bytes 153608 | tf_op jit(solution)/shard_map/ppermute | solution.py:92
  50.4 19.7 %collective-permute-start.11 = (bf16[2,2,16,400]{3,0,2,1:T(2,128)(2,1)S(1)}, bf16[2,2,16,400]{3,0,2,1:T(2,128)(2,1)S(1)}, u32[]{:S(2)}, u32[]{:S(2)}) collective-permute-start(bf16[2,2,16,400]{3,0,2,1:T(2,128)(2,1)S(1)} %get-tuple-element.19), channel_id=1, source_target_pairs={{0,3},{1,4},{2,5},{3,6},{4,7},{5,0},{6,1},{7,2},{8,11},{9,12},{10,... | collective-permute-start | bytes 153608 | tf_op jit(solution)/shard_map/ppermute | solution.py:92
  57.1 23.1 %all-to-all-start.1 = ((f32[32,1,2525]{2,1,0:T(1,128)}), f32[32,1,2525]{2,1,0:T(1,128)}, u32[]{:S(2)}, u32[]{:S(2)}) async-start(f32[32,1,2525]{2,1,0:T(1,128)} %broadcast_in_dim.44), calls=%async_computation.1 | async-start | bytes 655360 | tf_op jit(solution)/shard_map/all_to_all | solution.py:82
  63.2 12.0 %collective-permute-start.12 = (bf16[2,2,16,400]{3,0,2,1:T(2,128)(2,1)}, bf16[2,2,16,400]{3,0,2,1:T(2,128)(2,1)}, u32[]{:S(2)}, u32[]{:S(2)}) collective-permute-start(bf16[2,2,16,400]{3,0,2,1:T(2,128)(2,1)} %get-tuple-element.18), channel_id=1, source_target_pairs={{0,2},{1,3},{2,4},{3,5},{4,6},{5,7},{6,0},{7,1},{8,10},{9,11},{10,... | collective-permute-start | bytes 153608 | tf_op jit(solution)/shard_map/ppermute | solution.py:92
  64.9 10.3 %collective-permute-start.13 = (bf16[2,2,16,400]{3,0,2,1:T(2,128)(2,1)}, bf16[2,2,16,400]{3,0,2,1:T(2,128)(2,1)}, u32[]{:S(2)}, u32[]{:S(2)}) collective-permute-start(bf16[2,2,16,400]{3,0,2,1:T(2,128)(2,1)} %get-tuple-element.17), channel_id=1, source_target_pairs={{0,1},{1,2},{2,3},{3,4},{4,5},{5,6},{6,7},{7,0},{8,9},{9,10},{10,1... | collective-permute-start | bytes 153608 | tf_op jit(solution)/shard_map/ppermute | solution.py:92
  66.4 8.9 %collective-permute-start.7 = (bf16[2,2,16,400]{3,0,2,1:T(2,128)(2,1)}, bf16[2,2,16,400]{3,0,2,1:T(2,128)(2,1)}, u32[]{:S(2)}, u32[]{:S(2)}) collective-permute-start(bf16[2,2,16,400]{3,0,2,1:T(2,128)(2,1)} %get-tuple-element.23), channel_id=1, source_target_pairs={{0,7},{1,0},{2,1},{3,2},{4,3},{5,4},{6,5},{7,6},{8,15},{9,8},{10,9... | collective-permute-start | bytes 153608 | tf_op jit(solution)/shard_map/ppermute | solution.py:92
  69.6 5.6 %collective-permute-start.8 = (bf16[2,2,16,400]{3,0,2,1:T(2,128)(2,1)}, bf16[2,2,16,400]{3,0,2,1:T(2,128)(2,1)}, u32[]{:S(2)}, u32[]{:S(2)}) collective-permute-start(bf16[2,2,16,400]{3,0,2,1:T(2,128)(2,1)} %get-tuple-element.22), channel_id=1, source_target_pairs={{0,6},{1,7},{2,0},{3,1},{4,2},{5,3},{6,4},{7,5},{8,14},{9,15},{10,... | collective-permute-start | bytes 153608 | tf_op jit(solution)/shard_map/ppermute | solution.py:92
  70.0 6.6 %collective-permute-start.9 = (bf16[2,2,16,400]{3,0,2,1:T(2,128)(2,1)S(1)}, bf16[2,2,16,400]{3,0,2,1:T(2,128)(2,1)}, u32[]{:S(2)}, u32[]{:S(2)}) collective-permute-start(bf16[2,2,16,400]{3,0,2,1:T(2,128)(2,1)S(1)} %get-tuple-element.21), channel_id=1, source_target_pairs={{0,5},{1,6},{2,7},{3,0},{4,1},{5,2},{6,3},{7,4},{8,13},{9,14},{10,... | collective-permute-start | bytes 153608 | tf_op jit(solution)/shard_map/ppermute | solution.py:92
  73.7 5.4 %copy-start.22 = (s32[8]{0:T(128)S(1)}, s32[8]{0:T(128)}, u32[]{:S(2)}) copy-start(s32[8]{0:T(128)} %copy-done.21) | copy-start | bytes 100
  90.7 3.8 %copy-start.16 = (f32[16]{0:T(128)S(1)}, f32[16]{0:T(128)}, u32[]{:S(2)}) copy-start(f32[16]{0:T(128)} %copy-done.15) | copy-start | bytes 196
  90.7 3.8 %copy-start.18 = (f32[16]{0:T(128)S(1)}, f32[16]{0:T(128)}, u32[]{:S(2)}) copy-start(f32[16]{0:T(128)} %copy-done.17) | copy-start | bytes 196
  90.7 3.8 %copy-start.27 = (pred[800]{0:T(1024)(128)(4,1)S(1)}, pred[800]{0:T(1024)(128)(4,1)}, u32[]{:S(2)}) copy-start(pred[800]{0:T(1024)(128)(4,1)} %get-tuple-element.39) | copy-start | bytes 2404
  90.7 3.8 %copy-start.28 = (pred[800]{0:T(1024)(128)(4,1)S(1)}, pred[800]{0:T(1024)(128)(4,1)}, u32[]{:S(2)}) copy-start(pred[800]{0:T(1024)(128)(4,1)} %get-tuple-element.40) | copy-start | bytes 2404
  92.4 3.5 %copy-start.26 = (f32[16]{0:T(128)S(1)}, f32[16]{0:T(128)}, u32[]{:S(2)}) copy-start(f32[16]{0:T(128)} %copy-done.25) | copy-start | bytes 196
  95.9 4.2 %copy-start.5 = (f32[400,400]{1,0:T(8,128)S(1)}, f32[400,400]{1,0:T(8,128)}, u32[]{:S(2)}) copy-start(f32[400,400]{1,0:T(8,128)} %fusion.38) | copy-start | bytes 1920004
  97.1 6.1 %collective-permute-start.14 = (bf16[2,32,1200]{2,1,0:T(8,128)(2,1)S(1)}, bf16[2,32,1200]{2,1,0:T(8,128)(2,1)S(1)}, u32[]{:S(2)}, u32[]{:S(2)}) collective-permute-start(bf16[2,32,1200]{2,1,0:T(8,128)(2,1)S(1)} %get-tuple-element.14), channel_id=1, source_target_pairs={{0,8},{8,16},{16,24},{24,0},{1,9},{9,17},{17,25},{25,1},{2,10},{10... | collective-permute-start | bytes 460808 | tf_op jit(solution)/shard_map/ppermute | solution.py:102
  97.1 7.1 %collective-permute-start.15 = (bf16[2,32,1200]{2,1,0:T(8,128)(2,1)S(1)}, bf16[2,32,1200]{2,1,0:T(8,128)(2,1)S(1)}, u32[]{:S(2)}, u32[]{:S(2)}) collective-permute-start(bf16[2,32,1200]{2,1,0:T(8,128)(2,1)S(1)} %get-tuple-element.16), channel_id=1, source_target_pairs={{0,16},{8,24},{16,0},{24,8},{1,17},{9,25},{17,1},{25,9},{2,18},{10... | collective-permute-start | bytes 460808 | tf_op jit(solution)/shard_map/ppermute | solution.py:102
  98.7 7.5 %collective-permute-start.16 = (bf16[2,32,1200]{2,1,0:T(8,128)(2,1)S(1)}, bf16[2,32,1200]{2,1,0:T(8,128)(2,1)S(1)}, u32[]{:S(2)}, u32[]{:S(2)}) collective-permute-start(bf16[2,32,1200]{2,1,0:T(8,128)(2,1)S(1)} %get-tuple-element.15), channel_id=1, source_target_pairs={{0,24},{8,0},{16,8},{24,16},{1,25},{9,1},{17,9},{25,17},{2,26},{10... | collective-permute-start | bytes 460808 | tf_op jit(solution)/shard_map/ppermute | solution.py:102
  (22 other events, 45.9 us)

commit v7 on v6

--- a/solution.py
+++ b/solution.py
@@ -80,9 +80,17 @@
 def power_gather(total, device_count, rows, box_size):
     spread = jnp.broadcast_to(total, (device_count, total.shape[1]))
     back = lax.all_to_all(spread, ("img", "slab"), 0, 0, tiled=True)
-    half = back.reshape(rows, box_size)[: box_size // 2 + 1]
-    mirrored = jnp.roll(half[1 : box_size // 2][::-1, ::-1], 1, axis=1)
-    return jnp.concatenate([half, mirrored], axis=0)
+    half = back.reshape(rows, box_size)
+    zero = lax.optimization_barrier(jnp.zeros((), jnp.int32))
+    n = lax.broadcasted_iota(jnp.int32, (box_size, box_size), 0) + zero
+    m = lax.broadcasted_iota(jnp.int32, (box_size, box_size), 1)
+    flip_columns = (n == (box_size - m) % box_size).astype(jnp.float32)
+    flipped = jnp.dot(half, flip_columns, precision=HI)
+    k = lax.broadcasted_iota(jnp.int32, (box_size, rows), 0) + zero
+    j = lax.broadcasted_iota(jnp.int32, (box_size, rows), 1)
+    keep = ((j == k) & (k <= box_size // 2)).astype(jnp.float32)
+    turn = ((j == box_size - k) & (k > box_size // 2)).astype(jnp.float32)
+    return jnp.dot(keep, half, precision=HI) + jnp.dot(turn, flipped, precision=HI)
 
 
 def shift_exchange(values, count, capacity, direction):

time: 109 us -> 107 us (0.982)
  local copies, waits for them, and re-layouts: 27.2 us -> 20.7 us
  matrix products: 9.21 us -> 11.6 us
  other arithmetic: 25.2 us -> 27.4 us
    unnamed x73 -> x85, local copies, waits for them, and re-layouts: 5.64 us -> 1.71 us
    slice x3 -> x0, local copies, waits for them, and re-layouts: 2.55 us -> none  [power_gather(): mirrored = jnp.roll(half[1:box_size // 2][::-1, ::-1], 1, axis=1)]
    dot_general x0 -> x3, matrix products: none -> 2.33 us  [the longest x1 1.02 us: power_gather(): flipped = jnp.dot(half, flip_columns, precision=HI)]
    sqrt x1 -> x0, other arithmetic: 1.31 us -> none  [body(): noise_level = jnp.sqrt(power / (particles * device_count) + 1e-06)]
  transfers between devices with their start and end apart: 19 -> 19, of which waited for: 4 -> 4; matrix products, arithmetic and copies ran while one was open for 29% -> 33% of each run, Pallas kernels for 0% -> 0%
where the time goes in v7:
time: 107 us; the launch traced here: 106 us
  starting transfers between devices  38 us (36%)
  other arithmetic  27.4 us (26%)
  local copies, waits for them, and re-layouts  20.7 us (19%)
  matrix products  11.6 us (11%)
  waiting for transfers between devices  5.09 us (5%)
  between operations  2.75 us (3%)
    ppermute x14, starting transfers between devices, shift_exchange(): lax.ppermute(values[d * capacity:(d + 1) * capacity], 'slab', pairs)  28.4 us
    concatenate x2, local copies, waits for them, and re-layouts, shift_exchange(): return jnp.concatenate(pieces, axis=0)  5.94 us
    dot_general x1, matrix products, transform(): jnp.einsum('gky,hym->ghkm', tables, rowwise, preferred_element_type=jnp.f...  4.61 us
    convert_element_type x1, other arithmetic, body(): contrast.astype(jnp.float32)[:, None] * full_projection.astype(jnp.float32)  3.74 us
    all_to_all x1, starting transfers between devices, power_gather(): back = lax.all_to_all(spread, ('img', 'slab'), 0, 0, tiled=True)  3.3 us
    all_to_all x1, starting transfers between devices, body(): gathered = lax.all_to_all(pieces, ('img', 'slab'), 0, 0, tiled=True)  3.3 us
    ppermute x3, starting transfers between devices, reduce_over_img(): total = total + lax.ppermute(piece, 'img', pairs).astype(jnp.float32)  3.01 us
    ppermute x3, waiting for transfers between devices, reduce_over_img(): total = total + lax.ppermute(piece, 'img', pairs).astype(jnp.float32)  2.93 us
  transfers between devices with their start and end apart: 19, of which 4 were waited for; matrix products, arithmetic and copies ran while one was open for 33% of the time, Pallas kernels for 0%

profile of v7, /device:TPU:0, one launch (start us, length us, event | category | flops | bytes accessed | tf_op | source)
XLA Modules:
  0.0 105.5 jit_solution(14944644187293485754)
XLA Ops:
  1.6 4.6 %convolution_bitcast_fusion.1 = f32[2,2,400,400]{3,2,0,1:T(8,128)} fusion(bf16[2,400,400]{2,1,0:T(8,128)(2,1)} %constant.132.clone, bf16[1,400,400]{2,1,0:T(8,128)(2,1)S(1)} %copy-done), kind=kOutput, calls=%fused_computation.3 | convolution fusion | flops 768320000 | bytes 3520000 | tf_op jit(solution)/shard_map/gky,hym->ghkm/dot_general | solution.py:27
  6.2 1.6 %fusion.21 = f32[1,400,400]{2,1,0:T(8,128)S(1)} fusion(f32[2,2,400,400]{3,2,0,1:T(8,128)} %convolution_bitcast_fusion.1), kind=kLoop, calls=%fused_computation.40 | loop fusion | flops 320000 | bytes 1920000 | tf_op jit(solution)/shard_map/neg | solution.py:29
  7.8 1.5 %fusion.23 = f32[1,400,400]{2,1,0:T(8,128)S(1)} fusion(f32[2,2,400,400]{3,2,0,1:T(8,128)} %convolution_bitcast_fusion.1), kind=kLoop, calls=%fused_computation.43 | loop fusion | flops 160000 | bytes 1920000 | tf_op jit(solution)/shard_map/sub | solution.py:28
  13.0 2.9 %collective-permute-start = (bf16[2,12928]{1,0:T(2,128)(2,1)S(1)}, bf16[2,12928]{1,0:T(2,128)(2,1)S(1)}, u32[]{:S(2)}, u32[]{:S(2)}) collective-permute-start(bf16[2,12928]{1,0:T(2,128)(2,1)S(1)} %get-tuple-element.31), channel_id=1, source_target_pairs={{0,1},{1,2},{2,3},{3,4},{4,5},{5,6},{6,7},{7,0},{8,9},{9,10},{10,1... | collective-permute-start | bytes 155144 | tf_op jit(solution)/shard_map/ppermute | solution.py:100
  15.9 1.6 %collective-permute-start.1 = (bf16[2,12928]{1,0:T(2,128)(2,1)S(1)}, bf16[2,12928]{1,0:T(2,128)(2,1)S(1)}, u32[]{:S(2)}, u32[]{:S(2)}) collective-permute-start(bf16[2,12928]{1,0:T(2,128)(2,1)S(1)} %get-tuple-element.30), channel_id=1, source_target_pairs={{0,2},{1,3},{2,4},{3,5},{4,6},{5,7},{6,0},{7,1},{8,10},{9,11},{10,... | collective-permute-start | bytes 155144 | tf_op jit(solution)/shard_map/ppermute | solution.py:100
  17.5 2.6 %collective-permute-start.2 = (bf16[2,12928]{1,0:T(2,128)(2,1)}, bf16[2,12928]{1,0:T(2,128)(2,1)}, u32[]{:S(2)}, u32[]{:S(2)}) collective-permute-start(bf16[2,12928]{1,0:T(2,128)(2,1)} %get-tuple-element.29), channel_id=1, source_target_pairs={{0,3},{1,4},{2,5},{3,6},{4,7},{5,0},{6,1},{7,2},{8,11},{9,12},{10,... | collective-permute-start | bytes 155144 | tf_op jit(solution)/shard_map/ppermute | solution.py:100
  20.1 1.2 %collective-permute-start.3 = (bf16[2,12928]{1,0:T(2,128)(2,1)}, bf16[2,12928]{1,0:T(2,128)(2,1)}, u32[]{:S(2)}, u32[]{:S(2)}) collective-permute-start(bf16[2,12928]{1,0:T(2,128)(2,1)} %get-tuple-element.28), channel_id=1, source_target_pairs={{0,4},{1,5},{2,6},{3,7},{4,0},{5,1},{6,2},{7,3},{8,12},{9,13},{10,... | collective-permute-start | bytes 155144 | tf_op jit(solution)/shard_map/ppermute | solution.py:100
  21.3 2.6 %collective-permute-start.4 = (bf16[2,12928]{1,0:T(2,128)(2,1)}, bf16[2,12928]{1,0:T(2,128)(2,1)}, u32[]{:S(2)}, u32[]{:S(2)}) collective-permute-start(bf16[2,12928]{1,0:T(2,128)(2,1)} %get-tuple-element.27), channel_id=1, source_target_pairs={{0,5},{1,6},{2,7},{3,0},{4,1},{5,2},{6,3},{7,4},{8,13},{9,14},{10,... | collective-permute-start | bytes 155144 | tf_op jit(solution)/shard_map/ppermute | solution.py:100
  24.2 1.4 %all_to_all.13 = f32[32,1,2525]{2,1,0:T(1,128)} reshape(f32[202,400]{1,0:T(8,128)S(1)} %fusion.14) | data formatting | bytes 646400 | tf_op jit(solution)/shard_map/all_to_all | solution.py:175
  25.5 3.3 %all-to-all-start = ((f32[32,1,2525]{2,1,0:T(1,128)}), f32[32,1,2525]{2,1,0:T(1,128)}, u32[]{:S(2)}, u32[]{:S(2)}) async-start(f32[32,1,2525]{2,1,0:T(1,128)} %all_to_all.13), calls=%async_computation | async-start | bytes 655360 | tf_op jit(solution)/shard_map/all_to_all | solution.py:175
  33.1 3.7 %fusion.40 = f32[400,400]{1,0:T(8,128)} fusion(f32[]{:T(128)S(6)} %mul.155, s32[400]{0:T(512)S(1)} %fusion.84), kind=kLoop, calls=%fused_computation.71 | loop fusion | flops 1120000 | bytes 641604 | tf_op jit(solution)/shard_map/convert_element_type | solution.py:247
  37.3 3.6 %collective-permute-start.5 = (bf16[2,12928]{1,0:T(2,128)(2,1)}, bf16[2,12928]{1,0:T(2,128)(2,1)}, u32[]{:S(2)}, u32[]{:S(2)}) collective-permute-start(bf16[2,12928]{1,0:T(2,128)(2,1)} %get-tuple-element.26), channel_id=1, source_target_pairs={{0,6},{1,7},{2,0},{3,1},{4,2},{5,3},{6,4},{7,5},{8,14},{9,15},{10,... | collective-permute-start | bytes 155144 | tf_op jit(solution)/shard_map/ppermute | solution.py:100
  40.9 1.4 %collective-permute-start.6 = (bf16[2,12928]{1,0:T(2,128)(2,1)S(1)}, bf16[2,12928]{1,0:T(2,128)(2,1)}, u32[]{:S(2)}, u32[]{:S(2)}) collective-permute-start(bf16[2,12928]{1,0:T(2,128)(2,1)S(1)} %get-tuple-element.25), channel_id=1, source_target_pairs={{0,7},{1,0},{2,1},{3,2},{4,3},{5,4},{6,5},{7,6},{8,15},{9,8},{10,9... | collective-permute-start | bytes 155144 | tf_op jit(solution)/shard_map/ppermute | solution.py:100
  45.1 3.5 %concatenate.62 = bf16[16,12928]{1,0:T(8,128)(2,1)} concatenate(bf16[2,12928]{1,0:T(2,128)(2,1)S(1)} %get-tuple-element.32, bf16[2,12928]{1,0:T(2,128)(2,1)S(1)} %collective-permute-done, bf16[2,12928]{1,0:T(2,128)(2,1)} %copy-done.12, bf16[2,12928]{1,0:T(2,128)(2,1)} %collective-permute-done.2, bf16[2,12928]{1,0:T(2,128)(2,1)} %collective-permute-done.3, ...), dimensions={0} | concatenate | bytes 827392 | tf_op jit(solution)/shard_map/concatenate | solution.py:101
  52.9 1.1 %fusion.106 = (bf16[2,2,16,400]{3,0,2,1:T(2,128)(2,1)}, bf16[2,2,16,400]{3,0,2,1:T(2,128)(2,1)}, bf16[2,2,16,400]{3,0,2,1:T(2,128)(2,1)S(1)}, bf16[2,2,16,400]{3...) fusion(bf16[16,2,16,400]{3,0,2,1:T(8,128)(2,1)S(1)} %fusion.10), kind=kLoop, calls=%fused_computation.173 | loop fusion | bytes 819200 | tf_op jit(solution)/shard_map/slice | solution.py:100
  54.0 4.7 %collective-permute-start.11 = (bf16[2,2,16,400]{3,0,2,1:T(2,128)(2,1)S(1)}, bf16[2,2,16,400]{3,0,2,1:T(2,128)(2,1)S(1)}, u32[]{:S(2)}, u32[]{:S(2)}) collective-permute-start(bf16[2,2,16,400]{3,0,2,1:T(2,128)(2,1)S(1)} %get-tuple-element.19), channel_id=1, source_target_pairs={{0,3},{1,4},{2,5},{3,6},{4,7},{5,0},{6,1},{7,2},{8,11},{9,12},{10,... | collective-permute-start | bytes 153608 | tf_op jit(solution)/shard_map/ppermute | solution.py:100
  58.7 1.2 %reduce_sum.46 = f32[2525]{0:T(1024)S(1)} reduce(f32[32,1,2525]{2,1,0:T(1,128)} %all-to-all-done, f32[]{:T(128)} %constant.109.clone.1), dimensions={0,1}, to_apply=%region_1.2 | reduce | flops 78275 | bytes 333304 | tf_op jit(solution)/shard_map/reduce_sum | solution.py:196
  60.7 3.3 %all-to-all-start.1 = ((f32[32,1,2525]{2,1,0:T(1,128)}), f32[32,1,2525]{2,1,0:T(1,128)}, u32[]{:S(2)}, u32[]{:S(2)}) async-start(f32[32,1,2525]{2,1,0:T(1,128)} %broadcast_in_dim.44), calls=%async_computation.1 | async-start | bytes 655360 | tf_op jit(solution)/shard_map/all_to_all | solution.py:82
  64.1 2.7 %negate_convert_fusion.1 = (bf16[16,16,400]{2,0,1:T(8,128)(2,1)}, f32[16,16,400]{2,0,1:T(8,128)S(1)}) fusion(f32[16]{0:T(128)S(1)} %get-tuple-element.39, s32[400]{0:T(512)S(1)} %copy-done.14, s32[16,16]{0,1:T(8,128)S(1)} %fusion.67), kind=kLoop, calls=%fused_computation.62 | loop fusion | flops 819200 | bytes 617088 | tf_op jit(solution)/shard_map/convert_element_type | solution.py:55
  66.8 1.9 %collective-permute-start.12 = (bf16[2,2,16,400]{3,0,2,1:T(2,128)(2,1)}, bf16[2,2,16,400]{3,0,2,1:T(2,128)(2,1)}, u32[]{:S(2)}, u32[]{:S(2)}) collective-permute-start(bf16[2,2,16,400]{3,0,2,1:T(2,128)(2,1)} %get-tuple-element.18), channel_id=1, source_target_pairs={{0,2},{1,3},{2,4},{3,5},{4,6},{5,7},{6,0},{7,1},{8,10},{9,11},{10,... | collective-permute-start | bytes 153608 | tf_op jit(solution)/shard_map/ppermute | solution.py:100
  68.7 1.5 %collective-permute-start.13 = (bf16[2,2,16,400]{3,0,2,1:T(2,128)(2,1)}, bf16[2,2,16,400]{3,0,2,1:T(2,128)(2,1)}, u32[]{:S(2)}, u32[]{:S(2)}) collective-permute-start(bf16[2,2,16,400]{3,0,2,1:T(2,128)(2,1)} %get-tuple-element.17), channel_id=1, source_target_pairs={{0,1},{1,2},{2,3},{3,4},{4,5},{5,6},{6,7},{7,0},{8,9},{9,10},{10,1... | collective-permute-start | bytes 153608 | tf_op jit(solution)/shard_map/ppermute | solution.py:100
  70.2 3.2 %collective-permute-start.7 = (bf16[2,2,16,400]{3,0,2,1:T(2,128)(2,1)}, bf16[2,2,16,400]{3,0,2,1:T(2,128)(2,1)}, u32[]{:S(2)}, u32[]{:S(2)}) collective-permute-start(bf16[2,2,16,400]{3,0,2,1:T(2,128)(2,1)} %get-tuple-element.23), channel_id=1, source_target_pairs={{0,7},{1,0},{2,1},{3,2},{4,3},{5,4},{6,5},{7,6},{8,15},{9,8},{10,9... | collective-permute-start | bytes 153608 | tf_op jit(solution)/shard_map/ppermute | solution.py:100
  74.6 2.8 %fusion.34 = f32[16,16,400]{2,0,1:T(8,128)S(1)} fusion(f32[16,16,399]{2,0,1:T(8,128)S(1)} %bitcast.112, f32[16,16,1]{2,0,1:T(8,128)S(1)} %slice.254, f32[16]{0:T(128)} %copy-done.15, f32[16]{0:T(128)} %copy-done.17, f32[16]{0:T(128)} %copy-done.21, s32[400]{0:T(512)} %copy-done.13, s32[16,16]{0,1:T(8,128)S(1)} %fusion.67), kind=kLoop, calls=%fused_computation.58 | loop fusion | flops 1228800 | bytes 822016 | tf_op jit(solution)/shard_map/add | solution.py:219
  77.5 1.6 %reshape.373 = f32[16,16,800]{2,1,0:T(8,128)} reshape(f32[16,12800]{1,0:T(8,128)S(1)} %slice_convert_fusion) | data formatting | bytes 1638400 | tf_op jit(solution)/shard_map/convert_element_type | solution.py:215
  79.0 1.4 %collective-permute-done.9 = bf16[2,2,16,400]{3,0,2,1:T(2,128)(2,1)} collective-permute-done((bf16[2,2,16,400]{3,0,2,1:T(2,128)(2,1)S(1)}, bf16[2,2,16,400]{3,0,2,1:T(2,128)(2,1)}, u32[]{:S(2)}, u32[]{:S(2)}) %collective-permute-start.9) | collective-permute-done | bytes 51232 | tf_op jit(solution)/shard_map/ppermute | solution.py:100
  80.4 2.4 %concatenate.64 = bf16[16,2,16,400]{3,0,2,1:T(8,128)(2,1)S(1)} concatenate(bf16[2,2,16,400]{3,0,2,1:T(2,128)(2,1)S(1)} %get-tuple-element.24, bf16[2,2,16,400]{3,0,2,1:T(2,128)(2,1)} %collective-permute-done.7, bf16[2,2,16,400]{3,0,2,1:T(2,128)(2,1)} %collective-permute-done.8, bf16[2,2,16,400]{3,0,2,1:T(2,128)(2,1)} %collective-permute-done.9, ...), dimensions={0} | concatenate | bytes 819200 | tf_op jit(solution)/shard_map/concatenate | solution.py:101
  84.0 1.8 %reduce.3 = f32[32,2525]{1,0:T(8,128)S(1)} reduce(f32[32,1,2525]{2,1,0:T(1,128)} %all-to-all-done.1, f32[]{:T(128)} %constant.142), dimensions={1}, to_apply=%all_to_all.12.reduce_sub_computation | reduce | bytes 646404 | tf_op jit(solution)/shard_map/all_to_all | solution.py:82
  92.9 1.3 %fusion.13 = f32[16,16,800]{2,0,1:T(8,128)S(1)} fusion(f32[16,16,799]{2,0,1:T(8,128)S(1)} %bitcast.111, f32[16,16,1]{2,0,1:T(8,128)} %get-tuple-element.11, f32[16,16,800]{2,0,1:T(8,128)S(1)} %convolution_divide_fusion, f32[16,16]{0,1:T(8,128)S(1)} %bitcast.119, f32[16,16]{0,1:T(8,128)S(1)} %bitcast.118, f32[16]{0:T(128)S(1)} %copy-done.16, ...), kind=kLoop, calls=%fused_computation.26 | loop fusion | flops 1228800 | bytes 2461376 | tf_op jit(solution)/shard_map/add | solution.py:216
  95.5 1.6 %collective-permute-start.15 = (bf16[2,32,1200]{2,1,0:T(8,128)(2,1)S(1)}, bf16[2,32,1200]{2,1,0:T(8,128)(2,1)S(1)}, u32[]{:S(2)}, u32[]{:S(2)}) collective-permute-start(bf16[2,32,1200]{2,1,0:T(8,128)(2,1)S(1)} %get-tuple-element.16), channel_id=1, source_target_pairs={{0,16},{8,24},{16,0},{24,8},{1,17},{9,25},{17,1},{25,9},{2,18},{10... | collective-permute-start | bytes 460808 | tf_op jit(solution)/shard_map/ppermute | solution.py:110
  97.1 1.4 %collective-permute-start.16 = (bf16[2,32,1200]{2,1,0:T(8,128)(2,1)S(1)}, bf16[2,32,1200]{2,1,0:T(8,128)(2,1)S(1)}, u32[]{:S(2)}, u32[]{:S(2)}) collective-permute-start(bf16[2,32,1200]{2,1,0:T(8,128)(2,1)S(1)} %get-tuple-element.15), channel_id=1, source_target_pairs={{0,24},{8,0},{16,8},{24,16},{1,25},{9,1},{17,9},{25,17},{2,26},{10... | collective-permute-start | bytes 460808 | tf_op jit(solution)/shard_map/ppermute | solution.py:110
  98.5 1.1 %convolution_bitcast_fusion = f32[2,2,400,400]{3,2,1,0:T(8,128)S(1)} fusion(bf16[2,400,400]{2,1,0:T(8,128)(2,1)S(1)} %copy-done.4, f32[1,400,400]{2,1,0:T(8,128)S(1)} %fusion.21, f32[1,400,400]{2,1,0:T(8,128)S(1)} %fusion.23, bf16[2,64,400]{2,1,0:T(8,128)(2,1)S(1)} %copy-done.9, bf16[2,64,400]{2,1,0:T(8,128)(2,1)S(1)} %copy-done.8, ...), kind=kOutput, calls=%fused_computation.2 | convolution fusion | flops 515520000 | bytes 5965600 | tf_op jit(solution)/shard_map/hyj,gmj->hgym/dot_general | solution.py:34
  102.6 1.9 %collective-permute-done.16 = bf16[2,32,1200]{2,1,0:T(8,128)(2,1)S(1)} collective-permute-done((bf16[2,32,1200]{2,1,0:T(8,128)(2,1)S(1)}, bf16[2,32,1200]{2,1,0:T(8,128)(2,1)S(1)}, u32[]{:S(2)}, u32[]{:S(2)}) %collective-permute-start.16) | collective-permute-done | bytes 153632 | tf_op jit(solution)/shard_map/ppermute | solution.py:110
  (175 shorter events, 30.5 us)
Async XLA Ops:
  11.5 12.4 %copy-start.23 = (s32[8]{0:T(128)}, s32[8]{0:T(128)S(1)}, u32[]{:S(2)}) copy-start(s32[8]{0:T(128)S(1)} %fusion.94) | copy-start | bytes 100
  13.0 24.3 %collective-permute-start = (bf16[2,12928]{1,0:T(2,128)(2,1)S(1)}, bf16[2,12928]{1,0:T(2,128)(2,1)S(1)}, u32[]{:S(2)}, u32[]{:S(2)}) collective-permute-start(bf16[2,12928]{1,0:T(2,128)(2,1)S(1)} %get-tuple-element.31), channel_id=1, source_target_pairs={{0,1},{1,2},{2,3},{3,4},{4,5},{5,6},{6,7},{7,0},{8,9},{9,10},{10,1... | collective-permute-start | bytes 155144 | tf_op jit(solution)/shard_map/ppermute | solution.py:100
  15.9 25.0 %collective-permute-start.1 = (bf16[2,12928]{1,0:T(2,128)(2,1)S(1)}, bf16[2,12928]{1,0:T(2,128)(2,1)S(1)}, u32[]{:S(2)}, u32[]{:S(2)}) collective-permute-start(bf16[2,12928]{1,0:T(2,128)(2,1)S(1)} %get-tuple-element.30), channel_id=1, source_target_pairs={{0,2},{1,3},{2,4},{3,5},{4,6},{5,7},{6,0},{7,1},{8,10},{9,11},{10,... | collective-permute-start | bytes 155144 | tf_op jit(solution)/shard_map/ppermute | solution.py:100
  17.5 26.9 %collective-permute-start.2 = (bf16[2,12928]{1,0:T(2,128)(2,1)}, bf16[2,12928]{1,0:T(2,128)(2,1)}, u32[]{:S(2)}, u32[]{:S(2)}) collective-permute-start(bf16[2,12928]{1,0:T(2,128)(2,1)} %get-tuple-element.29), channel_id=1, source_target_pairs={{0,3},{1,4},{2,5},{3,6},{4,7},{5,0},{6,1},{7,2},{8,11},{9,12},{10,... | collective-permute-start | bytes 155144 | tf_op jit(solution)/shard_map/ppermute | solution.py:100
  20.1 24.3 %collective-permute-start.3 = (bf16[2,12928]{1,0:T(2,128)(2,1)}, bf16[2,12928]{1,0:T(2,128)(2,1)}, u32[]{:S(2)}, u32[]{:S(2)}) collective-permute-start(bf16[2,12928]{1,0:T(2,128)(2,1)} %get-tuple-element.28), channel_id=1, source_target_pairs={{0,4},{1,5},{2,6},{3,7},{4,0},{5,1},{6,2},{7,3},{8,12},{9,13},{10,... | collective-permute-start | bytes 155144 | tf_op jit(solution)/shard_map/ppermute | solution.py:100
  21.3 23.1 %collective-permute-start.4 = (bf16[2,12928]{1,0:T(2,128)(2,1)}, bf16[2,12928]{1,0:T(2,128)(2,1)}, u32[]{:S(2)}, u32[]{:S(2)}) collective-permute-start(bf16[2,12928]{1,0:T(2,128)(2,1)} %get-tuple-element.27), channel_id=1, source_target_pairs={{0,5},{1,6},{2,7},{3,0},{4,1},{5,2},{6,3},{7,4},{8,13},{9,14},{10,... | collective-permute-start | bytes 155144 | tf_op jit(solution)/shard_map/ppermute | solution.py:100
  24.1 7.8 %copy-start.40 = (f32[64]{0:T(128)S(1)}, f32[64]{0:T(128)}, u32[]{:S(2)}) copy-start(f32[64]{0:T(128)} %param.11) | copy-start | bytes 772
  24.1 18.8 %copy-start.6 = (bf16[2,128,800]{1,2,0:T(8,128)(2,1)S(1)}, bf16[2,128,800]{1,2,0:T(8,128)(2,1)}, u32[]{:S(2)}) copy-start(bf16[2,128,800]{1,2,0:T(8,128)(2,1)} %param.16) | copy-start | bytes 1228804
  25.5 33.1 %all-to-all-start = ((f32[32,1,2525]{2,1,0:T(1,128)}), f32[32,1,2525]{2,1,0:T(1,128)}, u32[]{:S(2)}, u32[]{:S(2)}) async-start(f32[32,1,2525]{2,1,0:T(1,128)} %all_to_all.13), calls=%async_computation | async-start | bytes 655360 | tf_op jit(solution)/shard_map/all_to_all | solution.py:175
  28.9 14.0 %copy-start.13 = (s32[400]{0:T(512)}, s32[400]{0:T(512)S(1)}, u32[]{:S(2)}) copy-start(s32[400]{0:T(512)S(1)} %fusion.84) | copy-start | bytes 4804
  37.3 7.1 %collective-permute-start.5 = (bf16[2,12928]{1,0:T(2,128)(2,1)}, bf16[2,12928]{1,0:T(2,128)(2,1)}, u32[]{:S(2)}, u32[]{:S(2)}) collective-permute-start(bf16[2,12928]{1,0:T(2,128)(2,1)} %get-tuple-element.26), channel_id=1, source_target_pairs={{0,6},{1,7},{2,0},{3,1},{4,2},{5,3},{6,4},{7,5},{8,14},{9,15},{10,... | collective-permute-start | bytes 155144 | tf_op jit(solution)/shard_map/ppermute | solution.py:100
  40.9 4.2 %collective-permute-start.6 = (bf16[2,12928]{1,0:T(2,128)(2,1)S(1)}, bf16[2,12928]{1,0:T(2,128)(2,1)}, u32[]{:S(2)}, u32[]{:S(2)}) collective-permute-start(bf16[2,12928]{1,0:T(2,128)(2,1)S(1)} %get-tuple-element.25), channel_id=1, source_target_pairs={{0,7},{1,0},{2,1},{3,2},{4,3},{5,4},{6,5},{7,6},{8,15},{9,8},{10,9... | collective-permute-start | bytes 155144 | tf_op jit(solution)/shard_map/ppermute | solution.py:100
  52.6 11.5 %copy-start.21 = (f32[16]{0:T(128)}, f32[16]{0:T(128)S(1)}, u32[]{:S(2)}) copy-start(f32[16]{0:T(128)S(1)} %get-tuple-element.39) | copy-start | bytes 196
  52.9 11.2 %copy-start.14 = (s32[400]{0:T(512)S(1)}, s32[400]{0:T(512)}, u32[]{:S(2)}) copy-start(s32[400]{0:T(512)} %copy-done.13) | copy-start | bytes 4804
  54.0 19.4 %collective-permute-start.10 = (bf16[2,2,16,400]{3,0,2,1:T(2,128)(2,1)S(1)}, bf16[2,2,16,400]{3,0,2,1:T(2,128)(2,1)S(1)}, u32[]{:S(2)}, u32[]{:S(2)}) collective-permute-start(bf16[2,2,16,400]{3,0,2,1:T(2,128)(2,1)S(1)} %get-tuple-element.20), channel_id=1, source_target_pairs={{0,4},{1,5},{2,6},{3,7},{4,0},{5,1},{6,2},{7,3},{8,12},{9,13},{10,... | collective-permute-start | bytes 153608 | tf_op jit(solution)/shard_map/ppermute | solution.py:100
  54.0 19.8 %collective-permute-start.11 = (bf16[2,2,16,400]{3,0,2,1:T(2,128)(2,1)S(1)}, bf16[2,2,16,400]{3,0,2,1:T(2,128)(2,1)S(1)}, u32[]{:S(2)}, u32[]{:S(2)}) collective-permute-start(bf16[2,2,16,400]{3,0,2,1:T(2,128)(2,1)S(1)} %get-tuple-element.19), channel_id=1, source_target_pairs={{0,3},{1,4},{2,5},{3,6},{4,7},{5,0},{6,1},{7,2},{8,11},{9,12},{10,... | collective-permute-start | bytes 153608 | tf_op jit(solution)/shard_map/ppermute | solution.py:100
  60.7 23.3 %all-to-all-start.1 = ((f32[32,1,2525]{2,1,0:T(1,128)}), f32[32,1,2525]{2,1,0:T(1,128)}, u32[]{:S(2)}, u32[]{:S(2)}) async-start(f32[32,1,2525]{2,1,0:T(1,128)} %broadcast_in_dim.44), calls=%async_computation.1 | async-start | bytes 655360 | tf_op jit(solution)/shard_map/all_to_all | solution.py:82
  66.8 12.2 %collective-permute-start.12 = (bf16[2,2,16,400]{3,0,2,1:T(2,128)(2,1)}, bf16[2,2,16,400]{3,0,2,1:T(2,128)(2,1)}, u32[]{:S(2)}, u32[]{:S(2)}) collective-permute-start(bf16[2,2,16,400]{3,0,2,1:T(2,128)(2,1)} %get-tuple-element.18), channel_id=1, source_target_pairs={{0,2},{1,3},{2,4},{3,5},{4,6},{5,7},{6,0},{7,1},{8,10},{9,11},{10,... | collective-permute-start | bytes 153608 | tf_op jit(solution)/shard_map/ppermute | solution.py:100
  68.7 10.3 %collective-permute-start.13 = (bf16[2,2,16,400]{3,0,2,1:T(2,128)(2,1)}, bf16[2,2,16,400]{3,0,2,1:T(2,128)(2,1)}, u32[]{:S(2)}, u32[]{:S(2)}) collective-permute-start(bf16[2,2,16,400]{3,0,2,1:T(2,128)(2,1)} %get-tuple-element.17), channel_id=1, source_target_pairs={{0,1},{1,2},{2,3},{3,4},{4,5},{5,6},{6,7},{7,0},{8,9},{9,10},{10,1... | collective-permute-start | bytes 153608 | tf_op jit(solution)/shard_map/ppermute | solution.py:100
  70.2 8.9 %collective-permute-start.7 = (bf16[2,2,16,400]{3,0,2,1:T(2,128)(2,1)}, bf16[2,2,16,400]{3,0,2,1:T(2,128)(2,1)}, u32[]{:S(2)}, u32[]{:S(2)}) collective-permute-start(bf16[2,2,16,400]{3,0,2,1:T(2,128)(2,1)} %get-tuple-element.23), channel_id=1, source_target_pairs={{0,7},{1,0},{2,1},{3,2},{4,3},{5,4},{6,5},{7,6},{8,15},{9,8},{10,9... | collective-permute-start | bytes 153608 | tf_op jit(solution)/shard_map/ppermute | solution.py:100
  73.4 5.6 %collective-permute-start.8 = (bf16[2,2,16,400]{3,0,2,1:T(2,128)(2,1)}, bf16[2,2,16,400]{3,0,2,1:T(2,128)(2,1)}, u32[]{:S(2)}, u32[]{:S(2)}) collective-permute-start(bf16[2,2,16,400]{3,0,2,1:T(2,128)(2,1)} %get-tuple-element.22), channel_id=1, source_target_pairs={{0,6},{1,7},{2,0},{3,1},{4,2},{5,3},{6,4},{7,5},{8,14},{9,15},{10,... | collective-permute-start | bytes 153608 | tf_op jit(solution)/shard_map/ppermute | solution.py:100
  73.8 6.6 %collective-permute-start.9 = (bf16[2,2,16,400]{3,0,2,1:T(2,128)(2,1)S(1)}, bf16[2,2,16,400]{3,0,2,1:T(2,128)(2,1)}, u32[]{:S(2)}, u32[]{:S(2)}) collective-permute-start(bf16[2,2,16,400]{3,0,2,1:T(2,128)(2,1)S(1)} %get-tuple-element.21), channel_id=1, source_target_pairs={{0,5},{1,6},{2,7},{3,0},{4,1},{5,2},{6,3},{7,4},{8,13},{9,14},{10,... | collective-permute-start | bytes 153608 | tf_op jit(solution)/shard_map/ppermute | solution.py:100
  77.5 5.4 %copy-start.24 = (s32[8]{0:T(128)S(1)}, s32[8]{0:T(128)}, u32[]{:S(2)}) copy-start(s32[8]{0:T(128)} %copy-done.23) | copy-start | bytes 100
  84.0 3.9 %copy-start.20 = (s32[400]{0:T(512)S(1)}, s32[400]{0:T(512)}, u32[]{:S(2)}) copy-start(s32[400]{0:T(512)} %fusion.89) | copy-start | bytes 4804
  84.0 3.9 %copy-start.36 = (pred[400]{0:T(512)(128)(4,1)S(1)}, pred[400]{0:T(512)(128)(4,1)}, u32[]{:S(2)}) copy-start(pred[400]{0:T(512)(128)(4,1)} %fusion.88) | copy-start | bytes 1204
  89.1 3.8 %copy-start.18 = (f32[16]{0:T(128)S(1)}, f32[16]{0:T(128)}, u32[]{:S(2)}) copy-start(f32[16]{0:T(128)} %copy-done.17) | copy-start | bytes 196
  89.1 3.8 %copy-start.29 = (pred[800]{0:T(1024)(128)(4,1)S(1)}, pred[800]{0:T(1024)(128)(4,1)}, u32[]{:S(2)}) copy-start(pred[800]{0:T(1024)(128)(4,1)} %get-tuple-element.41) | copy-start | bytes 2404
  89.1 3.8 %copy-start.30 = (pred[800]{0:T(1024)(128)(4,1)S(1)}, pred[800]{0:T(1024)(128)(4,1)}, u32[]{:S(2)}) copy-start(pred[800]{0:T(1024)(128)(4,1)} %get-tuple-element.42) | copy-start | bytes 2404
  94.3 4.2 %copy-start.5 = (f32[400,400]{1,0:T(8,128)S(1)}, f32[400,400]{1,0:T(8,128)}, u32[]{:S(2)}) copy-start(f32[400,400]{1,0:T(8,128)} %fusion.40) | copy-start | bytes 1920004
  95.5 6.2 %collective-permute-start.14 = (bf16[2,32,1200]{2,1,0:T(8,128)(2,1)S(1)}, bf16[2,32,1200]{2,1,0:T(8,128)(2,1)S(1)}, u32[]{:S(2)}, u32[]{:S(2)}) collective-permute-start(bf16[2,32,1200]{2,1,0:T(8,128)(2,1)S(1)} %get-tuple-element.14), channel_id=1, source_target_pairs={{0,8},{8,16},{16,24},{24,0},{1,9},{9,17},{17,25},{25,1},{2,10},{10... | collective-permute-start | bytes 460808 | tf_op jit(solution)/shard_map/ppermute | solution.py:110
  95.5 7.1 %collective-permute-start.15 = (bf16[2,32,1200]{2,1,0:T(8,128)(2,1)S(1)}, bf16[2,32,1200]{2,1,0:T(8,128)(2,1)S(1)}, u32[]{:S(2)}, u32[]{:S(2)}) collective-permute-start(bf16[2,32,1200]{2,1,0:T(8,128)(2,1)S(1)} %get-tuple-element.16), channel_id=1, source_target_pairs={{0,16},{8,24},{16,0},{24,8},{1,17},{9,25},{17,1},{25,9},{2,18},{10... | collective-permute-start | bytes 460808 | tf_op jit(solution)/shard_map/ppermute | solution.py:110
  97.1 7.5 %collective-permute-start.16 = (bf16[2,32,1200]{2,1,0:T(8,128)(2,1)S(1)}, bf16[2,32,1200]{2,1,0:T(8,128)(2,1)S(1)}, u32[]{:S(2)}, u32[]{:S(2)}) collective-permute-start(bf16[2,32,1200]{2,1,0:T(8,128)(2,1)S(1)} %get-tuple-element.15), channel_id=1, source_target_pairs={{0,24},{8,0},{16,8},{24,16},{1,25},{9,1},{17,9},{25,17},{2,26},{10... | collective-permute-start | bytes 460808 | tf_op jit(solution)/shard_map/ppermute | solution.py:110
  (29 other events, 68.4 us)

commit v8 on v7

--- a/solution.py
+++ b/solution.py
@@ -61,15 +61,11 @@
 
 
 def shift_halves(values, steps, box_size):
+    column = lax.broadcasted_iota(jnp.int32, values.shape, values.ndim - 1) % box_size
+    seam = 0 if steps == 1 else box_size - 1
     rolled = jnp.roll(values, steps, axis=-1)
-    column = lax.broadcasted_iota(jnp.int32, values.shape, values.ndim - 1)
-    if steps == 1:
-        first, second = values[..., box_size - 1 : box_size], values[..., 2 * box_size - 1 :]
-        rolled = jnp.where(column == 0, first, rolled)
-        return jnp.where(column == box_size, second, rolled)
-    first, second = values[..., 0:1], values[..., box_size : box_size + 1]
-    rolled = jnp.where(column == box_size - 1, first, rolled)
-    return jnp.where(column == 2 * box_size - 1, second, rolled)
+    wrapped = jnp.roll(values, -steps * (box_size - 1), axis=-1)
+    return jnp.where(column == seam, wrapped, rolled)
 
 
 def low_row_ids(block_ids, box_size):

time: 107 us -> 104 us (0.972)
  local copies, waits for them, and re-layouts: 20.7 us -> 18.1 us
  other arithmetic: 27.4 us -> 26.3 us
    broadcast_in_dim x2 -> x0, local copies, waits for them, and re-layouts: 2.12 us -> none  [the longest x1 1.07 us: shift_halves(): rolled = jnp.where(column == 0, first, rolled)]
    unnamed x85 -> x69, local copies, waits for them, and re-layouts: 1.71 us -> 2.41 us
where the time goes in v8:
time: 104 us; the launch traced here: 102 us
  starting transfers between devices  37.8 us (36%)
  other arithmetic  26.3 us (25%)
  local copies, waits for them, and re-layouts  18.1 us (17%)
  matrix products  11.6 us (11%)
  waiting for transfers between devices  5.29 us (5%)
  between operations  2.65 us (3%)
    ppermute x14, starting transfers between devices, shift_exchange(): lax.ppermute(values[d * capacity:(d + 1) * capacity], 'slab', pairs)  28 us
    concatenate x2, local copies, waits for them, and re-layouts, shift_exchange(): return jnp.concatenate(pieces, axis=0)  5.3 us
    dot_general x1, matrix products, transform(): jnp.einsum('gky,hym->ghkm', tables, rowwise, preferred_element_type=jnp.f...  4.52 us
    convert_element_type x1, other arithmetic, body(): contrast.astype(jnp.float32)[:, None] * full_projection.astype(jnp.float32)  3.71 us
    all_to_all x1, starting transfers between devices, power_gather(): back = lax.all_to_all(spread, ('img', 'slab'), 0, 0, tiled=True)  3.47 us
    all_to_all x1, starting transfers between devices, body(): gathered = lax.all_to_all(pieces, ('img', 'slab'), 0, 0, tiled=True)  3.3 us
    ppermute x3, starting transfers between devices, reduce_over_img(): total = total + lax.ppermute(piece, 'img', pairs).astype(jnp.float32)  3 us
    ppermute x3, waiting for transfers between devices, reduce_over_img(): total = total + lax.ppermute(piece, 'img', pairs).astype(jnp.float32)  2.96 us
  transfers between devices with their start and end apart: 19, of which 4 were waited for; matrix products, arithmetic and copies ran while one was open for 33% of the time, Pallas kernels for 0%

profile of v8, /device:TPU:0, one launch (start us, length us, event | category | flops | bytes accessed | tf_op | source)
XLA Modules:
  0.0 101.8 jit_solution(1445311514442749736)
XLA Ops:
  1.6 4.5 %convolution_bitcast_fusion.1 = f32[2,2,400,400]{3,2,0,1:T(8,128)} fusion(bf16[2,400,400]{2,1,0:T(8,128)(2,1)} %constant.137.clone, bf16[1,400,400]{2,1,0:T(8,128)(2,1)S(1)} %copy-done), kind=kOutput, calls=%fused_computation.3 | convolution fusion | flops 768320000 | bytes 3520000 | tf_op jit(solution)/shard_map/gky,hym->ghkm/dot_general | solution.py:27
  6.2 1.6 %fusion.20 = f32[1,400,400]{2,1,0:T(8,128)S(1)} fusion(f32[2,2,400,400]{3,2,0,1:T(8,128)} %convolution_bitcast_fusion.1), kind=kLoop, calls=%fused_computation.40 | loop fusion | flops 320000 | bytes 1920000 | tf_op jit(solution)/shard_map/neg | solution.py:29
  7.7 1.5 %fusion.22 = f32[1,400,400]{2,1,0:T(8,128)S(1)} fusion(f32[2,2,400,400]{3,2,0,1:T(8,128)} %convolution_bitcast_fusion.1), kind=kLoop, calls=%fused_computation.43 | loop fusion | flops 160000 | bytes 1920000 | tf_op jit(solution)/shard_map/sub | solution.py:28
  12.9 2.9 %collective-permute-start = (bf16[2,12928]{1,0:T(2,128)(2,1)S(1)}, bf16[2,12928]{1,0:T(2,128)(2,1)S(1)}, u32[]{:S(2)}, u32[]{:S(2)}) collective-permute-start(bf16[2,12928]{1,0:T(2,128)(2,1)S(1)} %get-tuple-element.29), channel_id=1, source_target_pairs={{0,1},{1,2},{2,3},{3,4},{4,5},{5,6},{6,7},{7,0},{8,9},{9,10},{10,1... | collective-permute-start | bytes 155144 | tf_op jit(solution)/shard_map/ppermute | solution.py:96
  15.8 1.6 %collective-permute-start.1 = (bf16[2,12928]{1,0:T(2,128)(2,1)S(1)}, bf16[2,12928]{1,0:T(2,128)(2,1)S(1)}, u32[]{:S(2)}, u32[]{:S(2)}) collective-permute-start(bf16[2,12928]{1,0:T(2,128)(2,1)S(1)} %get-tuple-element.28), channel_id=1, source_target_pairs={{0,2},{1,3},{2,4},{3,5},{4,6},{5,7},{6,0},{7,1},{8,10},{9,11},{10,... | collective-permute-start | bytes 155144 | tf_op jit(solution)/shard_map/ppermute | solution.py:96
  17.4 2.6 %collective-permute-start.2 = (bf16[2,12928]{1,0:T(2,128)(2,1)}, bf16[2,12928]{1,0:T(2,128)(2,1)}, u32[]{:S(2)}, u32[]{:S(2)}) collective-permute-start(bf16[2,12928]{1,0:T(2,128)(2,1)} %get-tuple-element.27), channel_id=1, source_target_pairs={{0,3},{1,4},{2,5},{3,6},{4,7},{5,0},{6,1},{7,2},{8,11},{9,12},{10,... | collective-permute-start | bytes 155144 | tf_op jit(solution)/shard_map/ppermute | solution.py:96
  20.0 1.2 %collective-permute-start.3 = (bf16[2,12928]{1,0:T(2,128)(2,1)}, bf16[2,12928]{1,0:T(2,128)(2,1)}, u32[]{:S(2)}, u32[]{:S(2)}) collective-permute-start(bf16[2,12928]{1,0:T(2,128)(2,1)} %get-tuple-element.26), channel_id=1, source_target_pairs={{0,4},{1,5},{2,6},{3,7},{4,0},{5,1},{6,2},{7,3},{8,12},{9,13},{10,... | collective-permute-start | bytes 155144 | tf_op jit(solution)/shard_map/ppermute | solution.py:96
  21.2 2.6 %collective-permute-start.4 = (bf16[2,12928]{1,0:T(2,128)(2,1)}, bf16[2,12928]{1,0:T(2,128)(2,1)}, u32[]{:S(2)}, u32[]{:S(2)}) collective-permute-start(bf16[2,12928]{1,0:T(2,128)(2,1)} %get-tuple-element.25), channel_id=1, source_target_pairs={{0,5},{1,6},{2,7},{3,0},{4,1},{5,2},{6,3},{7,4},{8,13},{9,14},{10,... | collective-permute-start | bytes 155144 | tf_op jit(solution)/shard_map/ppermute | solution.py:96
  24.1 1.4 %all_to_all.13 = f32[32,1,2525]{2,1,0:T(1,128)} reshape(f32[202,400]{1,0:T(8,128)S(1)} %fusion.13) | data formatting | bytes 646400 | tf_op jit(solution)/shard_map/all_to_all | solution.py:171
  25.4 3.3 %all-to-all-start = ((f32[32,1,2525]{2,1,0:T(1,128)}), f32[32,1,2525]{2,1,0:T(1,128)}, u32[]{:S(2)}, u32[]{:S(2)}) async-start(f32[32,1,2525]{2,1,0:T(1,128)} %all_to_all.13), calls=%async_computation | async-start | bytes 655360 | tf_op jit(solution)/shard_map/all_to_all | solution.py:171
  33.5 3.7 %fusion.39 = f32[400,400]{1,0:T(8,128)} fusion(f32[]{:T(128)S(6)} %mul.155, s32[400]{0:T(512)S(1)} %fusion.87), kind=kLoop, calls=%fused_computation.71 | loop fusion | flops 1120000 | bytes 641604 | tf_op jit(solution)/shard_map/convert_element_type | solution.py:243
  37.7 3.6 %collective-permute-start.5 = (bf16[2,12928]{1,0:T(2,128)(2,1)}, bf16[2,12928]{1,0:T(2,128)(2,1)}, u32[]{:S(2)}, u32[]{:S(2)}) collective-permute-start(bf16[2,12928]{1,0:T(2,128)(2,1)} %get-tuple-element.24), channel_id=1, source_target_pairs={{0,6},{1,7},{2,0},{3,1},{4,2},{5,3},{6,4},{7,5},{8,14},{9,15},{10,... | collective-permute-start | bytes 155144 | tf_op jit(solution)/shard_map/ppermute | solution.py:96
  41.2 1.4 %collective-permute-start.6 = (bf16[2,12928]{1,0:T(2,128)(2,1)S(1)}, bf16[2,12928]{1,0:T(2,128)(2,1)}, u32[]{:S(2)}, u32[]{:S(2)}) collective-permute-start(bf16[2,12928]{1,0:T(2,128)(2,1)S(1)} %get-tuple-element.23), channel_id=1, source_target_pairs={{0,7},{1,0},{2,1},{3,2},{4,3},{5,4},{6,5},{7,6},{8,15},{9,8},{10,9... | collective-permute-start | bytes 155144 | tf_op jit(solution)/shard_map/ppermute | solution.py:96
  45.5 2.9 %concatenate.66 = bf16[16,12928]{1,0:T(8,128)(2,1)S(1)} concatenate(bf16[2,12928]{1,0:T(2,128)(2,1)S(1)} %get-tuple-element.30, bf16[2,12928]{1,0:T(2,128)(2,1)S(1)} %collective-permute-done, bf16[2,12928]{1,0:T(2,128)(2,1)} %copy-done.8, bf16[2,12928]{1,0:T(2,128)(2,1)} %collective-permute-done.2, bf16[2,12928]{1,0:T(2,128)(2,1)} %collective-permute-done.3, ...), dimensions={0} | concatenate | bytes 827392 | tf_op jit(solution)/shard_map/concatenate | solution.py:97
  49.4 1.1 %slice_convert_fusion = f32[16,12800]{1,0:T(8,128)S(1)} fusion(bf16[16,12928]{1,0:T(8,128)(2,1)} %copy-done.1), kind=kLoop, calls=%fused_computation.74 | loop fusion | flops 204800 | bytes 1228800 | tf_op jit(solution)/shard_map/convert_element_type | solution.py:211
  52.3 1.1 %fusion.108 = (bf16[2,2,16,400]{3,0,2,1:T(2,128)(2,1)}, bf16[2,2,16,400]{3,0,2,1:T(2,128)(2,1)}, bf16[2,2,16,400]{3,0,2,1:T(2,128)(2,1)S(1)}, bf16[2,2,16,400]{3...) fusion(bf16[16,2,16,400]{3,0,2,1:T(8,128)(2,1)S(1)} %fusion.10), kind=kLoop, calls=%fused_computation.175 | loop fusion | bytes 819200 | tf_op jit(solution)/shard_map/slice | solution.py:96
  53.4 4.7 %collective-permute-start.11 = (bf16[2,2,16,400]{3,0,2,1:T(2,128)(2,1)S(1)}, bf16[2,2,16,400]{3,0,2,1:T(2,128)(2,1)}, u32[]{:S(2)}, u32[]{:S(2)}) collective-permute-start(bf16[2,2,16,400]{3,0,2,1:T(2,128)(2,1)S(1)} %get-tuple-element.17), channel_id=1, source_target_pairs={{0,3},{1,4},{2,5},{3,6},{4,7},{5,0},{6,1},{7,2},{8,11},{9,12},{10,... | collective-permute-start | bytes 153608 | tf_op jit(solution)/shard_map/ppermute | solution.py:96
  58.1 1.2 %reduce_sum.46 = f32[2525]{0:T(1024)S(1)} reduce(f32[32,1,2525]{2,1,0:T(1,128)} %all-to-all-done, f32[]{:T(128)} %constant.114.clone.1), dimensions={0,1}, to_apply=%region_1.2 | reduce | flops 78275 | bytes 333304 | tf_op jit(solution)/shard_map/reduce_sum | solution.py:192
  60.1 3.5 %all-to-all-start.1 = ((f32[32,1,2525]{2,1,0:T(1,128)}), f32[32,1,2525]{2,1,0:T(1,128)}, u32[]{:S(2)}, u32[]{:S(2)}) async-start(f32[32,1,2525]{2,1,0:T(1,128)} %broadcast_in_dim.23), calls=%async_computation.1 | async-start | bytes 655360 | tf_op jit(solution)/shard_map/all_to_all | solution.py:78
  63.6 2.7 %negate_convert_fusion.1 = (bf16[16,16,400]{2,0,1:T(8,128)(2,1)}, f32[16,16,400]{2,0,1:T(8,128)S(1)}) fusion(f32[16]{0:T(128)S(1)} %get-tuple-element.37, s32[400]{0:T(512)S(1)} %fusion.87, s32[16,16]{0,1:T(8,128)S(1)} %fusion.66), kind=kLoop, calls=%fused_computation.62 | loop fusion | flops 819200 | bytes 617088 | tf_op jit(solution)/shard_map/convert_element_type | solution.py:55
  66.4 1.5 %collective-permute-start.12 = (bf16[2,2,16,400]{3,0,2,1:T(2,128)(2,1)}, bf16[2,2,16,400]{3,0,2,1:T(2,128)(2,1)}, u32[]{:S(2)}, u32[]{:S(2)}) collective-permute-start(bf16[2,2,16,400]{3,0,2,1:T(2,128)(2,1)} %get-tuple-element.16), channel_id=1, source_target_pairs={{0,2},{1,3},{2,4},{3,5},{4,6},{5,7},{6,0},{7,1},{8,10},{9,11},{10,... | collective-permute-start | bytes 153608 | tf_op jit(solution)/shard_map/ppermute | solution.py:96
  67.9 1.5 %collective-permute-start.13 = (bf16[2,2,16,400]{3,0,2,1:T(2,128)(2,1)}, bf16[2,2,16,400]{3,0,2,1:T(2,128)(2,1)}, u32[]{:S(2)}, u32[]{:S(2)}) collective-permute-start(bf16[2,2,16,400]{3,0,2,1:T(2,128)(2,1)} %get-tuple-element.15), channel_id=1, source_target_pairs={{0,1},{1,2},{2,3},{3,4},{4,5},{5,6},{6,7},{7,0},{8,9},{9,10},{10,1... | collective-permute-start | bytes 153608 | tf_op jit(solution)/shard_map/ppermute | solution.py:96
  69.4 3.2 %collective-permute-start.7 = (bf16[2,2,16,400]{3,0,2,1:T(2,128)(2,1)}, bf16[2,2,16,400]{3,0,2,1:T(2,128)(2,1)}, u32[]{:S(2)}, u32[]{:S(2)}) collective-permute-start(bf16[2,2,16,400]{3,0,2,1:T(2,128)(2,1)} %get-tuple-element.21), channel_id=1, source_target_pairs={{0,7},{1,0},{2,1},{3,2},{4,3},{5,4},{6,5},{7,6},{8,15},{9,8},{10,9... | collective-permute-start | bytes 153608 | tf_op jit(solution)/shard_map/ppermute | solution.py:96
  73.8 2.7 %fusion.33 = f32[16,16,400]{2,0,1:T(8,128)S(1)} fusion(f32[16,16,399]{2,0,1:T(8,128)S(1)} %bitcast.108, f32[16,16,1]{2,0,1:T(8,128)S(1)} %slice.260, f32[16]{0:T(128)S(1)} %get-tuple-element.6, f32[16]{0:T(128)S(1)} %get-tuple-element.38, f32[16]{0:T(128)} %copy-done.13, s32[400]{0:T(512)S(1)} %fusion.87, s32[16,16]{0,1:T(8,128)S(1)} %fusion.66), kind=kLoop, calls=%fused_computation.58 | loop fusion | flops 1228800 | bytes 822016 | tf_op jit(solution)/shard_map/add | solution.py:215
  76.6 1.6 %reshape.373 = f32[16,16,800]{2,1,0:T(8,128)} reshape(f32[16,12800]{1,0:T(8,128)S(1)} %slice_convert_fusion) | data formatting | bytes 1638400 | tf_op jit(solution)/shard_map/convert_element_type | solution.py:211
  78.2 1.5 %collective-permute-done.9 = bf16[2,2,16,400]{3,0,2,1:T(2,128)(2,1)} collective-permute-done((bf16[2,2,16,400]{3,0,2,1:T(2,128)(2,1)S(1)}, bf16[2,2,16,400]{3,0,2,1:T(2,128)(2,1)}, u32[]{:S(2)}, u32[]{:S(2)}) %collective-permute-start.9) | collective-permute-done | bytes 51232 | tf_op jit(solution)/shard_map/ppermute | solution.py:96
  79.7 2.4 %concatenate.68 = bf16[16,2,16,400]{3,0,2,1:T(8,128)(2,1)S(1)} concatenate(bf16[2,2,16,400]{3,0,2,1:T(2,128)(2,1)S(1)} %get-tuple-element.22, bf16[2,2,16,400]{3,0,2,1:T(2,128)(2,1)} %collective-permute-done.7, bf16[2,2,16,400]{3,0,2,1:T(2,128)(2,1)} %collective-permute-done.8, bf16[2,2,16,400]{3,0,2,1:T(2,128)(2,1)} %collective-permute-done.9, ...), dimensions={0} | concatenate | bytes 819200 | tf_op jit(solution)/shard_map/concatenate | solution.py:97
  83.2 1.8 %reduce.3 = f32[32,2525]{1,0:T(8,128)S(1)} reduce(f32[32,1,2525]{2,1,0:T(1,128)} %all-to-all-done.1, f32[]{:T(128)} %constant.147), dimensions={1}, to_apply=%all_to_all.12.reduce_sub_computation | reduce | bytes 646404 | tf_op jit(solution)/shard_map/all_to_all | solution.py:78
  91.8 1.6 %collective-permute-start.15 = (bf16[2,32,1200]{2,1,0:T(8,128)(2,1)S(1)}, bf16[2,32,1200]{2,1,0:T(8,128)(2,1)S(1)}, u32[]{:S(2)}, u32[]{:S(2)}) collective-permute-start(bf16[2,32,1200]{2,1,0:T(8,128)(2,1)S(1)} %get-tuple-element.14), channel_id=1, source_target_pairs={{0,16},{8,24},{16,0},{24,8},{1,17},{9,25},{17,1},{25,9},{2,18},{10... | collective-permute-start | bytes 460808 | tf_op jit(solution)/shard_map/ppermute | solution.py:106
  93.3 1.4 %collective-permute-start.16 = (bf16[2,32,1200]{2,1,0:T(8,128)(2,1)S(1)}, bf16[2,32,1200]{2,1,0:T(8,128)(2,1)S(1)}, u32[]{:S(2)}, u32[]{:S(2)}) collective-permute-start(bf16[2,32,1200]{2,1,0:T(8,128)(2,1)S(1)} %get-tuple-element.13), channel_id=1, source_target_pairs={{0,24},{8,0},{16,8},{24,16},{1,25},{9,1},{17,9},{25,17},{2,26},{10... | collective-permute-start | bytes 460808 | tf_op jit(solution)/shard_map/ppermute | solution.py:106
  94.7 1.1 %convolution_bitcast_fusion = f32[2,2,400,400]{3,2,1,0:T(8,128)S(1)} fusion(bf16[2,400,400]{2,1,0:T(8,128)(2,1)S(1)} %copy-done.3, f32[1,400,400]{2,1,0:T(8,128)S(1)} %fusion.20, f32[1,400,400]{2,1,0:T(8,128)S(1)} %fusion.22, bf16[2,64,400]{2,1,0:T(8,128)(2,1)S(1)} %copy-done.7, bf16[2,64,400]{2,1,0:T(8,128)(2,1)S(1)} %get-tuple-element.31, ...), kind=kOutput, calls=%fused_computation.2 | convolution fusion | flops 515520000 | bytes 5965600 | tf_op jit(solution)/shard_map/hyj,gmj->hgym/dot_general | solution.py:34
  98.9 1.9 %collective-permute-done.16 = bf16[2,32,1200]{2,1,0:T(8,128)(2,1)S(1)} collective-permute-done((bf16[2,32,1200]{2,1,0:T(8,128)(2,1)S(1)}, bf16[2,32,1200]{2,1,0:T(8,128)(2,1)S(1)}, u32[]{:S(2)}, u32[]{:S(2)}) %collective-permute-start.16) | collective-permute-done | bytes 153632 | tf_op jit(solution)/shard_map/ppermute | solution.py:106
  (160 shorter events, 28.0 us)
Async XLA Ops:
  11.4 12.4 %copy-start.15 = (s32[8]{0:T(128)}, s32[8]{0:T(128)S(1)}, u32[]{:S(2)}) copy-start(s32[8]{0:T(128)S(1)} %fusion.97) | copy-start | bytes 100
  12.9 24.8 %collective-permute-start = (bf16[2,12928]{1,0:T(2,128)(2,1)S(1)}, bf16[2,12928]{1,0:T(2,128)(2,1)S(1)}, u32[]{:S(2)}, u32[]{:S(2)}) collective-permute-start(bf16[2,12928]{1,0:T(2,128)(2,1)S(1)} %get-tuple-element.29), channel_id=1, source_target_pairs={{0,1},{1,2},{2,3},{3,4},{4,5},{5,6},{6,7},{7,0},{8,9},{9,10},{10,1... | collective-permute-start | bytes 155144 | tf_op jit(solution)/shard_map/ppermute | solution.py:96
  15.8 25.4 %collective-permute-start.1 = (bf16[2,12928]{1,0:T(2,128)(2,1)S(1)}, bf16[2,12928]{1,0:T(2,128)(2,1)S(1)}, u32[]{:S(2)}, u32[]{:S(2)}) collective-permute-start(bf16[2,12928]{1,0:T(2,128)(2,1)S(1)} %get-tuple-element.28), channel_id=1, source_target_pairs={{0,2},{1,3},{2,4},{3,5},{4,6},{5,7},{6,0},{7,1},{8,10},{9,11},{10,... | collective-permute-start | bytes 155144 | tf_op jit(solution)/shard_map/ppermute | solution.py:96
  17.4 27.3 %collective-permute-start.2 = (bf16[2,12928]{1,0:T(2,128)(2,1)}, bf16[2,12928]{1,0:T(2,128)(2,1)}, u32[]{:S(2)}, u32[]{:S(2)}) collective-permute-start(bf16[2,12928]{1,0:T(2,128)(2,1)} %get-tuple-element.27), channel_id=1, source_target_pairs={{0,3},{1,4},{2,5},{3,6},{4,7},{5,0},{6,1},{7,2},{8,11},{9,12},{10,... | collective-permute-start | bytes 155144 | tf_op jit(solution)/shard_map/ppermute | solution.py:96
  20.0 24.7 %collective-permute-start.3 = (bf16[2,12928]{1,0:T(2,128)(2,1)}, bf16[2,12928]{1,0:T(2,128)(2,1)}, u32[]{:S(2)}, u32[]{:S(2)}) collective-permute-start(bf16[2,12928]{1,0:T(2,128)(2,1)} %get-tuple-element.26), channel_id=1, source_target_pairs={{0,4},{1,5},{2,6},{3,7},{4,0},{5,1},{6,2},{7,3},{8,12},{9,13},{10,... | collective-permute-start | bytes 155144 | tf_op jit(solution)/shard_map/ppermute | solution.py:96
  21.2 23.5 %collective-permute-start.4 = (bf16[2,12928]{1,0:T(2,128)(2,1)}, bf16[2,12928]{1,0:T(2,128)(2,1)}, u32[]{:S(2)}, u32[]{:S(2)}) collective-permute-start(bf16[2,12928]{1,0:T(2,128)(2,1)} %get-tuple-element.25), channel_id=1, source_target_pairs={{0,5},{1,6},{2,7},{3,0},{4,1},{5,2},{6,3},{7,4},{8,13},{9,14},{10,... | collective-permute-start | bytes 155144 | tf_op jit(solution)/shard_map/ppermute | solution.py:96
  24.0 8.3 %copy-start.31 = (f32[64]{0:T(128)S(1)}, f32[64]{0:T(128)}, u32[]{:S(2)}) copy-start(f32[64]{0:T(128)} %param.11) | copy-start | bytes 772
  24.0 19.3 %copy-start.5 = (bf16[2,128,800]{1,2,0:T(8,128)(2,1)S(1)}, bf16[2,128,800]{1,2,0:T(8,128)(2,1)}, u32[]{:S(2)}) copy-start(bf16[2,128,800]{1,2,0:T(8,128)(2,1)} %param.16) | copy-start | bytes 1228804
  25.4 32.6 %all-to-all-start = ((f32[32,1,2525]{2,1,0:T(1,128)}), f32[32,1,2525]{2,1,0:T(1,128)}, u32[]{:S(2)}, u32[]{:S(2)}) async-start(f32[32,1,2525]{2,1,0:T(1,128)} %all_to_all.13), calls=%async_computation | async-start | bytes 655360 | tf_op jit(solution)/shard_map/all_to_all | solution.py:171
  37.7 7.0 %collective-permute-start.5 = (bf16[2,12928]{1,0:T(2,128)(2,1)}, bf16[2,12928]{1,0:T(2,128)(2,1)}, u32[]{:S(2)}, u32[]{:S(2)}) collective-permute-start(bf16[2,12928]{1,0:T(2,128)(2,1)} %get-tuple-element.24), channel_id=1, source_target_pairs={{0,6},{1,7},{2,0},{3,1},{4,2},{5,3},{6,4},{7,5},{8,14},{9,15},{10,... | collective-permute-start | bytes 155144 | tf_op jit(solution)/shard_map/ppermute | solution.py:96
  41.2 4.2 %collective-permute-start.6 = (bf16[2,12928]{1,0:T(2,128)(2,1)S(1)}, bf16[2,12928]{1,0:T(2,128)(2,1)}, u32[]{:S(2)}, u32[]{:S(2)}) collective-permute-start(bf16[2,12928]{1,0:T(2,128)(2,1)S(1)} %get-tuple-element.23), channel_id=1, source_target_pairs={{0,7},{1,0},{2,1},{3,2},{4,3},{5,4},{6,5},{7,6},{8,15},{9,8},{10,9... | collective-permute-start | bytes 155144 | tf_op jit(solution)/shard_map/ppermute | solution.py:96
  52.0 11.7 %copy-start.13 = (f32[16]{0:T(128)}, f32[16]{0:T(128)S(1)}, u32[]{:S(2)}) copy-start(f32[16]{0:T(128)S(1)} %get-tuple-element.37) | copy-start | bytes 196
  53.4 19.2 %collective-permute-start.10 = (bf16[2,2,16,400]{3,0,2,1:T(2,128)(2,1)S(1)}, bf16[2,2,16,400]{3,0,2,1:T(2,128)(2,1)}, u32[]{:S(2)}, u32[]{:S(2)}) collective-permute-start(bf16[2,2,16,400]{3,0,2,1:T(2,128)(2,1)S(1)} %get-tuple-element.18), channel_id=1, source_target_pairs={{0,4},{1,5},{2,6},{3,7},{4,0},{5,1},{6,2},{7,3},{8,12},{9,13},{10,... | collective-permute-start | bytes 153608 | tf_op jit(solution)/shard_map/ppermute | solution.py:96
  53.4 19.8 %collective-permute-start.11 = (bf16[2,2,16,400]{3,0,2,1:T(2,128)(2,1)S(1)}, bf16[2,2,16,400]{3,0,2,1:T(2,128)(2,1)}, u32[]{:S(2)}, u32[]{:S(2)}) collective-permute-start(bf16[2,2,16,400]{3,0,2,1:T(2,128)(2,1)S(1)} %get-tuple-element.17), channel_id=1, source_target_pairs={{0,3},{1,4},{2,5},{3,6},{4,7},{5,0},{6,1},{7,2},{8,11},{9,12},{10,... | collective-permute-start | bytes 153608 | tf_op jit(solution)/shard_map/ppermute | solution.py:96
  60.1 23.1 %all-to-all-start.1 = ((f32[32,1,2525]{2,1,0:T(1,128)}), f32[32,1,2525]{2,1,0:T(1,128)}, u32[]{:S(2)}, u32[]{:S(2)}) async-start(f32[32,1,2525]{2,1,0:T(1,128)} %broadcast_in_dim.23), calls=%async_computation.1 | async-start | bytes 655360 | tf_op jit(solution)/shard_map/all_to_all | solution.py:78
  66.4 11.8 %collective-permute-start.12 = (bf16[2,2,16,400]{3,0,2,1:T(2,128)(2,1)}, bf16[2,2,16,400]{3,0,2,1:T(2,128)(2,1)}, u32[]{:S(2)}, u32[]{:S(2)}) collective-permute-start(bf16[2,2,16,400]{3,0,2,1:T(2,128)(2,1)} %get-tuple-element.16), channel_id=1, source_target_pairs={{0,2},{1,3},{2,4},{3,5},{4,6},{5,7},{6,0},{7,1},{8,10},{9,11},{10,... | collective-permute-start | bytes 153608 | tf_op jit(solution)/shard_map/ppermute | solution.py:96
  67.9 10.3 %collective-permute-start.13 = (bf16[2,2,16,400]{3,0,2,1:T(2,128)(2,1)}, bf16[2,2,16,400]{3,0,2,1:T(2,128)(2,1)}, u32[]{:S(2)}, u32[]{:S(2)}) collective-permute-start(bf16[2,2,16,400]{3,0,2,1:T(2,128)(2,1)} %get-tuple-element.15), channel_id=1, source_target_pairs={{0,1},{1,2},{2,3},{3,4},{4,5},{5,6},{6,7},{7,0},{8,9},{9,10},{10,1... | collective-permute-start | bytes 153608 | tf_op jit(solution)/shard_map/ppermute | solution.py:96
  69.4 8.8 %collective-permute-start.7 = (bf16[2,2,16,400]{3,0,2,1:T(2,128)(2,1)}, bf16[2,2,16,400]{3,0,2,1:T(2,128)(2,1)}, u32[]{:S(2)}, u32[]{:S(2)}) collective-permute-start(bf16[2,2,16,400]{3,0,2,1:T(2,128)(2,1)} %get-tuple-element.21), channel_id=1, source_target_pairs={{0,7},{1,0},{2,1},{3,2},{4,3},{5,4},{6,5},{7,6},{8,15},{9,8},{10,9... | collective-permute-start | bytes 153608 | tf_op jit(solution)/shard_map/ppermute | solution.py:96
  72.6 5.5 %collective-permute-start.8 = (bf16[2,2,16,400]{3,0,2,1:T(2,128)(2,1)}, bf16[2,2,16,400]{3,0,2,1:T(2,128)(2,1)}, u32[]{:S(2)}, u32[]{:S(2)}) collective-permute-start(bf16[2,2,16,400]{3,0,2,1:T(2,128)(2,1)} %get-tuple-element.20), channel_id=1, source_target_pairs={{0,6},{1,7},{2,0},{3,1},{4,2},{5,3},{6,4},{7,5},{8,14},{9,15},{10,... | collective-permute-start | bytes 153608 | tf_op jit(solution)/shard_map/ppermute | solution.py:96
  73.2 6.5 %collective-permute-start.9 = (bf16[2,2,16,400]{3,0,2,1:T(2,128)(2,1)S(1)}, bf16[2,2,16,400]{3,0,2,1:T(2,128)(2,1)}, u32[]{:S(2)}, u32[]{:S(2)}) collective-permute-start(bf16[2,2,16,400]{3,0,2,1:T(2,128)(2,1)S(1)} %get-tuple-element.19), channel_id=1, source_target_pairs={{0,5},{1,6},{2,7},{3,0},{4,1},{5,2},{6,3},{7,4},{8,13},{9,14},{10,... | collective-permute-start | bytes 153608 | tf_op jit(solution)/shard_map/ppermute | solution.py:96
  76.6 5.5 %copy-start.16 = (s32[8]{0:T(128)S(1)}, s32[8]{0:T(128)}, u32[]{:S(2)}) copy-start(s32[8]{0:T(128)} %copy-done.15) | copy-start | bytes 100
  82.1 3.3 %copy-start.11 = (s32[400]{0:T(512)S(1)}, s32[400]{0:T(512)}, u32[]{:S(2)}) copy-start(s32[400]{0:T(512)} %get-tuple-element.36) | copy-start | bytes 4804
  82.1 3.3 %copy-start.25 = (pred[400]{0:T(512)(128)(4,1)S(1)}, pred[400]{0:T(512)(128)(4,1)}, u32[]{:S(2)}) copy-start(pred[400]{0:T(512)(128)(4,1)} %fusion.93) | copy-start | bytes 1204
  82.5 3.5 %copy-start.21 = (s32[400]{0:T(512)S(1)}, s32[400]{0:T(512)}, u32[]{:S(2)}) copy-start(s32[400]{0:T(512)} %fusion.94) | copy-start | bytes 4804
  82.5 3.5 %copy-start.22 = (s32[400]{0:T(512)S(1)}, s32[400]{0:T(512)}, u32[]{:S(2)}) copy-start(s32[400]{0:T(512)} %get-tuple-element.35) | copy-start | bytes 4804
  82.5 3.5 %copy-start.33 = (pred[400]{0:T(512)(128)(4,1)S(1)}, pred[400]{0:T(512)(128)(4,1)}, u32[]{:S(2)}) copy-start(pred[400]{0:T(512)(128)(4,1)} %compare_and_fusion) | copy-start | bytes 1204
  83.2 3.9 %copy-start.12 = (s32[400]{0:T(512)S(1)}, s32[400]{0:T(512)}, u32[]{:S(2)}) copy-start(s32[400]{0:T(512)} %fusion.92) | copy-start | bytes 4804
  83.2 3.9 %copy-start.27 = (pred[400]{0:T(512)(128)(4,1)S(1)}, pred[400]{0:T(512)(128)(4,1)}, u32[]{:S(2)}) copy-start(pred[400]{0:T(512)(128)(4,1)} %fusion.91) | copy-start | bytes 1204
  91.4 3.3 %copy-start.3 = (bf16[2,400,400]{2,1,0:T(8,128)(2,1)S(1)}, bf16[2,400,400]{2,1,0:T(8,128)(2,1)}, u32[]{:S(2)}) copy-start(bf16[2,400,400]{2,1,0:T(8,128)(2,1)} %constant.137.clone) | copy-start | bytes 1920004
  91.7 6.1 %collective-permute-start.14 = (bf16[2,32,1200]{2,1,0:T(8,128)(2,1)S(1)}, bf16[2,32,1200]{2,1,0:T(8,128)(2,1)S(1)}, u32[]{:S(2)}, u32[]{:S(2)}) collective-permute-start(bf16[2,32,1200]{2,1,0:T(8,128)(2,1)S(1)} %get-tuple-element.12), channel_id=1, source_target_pairs={{0,8},{8,16},{16,24},{24,0},{1,9},{9,17},{17,25},{25,1},{2,10},{10... | collective-permute-start | bytes 460808 | tf_op jit(solution)/shard_map/ppermute | solution.py:106
  91.8 7.1 %collective-permute-start.15 = (bf16[2,32,1200]{2,1,0:T(8,128)(2,1)S(1)}, bf16[2,32,1200]{2,1,0:T(8,128)(2,1)S(1)}, u32[]{:S(2)}, u32[]{:S(2)}) collective-permute-start(bf16[2,32,1200]{2,1,0:T(8,128)(2,1)S(1)} %get-tuple-element.14), channel_id=1, source_target_pairs={{0,16},{8,24},{16,0},{24,8},{1,17},{9,25},{17,1},{25,9},{2,18},{10... | collective-permute-start | bytes 460808 | tf_op jit(solution)/shard_map/ppermute | solution.py:106
  93.3 7.5 %collective-permute-start.16 = (bf16[2,32,1200]{2,1,0:T(8,128)(2,1)S(1)}, bf16[2,32,1200]{2,1,0:T(8,128)(2,1)S(1)}, u32[]{:S(2)}, u32[]{:S(2)}) collective-permute-start(bf16[2,32,1200]{2,1,0:T(8,128)(2,1)S(1)} %get-tuple-element.13), channel_id=1, source_target_pairs={{0,24},{8,0},{16,8},{24,16},{1,25},{9,1},{17,9},{25,17},{2,26},{10... | collective-permute-start | bytes 460808 | tf_op jit(solution)/shard_map/ppermute | solution.py:106
  (21 other events, 32.4 us)

commit v9 on v8

--- a/solution.py
+++ b/solution.py
@@ -135,7 +135,7 @@
     before = jnp.cumsum(member, axis=0) - member
     slot_rank = jnp.sum(member * before, axis=1)
     me = lax.axis_index("slab")
-    seat_index = ((destination - me) % slab_count) * capacity + slot_rank
+    seat_index = destination * capacity + slot_rank
     seat_count = slab_count * capacity
     seat_pick = (seat_index[:, None] == jnp.arange(seat_count, dtype=jnp.int32)[None, :]).astype(
         jnp.bfloat16
@@ -169,7 +169,7 @@
     power_half = jnp.sum(low_half * low_half, axis=(0, 1))
     pieces = power_half.reshape(device_count, rows_half * box_size // device_count)
     gathered = lax.all_to_all(pieces, ("img", "slab"), 0, 0, tiled=True)
-    got = shift_exchange(send, slab_count, capacity, 1)
+    got = lax.all_to_all(send, "slab", 0, 0, tiled=True)
     got_blocks = got[:, : RB * 2 * box_size].reshape(seat_count, RB, 2 * box_size)
     got_info = got[:, RB * 2 * box_size : RB * 2 * box_size + 6].astype(jnp.int32)
 
@@ -194,7 +194,7 @@
     noise_level = jnp.sqrt(power / (particles * device_count) + 1e-06)
     level_both = jnp.concatenate([noise_level, noise_level], axis=1)
 
-    returned_rows = shift_exchange(projected, slab_count, capacity, -1)
+    returned_rows = lax.all_to_all(projected, "slab", 0, 0, tiled=True)
 
     got_rows = low_row_ids(got_info[:, 4], box_size)
     got_contrast = contrast_curve(lookup_defocus(got_info[:, 5], defocus), got_rows, box_size)

time: 104 us -> 102 us (0.981); the launches traced: 102 us -> 101 us
  waiting for transfers between devices: 5.29 us -> 24.3 us
  starting transfers between devices: 37.8 us -> 23.1 us
  other arithmetic: 26.3 us -> 20.6 us
  matrix products: 11.6 us -> 14 us
  local copies, waits for them, and re-layouts: 18.1 us -> 16.9 us
    ppermute x14 -> x0, starting transfers between devices: 28 us -> none  [shift_exchange(): lax.ppermute(values[d * capacity:(d + 1) * capacity], 'slab', pairs)]
    all_to_all x0 -> x2, waiting for transfers between devices: none -> 16.4 us  [the longest x1 11.9 us: body(): returned_rows = lax.all_to_all(projected, 'slab', 0, 0, tiled=True)]
    all_to_all x0 -> x2, starting transfers between devices: none -> 9 us  [the longest x1 5.54 us: body(): returned_rows = lax.all_to_all(projected, 'slab', 0, 0, tiled=True)]
    all_to_all x1, waiting for transfers between devices: 0.01 us -> 7.85 us  [body(): gathered = lax.all_to_all(pieces, ('img', 'slab'), 0, 0, tiled=True)]
    concatenate x2 -> x0, local copies, waits for them, and re-layouts: 5.3 us -> none  [shift_exchange(): return jnp.concatenate(pieces, axis=0)]
    all_to_all x1, starting transfers between devices: 3.3 us -> 7.3 us  [body(): gathered = lax.all_to_all(pieces, ('img', 'slab'), 0, 0, tiled=True)]
    ppermute x3, waiting for transfers between devices: 2.96 us -> 0.01 us  [reduce_over_img(): total = total + lax.ppermute(piece, 'img', pairs).astype(jnp.float32)]
    ppermute x14 -> x0, waiting for transfers between devices: 2.33 us -> none  [shift_exchange(): lax.ppermute(values[d * capacity:(d + 1) * capacity], 'slab', pairs)]
  transfers between devices with their start and end apart: 19 -> 7, of which waited for: 4 -> 3; matrix products, arithmetic and copies ran while one was open for 33% -> 25% of each run, Pallas kernels for 0% -> 0%
where the time goes in v9:
time: 102 us; the launch traced here: 101 us
  waiting for transfers between devices  24.3 us (24%)
  starting transfers between devices  23.1 us (23%)
  other arithmetic  20.6 us (20%)
  local copies, waits for them, and re-layouts  16.9 us (17%)
  matrix products  14 us (14%)
  between operations  2.53 us (2%)
    all_to_all x1, waiting for transfers between devices, body(): returned_rows = lax.all_to_all(projected, 'slab', 0, 0, tiled=True)  11.9 us
    all_to_all x1, waiting for transfers between devices, body(): gathered = lax.all_to_all(pieces, ('img', 'slab'), 0, 0, tiled=True)  7.85 us
    all_to_all x1, starting transfers between devices, body(): gathered = lax.all_to_all(pieces, ('img', 'slab'), 0, 0, tiled=True)  7.3 us
    all_to_all x1, starting transfers between devices, body(): returned_rows = lax.all_to_all(projected, 'slab', 0, 0, tiled=True)  5.54 us
    dot_general x1, matrix products, transform(): jnp.einsum('gky,hym->ghkm', tables, rowwise, preferred_element_type=jnp.f...  4.59 us
    all_to_all x1, waiting for transfers between devices, body(): got = lax.all_to_all(send, 'slab', 0, 0, tiled=True)  4.54 us
    unnamed x35, local copies, waits for them, and re-layouts  3.96 us
    all_to_all x1, starting transfers between devices, power_gather(): back = lax.all_to_all(spread, ('img', 'slab'), 0, 0, tiled=True)  3.77 us
  transfers between devices with their start and end apart: 7, of which 3 were waited for; matrix products, arithmetic and copies ran while one was open for 25% of the time, Pallas kernels for 0%

profile of v9, /device:TPU:0, one launch (start us, length us, event | category | flops | bytes accessed | tf_op | source)
XLA Modules:
  0.0 101.4 jit_solution(15941024486882521175)
XLA Ops:
  0.6 1.0 copy-done
  1.6 4.6 %convolution_bitcast_fusion.1 = f32[2,2,400,400]{3,2,0,1:T(8,128)} fusion(bf16[2,400,400]{2,1,0:T(8,128)(2,1)} %constant.121.clone, bf16[1,400,400]{2,1,0:T(8,128)(2,1)S(1)} %copy-done), kind=kOutput, calls=%fused_computation.3 | convolution fusion | flops 768320000 | bytes 3520000 | tf_op jit(solution)/shard_map/gky,hym->ghkm/dot_general | solution.py:27
  6.2 1.6 %fusion.20 = f32[1,400,400]{2,1,0:T(8,128)S(1)} fusion(f32[2,2,400,400]{3,2,0,1:T(8,128)} %convolution_bitcast_fusion.1), kind=kLoop, calls=%fused_computation.40 | loop fusion | flops 320000 | bytes 1920000 | tf_op jit(solution)/shard_map/neg | solution.py:29
  7.8 1.5 %fusion.22 = f32[1,400,400]{2,1,0:T(8,128)S(1)} fusion(f32[2,2,400,400]{3,2,0,1:T(8,128)} %convolution_bitcast_fusion.1), kind=kLoop, calls=%fused_computation.43 | loop fusion | flops 160000 | bytes 1920000 | tf_op jit(solution)/shard_map/sub | solution.py:28
  9.6 1.4 %all_to_all.28 = f32[32,1,2525]{2,1,0:T(1,128)} reshape(f32[202,400]{1,0:T(8,128)S(1)} %fusion.13) | data formatting | bytes 646400 | tf_op jit(solution)/shard_map/all_to_all | solution.py:171
  10.9 7.3 %all-to-all-start = ((f32[32,1,2525]{2,1,0:T(1,128)}), f32[32,1,2525]{2,1,0:T(1,128)S(1)}, u32[]{:S(2)}, u32[]{:S(2)}) async-start(f32[32,1,2525]{2,1,0:T(1,128)} %all_to_all.28), calls=%async_computation | async-start | bytes 655360 | tf_op jit(solution)/shard_map/all_to_all | solution.py:171
  20.9 0.9 all_to_all.24
  22.5 7.8 %all-to-all-done = f32[32,1,2525]{2,1,0:T(1,128)S(1)} async-done(((f32[32,1,2525]{2,1,0:T(1,128)}), f32[32,1,2525]{2,1,0:T(1,128)S(1)}, u32[]{:S(2)}, u32[]{:S(2)}) %all-to-all-start) | async-done | bytes 323232 | tf_op jit(solution)/shard_map/all_to_all | solution.py:171
  30.4 3.5 %all-to-all-start.2 = ((bf16[8,2,12928]{2,1,0:T(2,128)(2,1)}), bf16[8,2,12928]{2,1,0:T(2,128)(2,1)S(1)}, u32[]{:S(2)}, u32[]{:S(2)}) async-start(bf16[8,2,12928]{2,1,0:T(2,128)(2,1)} %all_to_all.24), calls=%async_computation.2 | async-start | bytes 827392 | tf_op jit(solution)/shard_map/all_to_all | solution.py:172
  33.9 1.2 %copy.71 = bf16[2,128,800]{2,1,0:T(8,128)(2,1)S(1)} copy(bf16[2,128,800]{1,2,0:T(8,128)(2,1)} %param.16) | data formatting | bytes 819200 | tf_op args[7]
  35.1 1.3 %reshape.358 = bf16[2,8,16,2,400]{4,3,2,1,0:T(2,128)(2,1)} reshape(bf16[2,128,800]{2,1,0:T(8,128)(2,1)S(1)} %copy.71) | data formatting | bytes 819200 | tf_op jit(solution)/shard_map/reshape | solution.py:182
  37.3 3.7 %fusion.40 = f32[400,400]{1,0:T(8,128)} fusion(f32[]{:T(128)S(6)} %mul.155, s32[400]{0:T(512)S(1)} %fusion.88), kind=kLoop, calls=%fused_computation.72 | loop fusion | flops 1120000 | bytes 641604 | tf_op jit(solution)/shard_map/convert_element_type | solution.py:243
  41.2 4.5 %all-to-all-done.2 = bf16[8,2,12928]{2,1,0:T(2,128)(2,1)S(1)} async-done(((bf16[8,2,12928]{2,1,0:T(2,128)(2,1)}), bf16[8,2,12928]{2,1,0:T(2,128)(2,1)S(1)}, u32[]{:S(2)}, u32[]{:S(2)}) %all-to-all-start.2) | async-done | bytes 413728 | tf_op jit(solution)/shard_map/all_to_all | solution.py:172
  45.7 0.9 broadcast_in_dim.23
  46.6 3.8 %all-to-all-start.1 = ((f32[32,1,2525]{2,1,0:T(1,128)}), f32[32,1,2525]{2,1,0:T(1,128)S(1)}, u32[]{:S(2)}, u32[]{:S(2)}) async-start(f32[32,1,2525]{2,1,0:T(1,128)} %broadcast_in_dim.23), calls=%async_computation.1 | async-start | bytes 655360 | tf_op jit(solution)/shard_map/all_to_all | solution.py:78
  51.0 0.9 slice_convert_fusion
  51.9 1.7 %fusion.35 = f32[16,2,16,400]{3,0,2,1:T(8,128)S(1)} fusion(bf16[16,2,16,400]{3,1,2,0:T(2,128)(2,1)} %bitcast.110, s32[16]{0:T(128)S(1)} %get-tuple-element.4), kind=kOutput, calls=%fused_computation.60 | convolution fusion | flops 6553856 | bytes 1228864 | tf_op jit(solution)/shard_map/sq,qhix->shix/dot_general | solution.py:184
  53.7 1.4 %slice.162 = f32[16,2,16,399]{3,0,2,1:T(8,128)} slice(f32[16,2,16,400]{3,0,2,1:T(8,128)S(1)} %fusion.35), slice={[0:16], [0:2], [0:16], [1:400]} | slice | bytes 1634304 | tf_op jit(solution)/shard_map/jit(_roll_static)/slice | solution.py:189
  55.2 2.7 %reshape.363 = f32[16,16,800]{2,1,0:T(8,128)} reshape(f32[16,12800]{1,0:T(8,128)} %slice_convert_fusion) | data formatting | bytes 1638400 | tf_op jit(solution)/shard_map/convert_element_type | solution.py:211
  57.9 2.7 %negate_convert_fusion.1 = (bf16[16,16,400]{2,0,1:T(8,128)(2,1)}, f32[16,16,400]{2,0,1:T(8,128)S(1)}) fusion(f32[16]{0:T(128)S(1)} %get-tuple-element.21, s32[400]{0:T(512)S(1)} %fusion.88, s32[16,16]{0,1:T(8,128)S(1)} %fusion.67), kind=kLoop, calls=%fused_computation.63 | loop fusion | flops 819200 | bytes 617088 | tf_op jit(solution)/shard_map/convert_element_type | solution.py:55
  60.7 2.9 %fusion.33 = f32[16,16,400]{2,0,1:T(8,128)} fusion(f32[16,16,399]{2,0,1:T(8,128)S(1)} %bitcast.107, f32[16,16,1]{2,0,1:T(8,128)S(1)} %slice.180, f32[16]{0:T(128)S(1)} %get-tuple-element.6, f32[16]{0:T(128)S(1)} %get-tuple-element.22, f32[16]{0:T(128)S(1)} %get-tuple-element.21, s32[400]{0:T(512)S(1)} %fusion.88, s32[16,16]{0,1:T(8,128)S(1)} %fusion.67), kind=kLoop, calls=%fused_computation.58 | loop fusion | flops 1228800 | bytes 822016 | tf_op jit(solution)/shard_map/add | solution.py:215
  65.4 1.0 %fusion.31 = f32[202,400]{0,1:T(8,128)S(1)} fusion(f32[202,400]{1,0:T(8,128)S(1)} %reshape.355, s32[400]{0:T(512)S(1)} %get-tuple-element.19, s32[400]{0:T(512)S(1)} %fusion.95, s32[400]{0:T(512)S(1)} %get-tuple-element.20, pred[400]{0:T(512)(128)(4,1)S(1)} %compare_and_fusion), kind=kOutput, calls=%fused_computation.55 | convolution fusion | flops 388160000 | bytes 651600 | tf_op jit(solution)/shard_map/dot_general | solution.py:84
  69.9 0.9 convolution_convert_fusion.1
  72.7 1.7 %collective-permute-start.1 = (bf16[2,32,1200]{2,1,0:T(8,128)(2,1)}, bf16[2,32,1200]{2,1,0:T(8,128)(2,1)S(1)}, u32[]{:S(2)}, u32[]{:S(2)}) collective-permute-start(bf16[2,32,1200]{2,1,0:T(8,128)(2,1)} %get-tuple-element.14), channel_id=1, source_target_pairs={{0,16},{8,24},{16,0},{24,8},{1,17},{9,25},{17,1},{25,9},{2,18},{10... | collective-permute-start | bytes 460808 | tf_op jit(solution)/shard_map/ppermute | solution.py:106
  74.4 1.3 %collective-permute-start.2 = (bf16[2,32,1200]{2,1,0:T(8,128)(2,1)}, bf16[2,32,1200]{2,1,0:T(8,128)(2,1)}, u32[]{:S(2)}, u32[]{:S(2)}) collective-permute-start(bf16[2,32,1200]{2,1,0:T(8,128)(2,1)} %get-tuple-element.13), channel_id=1, source_target_pairs={{0,24},{8,0},{16,8},{24,16},{1,25},{9,1},{17,9},{25,17},{2,26},{10... | collective-permute-start | bytes 460808 | tf_op jit(solution)/shard_map/ppermute | solution.py:106
  76.0 1.1 %copy.74 = bf16[16,2,16,400]{3,2,1,0:T(8,128)(2,1)} copy(bf16[16,2,16,400]{3,0,2,1:T(8,128)(2,1)S(1)} %fusion.10) | data formatting | bytes 819200 | tf_op jit(solution)/shard_map/convert_element_type | solution.py:190
  77.1 5.5 %all-to-all-start.3 = ((bf16[16,2,16,400]{3,2,1,0:T(8,128)(2,1)}), bf16[16,2,16,400]{3,2,1,0:T(8,128)(2,1)}, u32[]{:S(2)}, u32[]{:S(2)}) async-start(bf16[16,2,16,400]{3,2,1,0:T(8,128)(2,1)} %copy.74), calls=%async_computation.3 | async-start | bytes 1048576 | tf_op jit(solution)/shard_map/all_to_all | solution.py:197
  82.7 1.1 %fusion.56 = f32[2,32,1200]{2,1,0:T(8,128)S(1)} fusion(bf16[2,32,1200]{2,1,0:T(8,128)(2,1)} %collective-permute-done.2, bf16[2,32,1200]{2,1,0:T(8,128)(2,1)S(1)} %collective-permute-done.1, bf16[2,32,1200]{2,1,0:T(8,128)(2,1)S(1)} %collective-permute-done, bf16[2,4,32,1200]{3,2,1,0:T(8,128)(2,1)} %bitcast.109, s32[]{:T(128)S(6)} %select_n.93), kind=kLoop, calls=%fused_computation.89 | loop fusion | flops 537600 | bytes 921604 | tf_op jit(solution)/shard_map/add | solution.py:106
  84.7 11.9 %all-to-all-done.3 = bf16[16,2,16,400]{3,2,1,0:T(8,128)(2,1)} async-done(((bf16[16,2,16,400]{3,2,1,0:T(8,128)(2,1)}), bf16[16,2,16,400]{3,2,1,0:T(8,128)(2,1)}, u32[]{:S(2)}, u32[]{:S(2)}) %all-to-all-start.3) | async-done | bytes 409632 | tf_op jit(solution)/shard_map/all_to_all | solution.py:197
  96.6 1.6 %fusion.7 = bf16[1,2,8,16,400]{4,2,3,1,0:T(8,128)(2,1)S(1)} fusion(bf16[16,2,16,400]{3,2,1,0:T(8,128)(2,1)} %all-to-all-done.3, s32[8]{0:T(128)S(1)} %multiply_add_fusion), kind=kOutput, calls=%fused_computation.18 | convolution fusion | flops 3379328 | bytes 614432 | tf_op jit(solution)/shard_map/rs,shix->rhix/dot_general | solution.py:233
  98.3 1.1 %convolution_bitcast_fusion = f32[2,2,400,400]{3,2,1,0:T(8,128)S(1)} fusion(bf16[2,400,400]{2,1,0:T(8,128)(2,1)S(1)} %copy-done.9, f32[1,400,400]{2,1,0:T(8,128)S(1)} %fusion.20, f32[1,400,400]{2,1,0:T(8,128)S(1)} %fusion.22, bf16[2,64,400]{2,1,0:T(8,128)(2,1)S(1)} %get-tuple-element.16, bf16[2,64,400]{2,1,0:T(8,128)(2,1)S(1)} %get-tuple-element.15, ...), kind=kOutput, calls=%fused_computation.2 | convolution fusion | flops 515520000 | bytes 5965600 | tf_op jit(solution)/shard_map/hyj,gmj->hgym/dot_general | solution.py:34
  100.5 0.9 fusion.15
  (102 shorter events, 13.4 us)
Async XLA Ops:
  0.6 1.0 copy-start
  10.9 19.4 %all-to-all-start = ((f32[32,1,2525]{2,1,0:T(1,128)}), f32[32,1,2525]{2,1,0:T(1,128)S(1)}, u32[]{:S(2)}, u32[]{:S(2)}) async-start(f32[32,1,2525]{2,1,0:T(1,128)} %all_to_all.28), calls=%async_computation | async-start | bytes 655360 | tf_op jit(solution)/shard_map/all_to_all | solution.py:171
  18.2 0.9 copy-start.12
  18.4 1.7 %copy-start.13 = (s32[1,8]{1,0:T(1,128)S(1)}, s32[1,8]{1,0:T(1,128)}, u32[]{:S(2)}) copy-start(s32[1,8]{1,0:T(1,128)} %param.13) | copy-start | bytes 100
  18.4 1.8 %copy-start.14 = (s32[1,8]{1,0:T(1,128)S(1)}, s32[1,8]{1,0:T(1,128)}, u32[]{:S(2)}) copy-start(s32[1,8]{1,0:T(1,128)} %param.14) | copy-start | bytes 100
  18.4 1.9 %copy-start.15 = (s32[1,8]{1,0:T(1,128)S(1)}, s32[1,8]{1,0:T(1,128)}, u32[]{:S(2)}) copy-start(s32[1,8]{1,0:T(1,128)} %param.15) | copy-start | bytes 100
  18.4 3.4 %copy-start.16 = (f32[64]{0:T(128)S(1)}, f32[64]{0:T(128)}, u32[]{:S(2)}) copy-start(f32[64]{0:T(128)} %param.11) | copy-start | bytes 772
  30.4 15.4 %all-to-all-start.2 = ((bf16[8,2,12928]{2,1,0:T(2,128)(2,1)}), bf16[8,2,12928]{2,1,0:T(2,128)(2,1)S(1)}, u32[]{:S(2)}, u32[]{:S(2)}) async-start(bf16[8,2,12928]{2,1,0:T(2,128)(2,1)} %all_to_all.24), calls=%async_computation.2 | async-start | bytes 827392 | tf_op jit(solution)/shard_map/all_to_all | solution.py:172
  46.6 16.9 %all-to-all-start.1 = ((f32[32,1,2525]{2,1,0:T(1,128)}), f32[32,1,2525]{2,1,0:T(1,128)S(1)}, u32[]{:S(2)}, u32[]{:S(2)}) async-start(f32[32,1,2525]{2,1,0:T(1,128)} %broadcast_in_dim.23), calls=%async_computation.1 | async-start | bytes 655360 | tf_op jit(solution)/shard_map/all_to_all | solution.py:78
  53.7 4.3 %copy-start.1 = (f32[16,2,16,400]{3,0,2,1:T(8,128)}, f32[16,2,16,400]{3,0,2,1:T(8,128)S(1)}, u32[]{:S(2)}) copy-start(f32[16,2,16,400]{3,0,2,1:T(8,128)S(1)} %fusion.35) | copy-start | bytes 2457604
  66.4 1.2 %copy-start.8 = (f32[16,16,800]{2,1,0:T(8,128)S(1)}, f32[16,16,800]{2,1,0:T(8,128)}, u32[]{:S(2)}) copy-start(f32[16,16,800]{2,1,0:T(8,128)} %reshape.363) | copy-start | bytes 2457604
  66.4 1.2 %copy-start.11 = (bf16[16,16,400]{2,0,1:T(8,128)(2,1)S(1)}, bf16[16,16,400]{2,0,1:T(8,128)(2,1)}, u32[]{:S(2)}) copy-start(bf16[16,16,400]{2,0,1:T(8,128)(2,1)} %get-tuple-element.17) | copy-start | bytes 614404
  67.2 1.3 %copy-start.4 = (f32[400,400]{1,0:T(8,128)}, f32[400,400]{1,0:T(8,128)S(1)}, u32[]{:S(2)}) copy-start(f32[400,400]{1,0:T(8,128)S(1)} %fusion.6) | copy-start | bytes 1920004
  68.9 1.0 %copy-start.7 = (f32[16,16,400]{2,0,1:T(8,128)S(1)}, f32[16,16,400]{2,0,1:T(8,128)}, u32[]{:S(2)}) copy-start(f32[16,16,400]{2,0,1:T(8,128)} %fusion.33) | copy-start | bytes 1228804
  69.9 5.8 %copy-start.3 = (f32[16,2,16,399]{3,0,2,1:T(8,128)S(1)}, f32[16,2,16,399]{3,0,2,1:T(8,128)}, u32[]{:S(2)}) copy-start(f32[16,2,16,399]{3,0,2,1:T(8,128)} %slice.162) | copy-start | bytes 2451460
  70.8 4.9 %copy-start.2 = (f32[16,2,16,400]{3,0,2,1:T(8,128)S(1)}, f32[16,2,16,400]{3,0,2,1:T(8,128)}, u32[]{:S(2)}) copy-start(f32[16,2,16,400]{3,0,2,1:T(8,128)} %copy-done.1) | copy-start | bytes 2457604
  70.8 4.9 %slice-start = ((f32[16,2,16,400]{3,0,2,1:T(8,128)}), f32[16,2,16,1]{3,0,2,1:T(8,128)S(1)}, s32[]{:S(2)}) async-start(f32[16,2,16,400]{3,0,2,1:T(8,128)} %copy-done.1), calls=%async_computation.4 | async-start | bytes 524288 | tf_op jit(solution)/shard_map/jit(_roll_static)/slice | solution.py:189
  71.0 0.8 copy-start.6
  72.6 10.0 %collective-permute-start = (bf16[2,32,1200]{2,1,0:T(8,128)(2,1)}, bf16[2,32,1200]{2,1,0:T(8,128)(2,1)S(1)}, u32[]{:S(2)}, u32[]{:S(2)}) collective-permute-start(bf16[2,32,1200]{2,1,0:T(8,128)(2,1)} %get-tuple-element.12), channel_id=1, source_target_pairs={{0,8},{8,16},{16,24},{24,0},{1,9},{9,17},{17,25},{25,1},{2,10},{10... | collective-permute-start | bytes 460808 | tf_op jit(solution)/shard_map/ppermute | solution.py:106
  72.7 9.9 %collective-permute-start.1 = (bf16[2,32,1200]{2,1,0:T(8,128)(2,1)}, bf16[2,32,1200]{2,1,0:T(8,128)(2,1)S(1)}, u32[]{:S(2)}, u32[]{:S(2)}) collective-permute-start(bf16[2,32,1200]{2,1,0:T(8,128)(2,1)} %get-tuple-element.14), channel_id=1, source_target_pairs={{0,16},{8,24},{16,0},{24,8},{1,17},{9,25},{17,1},{25,9},{2,18},{10... | collective-permute-start | bytes 460808 | tf_op jit(solution)/shard_map/ppermute | solution.py:106
  74.4 8.3 %collective-permute-start.2 = (bf16[2,32,1200]{2,1,0:T(8,128)(2,1)}, bf16[2,32,1200]{2,1,0:T(8,128)(2,1)}, u32[]{:S(2)}, u32[]{:S(2)}) collective-permute-start(bf16[2,32,1200]{2,1,0:T(8,128)(2,1)} %get-tuple-element.13), channel_id=1, source_target_pairs={{0,24},{8,0},{16,8},{24,16},{1,25},{9,1},{17,9},{25,17},{2,26},{10... | collective-permute-start | bytes 460808 | tf_op jit(solution)/shard_map/ppermute | solution.py:106
  77.1 19.5 %all-to-all-start.3 = ((bf16[16,2,16,400]{3,2,1,0:T(8,128)(2,1)}), bf16[16,2,16,400]{3,2,1,0:T(8,128)(2,1)}, u32[]{:S(2)}, u32[]{:S(2)}) async-start(bf16[16,2,16,400]{3,2,1,0:T(8,128)(2,1)} %copy.74), calls=%async_computation.3 | async-start | bytes 1048576 | tf_op jit(solution)/shard_map/all_to_all | solution.py:197
  82.6 15.7 %copy-start.5 = (f32[400,400]{1,0:T(8,128)S(1)}, f32[400,400]{1,0:T(8,128)}, u32[]{:S(2)}) copy-start(f32[400,400]{1,0:T(8,128)} %copy-done.4) | copy-start | bytes 1920004
  96.6 1.7 %copy-start.9 = (bf16[2,400,400]{2,1,0:T(8,128)(2,1)S(1)}, bf16[2,400,400]{2,1,0:T(8,128)(2,1)}, u32[]{:S(2)}) copy-start(bf16[2,400,400]{2,1,0:T(8,128)(2,1)} %constant.121.clone) | copy-start | bytes 1920004
  96.6 1.7 %copy-start.10 = (f32[400,400]{1,0:T(8,128)S(1)}, f32[400,400]{1,0:T(8,128)}, u32[]{:S(2)}) copy-start(f32[400,400]{1,0:T(8,128)} %fusion.40) | copy-start | bytes 1920004

commit v10 on v9

--- a/solution.py
+++ b/solution.py
@@ -194,7 +194,12 @@
     noise_level = jnp.sqrt(power / (particles * device_count) + 1e-06)
     level_both = jnp.concatenate([noise_level, noise_level], axis=1)
 
-    returned_rows = lax.all_to_all(projected, "slab", 0, 0, tiled=True)
+    groups = projected.reshape((slab_count, capacity) + projected.shape[1:])
+    steps = jnp.arange(slab_count, dtype=jnp.int32)
+    by_shift = jnp.take(groups, (me - steps) % slab_count, axis=0).reshape(projected.shape)
+    came_back = shift_exchange(by_shift, slab_count, capacity, -1)
+    came_back = came_back.reshape((slab_count, capacity) + projected.shape[1:])
+    returned_rows = jnp.take(came_back, (steps - me) % slab_count, axis=0).reshape(projected.shape)
 
     got_rows = low_row_ids(got_info[:, 4], box_size)
     got_contrast = contrast_curve(lookup_defocus(got_info[:, 5], defocus), got_rows, box_size)

time: 102 us -> 112 us (1.098)
  waiting for transfers between devices: 24.3 us -> 16.2 us
  other arithmetic: 20.6 us -> 28.3 us
  local copies, waits for them, and re-layouts: 16.9 us -> 23.1 us
  starting transfers between devices: 23.1 us -> 29.1 us
  matrix products: 14 us -> 11.7 us
    all_to_all x1 -> x0, waiting for transfers between devices: 11.9 us -> none  [body(): returned_rows = lax.all_to_all(projected, 'slab', 0, 0, tiled=True)]
    ppermute x0 -> x7, starting transfers between devices: none -> 11 us  [shift_exchange(): lax.ppermute(values[d * capacity:(d + 1) * capacity], 'slab', pairs)]
    all_to_all x1 -> x0, starting transfers between devices: 5.54 us -> none  [body(): returned_rows = lax.all_to_all(projected, 'slab', 0, 0, tiled=True)]
    ppermute x0 -> x7, waiting for transfers between devices: none -> 4.55 us  [shift_exchange(): lax.ppermute(values[d * capacity:(d + 1) * capacity], 'slab', pairs)]
    gather x0 -> x2, local copies, waits for them, and re-layouts: none -> 4.21 us  [the longest x1 2.47 us: body(): jnp.take(groups, (me - steps) % slab_count, axis=0).reshape(projected.shape)]
    all_to_all x1, waiting for transfers between devices: 7.85 us -> 3.94 us  [body(): gathered = lax.all_to_all(pieces, ('img', 'slab'), 0, 0, tiled=True)]
    concatenate x0 -> x2, local copies, waits for them, and re-layouts: none -> 3.5 us  [shift_exchange(): return jnp.concatenate(pieces, axis=0)]
    ppermute x3, waiting for transfers between devices: 0.01 us -> 2.96 us  [reduce_over_img(): total = total + lax.ppermute(piece, 'img', pairs).astype(jnp.float32)]
  transfers between devices with their start and end apart: 7 -> 13, of which waited for: 3 -> 5; matrix products, arithmetic and copies ran while one was open for 25% -> 36% of each run, Pallas kernels for 0% -> 0%
where the time goes in v10:
time: 112 us; the launch traced here: 111 us
  starting transfers between devices  29.1 us (26%)
  other arithmetic  28.3 us (25%)
  local copies, waits for them, and re-layouts  23.1 us (21%)
  waiting for transfers between devices  16.2 us (14%)
  matrix products  11.7 us (10%)
  between operations  2.63 us (2%)
    ppermute x7, starting transfers between devices, shift_exchange(): lax.ppermute(values[d * capacity:(d + 1) * capacity], 'slab', pairs)  11 us
    all_to_all x1, starting transfers between devices, body(): gathered = lax.all_to_all(pieces, ('img', 'slab'), 0, 0, tiled=True)  7.3 us
    all_to_all x1, waiting for transfers between devices, body(): got = lax.all_to_all(send, 'slab', 0, 0, tiled=True)  4.72 us
    ppermute x7, waiting for transfers between devices, shift_exchange(): lax.ppermute(values[d * capacity:(d + 1) * capacity], 'slab', pairs)  4.55 us
    dot_general x1, matrix products, transform(): jnp.einsum('gky,hym->ghkm', tables, rowwise, preferred_element_type=jnp.f...  4.52 us
    all_to_all x1, starting transfers between devices, body(): got = lax.all_to_all(send, 'slab', 0, 0, tiled=True)  4.1 us
    all_to_all x1, waiting for transfers between devices, body(): gathered = lax.all_to_all(pieces, ('img', 'slab'), 0, 0, tiled=True)  3.94 us
    all_to_all x1, starting transfers between devices, power_gather(): back = lax.all_to_all(spread, ('img', 'slab'), 0, 0, tiled=True)  3.7 us
  transfers between devices with their start and end apart: 13, of which 5 were waited for; matrix products, arithmetic and copies ran while one was open for 36% of the time, Pallas kernels for 0%

profile of v10, /device:TPU:0, one launch (start us, length us, event | category | flops | bytes accessed | tf_op | source)
XLA Modules:
  0.0 111.0 jit_solution(1492311133764914827)
XLA Ops:
  1.6 4.5 %convolution_bitcast_fusion.1 = f32[2,2,400,400]{3,2,0,1:T(8,128)} fusion(bf16[2,400,400]{2,1,0:T(8,128)(2,1)} %constant.152.clone, bf16[1,400,400]{2,1,0:T(8,128)(2,1)S(1)} %copy-done), kind=kOutput, calls=%fused_computation.5 | convolution fusion | flops 768320000 | bytes 3520000 | tf_op jit(solution)/shard_map/gky,hym->ghkm/dot_general | solution.py:27
  6.2 1.6 %fusion.20 = f32[1,400,400]{2,1,0:T(8,128)S(1)} fusion(f32[2,2,400,400]{3,2,0,1:T(8,128)} %convolution_bitcast_fusion.1), kind=kLoop, calls=%fused_computation.43 | loop fusion | flops 320000 | bytes 1920000 | tf_op jit(solution)/shard_map/neg | solution.py:29
  7.7 1.5 %fusion.22 = f32[1,400,400]{2,1,0:T(8,128)S(1)} fusion(f32[2,2,400,400]{3,2,0,1:T(8,128)} %convolution_bitcast_fusion.1), kind=kLoop, calls=%fused_computation.46 | loop fusion | flops 160000 | bytes 1920000 | tf_op jit(solution)/shard_map/sub | solution.py:28
  9.5 1.4 %all_to_all.24 = f32[32,1,2525]{2,1,0:T(1,128)} reshape(f32[202,400]{1,0:T(8,128)S(1)} %fusion.13) | data formatting | bytes 646400 | tf_op jit(solution)/shard_map/all_to_all | solution.py:171
  10.9 7.3 %all-to-all-start = ((f32[32,1,2525]{2,1,0:T(1,128)}), f32[32,1,2525]{2,1,0:T(1,128)S(1)}, u32[]{:S(2)}, u32[]{:S(2)}) async-start(f32[32,1,2525]{2,1,0:T(1,128)} %all_to_all.24), calls=%async_computation | async-start | bytes 655360 | tf_op jit(solution)/shard_map/all_to_all | solution.py:171
  26.4 3.9 %all-to-all-done = f32[32,1,2525]{2,1,0:T(1,128)S(1)} async-done(((f32[32,1,2525]{2,1,0:T(1,128)}), f32[32,1,2525]{2,1,0:T(1,128)S(1)}, u32[]{:S(2)}, u32[]{:S(2)}) %all-to-all-start) | async-done | bytes 323232 | tf_op jit(solution)/shard_map/all_to_all | solution.py:171
  30.3 4.1 %all-to-all-start.2 = ((bf16[8,2,12928]{2,1,0:T(2,128)(2,1)}), bf16[8,2,12928]{2,1,0:T(2,128)(2,1)}, u32[]{:S(2)}, u32[]{:S(2)}) async-start(bf16[8,2,12928]{2,1,0:T(2,128)(2,1)} %all_to_all.21), calls=%async_computation.2 | async-start | bytes 827392 | tf_op jit(solution)/shard_map/all_to_all | solution.py:172
  37.8 3.7 %fusion.40 = f32[400,400]{1,0:T(8,128)} fusion(f32[]{:T(128)S(6)} %mul.155, s32[400]{0:T(512)S(1)} %fusion.88), kind=kLoop, calls=%fused_computation.76 | loop fusion | flops 1120000 | bytes 641604 | tf_op jit(solution)/shard_map/convert_element_type | solution.py:248
  41.7 4.7 %all-to-all-done.2 = bf16[8,2,12928]{2,1,0:T(2,128)(2,1)} async-done(((bf16[8,2,12928]{2,1,0:T(2,128)(2,1)}), bf16[8,2,12928]{2,1,0:T(2,128)(2,1)}, u32[]{:S(2)}, u32[]{:S(2)}) %all-to-all-start.2) | async-done | bytes 413728 | tf_op jit(solution)/shard_map/all_to_all | solution.py:172
  47.3 3.7 %all-to-all-start.1 = ((f32[32,1,2525]{2,1,0:T(1,128)}), f32[32,1,2525]{2,1,0:T(1,128)}, u32[]{:S(2)}, u32[]{:S(2)}) async-start(f32[32,1,2525]{2,1,0:T(1,128)} %broadcast_in_dim.36), calls=%async_computation.1 | async-start | bytes 655360 | tf_op jit(solution)/shard_map/all_to_all | solution.py:78
  51.0 1.2 %all_to_all.23 = bf16[16,12928]{1,0:T(8,128)(2,1)S(1)} reshape(bf16[8,2,12928]{2,1,0:T(2,128)(2,1)} %all-to-all-done.2) | data formatting | bytes 827392 | tf_op jit(solution)/shard_map/all_to_all | solution.py:172
  53.6 1.1 slice_convert_fusion
  56.5 1.1 fusion.10
  57.6 1.3 %reshape.383 = bf16[8,2,2,16,400]{4,1,0,3,2:T(2,128)(2,1)S(1)} reshape(bf16[16,2,16,400]{3,0,2,1:T(8,128)(2,1)} %fusion.10) | data formatting | bytes 819200 | tf_op jit(solution)/shard_map/reshape | solution.py:197
  58.9 2.5 %gather_fusion = bf16[8,2,2,16,400]{4,1,3,2,0:T(2,128)(2,1)} fusion(bf16[8,2,2,16,400]{4,1,0,3,2:T(2,128)(2,1)S(1)} %reshape.383, s32[1024]{0:T(1024)S(1)} %pad_clamp_fusion.1), kind=kCustom, calls=%fused_computation.clone | custom fusion | bytes 819232 | tf_op jit(solution)/shard_map/jit(_take)/gather | solution.py:199
  61.3 1.6 %broadcast_select_fusion = bf16[8,2,2,16,400]{4,1,3,2,0:T(2,128)(2,1)S(1)} fusion(bf16[8,2,2,16,400]{4,1,3,2,0:T(2,128)(2,1)} %gather_fusion, pred[8]{0:T(512)(128)(4,1)S(1)} %get-tuple-element.29), kind=kLoop, calls=%fused_computation.25 | loop fusion | flops 204800 | bytes 819208 | tf_op jit(solution)/shard_map/jit(_take)/select_n | solution.py:199
  62.9 1.1 slice_bitcast_fusion.4
  64.0 4.5 %collective-permute-start = (bf16[2,2,16,400]{3,0,2,1:T(2,128)(2,1)S(1)}, bf16[2,2,16,400]{3,0,2,1:T(2,128)(2,1)S(1)}, u32[]{:S(2)}, u32[]{:S(2)}) collective-permute-start(bf16[2,2,16,400]{3,0,2,1:T(2,128)(2,1)S(1)} %get-tuple-element.22), channel_id=1, source_target_pairs={{0,7},{1,0},{2,1},{3,2},{4,3},{5,4},{6,5},{7,6},{8,15},{9,8},{10,9... | collective-permute-start | bytes 153608 | tf_op jit(solution)/shard_map/ppermute | solution.py:96
  69.0 2.7 %negate_convert_fusion.1 = (bf16[16,16,400]{2,0,1:T(8,128)(2,1)}, f32[16,16,400]{2,0,1:T(8,128)S(1)}) fusion(f32[16]{0:T(128)S(1)} %copy-done.11, s32[400]{0:T(512)S(1)} %fusion.88, s32[16,16]{0,1:T(8,128)S(1)} %fusion.67), kind=kLoop, calls=%fused_computation.66 | loop fusion | flops 819200 | bytes 617088 | tf_op jit(solution)/shard_map/convert_element_type | solution.py:55
  71.8 3.0 %collective-permute-start.3 = (bf16[2,2,16,400]{3,0,2,1:T(2,128)(2,1)}, bf16[2,2,16,400]{3,0,2,1:T(2,128)(2,1)}, u32[]{:S(2)}, u32[]{:S(2)}) collective-permute-start(bf16[2,2,16,400]{3,0,2,1:T(2,128)(2,1)} %get-tuple-element.19), channel_id=1, source_target_pairs={{0,4},{1,5},{2,6},{3,7},{4,0},{5,1},{6,2},{7,3},{8,12},{9,13},{10,... | collective-permute-start | bytes 153608 | tf_op jit(solution)/shard_map/ppermute | solution.py:96
  74.7 2.0 %collective-permute-start.5 = (bf16[2,2,16,400]{3,0,2,1:T(2,128)(2,1)}, bf16[2,2,16,400]{3,0,2,1:T(2,128)(2,1)}, u32[]{:S(2)}, u32[]{:S(2)}) collective-permute-start(bf16[2,2,16,400]{3,0,2,1:T(2,128)(2,1)} %get-tuple-element.17), channel_id=1, source_target_pairs={{0,2},{1,3},{2,4},{3,5},{4,6},{5,7},{6,0},{7,1},{8,10},{9,11},{10,... | collective-permute-start | bytes 153608 | tf_op jit(solution)/shard_map/ppermute | solution.py:96
  77.8 2.1 %fusion.33 = f32[16,16,400]{2,0,1:T(8,128)S(1)} fusion(f32[16,16,399]{2,0,1:T(8,128)S(1)} %bitcast.129, f32[16,16,1]{2,0,1:T(8,128)S(1)} %slice.256, f32[16]{0:T(128)S(1)} %get-tuple-element.7, f32[16]{0:T(128)S(1)} %get-tuple-element.33, f32[16]{0:T(128)S(1)} %copy-done.11, s32[400]{0:T(512)S(1)} %fusion.88, s32[16,16]{0,1:T(8,128)S(1)} %fusion.67), kind=kLoop, calls=%fused_computation.61 | loop fusion | flops 1228800 | bytes 822016 | tf_op jit(solution)/shard_map/add | solution.py:220
  79.9 1.5 %reshape.389 = f32[16,16,800]{2,1,0:T(8,128)} reshape(f32[16,12800]{1,0:T(8,128)S(1)} %slice_convert_fusion) | data formatting | bytes 1638400 | tf_op jit(solution)/shard_map/convert_element_type | solution.py:216
  81.4 4.5 %collective-permute-done.4 = bf16[2,2,16,400]{3,0,2,1:T(2,128)(2,1)} collective-permute-done((bf16[2,2,16,400]{3,0,2,1:T(2,128)(2,1)}, bf16[2,2,16,400]{3,0,2,1:T(2,128)(2,1)}, u32[]{:S(2)}, u32[]{:S(2)}) %collective-permute-start.4) | collective-permute-done | bytes 51232 | tf_op jit(solution)/shard_map/ppermute | solution.py:96
  86.0 2.4 %concatenate.64 = bf16[16,2,16,400]{3,0,2,1:T(8,128)(2,1)S(1)} concatenate(bf16[2,2,16,400]{3,0,2,1:T(2,128)(2,1)S(1)} %get-tuple-element.23, bf16[2,2,16,400]{3,0,2,1:T(2,128)(2,1)} %copy-done.8, bf16[2,2,16,400]{3,0,2,1:T(2,128)(2,1)} %copy-done.9, bf16[2,2,16,400]{3,0,2,1:T(2,128)(2,1)} %collective-permute-done.2, bf16[2,2,16,400]{3,0,2,1:T(2,128)(2,1)} %collective-permute-done.3, ...), dimensions={0} | concatenate | bytes 819200 | tf_op jit(solution)/shard_map/concatenate | solution.py:97
  88.4 1.1 copy.78
  89.5 1.7 %gather_fusion.1 = bf16[8,2,2,16,400]{4,3,2,1,0:T(8,128)(2,1)S(1)} fusion(bf16[8,2,2,16,400]{4,3,2,1,0:T(8,128)(2,1)} %bitcast.134, s32[1024]{0:T(1024)} %pad_clamp_fusion), kind=kCustom, calls=%fused_computation.1.clone | custom fusion | bytes 819232 | tf_op jit(solution)/shard_map/jit(_take)/gather | solution.py:202
  92.6 1.8 %reduce.3 = f32[32,2525]{1,0:T(8,128)S(1)} reduce(f32[32,1,2525]{2,1,0:T(1,128)} %all-to-all-done.1, f32[]{:T(128)} %constant.162), dimensions={1}, to_apply=%all_to_all.20.reduce_sub_computation | reduce | bytes 646404 | tf_op jit(solution)/shard_map/all_to_all | solution.py:78
  101.0 1.6 %collective-permute-start.8 = (bf16[2,32,1200]{2,1,0:T(8,128)(2,1)S(1)}, bf16[2,32,1200]{2,1,0:T(8,128)(2,1)S(1)}, u32[]{:S(2)}, u32[]{:S(2)}) collective-permute-start(bf16[2,32,1200]{2,1,0:T(8,128)(2,1)S(1)} %get-tuple-element.15), channel_id=1, source_target_pairs={{0,16},{8,24},{16,0},{24,8},{1,17},{9,25},{17,1},{25,9},{2,18},{10... | collective-permute-start | bytes 460808 | tf_op jit(solution)/shard_map/ppermute | solution.py:106
  102.6 1.4 %collective-permute-start.9 = (bf16[2,32,1200]{2,1,0:T(8,128)(2,1)S(1)}, bf16[2,32,1200]{2,1,0:T(8,128)(2,1)S(1)}, u32[]{:S(2)}, u32[]{:S(2)}) collective-permute-start(bf16[2,32,1200]{2,1,0:T(8,128)(2,1)S(1)} %get-tuple-element.14), channel_id=1, source_target_pairs={{0,24},{8,0},{16,8},{24,16},{1,25},{9,1},{17,9},{25,17},{2,26},{10... | collective-permute-start | bytes 460808 | tf_op jit(solution)/shard_map/ppermute | solution.py:106
  104.0 1.1 %convolution_bitcast_fusion = f32[2,2,400,400]{3,2,1,0:T(8,128)S(1)} fusion(bf16[2,400,400]{2,1,0:T(8,128)(2,1)S(1)} %copy-done.3, f32[1,400,400]{2,1,0:T(8,128)S(1)} %fusion.20, f32[1,400,400]{2,1,0:T(8,128)S(1)} %fusion.22, bf16[2,64,400]{2,1,0:T(8,128)(2,1)S(1)} %copy-done.7, bf16[2,64,400]{2,1,0:T(8,128)(2,1)S(1)} %get-tuple-element.24, ...), kind=kOutput, calls=%fused_computation.4 | convolution fusion | flops 515520000 | bytes 5965600 | tf_op jit(solution)/shard_map/hyj,gmj->hgym/dot_general | solution.py:34
  108.1 1.9 %collective-permute-done.9 = bf16[2,32,1200]{2,1,0:T(8,128)(2,1)S(1)} collective-permute-done((bf16[2,32,1200]{2,1,0:T(8,128)(2,1)S(1)}, bf16[2,32,1200]{2,1,0:T(8,128)(2,1)S(1)}, u32[]{:S(2)}, u32[]{:S(2)}) %collective-permute-start.9) | collective-permute-done | bytes 153632 | tf_op jit(solution)/shard_map/ppermute | solution.py:106
  (155 shorter events, 29.1 us)
Async XLA Ops:
  10.9 19.4 %all-to-all-start = ((f32[32,1,2525]{2,1,0:T(1,128)}), f32[32,1,2525]{2,1,0:T(1,128)S(1)}, u32[]{:S(2)}, u32[]{:S(2)}) async-start(f32[32,1,2525]{2,1,0:T(1,128)} %all_to_all.24), calls=%async_computation | async-start | bytes 655360 | tf_op jit(solution)/shard_map/all_to_all | solution.py:171
  18.3 3.9 %copy-start.27 = (s32[1,8]{1,0:T(1,128)S(1)}, s32[1,8]{1,0:T(1,128)}, u32[]{:S(2)}) copy-start(s32[1,8]{1,0:T(1,128)} %param.15) | copy-start | bytes 100
  18.3 4.1 %copy-start.28 = (s32[1,8]{1,0:T(1,128)S(1)}, s32[1,8]{1,0:T(1,128)}, u32[]{:S(2)}) copy-start(s32[1,8]{1,0:T(1,128)} %param.16) | copy-start | bytes 100
  18.3 4.1 %copy-start.29 = (s32[1,8]{1,0:T(1,128)S(1)}, s32[1,8]{1,0:T(1,128)}, u32[]{:S(2)}) copy-start(s32[1,8]{1,0:T(1,128)} %param.17) | copy-start | bytes 100
  20.6 5.1 %copy-start.30 = (f32[64]{0:T(128)S(1)}, f32[64]{0:T(128)}, u32[]{:S(2)}) copy-start(f32[64]{0:T(128)} %param.13) | copy-start | bytes 772
  20.6 13.9 %copy-start.5 = (bf16[2,128,800]{1,2,0:T(8,128)(2,1)S(1)}, bf16[2,128,800]{1,2,0:T(8,128)(2,1)}, u32[]{:S(2)}) copy-start(bf16[2,128,800]{1,2,0:T(8,128)(2,1)} %param.18) | copy-start | bytes 1228804
  21.6 12.9 %copy-start.19 = (s32[8]{0:T(128)}, s32[8]{0:T(128)S(1)}, u32[]{:S(2)}) copy-start(s32[8]{0:T(128)S(1)} %multiply_add_fusion) | copy-start | bytes 100
  30.3 16.1 %all-to-all-start.2 = ((bf16[8,2,12928]{2,1,0:T(2,128)(2,1)}), bf16[8,2,12928]{2,1,0:T(2,128)(2,1)}, u32[]{:S(2)}, u32[]{:S(2)}) async-start(bf16[8,2,12928]{2,1,0:T(2,128)(2,1)} %all_to_all.21), calls=%async_computation.2 | async-start | bytes 827392 | tf_op jit(solution)/shard_map/all_to_all | solution.py:172
  47.3 45.3 %all-to-all-start.1 = ((f32[32,1,2525]{2,1,0:T(1,128)}), f32[32,1,2525]{2,1,0:T(1,128)}, u32[]{:S(2)}, u32[]{:S(2)}) async-start(f32[32,1,2525]{2,1,0:T(1,128)} %broadcast_in_dim.36), calls=%async_computation.1 | async-start | bytes 655360 | tf_op jit(solution)/shard_map/all_to_all | solution.py:78
  52.9 3.6 %copy-start.14 = (f32[16]{0:T(128)}, f32[16]{0:T(128)S(1)}, u32[]{:S(2)}) copy-start(f32[16]{0:T(128)S(1)} %get-tuple-element.8) | copy-start | bytes 196
  61.3 7.6 %copy-start.11 = (f32[16]{0:T(128)S(1)}, f32[16]{0:T(128)}, u32[]{:S(2)}) copy-start(f32[16]{0:T(128)} %get-tuple-element.32) | copy-start | bytes 196
  64.0 10.8 %collective-permute-start = (bf16[2,2,16,400]{3,0,2,1:T(2,128)(2,1)S(1)}, bf16[2,2,16,400]{3,0,2,1:T(2,128)(2,1)S(1)}, u32[]{:S(2)}, u32[]{:S(2)}) collective-permute-start(bf16[2,2,16,400]{3,0,2,1:T(2,128)(2,1)S(1)} %get-tuple-element.22), channel_id=1, source_target_pairs={{0,7},{1,0},{2,1},{3,2},{4,3},{5,4},{6,5},{7,6},{8,15},{9,8},{10,9... | collective-permute-start | bytes 153608 | tf_op jit(solution)/shard_map/ppermute | solution.py:96
  68.5 8.3 %collective-permute-start.1 = (bf16[2,2,16,400]{3,0,2,1:T(2,128)(2,1)S(1)}, bf16[2,2,16,400]{3,0,2,1:T(2,128)(2,1)S(1)}, u32[]{:S(2)}, u32[]{:S(2)}) collective-permute-start(bf16[2,2,16,400]{3,0,2,1:T(2,128)(2,1)S(1)} %get-tuple-element.21), channel_id=1, source_target_pairs={{0,6},{1,7},{2,0},{3,1},{4,2},{5,3},{6,4},{7,5},{8,14},{9,15},{10,... | collective-permute-start | bytes 153608 | tf_op jit(solution)/shard_map/ppermute | solution.py:96
  71.7 9.7 %collective-permute-start.2 = (bf16[2,2,16,400]{3,0,2,1:T(2,128)(2,1)}, bf16[2,2,16,400]{3,0,2,1:T(2,128)(2,1)}, u32[]{:S(2)}, u32[]{:S(2)}) collective-permute-start(bf16[2,2,16,400]{3,0,2,1:T(2,128)(2,1)} %get-tuple-element.20), channel_id=1, source_target_pairs={{0,5},{1,6},{2,7},{3,0},{4,1},{5,2},{6,3},{7,4},{8,13},{9,14},{10,... | collective-permute-start | bytes 153608 | tf_op jit(solution)/shard_map/ppermute | solution.py:96
  71.8 9.6 %collective-permute-start.3 = (bf16[2,2,16,400]{3,0,2,1:T(2,128)(2,1)}, bf16[2,2,16,400]{3,0,2,1:T(2,128)(2,1)}, u32[]{:S(2)}, u32[]{:S(2)}) collective-permute-start(bf16[2,2,16,400]{3,0,2,1:T(2,128)(2,1)} %get-tuple-element.19), channel_id=1, source_target_pairs={{0,4},{1,5},{2,6},{3,7},{4,0},{5,1},{6,2},{7,3},{8,12},{9,13},{10,... | collective-permute-start | bytes 153608 | tf_op jit(solution)/shard_map/ppermute | solution.py:96
  74.7 11.2 %collective-permute-start.4 = (bf16[2,2,16,400]{3,0,2,1:T(2,128)(2,1)}, bf16[2,2,16,400]{3,0,2,1:T(2,128)(2,1)}, u32[]{:S(2)}, u32[]{:S(2)}) collective-permute-start(bf16[2,2,16,400]{3,0,2,1:T(2,128)(2,1)} %get-tuple-element.18), channel_id=1, source_target_pairs={{0,3},{1,4},{2,5},{3,6},{4,7},{5,0},{6,1},{7,2},{8,11},{9,12},{10,... | collective-permute-start | bytes 153608 | tf_op jit(solution)/shard_map/ppermute | solution.py:96
  74.7 11.2 %collective-permute-start.5 = (bf16[2,2,16,400]{3,0,2,1:T(2,128)(2,1)}, bf16[2,2,16,400]{3,0,2,1:T(2,128)(2,1)}, u32[]{:S(2)}, u32[]{:S(2)}) collective-permute-start(bf16[2,2,16,400]{3,0,2,1:T(2,128)(2,1)} %get-tuple-element.17), channel_id=1, source_target_pairs={{0,2},{1,3},{2,4},{3,5},{4,6},{5,7},{6,0},{7,1},{8,10},{9,11},{10,... | collective-permute-start | bytes 153608 | tf_op jit(solution)/shard_map/ppermute | solution.py:96
  76.7 9.2 %collective-permute-start.6 = (bf16[2,2,16,400]{3,0,2,1:T(2,128)(2,1)S(1)}, bf16[2,2,16,400]{3,0,2,1:T(2,128)(2,1)}, u32[]{:S(2)}, u32[]{:S(2)}) collective-permute-start(bf16[2,2,16,400]{3,0,2,1:T(2,128)(2,1)S(1)} %get-tuple-element.16), channel_id=1, source_target_pairs={{0,1},{1,2},{2,3},{3,4},{4,5},{5,6},{6,7},{7,0},{8,9},{9,10},{10,1... | collective-permute-start | bytes 153608 | tf_op jit(solution)/shard_map/ppermute | solution.py:96
  81.4 9.8 %copy-start.24 = (pred[8]{0:T(512)(128)(4,1)S(1)}, pred[8]{0:T(512)(128)(4,1)}, u32[]{:S(2)}) copy-start(pred[8]{0:T(512)(128)(4,1)} %get-tuple-element.28) | copy-start | bytes 28
  91.4 3.5 %copy-start.23 = (pred[400]{0:T(512)(128)(4,1)S(1)}, pred[400]{0:T(512)(128)(4,1)}, u32[]{:S(2)}) copy-start(pred[400]{0:T(512)(128)(4,1)} %fusion.94) | copy-start | bytes 1204
  91.9 3.5 %copy-start.17 = (s32[400]{0:T(512)S(1)}, s32[400]{0:T(512)}, u32[]{:S(2)}) copy-start(s32[400]{0:T(512)} %fusion.95) | copy-start | bytes 4804
  91.9 3.5 %copy-start.18 = (s32[400]{0:T(512)S(1)}, s32[400]{0:T(512)}, u32[]{:S(2)}) copy-start(s32[400]{0:T(512)} %get-tuple-element.30) | copy-start | bytes 4804
  91.9 3.5 %copy-start.31 = (pred[400]{0:T(512)(128)(4,1)S(1)}, pred[400]{0:T(512)(128)(4,1)}, u32[]{:S(2)}) copy-start(pred[400]{0:T(512)(128)(4,1)} %compare_and_fusion.2) | copy-start | bytes 1204
  92.6 3.9 %copy-start.10 = (s32[400]{0:T(512)S(1)}, s32[400]{0:T(512)}, u32[]{:S(2)}) copy-start(s32[400]{0:T(512)} %fusion.93) | copy-start | bytes 4804
  92.6 3.9 %copy-start.26 = (pred[400]{0:T(512)(128)(4,1)S(1)}, pred[400]{0:T(512)(128)(4,1)}, u32[]{:S(2)}) copy-start(pred[400]{0:T(512)(128)(4,1)} %fusion.92) | copy-start | bytes 1204
  100.6 3.3 %copy-start.3 = (bf16[2,400,400]{2,1,0:T(8,128)(2,1)S(1)}, bf16[2,400,400]{2,1,0:T(8,128)(2,1)}, u32[]{:S(2)}) copy-start(bf16[2,400,400]{2,1,0:T(8,128)(2,1)} %constant.152.clone) | copy-start | bytes 1920004
  100.7 3.3 %copy-start.4 = (f32[400,400]{1,0:T(8,128)S(1)}, f32[400,400]{1,0:T(8,128)}, u32[]{:S(2)}) copy-start(f32[400,400]{1,0:T(8,128)} %fusion.40) | copy-start | bytes 1920004
  100.7 3.3 %copy-start.7 = (bf16[2,64,400]{2,1,0:T(8,128)(2,1)S(1)}, bf16[2,64,400]{2,1,0:T(8,128)(2,1)}, u32[]{:S(2)}) copy-start(bf16[2,64,400]{2,1,0:T(8,128)(2,1)} %get-tuple-element.25) | copy-start | bytes 307204
  100.7 3.3 %copy-start.22 = (bf16[400]{0:T(512)(128)(2,1)S(1)}, bf16[400]{0:T(512)(128)(2,1)}, u32[]{:S(2)}) copy-start(bf16[400]{0:T(512)(128)(2,1)} %pad.24.clone) | copy-start | bytes 2404
  100.9 6.1 %collective-permute-start.7 = (bf16[2,32,1200]{2,1,0:T(8,128)(2,1)S(1)}, bf16[2,32,1200]{2,1,0:T(8,128)(2,1)S(1)}, u32[]{:S(2)}, u32[]{:S(2)}) collective-permute-start(bf16[2,32,1200]{2,1,0:T(8,128)(2,1)S(1)} %get-tuple-element.13), channel_id=1, source_target_pairs={{0,8},{8,16},{16,24},{24,0},{1,9},{9,17},{17,25},{25,1},{2,10},{10... | collective-permute-start | bytes 460808 | tf_op jit(solution)/shard_map/ppermute | solution.py:106
  101.0 7.1 %collective-permute-start.8 = (bf16[2,32,1200]{2,1,0:T(8,128)(2,1)S(1)}, bf16[2,32,1200]{2,1,0:T(8,128)(2,1)S(1)}, u32[]{:S(2)}, u32[]{:S(2)}) collective-permute-start(bf16[2,32,1200]{2,1,0:T(8,128)(2,1)S(1)} %get-tuple-element.15), channel_id=1, source_target_pairs={{0,16},{8,24},{16,0},{24,8},{1,17},{9,25},{17,1},{25,9},{2,18},{10... | collective-permute-start | bytes 460808 | tf_op jit(solution)/shard_map/ppermute | solution.py:106
  102.6 7.5 %collective-permute-start.9 = (bf16[2,32,1200]{2,1,0:T(8,128)(2,1)S(1)}, bf16[2,32,1200]{2,1,0:T(8,128)(2,1)S(1)}, u32[]{:S(2)}, u32[]{:S(2)}) collective-permute-start(bf16[2,32,1200]{2,1,0:T(8,128)(2,1)S(1)} %get-tuple-element.14), channel_id=1, source_target_pairs={{0,24},{8,0},{16,8},{24,16},{1,25},{9,1},{17,9},{25,17},{2,26},{10... | collective-permute-start | bytes 460808 | tf_op jit(solution)/shard_map/ppermute | solution.py:106
  (13 other events, 19.4 us)

commit v11 on v9

--- a/solution.py
+++ b/solution.py
@@ -30,15 +30,18 @@
     return jnp.stack([real, imag])
 
 
-def invert(difference, tables, box_size):
+def back_rows_of(difference, tables):
     products = jnp.einsum(
         "hyj,gmj->hgym", difference, tables, preferred_element_type=jnp.float32
     )
     back_real = products[0, 0] - products[1, 1]
     back_imag = products[0, 1] + products[1, 0]
-    back_rows = jnp.stack([back_real, -back_imag]).astype(jnp.bfloat16)
+    return jnp.stack([back_real, -back_imag]).astype(jnp.bfloat16)
+
+
+def picture_of(back_rows, tables):
     picture = jnp.einsum("hxk,hkm->hxm", tables, back_rows, preferred_element_type=jnp.float32)
-    return ((picture[0] + picture[1]) / box_size).astype(jnp.bfloat16)
+    return picture[0] + picture[1]
 
 
 def radius_sq(row_ids, box_size):
@@ -235,14 +238,30 @@
     ).astype(jnp.bfloat16)
     own_rows = own_rows.reshape(particles, blocks_per, 2, RB, box_size)
     own_rows = jnp.moveaxis(own_rows, 2, 1).reshape(particles, 2, 2 * low_rows, box_size)
-    middle = jnp.zeros((particles, 2, box_size - 2 * low_rows, box_size), jnp.bfloat16)
-    full_projection = jnp.concatenate(
-        [own_rows[:, :, :low_rows], middle, own_rows[:, :, low_rows:]], axis=2
-    )
-    difference = (
-        whitened - contrast.astype(jnp.float32)[:, None] * full_projection.astype(jnp.float32)
-    ).astype(jnp.bfloat16)
-    residual = jnp.stack([invert(difference[n], tables, box_size) for n in range(particles)])
+    inner = box_size - 2 * low_rows
+    inner_rows = whitened[:, :, low_rows : box_size - low_rows].astype(jnp.bfloat16)
+    residual = []
+    for n in range(particles):
+        inner_back = back_rows_of(inner_rows[n], tables)
+        edge = jnp.zeros((2, low_rows, box_size), jnp.bfloat16)
+        inner_part = picture_of(jnp.concatenate([edge, inner_back, edge], axis=1), tables)
+        routed_white = jnp.concatenate(
+            [whitened[n, :, :low_rows], whitened[n, :, box_size - low_rows :]], axis=1
+        )
+        routed_contrast = jnp.concatenate(
+            [contrast[n, :low_rows], contrast[n, box_size - low_rows :]], axis=0
+        ).astype(jnp.float32)
+        routed_difference = (
+            routed_white - routed_contrast[None] * own_rows[n].astype(jnp.float32)
+        ).astype(jnp.bfloat16)
+        routed_back = back_rows_of(routed_difference, tables)
+        middle = jnp.zeros((2, inner, box_size), jnp.bfloat16)
+        routed_part = picture_of(
+            jnp.concatenate([routed_back[:, :low_rows], middle, routed_back[:, low_rows:]], axis=1),
+            tables,
+        )
+        residual.append(((inner_part + routed_part) / box_size).astype(jnp.bfloat16))
+    residual = jnp.stack(residual)
     return (residual, reconstruction)
 
 

time: 102 us -> 99.9 us (0.979)
  waiting for transfers between devices: 24.3 us -> 14 us
  other arithmetic: 20.6 us -> 27.7 us
  starting transfers between devices: 23.1 us -> 25.8 us
  matrix products: 14 us -> 12.5 us
    all_to_all x1, waiting for transfers between devices: 11.9 us -> 0.01 us  [body(): returned_rows = lax.all_to_all(projected, 'slab', 0, 0, tiled=True)]
    all_to_all x1, waiting for transfers between devices: 7.85 us -> 0.01 us  [body(): gathered = lax.all_to_all(pieces, ('img', 'slab'), 0, 0, tiled=True)]
    ppermute x3, waiting for transfers between devices: 0.01 us -> 5.33 us  [reduce_over_img(): total = total + lax.ppermute(piece, 'img', pairs).astype(jnp.float32)]
    all_to_all x1, waiting for transfers between devices: 4.54 us -> 8.53 us  [body(): got = lax.all_to_all(send, 'slab', 0, 0, tiled=True)]
    convert_element_type x2, other arithmetic: 4.69 us -> 1.89 us  [the longest x1 1.16 us: body(): ((inner_part + routed_part) / box_size).astype(jnp.bfloat16)]
    sub x1 -> x2, other arithmetic: 1.54 us -> 3.98 us  [transform(): real = products[0, 0] - products[1, 1]]
    all_to_all x1, starting transfers between devices: 3.46 us -> 5.82 us  [body(): got = lax.all_to_all(send, 'slab', 0, 0, tiled=True)]
    convert_element_type x1 -> x2, other arithmetic: 2.68 us -> 4.92 us  [contrast_curve(): (-jnp.sin(defocus_of[:, None, None] * radius + 0.1)).astype(jnp.bfloat16)]
  transfers between devices with their start and end apart: 7 -> 7, of which waited for: 3 -> 5; matrix products, arithmetic and copies ran while one was open for 25% -> 37% of each run, Pallas kernels for 0% -> 0%
where the time goes in v11:
time: 99.9 us; the launch traced here: 99.1 us
  other arithmetic  27.7 us (28%)
  starting transfers between devices  25.8 us (26%)
  local copies, waits for them, and re-layouts  16.4 us (16%)
  waiting for transfers between devices  14 us (14%)
  matrix products  12.5 us (13%)
  between operations  2.64 us (3%)
    all_to_all x1, waiting for transfers between devices, body(): got = lax.all_to_all(send, 'slab', 0, 0, tiled=True)  8.53 us
    all_to_all x1, starting transfers between devices, body(): gathered = lax.all_to_all(pieces, ('img', 'slab'), 0, 0, tiled=True)  7.3 us
    all_to_all x1, starting transfers between devices, body(): got = lax.all_to_all(send, 'slab', 0, 0, tiled=True)  5.82 us
    all_to_all x1, starting transfers between devices, body(): returned_rows = lax.all_to_all(projected, 'slab', 0, 0, tiled=True)  5.44 us
    ppermute x3, waiting for transfers between devices, reduce_over_img(): total = total + lax.ppermute(piece, 'img', pairs).astype(jnp.float32)  5.33 us
    convert_element_type x2, other arithmetic, contrast_curve(): (-jnp.sin(defocus_of[:, None, None] * radius + 0.1)).astype(jnp.bfloat16)  4.92 us
    dot_general x1, matrix products, transform(): jnp.einsum('gky,hym->ghkm', tables, rowwise, preferred_element_type=jnp.f...  4.56 us
    unnamed x67, local copies, waits for them, and re-layouts  4.54 us
  transfers between devices with their start and end apart: 7, of which 5 were waited for; matrix products, arithmetic and copies ran while one was open for 37% of the time, Pallas kernels for 0%

profile of v11, /device:TPU:0, one launch (start us, length us, event | category | flops | bytes accessed | tf_op | source)
XLA Modules:
  0.0 99.1 jit_solution(17976942875130131763)
XLA Ops:
  0.6 1.0 %copy-done = bf16[1,400,400]{2,1,0:T(8,128)(2,1)S(1)} copy-done((bf16[1,400,400]{2,1,0:T(8,128)(2,1)S(1)}, bf16[1,400,400]{2,1,0:T(8,128)(2,1)}, u32[]{:S(2)}) %copy-start) | copy-done | bytes 320024
  1.6 4.6 %convolution_bitcast_fusion = f32[2,2,400,400]{3,2,0,1:T(8,128)} fusion(bf16[2,400,400]{2,1,0:T(8,128)(2,1)} %constant.122.clone, bf16[1,400,400]{2,1,0:T(8,128)(2,1)S(1)} %copy-done), kind=kOutput, calls=%fused_computation.2 | convolution fusion | flops 768320000 | bytes 3520000 | tf_op jit(solution)/shard_map/gky,hym->ghkm/dot_general | solution.py:27
  6.2 1.5 %fusion.132 = f32[1,400,400]{2,1,0:T(8,128)S(1)} fusion(f32[2,2,400,400]{3,2,0,1:T(8,128)} %convolution_bitcast_fusion), kind=kLoop, calls=%fused_computation.200 | loop fusion | flops 160000 | bytes 1920000 | tf_op jit(solution)/shard_map/sub | solution.py:28
  7.7 2.5 %fusion.71 = (f32[1,1,400,400]{3,2,1,0:T(8,128)}, f32[1,400,400]{2,1,0:T(8,128)S(1)}) fusion(f32[2,2,400,400]{3,2,0,1:T(8,128)} %convolution_bitcast_fusion), kind=kLoop, calls=%fused_computation.111 | loop fusion | flops 320000 | bytes 2560000 | tf_op jit(solution)/shard_map/neg | solution.py:29
  10.5 1.4 %all_to_all.28 = f32[32,1,2525]{2,1,0:T(1,128)} reshape(f32[202,400]{1,0:T(8,128)S(1)} %fusion.14) | data formatting | bytes 646400 | tf_op jit(solution)/shard_map/all_to_all | solution.py:174
  11.8 7.3 %all-to-all-start = ((f32[32,1,2525]{2,1,0:T(1,128)}), f32[32,1,2525]{2,1,0:T(1,128)S(1)}, u32[]{:S(2)}, u32[]{:S(2)}) async-start(f32[32,1,2525]{2,1,0:T(1,128)} %all_to_all.28), calls=%async_computation | async-start | bytes 655360 | tf_op jit(solution)/shard_map/all_to_all | solution.py:174
  25.5 0.9 all_to_all.24
  28.9 3.0 %negate_convert_fusion = bf16[1,400,400]{2,1,0:T(8,128)(2,1)S(1)} fusion(f32[]{:T(128)S(6)} %mul.154, s32[400]{0:T(512)S(1)} %fusion.108), kind=kLoop, calls=%fused_computation.59 | loop fusion | flops 960000 | bytes 321604 | tf_op jit(solution)/shard_map/convert_element_type | solution.py:58
  31.9 5.8 %all-to-all-start.2 = ((bf16[8,2,12928]{2,1,0:T(2,128)(2,1)}), bf16[8,2,12928]{2,1,0:T(2,128)(2,1)S(1)}, u32[]{:S(2)}, u32[]{:S(2)}) async-start(bf16[8,2,12928]{2,1,0:T(2,128)(2,1)} %all_to_all.24), calls=%async_computation.2 | async-start | bytes 827392 | tf_op jit(solution)/shard_map/all_to_all | solution.py:175
  39.0 2.4 %fusion.19 = f32[1,1,400,400]{3,2,1,0:T(8,128)} fusion(f32[2,2,400,400]{3,2,0,1:T(8,128)} %convolution_bitcast_fusion), kind=kLoop, calls=%fused_computation.41 | loop fusion | flops 160000 | bytes 1920000 | tf_op jit(solution)/shard_map/sub | solution.py:28
  41.6 8.5 %all-to-all-done.2 = bf16[8,2,12928]{2,1,0:T(2,128)(2,1)S(1)} async-done(((bf16[8,2,12928]{2,1,0:T(2,128)(2,1)}), bf16[8,2,12928]{2,1,0:T(2,128)(2,1)S(1)}, u32[]{:S(2)}, u32[]{:S(2)}) %all-to-all-start.2) | async-done | bytes 413728 | tf_op jit(solution)/shard_map/all_to_all | solution.py:175
  50.1 0.9 broadcast_in_dim.30
  51.0 4.0 %all-to-all-start.1 = ((f32[32,1,2525]{2,1,0:T(1,128)}), f32[32,1,2525]{2,1,0:T(1,128)}, u32[]{:S(2)}, u32[]{:S(2)}) async-start(f32[32,1,2525]{2,1,0:T(1,128)} %broadcast_in_dim.30), calls=%async_computation.1 | async-start | bytes 655360 | tf_op jit(solution)/shard_map/all_to_all | solution.py:81
  58.7 1.5 %reshape.437 = f32[16,16,800]{2,1,0:T(8,128)} reshape(f32[16,12800]{1,0:T(8,128)S(1)} %slice_convert_fusion.1) | data formatting | bytes 1638400 | tf_op jit(solution)/shard_map/convert_element_type | solution.py:214
  60.3 1.9 %negate_convert_fusion.1 = (bf16[16,16,400]{2,0,1:T(8,128)(2,1)S(1)}, f32[16,16,400]{2,0,1:T(8,128)S(1)}) fusion(f32[16]{0:T(128)S(1)} %get-tuple-element.29, s32[400]{0:T(512)S(1)} %fusion.108, s32[16,16]{0,1:T(8,128)S(1)} %fusion.87), kind=kLoop, calls=%fused_computation.77 | loop fusion | flops 819200 | bytes 617088 | tf_op jit(solution)/shard_map/convert_element_type | solution.py:58
  62.3 1.2 %fusion.11 = bf16[16,2,16,400]{3,0,2,1:T(8,128)(2,1)S(1)} fusion(f32[16,2,16,1]{3,0,2,1:T(8,128)} %slice.219, f32[16,2,16,399]{3,0,2,1:T(8,128)S(1)} %slice.218, f32[16,2,16,400]{3,0,2,1:T(8,128)S(1)} %fusion.46, f32[16]{0:T(128)S(1)} %copy-done.15, f32[16]{0:T(128)S(1)} %copy-done.9, f32[16]{0:T(128)S(1)} %get-tuple-element.30), kind=kLoop, calls=%fused_computation.25 | loop fusion | flops 1228800 | bytes 2048192 | tf_op jit(solution)/shard_map/convert_element_type | solution.py:193
  63.6 1.1 %copy.91 = bf16[16,2,16,400]{3,2,1,0:T(8,128)(2,1)} copy(bf16[16,2,16,400]{3,0,2,1:T(8,128)(2,1)S(1)} %fusion.11) | data formatting | bytes 819200 | tf_op jit(solution)/shard_map/convert_element_type | solution.py:193
  64.7 2.1 %fusion.44 = f32[16,16,400]{2,0,1:T(8,128)S(1)} fusion(f32[16,16,399]{2,0,1:T(8,128)S(1)} %bitcast.135, f32[16,16,1]{2,0,1:T(8,128)S(1)} %slice.236, f32[16]{0:T(128)S(1)} %copy-done.9, f32[16]{0:T(128)S(1)} %get-tuple-element.30, f32[16]{0:T(128)S(1)} %get-tuple-element.29, s32[400]{0:T(512)S(1)} %fusion.108, s32[16,16]{0,1:T(8,128)S(1)} %fusion.87), kind=kLoop, calls=%fused_computation.72 | loop fusion | flops 1228800 | bytes 822016 | tf_op jit(solution)/shard_map/add | solution.py:218
  67.0 5.4 %all-to-all-start.3 = ((bf16[16,2,16,400]{3,2,1,0:T(8,128)(2,1)}), bf16[16,2,16,400]{3,2,1,0:T(8,128)(2,1)S(1)}, u32[]{:S(2)}, u32[]{:S(2)}) async-start(bf16[16,2,16,400]{3,2,1,0:T(8,128)(2,1)} %copy.91), calls=%async_computation.3 | async-start | bytes 1048576 | tf_op jit(solution)/shard_map/all_to_all | solution.py:200
  72.4 1.8 %reduce.3 = f32[32,2525]{1,0:T(8,128)S(1)} reduce(f32[32,1,2525]{2,1,0:T(1,128)} %all-to-all-done.1, f32[]{:T(128)} %constant.132), dimensions={1}, to_apply=%all_to_all.23.reduce_sub_computation | reduce | bytes 646404 | tf_op jit(solution)/shard_map/all_to_all | solution.py:81
  75.2 1.0 %fusion.36 = f32[202,400]{0,1:T(8,128)S(1)} fusion(f32[202,400]{1,0:T(8,128)S(1)} %reshape.430, s32[400]{0:T(512)S(1)} %copy-done.19, s32[400]{0:T(512)S(1)} %copy-done.18, s32[400]{0:T(512)S(1)} %copy-done.11, pred[400]{0:T(512)(128)(4,1)S(1)} %copy-done.32), kind=kOutput, calls=%fused_computation.61 | convolution fusion | flops 388160000 | bytes 651600 | tf_op jit(solution)/shard_map/dot_general | solution.py:87
  76.3 0.8 fusion.5
  77.5 0.9 convolution_divide_fusion
  80.0 0.9 copy-done.1
  82.9 0.9 convolution_convert_fusion.1
  84.1 1.7 %collective-permute-start.2 = (bf16[2,32,1200]{2,1,0:T(8,128)(2,1)S(1)}, bf16[2,32,1200]{2,1,0:T(8,128)(2,1)S(1)}, u32[]{:S(2)}, u32[]{:S(2)}) collective-permute-start(bf16[2,32,1200]{2,1,0:T(8,128)(2,1)S(1)} %get-tuple-element.19), channel_id=1, source_target_pairs={{0,24},{8,0},{16,8},{24,16},{1,25},{9,1},{17,9},{25,17},{2,26},{10... | collective-permute-start | bytes 460808 | tf_op jit(solution)/shard_map/ppermute | solution.py:109
  85.9 1.5 %collective-permute-start.1 = (bf16[2,32,1200]{2,1,0:T(8,128)(2,1)S(1)}, bf16[2,32,1200]{2,1,0:T(8,128)(2,1)S(1)}, u32[]{:S(2)}, u32[]{:S(2)}) collective-permute-start(bf16[2,32,1200]{2,1,0:T(8,128)(2,1)S(1)} %get-tuple-element.20), channel_id=1, source_target_pairs={{0,16},{8,24},{16,0},{24,8},{1,17},{9,25},{17,1},{25,9},{2,18},{10... | collective-permute-start | bytes 460808 | tf_op jit(solution)/shard_map/ppermute | solution.py:109
  88.0 0.8 slice_bitcast_fusion.3
  88.9 1.6 %collective-permute-done.2 = bf16[2,32,1200]{2,1,0:T(8,128)(2,1)S(1)} collective-permute-done((bf16[2,32,1200]{2,1,0:T(8,128)(2,1)S(1)}, bf16[2,32,1200]{2,1,0:T(8,128)(2,1)S(1)}, u32[]{:S(2)}, u32[]{:S(2)}) %collective-permute-start.2) | collective-permute-done | bytes 153632 | tf_op jit(solution)/shard_map/ppermute | solution.py:109
  90.4 3.7 %collective-permute-done.1 = bf16[2,32,1200]{2,1,0:T(8,128)(2,1)S(1)} collective-permute-done((bf16[2,32,1200]{2,1,0:T(8,128)(2,1)S(1)}, bf16[2,32,1200]{2,1,0:T(8,128)(2,1)S(1)}, u32[]{:S(2)}, u32[]{:S(2)}) %collective-permute-start.1) | collective-permute-done | bytes 153632 | tf_op jit(solution)/shard_map/ppermute | solution.py:109
  94.3 0.8 slice_divide_fusion
  98.0 1.2 %fusion.17 = bf16[1,400,400]{2,1,0:T(8,128)(2,1)} fusion(f32[2,400,400]{2,1,0:T(8,128)S(1)} %fusion.28, f32[2,400,400]{2,1,0:T(8,128)S(1)} %fusion.20), kind=kLoop, calls=%fused_computation.36 | loop fusion | flops 800000 | bytes 2880000 | tf_op jit(solution)/shard_map/convert_element_type | solution.py:263
  (144 shorter events, 22.0 us)
Async XLA Ops:
  11.8 9.8 %copy-start.27 = (s32[1,8]{1,0:T(1,128)S(1)}, s32[1,8]{1,0:T(1,128)}, u32[]{:S(2)}) copy-start(s32[1,8]{1,0:T(1,128)} %param.13) | copy-start | bytes 100
  11.8 9.9 %copy-start.28 = (s32[1,8]{1,0:T(1,128)S(1)}, s32[1,8]{1,0:T(1,128)}, u32[]{:S(2)}) copy-start(s32[1,8]{1,0:T(1,128)} %param.14) | copy-start | bytes 100
  11.8 9.9 %copy-start.29 = (s32[1,8]{1,0:T(1,128)S(1)}, s32[1,8]{1,0:T(1,128)}, u32[]{:S(2)}) copy-start(s32[1,8]{1,0:T(1,128)} %param.15) | copy-start | bytes 100
  11.8 10.2 %copy-start.17 = (s32[1,8,1]{1,2,0:T(1,128)S(1)}, s32[1,8,1]{1,2,0:T(1,128)}, u32[]{:S(2)}) copy-start(s32[1,8,1]{1,2,0:T(1,128)} %param.12) | copy-start | bytes 100
  11.8 20.0 %all-to-all-start = ((f32[32,1,2525]{2,1,0:T(1,128)}), f32[32,1,2525]{2,1,0:T(1,128)S(1)}, u32[]{:S(2)}, u32[]{:S(2)}) async-start(f32[32,1,2525]{2,1,0:T(1,128)} %all_to_all.28), calls=%async_computation | async-start | bytes 655360 | tf_op jit(solution)/shard_map/all_to_all | solution.py:174
  20.9 2.1 %copy-start.30 = (f32[64]{0:T(128)S(1)}, f32[64]{0:T(128)}, u32[]{:S(2)}) copy-start(f32[64]{0:T(128)} %param.11) | copy-start | bytes 772
  21.0 3.7 %copy-start.8 = (bf16[2,128,800]{1,2,0:T(8,128)(2,1)S(1)}, bf16[2,128,800]{1,2,0:T(8,128)(2,1)}, u32[]{:S(2)}) copy-start(bf16[2,128,800]{1,2,0:T(8,128)(2,1)} %param.16) | copy-start | bytes 1228804
  22.3 2.4 %copy-start.20 = (s32[8]{0:T(128)}, s32[8]{0:T(128)S(1)}, u32[]{:S(2)}) copy-start(s32[8]{0:T(128)S(1)} %multiply_add_fusion) | copy-start | bytes 100
  31.9 18.3 %all-to-all-start.2 = ((bf16[8,2,12928]{2,1,0:T(2,128)(2,1)}), bf16[8,2,12928]{2,1,0:T(2,128)(2,1)S(1)}, u32[]{:S(2)}, u32[]{:S(2)}) async-start(bf16[8,2,12928]{2,1,0:T(2,128)(2,1)} %all_to_all.24), calls=%async_computation.2 | async-start | bytes 827392 | tf_op jit(solution)/shard_map/all_to_all | solution.py:175
  51.0 15.9 %all-to-all-start.1 = ((f32[32,1,2525]{2,1,0:T(1,128)}), f32[32,1,2525]{2,1,0:T(1,128)}, u32[]{:S(2)}, u32[]{:S(2)}) async-start(f32[32,1,2525]{2,1,0:T(1,128)} %broadcast_in_dim.30), calls=%async_computation.1 | async-start | bytes 655360 | tf_op jit(solution)/shard_map/all_to_all | solution.py:81
  57.4 1.1 %copy-start.31 = (f32[64]{0:T(128)S(1)}, f32[64]{0:T(128)}, u32[]{:S(2)}) copy-start(f32[64]{0:T(128)} %param.11) | copy-start | bytes 772
  58.2 2.1 %copy-start.9 = (f32[16]{0:T(128)S(1)}, f32[16]{0:T(128)}, u32[]{:S(2)}) copy-start(f32[16]{0:T(128)} %get-tuple-element.6) | copy-start | bytes 196
  58.5 3.8 %copy-start.15 = (f32[16]{0:T(128)S(1)}, f32[16]{0:T(128)}, u32[]{:S(2)}) copy-start(f32[16]{0:T(128)} %get-tuple-element.7) | copy-start | bytes 196
  64.7 10.0 %copy-start.11 = (s32[400]{0:T(512)S(1)}, s32[400]{0:T(512)}, u32[]{:S(2)}) copy-start(s32[400]{0:T(512)} %get-tuple-element.28) | copy-start | bytes 4804
  64.7 10.0 %copy-start.24 = (pred[400]{0:T(512)(128)(4,1)S(1)}, pred[400]{0:T(512)(128)(4,1)}, u32[]{:S(2)}) copy-start(pred[400]{0:T(512)(128)(4,1)} %fusion.114) | copy-start | bytes 1204
  66.8 8.5 %copy-start.18 = (s32[400]{0:T(512)S(1)}, s32[400]{0:T(512)}, u32[]{:S(2)}) copy-start(s32[400]{0:T(512)} %fusion.115) | copy-start | bytes 4804
  66.8 8.5 %copy-start.19 = (s32[400]{0:T(512)S(1)}, s32[400]{0:T(512)}, u32[]{:S(2)}) copy-start(s32[400]{0:T(512)} %get-tuple-element.27) | copy-start | bytes 4804
  66.8 8.5 %copy-start.32 = (pred[400]{0:T(512)(128)(4,1)S(1)}, pred[400]{0:T(512)(128)(4,1)}, u32[]{:S(2)}) copy-start(pred[400]{0:T(512)(128)(4,1)} %compare_and_fusion) | copy-start | bytes 1204
  67.0 28.2 %all-to-all-start.3 = ((bf16[16,2,16,400]{3,2,1,0:T(8,128)(2,1)}), bf16[16,2,16,400]{3,2,1,0:T(8,128)(2,1)S(1)}, u32[]{:S(2)}, u32[]{:S(2)}) async-start(bf16[16,2,16,400]{3,2,1,0:T(8,128)(2,1)} %copy.91), calls=%async_computation.3 | async-start | bytes 1048576 | tf_op jit(solution)/shard_map/all_to_all | solution.py:200
  72.4 3.9 %copy-start.12 = (s32[400]{0:T(512)S(1)}, s32[400]{0:T(512)}, u32[]{:S(2)}) copy-start(s32[400]{0:T(512)} %fusion.113) | copy-start | bytes 4804
  72.4 3.9 %copy-start.26 = (pred[400]{0:T(512)(128)(4,1)S(1)}, pred[400]{0:T(512)(128)(4,1)}, u32[]{:S(2)}) copy-start(pred[400]{0:T(512)(128)(4,1)} %fusion.112) | copy-start | bytes 1204
  76.3 1.2 %copy-start.7 = (f32[16,16,800]{2,1,0:T(8,128)S(1)}, f32[16,16,800]{2,1,0:T(8,128)}, u32[]{:S(2)}) copy-start(f32[16,16,800]{2,1,0:T(8,128)} %reshape.437) | copy-start | bytes 2457604
  76.3 1.2 %copy-start.25 = (s32[16]{0:T(128)S(1)}, s32[16]{0:T(128)}, u32[]{:S(2)}) copy-start(s32[16]{0:T(128)} %get-tuple-element.2) | copy-start | bytes 196
  78.4 1.1 %copy-start.2 = (f32[1,1,400,400]{3,2,1,0:T(8,128)S(1)}, f32[1,1,400,400]{3,2,1,0:T(8,128)}, u32[]{:S(2)}) copy-start(f32[1,1,400,400]{3,2,1,0:T(8,128)} %get-tuple-element.8) | copy-start | bytes 1920004
  78.4 1.4 %copy-start.3 = (f32[1,1,400,400]{3,2,1,0:T(8,128)S(1)}, f32[1,1,400,400]{3,2,1,0:T(8,128)}, u32[]{:S(2)}) copy-start(f32[1,1,400,400]{3,2,1,0:T(8,128)} %fusion.19) | copy-start | bytes 1920004
  79.7 1.1 %copy-start.1 = (bf16[2,400,400]{2,1,0:T(8,128)(2,1)S(1)}, bf16[2,400,400]{2,1,0:T(8,128)(2,1)}, u32[]{:S(2)}) copy-start(bf16[2,400,400]{2,1,0:T(8,128)(2,1)} %constant.122.clone) | copy-start | bytes 1920004
  84.1 4.8 %collective-permute-start = (bf16[2,32,1200]{2,1,0:T(8,128)(2,1)S(1)}, bf16[2,32,1200]{2,1,0:T(8,128)(2,1)S(1)}, u32[]{:S(2)}, u32[]{:S(2)}) collective-permute-start(bf16[2,32,1200]{2,1,0:T(8,128)(2,1)S(1)} %get-tuple-element.18), channel_id=1, source_target_pairs={{0,8},{8,16},{16,24},{24,0},{1,9},{9,17},{17,25},{25,1},{2,10},{10... | collective-permute-start | bytes 460808 | tf_op jit(solution)/shard_map/ppermute | solution.py:109
  84.1 6.3 %collective-permute-start.2 = (bf16[2,32,1200]{2,1,0:T(8,128)(2,1)S(1)}, bf16[2,32,1200]{2,1,0:T(8,128)(2,1)S(1)}, u32[]{:S(2)}, u32[]{:S(2)}) collective-permute-start(bf16[2,32,1200]{2,1,0:T(8,128)(2,1)S(1)} %get-tuple-element.19), channel_id=1, source_target_pairs={{0,24},{8,0},{16,8},{24,16},{1,25},{9,1},{17,9},{25,17},{2,26},{10... | collective-permute-start | bytes 460808 | tf_op jit(solution)/shard_map/ppermute | solution.py:109
  85.9 8.3 %collective-permute-start.1 = (bf16[2,32,1200]{2,1,0:T(8,128)(2,1)S(1)}, bf16[2,32,1200]{2,1,0:T(8,128)(2,1)S(1)}, u32[]{:S(2)}, u32[]{:S(2)}) collective-permute-start(bf16[2,32,1200]{2,1,0:T(8,128)(2,1)S(1)} %get-tuple-element.20), channel_id=1, source_target_pairs={{0,16},{8,24},{16,0},{24,8},{1,17},{9,25},{17,1},{25,9},{2,18},{10... | collective-permute-start | bytes 460808 | tf_op jit(solution)/shard_map/ppermute | solution.py:109
  88.0 7.1 %copy-start.21 = (s32[8]{0:T(128)S(1)}, s32[8]{0:T(128)}, u32[]{:S(2)}) copy-start(s32[8]{0:T(128)} %copy-done.20) | copy-start | bytes 100
  95.1 1.0 %copy-start.5 = (f32[2,64,400]{2,1,0:T(8,128)S(1)}, f32[2,64,400]{2,1,0:T(8,128)}, u32[]{:S(2)}) copy-start(f32[2,64,400]{2,1,0:T(8,128)} %get-tuple-element.12) | copy-start | bytes 614404
  95.1 1.1 %copy-start.6 = (f32[2,64,400]{2,1,0:T(8,128)S(1)}, f32[2,64,400]{2,1,0:T(8,128)}, u32[]{:S(2)}) copy-start(f32[2,64,400]{2,1,0:T(8,128)} %get-tuple-element.13) | copy-start | bytes 614404
  (8 other events, 5.9 us)

commit v12 on v11

--- a/solution.py
+++ b/solution.py
@@ -172,6 +172,9 @@
     power_half = jnp.sum(low_half * low_half, axis=(0, 1))
     pieces = power_half.reshape(device_count, rows_half * box_size // device_count)
     gathered = lax.all_to_all(pieces, ("img", "slab"), 0, 0, tiled=True)
+    total = jnp.sum(gathered, axis=0, keepdims=True)
+    power = power_gather(total, device_count, rows_half, box_size)
+    send, power = lax.optimization_barrier((send, power))
     got = lax.all_to_all(send, "slab", 0, 0, tiled=True)
     got_blocks = got[:, : RB * 2 * box_size].reshape(seat_count, RB, 2 * box_size)
     got_info = got[:, RB * 2 * box_size : RB * 2 * box_size + 6].astype(jnp.int32)
@@ -192,8 +195,6 @@
         ((1.0 - blend_4) * nearby + blend_4 * jnp.roll(nearby, -1, axis=-1)) * live[..., None]
     ).astype(jnp.bfloat16)
 
-    total = jnp.sum(gathered, axis=0, keepdims=True)
-    power = power_gather(total, device_count, rows_half, box_size)
     noise_level = jnp.sqrt(power / (particles * device_count) + 1e-06)
     level_both = jnp.concatenate([noise_level, noise_level], axis=1)
 

time: 99.9 us -> 108 us (1.081)
  waiting for transfers between devices: 14 us -> 29.3 us
  starting transfers between devices: 25.8 us -> 21.1 us
  other arithmetic: 27.7 us -> 23.2 us
  matrix products: 12.5 us -> 14.6 us
    all_to_all x1, waiting for transfers between devices: 0.01 us -> 10.4 us  [body(): returned_rows = lax.all_to_all(projected, 'slab', 0, 0, tiled=True)]
    all_to_all x1, waiting for transfers between devices: 0.16 us -> 5.64 us  [power_gather(): back = lax.all_to_all(spread, ('img', 'slab'), 0, 0, tiled=True)]
    all_to_all x1, waiting for transfers between devices: 0.01 us -> 4.63 us  [body(): gathered = lax.all_to_all(pieces, ('img', 'slab'), 0, 0, tiled=True)]
    ppermute x3, waiting for transfers between devices: 5.33 us -> 1.9 us  [reduce_over_img(): total = total + lax.ppermute(piece, 'img', pairs).astype(jnp.float32)]
    all_to_all x1, waiting for transfers between devices: 8.53 us -> 6.69 us  [body(): got = lax.all_to_all(send, 'slab', 0, 0, tiled=True)]
    all_to_all x1, starting transfers between devices: 5.44 us -> 3.71 us  [body(): returned_rows = lax.all_to_all(projected, 'slab', 0, 0, tiled=True)]
    all_to_all x1, starting transfers between devices: 5.82 us -> 4.28 us  [body(): got = lax.all_to_all(send, 'slab', 0, 0, tiled=True)]
    unnamed x67 -> x27, local copies, waits for them, and re-layouts: 4.54 us -> 3.05 us
  transfers between devices with their start and end apart: 7 -> 7, of which waited for: 5 -> 5; matrix products, arithmetic and copies ran while one was open for 37% -> 19% of each run, Pallas kernels for 0% -> 0%
where the time goes in v12:
time: 108 us; the launch traced here: 107 us
  waiting for transfers between devices  29.3 us (27%)
  other arithmetic  23.2 us (21%)
  starting transfers between devices  21.1 us (20%)
  local copies, waits for them, and re-layouts  16.1 us (15%)
  matrix products  14.6 us (14%)
  between operations  2.61 us (2%)
    all_to_all x1, waiting for transfers between devices, body(): returned_rows = lax.all_to_all(projected, 'slab', 0, 0, tiled=True)  10.4 us
    all_to_all x1, starting transfers between devices, body(): gathered = lax.all_to_all(pieces, ('img', 'slab'), 0, 0, tiled=True)  7.3 us
    all_to_all x1, waiting for transfers between devices, body(): got = lax.all_to_all(send, 'slab', 0, 0, tiled=True)  6.69 us
    all_to_all x1, waiting for transfers between devices, power_gather(): back = lax.all_to_all(spread, ('img', 'slab'), 0, 0, tiled=True)  5.64 us
    convert_element_type x2, other arithmetic, contrast_curve(): (-jnp.sin(defocus_of[:, None, None] * radius + 0.1)).astype(jnp.bfloat16)  4.94 us
    all_to_all x1, waiting for transfers between devices, body(): gathered = lax.all_to_all(pieces, ('img', 'slab'), 0, 0, tiled=True)  4.63 us
    dot_general x1, matrix products, transform(): jnp.einsum('gky,hym->ghkm', tables, rowwise, preferred_element_type=jnp.f...  4.56 us
    all_to_all x1, starting transfers between devices, body(): got = lax.all_to_all(send, 'slab', 0, 0, tiled=True)  4.28 us
  transfers between devices with their start and end apart: 7, of which 5 were waited for; matrix products, arithmetic and copies ran while one was open for 19% of the time, Pallas kernels for 0%

profile of v12, /device:TPU:0, one launch (start us, length us, event | category | flops | bytes accessed | tf_op | source)
XLA Modules:
  0.0 106.9 jit_solution(15148783806139666845)
XLA Ops:
  0.6 1.0 copy-done
  1.6 4.6 %convolution_bitcast_fusion = f32[2,2,400,400]{3,2,0,1:T(8,128)} fusion(bf16[2,400,400]{2,1,0:T(8,128)(2,1)} %constant.122.clone, bf16[1,400,400]{2,1,0:T(8,128)(2,1)S(1)} %copy-done), kind=kOutput, calls=%fused_computation.2 | convolution fusion | flops 768320000 | bytes 3520000 | tf_op jit(solution)/shard_map/gky,hym->ghkm/dot_general | solution.py:27
  6.2 1.5 %fusion.129 = f32[1,400,400]{2,1,0:T(8,128)S(1)} fusion(f32[2,2,400,400]{3,2,0,1:T(8,128)} %convolution_bitcast_fusion), kind=kLoop, calls=%fused_computation.198 | loop fusion | flops 160000 | bytes 1920000 | tf_op jit(solution)/shard_map/sub | solution.py:28
  7.7 1.6 %fusion.68 = (f32[1,1,400,400]{3,2,1,0:T(8,128)S(1)}, f32[1,400,400]{2,1,0:T(8,128)S(1)}) fusion(f32[2,2,400,400]{3,2,0,1:T(8,128)} %convolution_bitcast_fusion), kind=kLoop, calls=%fused_computation.109 | loop fusion | flops 320000 | bytes 2560000 | tf_op jit(solution)/shard_map/neg | solution.py:29
  9.6 1.4 %all_to_all.28 = f32[32,1,2525]{2,1,0:T(1,128)} reshape(f32[202,400]{1,0:T(8,128)S(1)} %fusion.11) | data formatting | bytes 646400 | tf_op jit(solution)/shard_map/all_to_all | solution.py:174
  11.0 7.3 %all-to-all-start = ((f32[32,1,2525]{2,1,0:T(1,128)}), f32[32,1,2525]{2,1,0:T(1,128)S(1)}, u32[]{:S(2)}, u32[]{:S(2)}) async-start(f32[32,1,2525]{2,1,0:T(1,128)} %all_to_all.28), calls=%async_computation | async-start | bytes 655360 | tf_op jit(solution)/shard_map/all_to_all | solution.py:174
  18.4 1.0 fusion.121
  20.4 1.0 fusion.122
  22.7 3.0 %negate_convert_fusion = bf16[1,400,400]{2,1,0:T(8,128)(2,1)S(1)} fusion(f32[]{:T(128)S(6)} %mul.156, s32[400]{0:T(512)S(1)} %fusion.105), kind=kLoop, calls=%fused_computation.56 | loop fusion | flops 960000 | bytes 321604 | tf_op jit(solution)/shard_map/convert_element_type | solution.py:58
  25.8 4.6 %all-to-all-done = f32[32,1,2525]{2,1,0:T(1,128)S(1)} async-done(((f32[32,1,2525]{2,1,0:T(1,128)}), f32[32,1,2525]{2,1,0:T(1,128)S(1)}, u32[]{:S(2)}, u32[]{:S(2)}) %all-to-all-start) | async-done | bytes 323232 | tf_op jit(solution)/shard_map/all_to_all | solution.py:174
  31.5 2.6 %all-to-all-start.1 = ((f32[32,1,2525]{2,1,0:T(1,128)}), f32[32,1,2525]{2,1,0:T(1,128)S(1)}, u32[]{:S(2)}, u32[]{:S(2)}) async-start(f32[32,1,2525]{2,1,0:T(1,128)} %broadcast_in_dim.30), calls=%async_computation.1 | async-start | bytes 655360 | tf_op jit(solution)/shard_map/all_to_all | solution.py:81
  34.5 1.2 %copy.88 = bf16[2,128,800]{2,1,0:T(8,128)(2,1)S(1)} copy(bf16[2,128,800]{1,2,0:T(8,128)(2,1)} %param.16) | data formatting | bytes 819200 | tf_op args[7]
  38.2 2.4 %fusion.16 = f32[1,1,400,400]{3,2,1,0:T(8,128)} fusion(f32[2,2,400,400]{3,2,0,1:T(8,128)} %convolution_bitcast_fusion), kind=kLoop, calls=%fused_computation.38 | loop fusion | flops 160000 | bytes 1920000 | tf_op jit(solution)/shard_map/sub | solution.py:28
  40.6 5.6 %all-to-all-done.1 = f32[32,1,2525]{2,1,0:T(1,128)S(1)} async-done(((f32[32,1,2525]{2,1,0:T(1,128)}), f32[32,1,2525]{2,1,0:T(1,128)S(1)}, u32[]{:S(2)}, u32[]{:S(2)}) %all-to-all-start.1) | async-done | bytes 323232 | tf_op jit(solution)/shard_map/all_to_all | solution.py:81
  48.0 1.0 fusion.33
  50.8 0.9 all_to_all.24
  51.8 4.3 %all-to-all-start.2 = ((bf16[8,2,12928]{2,1,0:T(2,128)(2,1)}), bf16[8,2,12928]{2,1,0:T(2,128)(2,1)}, u32[]{:S(2)}, u32[]{:S(2)}) async-start(bf16[8,2,12928]{2,1,0:T(2,128)(2,1)} %all_to_all.24), calls=%async_computation.2 | async-start | bytes 827392 | tf_op jit(solution)/shard_map/all_to_all | solution.py:178
  56.1 1.5 %maximum_divide_fusion = f32[1,2,400,400]{3,2,1,0:T(8,128)S(1)} fusion(f32[1,1,400,400]{3,2,1,0:T(8,128)S(1)} %get-tuple-element.12, f32[1,1,400,400]{3,2,1,0:T(8,128)} %fusion.16, f32[400,400]{1,0:T(8,128)S(1)} %add_sqrt_fusion), kind=kLoop, calls=%fused_computation.4 | loop fusion | flops 640000 | bytes 3200000 | tf_op jit(solution)/shard_map/div | solution.py:234
  59.4 1.8 %fusion.17 = f32[2,400,400]{2,1,0:T(8,128)} fusion(bf16[2,400,400]{2,1,0:T(8,128)(2,1)S(1)} %copy-done.3, bf16[2,64,400]{2,1,0:T(8,128)(2,1)S(1)} %broadcast_in_dim.25, bf16[1,272,400]{2,1,0:T(8,128)(2,1)S(1)} %get-tuple-element.15, bf16[1,272,400]{2,1,0:T(8,128)(2,1)S(1)} %get-tuple-element.14), kind=kOutput, calls=%fused_computation.40 | convolution fusion | flops 258560000 | bytes 2457600 | tf_op jit(solution)/shard_map/hxk,hkm->hxm/dot_general | solution.py:43
  61.1 6.7 %all-to-all-done.2 = bf16[8,2,12928]{2,1,0:T(2,128)(2,1)} async-done(((bf16[8,2,12928]{2,1,0:T(2,128)(2,1)}), bf16[8,2,12928]{2,1,0:T(2,128)(2,1)}, u32[]{:S(2)}, u32[]{:S(2)}) %all-to-all-start.2) | async-done | bytes 413728 | tf_op jit(solution)/shard_map/all_to_all | solution.py:178
  67.8 1.2 %all_to_all.26 = bf16[16,12928]{1,0:T(8,128)(2,1)S(1)} reshape(bf16[8,2,12928]{2,1,0:T(2,128)(2,1)} %all-to-all-done.2) | data formatting | bytes 827392 | tf_op jit(solution)/shard_map/all_to_all | solution.py:178
  69.7 1.5 %reshape.437 = f32[16,16,800]{2,1,0:T(8,128)} reshape(f32[16,12800]{1,0:T(8,128)S(1)} %slice_convert_fusion.1) | data formatting | bytes 1638400 | tf_op jit(solution)/shard_map/convert_element_type | solution.py:215
  71.2 1.9 %negate_convert_fusion.1 = (bf16[16,16,400]{2,0,1:T(8,128)(2,1)S(1)}, f32[16,16,400]{2,0,1:T(8,128)S(1)}) fusion(f32[16]{0:T(128)S(1)} %broadcast_multiply_fusion, s32[400]{0:T(512)S(1)} %fusion.105, s32[16,16]{0,1:T(8,128)S(1)} %fusion.84), kind=kLoop, calls=%fused_computation.75 | loop fusion | flops 819200 | bytes 617088 | tf_op jit(solution)/shard_map/convert_element_type | solution.py:58
  73.1 2.0 %convolution_divide_fusion = f32[16,16,800]{2,0,1:T(8,128)S(1)} fusion(f32[16,16,800]{2,1,0:T(8,128)} %reshape.437, bf16[16,16,400]{2,0,1:T(8,128)(2,1)S(1)} %get-tuple-element.29, f32[8,16,800]{2,1,0:T(8,128)S(1)} %bitcast.140, s32[16]{0:T(128)S(1)} %get-tuple-element.6), kind=kOutput, calls=%fused_computation.7 | convolution fusion | flops 20889728 | bytes 2252864 | tf_op jit(solution)/shard_map/sj,jix->six/dot_general | solution.py:211
  76.7 2.1 %fusion.41 = f32[16,16,400]{2,0,1:T(8,128)S(1)} fusion(f32[16,16,399]{2,0,1:T(8,128)S(1)} %bitcast.135, f32[16,16,1]{2,0,1:T(8,128)S(1)} %slice.236, f32[16]{0:T(128)S(1)} %get-tuple-element.10, f32[16]{0:T(128)S(1)} %broadcast_subtract_fusion, f32[16]{0:T(128)S(1)} %broadcast_multiply_fusion, s32[400]{0:T(512)S(1)} %fusion.105, s32[16,16]{0,1:T(8,128)S(1)} %fusion.84), kind=kLoop, calls=%fused_computation.70 | loop fusion | flops 1228800 | bytes 822016 | tf_op jit(solution)/shard_map/add | solution.py:219
  81.1 1.7 %collective-permute-start.2 = (bf16[2,32,1200]{2,1,0:T(8,128)(2,1)S(1)}, bf16[2,32,1200]{2,1,0:T(8,128)(2,1)S(1)}, u32[]{:S(2)}, u32[]{:S(2)}) collective-permute-start(bf16[2,32,1200]{2,1,0:T(8,128)(2,1)S(1)} %get-tuple-element.23), channel_id=1, source_target_pairs={{0,24},{8,0},{16,8},{24,16},{1,25},{9,1},{17,9},{25,17},{2,26},{10... | collective-permute-start | bytes 460808 | tf_op jit(solution)/shard_map/ppermute | solution.py:109
  82.8 1.5 %collective-permute-start.1 = (bf16[2,32,1200]{2,1,0:T(8,128)(2,1)S(1)}, bf16[2,32,1200]{2,1,0:T(8,128)(2,1)S(1)}, u32[]{:S(2)}, u32[]{:S(2)}) collective-permute-start(bf16[2,32,1200]{2,1,0:T(8,128)(2,1)S(1)} %get-tuple-element.24), channel_id=1, source_target_pairs={{0,16},{8,24},{16,0},{24,8},{1,17},{9,25},{17,1},{25,9},{2,18},{10... | collective-permute-start | bytes 460808 | tf_op jit(solution)/shard_map/ppermute | solution.py:109
  84.6 1.1 %copy.91 = bf16[16,2,16,400]{3,2,1,0:T(8,128)(2,1)} copy(bf16[16,2,16,400]{3,0,2,1:T(8,128)(2,1)S(1)} %fusion.8) | data formatting | bytes 819200 | tf_op jit(solution)/shard_map/convert_element_type | solution.py:196
  85.7 3.7 %all-to-all-start.3 = ((bf16[16,2,16,400]{3,2,1,0:T(8,128)(2,1)}), bf16[16,2,16,400]{3,2,1,0:T(8,128)(2,1)S(1)}, u32[]{:S(2)}, u32[]{:S(2)}) async-start(bf16[16,2,16,400]{3,2,1,0:T(8,128)(2,1)} %copy.91), calls=%async_computation.3 | async-start | bytes 1048576 | tf_op jit(solution)/shard_map/all_to_all | solution.py:201
  89.4 1.9 %collective-permute-done.1 = bf16[2,32,1200]{2,1,0:T(8,128)(2,1)S(1)} collective-permute-done((bf16[2,32,1200]{2,1,0:T(8,128)(2,1)S(1)}, bf16[2,32,1200]{2,1,0:T(8,128)(2,1)S(1)}, u32[]{:S(2)}, u32[]{:S(2)}) %collective-permute-start.1) | collective-permute-done | bytes 153632 | tf_op jit(solution)/shard_map/ppermute | solution.py:109
  92.3 10.4 %all-to-all-done.3 = bf16[16,2,16,400]{3,2,1,0:T(8,128)(2,1)S(1)} async-done(((bf16[16,2,16,400]{3,2,1,0:T(8,128)(2,1)}), bf16[16,2,16,400]{3,2,1,0:T(8,128)(2,1)S(1)}, u32[]{:S(2)}, u32[]{:S(2)}) %all-to-all-start.3) | async-done | bytes 409632 | tf_op jit(solution)/shard_map/all_to_all | solution.py:201
  105.7 1.1 %fusion.14 = bf16[1,400,400]{2,1,0:T(8,128)(2,1)} fusion(f32[2,400,400]{2,1,0:T(8,128)S(1)} %fusion.25, f32[2,400,400]{2,1,0:T(8,128)S(1)} %copy-done.4), kind=kLoop, calls=%fused_computation.33 | loop fusion | flops 800000 | bytes 2880000 | tf_op jit(solution)/shard_map/convert_element_type | solution.py:264
  (107 shorter events, 19.0 us)
Async XLA Ops:
  0.6 1.0 copy-start
  11.0 9.1 %copy-start.9 = (s32[1,8]{1,0:T(1,128)S(1)}, s32[1,8]{1,0:T(1,128)}, u32[]{:S(2)}) copy-start(s32[1,8]{1,0:T(1,128)} %param.13) | copy-start | bytes 100
  11.0 9.1 %copy-start.10 = (s32[1,8]{1,0:T(1,128)S(1)}, s32[1,8]{1,0:T(1,128)}, u32[]{:S(2)}) copy-start(s32[1,8]{1,0:T(1,128)} %param.14) | copy-start | bytes 100
  11.0 9.1 %copy-start.11 = (s32[1,8]{1,0:T(1,128)S(1)}, s32[1,8]{1,0:T(1,128)}, u32[]{:S(2)}) copy-start(s32[1,8]{1,0:T(1,128)} %param.15) | copy-start | bytes 100
  11.0 9.2 %copy-start.8 = (s32[1,8,1]{1,2,0:T(1,128)S(1)}, s32[1,8,1]{1,2,0:T(1,128)}, u32[]{:S(2)}) copy-start(s32[1,8,1]{1,2,0:T(1,128)} %param.12) | copy-start | bytes 100
  11.0 19.4 %all-to-all-start = ((f32[32,1,2525]{2,1,0:T(1,128)}), f32[32,1,2525]{2,1,0:T(1,128)S(1)}, u32[]{:S(2)}, u32[]{:S(2)}) async-start(f32[32,1,2525]{2,1,0:T(1,128)} %all_to_all.28), calls=%async_computation | async-start | bytes 655360 | tf_op jit(solution)/shard_map/all_to_all | solution.py:174
  18.3 3.1 %copy-start.12 = (f32[64]{0:T(128)S(1)}, f32[64]{0:T(128)}, u32[]{:S(2)}) copy-start(f32[64]{0:T(128)} %param.11) | copy-start | bytes 772
  31.5 14.7 %all-to-all-start.1 = ((f32[32,1,2525]{2,1,0:T(1,128)}), f32[32,1,2525]{2,1,0:T(1,128)S(1)}, u32[]{:S(2)}, u32[]{:S(2)}) async-start(f32[32,1,2525]{2,1,0:T(1,128)} %broadcast_in_dim.30), calls=%async_computation.1 | async-start | bytes 655360 | tf_op jit(solution)/shard_map/all_to_all | solution.py:81
  51.8 16.1 %all-to-all-start.2 = ((bf16[8,2,12928]{2,1,0:T(2,128)(2,1)}), bf16[8,2,12928]{2,1,0:T(2,128)(2,1)}, u32[]{:S(2)}, u32[]{:S(2)}) async-start(bf16[8,2,12928]{2,1,0:T(2,128)(2,1)} %all_to_all.24), calls=%async_computation.2 | async-start | bytes 827392 | tf_op jit(solution)/shard_map/all_to_all | solution.py:178
  56.0 1.5 %copy-start.3 = (bf16[2,400,400]{2,1,0:T(8,128)(2,1)S(1)}, bf16[2,400,400]{2,1,0:T(8,128)(2,1)}, u32[]{:S(2)}) copy-start(bf16[2,400,400]{2,1,0:T(8,128)(2,1)} %constant.122.clone) | copy-start | bytes 1920004
  69.5 3.7 %copy-start.7 = (f32[128,800]{1,0:T(8,128)S(1)}, f32[128,800]{1,0:T(8,128)}, u32[]{:S(2)}) copy-start(f32[128,800]{1,0:T(8,128)} %fusion.45) | copy-start | bytes 1228804
  76.2 2.6 %copy-start.1 = (f32[16,2,16,400]{3,0,2,1:T(8,128)}, f32[16,2,16,400]{3,0,2,1:T(8,128)S(1)}, u32[]{:S(2)}) copy-start(f32[16,2,16,400]{3,0,2,1:T(8,128)S(1)} %fusion.43) | copy-start | bytes 2457604
  80.1 4.1 %copy-start.2 = (f32[16,2,16,400]{3,0,2,1:T(8,128)S(1)}, f32[16,2,16,400]{3,0,2,1:T(8,128)}, u32[]{:S(2)}) copy-start(f32[16,2,16,400]{3,0,2,1:T(8,128)} %copy-done.1) | copy-start | bytes 2457604
  80.1 4.1 %slice-start = ((f32[16,2,16,400]{3,0,2,1:T(8,128)}), f32[16,2,16,1]{3,0,2,1:T(8,128)S(1)}, s32[]{:S(2)}) async-start(f32[16,2,16,400]{3,0,2,1:T(8,128)} %copy-done.1), calls=%async_computation.4 | async-start | bytes 524288 | tf_op jit(solution)/shard_map/jit(_roll_static)/slice | solution.py:195
  81.1 8.3 %collective-permute-start = (bf16[2,32,1200]{2,1,0:T(8,128)(2,1)}, bf16[2,32,1200]{2,1,0:T(8,128)(2,1)S(1)}, u32[]{:S(2)}, u32[]{:S(2)}) collective-permute-start(bf16[2,32,1200]{2,1,0:T(8,128)(2,1)} %get-tuple-element.22), channel_id=1, source_target_pairs={{0,8},{8,16},{16,24},{24,0},{1,9},{9,17},{17,25},{25,1},{2,10},{10... | collective-permute-start | bytes 460808 | tf_op jit(solution)/shard_map/ppermute | solution.py:109
  81.1 8.3 %collective-permute-start.2 = (bf16[2,32,1200]{2,1,0:T(8,128)(2,1)S(1)}, bf16[2,32,1200]{2,1,0:T(8,128)(2,1)S(1)}, u32[]{:S(2)}, u32[]{:S(2)}) collective-permute-start(bf16[2,32,1200]{2,1,0:T(8,128)(2,1)S(1)} %get-tuple-element.23), channel_id=1, source_target_pairs={{0,24},{8,0},{16,8},{24,16},{1,25},{9,1},{17,9},{25,17},{2,26},{10... | collective-permute-start | bytes 460808 | tf_op jit(solution)/shard_map/ppermute | solution.py:109
  82.8 8.5 %collective-permute-start.1 = (bf16[2,32,1200]{2,1,0:T(8,128)(2,1)S(1)}, bf16[2,32,1200]{2,1,0:T(8,128)(2,1)S(1)}, u32[]{:S(2)}, u32[]{:S(2)}) collective-permute-start(bf16[2,32,1200]{2,1,0:T(8,128)(2,1)S(1)} %get-tuple-element.24), channel_id=1, source_target_pairs={{0,16},{8,24},{16,0},{24,8},{1,17},{9,25},{17,1},{25,9},{2,18},{10... | collective-permute-start | bytes 460808 | tf_op jit(solution)/shard_map/ppermute | solution.py:109
  85.7 17.0 %all-to-all-start.3 = ((bf16[16,2,16,400]{3,2,1,0:T(8,128)(2,1)}), bf16[16,2,16,400]{3,2,1,0:T(8,128)(2,1)S(1)}, u32[]{:S(2)}, u32[]{:S(2)}) async-start(bf16[16,2,16,400]{3,2,1,0:T(8,128)(2,1)} %copy.91), calls=%async_computation.3 | async-start | bytes 1048576 | tf_op jit(solution)/shard_map/all_to_all | solution.py:201
  91.4 12.0 %copy-start.5 = (f32[128,400]{1,0:T(8,128)S(1)}, f32[128,400]{1,0:T(8,128)}, u32[]{:S(2)}) copy-start(f32[128,400]{1,0:T(8,128)} %maximum_convert_fusion) | copy-start | bytes 614404
  91.4 12.0 %copy-start.6 = (f32[2,64,400]{2,1,0:T(8,128)S(1)}, f32[2,64,400]{2,1,0:T(8,128)}, u32[]{:S(2)}) copy-start(f32[2,64,400]{2,1,0:T(8,128)} %get-tuple-element.17) | copy-start | bytes 614404
  104.3 1.4 %copy-start.4 = (f32[2,400,400]{2,1,0:T(8,128)S(1)}, f32[2,400,400]{2,1,0:T(8,128)}, u32[]{:S(2)}) copy-start(f32[2,400,400]{2,1,0:T(8,128)} %fusion.17) | copy-start | bytes 3840004

commit v13 on v11

--- a/solution.py
+++ b/solution.py
@@ -20,10 +20,13 @@
     return jnp.asarray(both)
 
 
-def transform(image, tables):
-    rowwise = jnp.einsum(
+def rowwise_of(image, tables):
+    return jnp.einsum(
         "yx,hmx->hym", image, tables, preferred_element_type=jnp.float32
     ).astype(jnp.bfloat16)
+
+
+def transform(rowwise, tables):
     products = jnp.einsum("gky,hym->ghkm", tables, rowwise, preferred_element_type=jnp.float32)
     real = products[0, 0] - products[1, 1]
     imag = -(products[0, 1] + products[1, 0])
@@ -158,7 +161,8 @@
     info_width = 128
     block_info = jnp.pad(block_info, ((0, 0), (0, info_width - block_info.shape[1])))
 
-    spectrum = jnp.stack([transform(images[n], tables) for n in range(particles)])
+    rowwise = [rowwise_of(images[n], tables) for n in range(particles)]
+    spectrum = jnp.stack([transform(r, tables) for r in rowwise])
     low_spectrum = jnp.concatenate(
         [spectrum[:, :, :low_rows], spectrum[:, :, box_size - low_rows :]], axis=2
     ).astype(jnp.bfloat16)
@@ -168,7 +172,8 @@
         "rs,rx->sx", seat_pick, payload, preferred_element_type=jnp.float32
     ).astype(jnp.bfloat16)
     rows_half = half_rows(box_size, device_count)
-    low_half = spectrum[:, :, :rows_half]
+    top_rows = -(-rows_half // RB) * RB
+    low_half = jnp.stack([transform(r, tables[:, :top_rows]) for r in rowwise])[:, :, :rows_half]
     power_half = jnp.sum(low_half * low_half, axis=(0, 1))
     pieces = power_half.reshape(device_count, rows_half * box_size // device_count)
     gathered = lax.all_to_all(pieces, ("img", "slab"), 0, 0, tiled=True)

time: 99.9 us -> 90 us (0.901)
  other arithmetic: 27.7 us -> 23.2 us
  waiting for transfers between devices: 14 us -> 10.3 us
    dot_general x1 -> x2, matrix products: 4.56 us -> 1.68 us  [transform(): jnp.einsum('gky,hym->ghkm', tables, rowwise, preferred_element_type=jnp.f...]
    ppermute x3, waiting for transfers between devices: 5.33 us -> 3.27 us  [reduce_over_img(): total = total + lax.ppermute(piece, 'img', pairs).astype(jnp.float32)]
    all_to_all x1, waiting for transfers between devices: 8.53 us -> 6.59 us  [body(): got = lax.all_to_all(send, 'slab', 0, 0, tiled=True)]
    dot_general x0 -> x1, matrix products: none -> 1.9 us  [rowwise_of(): jnp.einsum('yx,hmx->hym', image, tables, preferred_element_type=jnp.float32)]
    sub x2 -> x3, other arithmetic: 3.98 us -> 2.67 us  [transform(): real = products[0, 0] - products[1, 1]]
    unnamed x67 -> x33, local copies, waits for them, and re-layouts: 4.54 us -> 3.32 us
    convert_element_type x1, local copies, waits for them, and re-layouts: 1.54 us -> 2.7 us  [body(): received = got_contrast_both * got_blocks.astype(jnp.float32) / got_level]
    neg x1 -> x3, other arithmetic: 2.48 us -> 2.7 us  [transform(): imag = -(products[0, 1] + products[1, 0])]
  transfers between devices with their start and end apart: 7 -> 7, of which waited for: 5 -> 5; matrix products, arithmetic and copies ran while one was open for 37% -> 43% of each run, Pallas kernels for 0% -> 0%
where the time goes in v13:
time: 90 us; the launch traced here: 89 us
  starting transfers between devices  25.2 us (28%)
  other arithmetic  23.2 us (26%)
  local copies, waits for them, and re-layouts  15.9 us (18%)
  matrix products  11.7 us (13%)
  waiting for transfers between devices  10.3 us (11%)
  between operations  2.58 us (3%)
    all_to_all x1, starting transfers between devices, body(): gathered = lax.all_to_all(pieces, ('img', 'slab'), 0, 0, tiled=True)  7.3 us
    all_to_all x1, waiting for transfers between devices, body(): got = lax.all_to_all(send, 'slab', 0, 0, tiled=True)  6.59 us
    convert_element_type x2, other arithmetic, contrast_curve(): (-jnp.sin(defocus_of[:, None, None] * radius + 0.1)).astype(jnp.bfloat16)  5.67 us
    all_to_all x1, starting transfers between devices, body(): returned_rows = lax.all_to_all(projected, 'slab', 0, 0, tiled=True)  5.59 us
    all_to_all x1, starting transfers between devices, body(): got = lax.all_to_all(send, 'slab', 0, 0, tiled=True)  5.39 us
    all_to_all x1, starting transfers between devices, power_gather(): back = lax.all_to_all(spread, ('img', 'slab'), 0, 0, tiled=True)  3.96 us
    unnamed x33, local copies, waits for them, and re-layouts  3.32 us
    ppermute x3, waiting for transfers between devices, reduce_over_img(): total = total + lax.ppermute(piece, 'img', pairs).astype(jnp.float32)  3.27 us
  transfers between devices with their start and end apart: 7, of which 5 were waited for; matrix products, arithmetic and copies ran while one was open for 43% of the time, Pallas kernels for 0%

profile of v13, /device:TPU:0, one launch (start us, length us, event | category | flops | bytes accessed | tf_op | source)
XLA Modules:
  0.0 89.0 jit_solution(15310109683059392179)
XLA Ops:
  0.7 1.0 %copy-done = bf16[1,400,400]{2,1,0:T(8,128)(2,1)S(1)} copy-done((bf16[1,400,400]{2,1,0:T(8,128)(2,1)S(1)}, bf16[1,400,400]{2,1,0:T(8,128)(2,1)}, u32[]{:S(2)}) %copy-start) | copy-done | bytes 320024
  1.6 1.9 %fusion.2 = bf16[2,400,400,1]{1,2,3,0:T(8,128)(2,1)S(1)} fusion(bf16[2,400,400]{1,2,0:T(8,128)(2,1)} %constant.122.clone, bf16[1,400,400]{2,1,0:T(8,128)(2,1)S(1)} %copy-done), kind=kOutput, calls=%fused_computation.12 | convolution fusion | flops 256320000 | bytes 1600000 | tf_op jit(solution)/shard_map/yx,hmx->hym/dot_general | solution.py:24
  4.6 1.4 %all_to_all.28 = f32[32,1,2525]{2,1,0:T(1,128)} reshape(f32[202,400]{1,0:T(8,128)S(1)} %copy.122) | data formatting | bytes 646400 | tf_op jit(solution)/shard_map/all_to_all | solution.py:179
  6.0 7.3 %all-to-all-start = ((f32[32,1,2525]{2,1,0:T(1,128)}), f32[32,1,2525]{2,1,0:T(1,128)S(1)}, u32[]{:S(2)}, u32[]{:S(2)}) async-start(f32[32,1,2525]{2,1,0:T(1,128)} %all_to_all.28), calls=%async_computation | async-start | bytes 655360 | tf_op jit(solution)/shard_map/all_to_all | solution.py:179
  13.3 1.1 %convolution_bitcast_fusion = f32[2,2,400,400]{3,2,0,1:T(8,128)S(1)} fusion(bf16[2,400,400,1]{1,2,3,0:T(8,128)(2,1)S(1)} %fusion.2, bf16[2,400,400]{1,2,0:T(8,128)(2,1)S(1)} %copy-done.2), kind=kOutput, calls=%fused_computation.2 | convolution fusion | flops 512000000 | bytes 3840000 | tf_op jit(solution)/shard_map/gky,hym->ghkm/dot_general | solution.py:30
  14.7 1.4 %copy-done.1 = f32[2,2,400,400]{3,2,0,1:T(8,128)} copy-done((f32[2,2,400,400]{3,2,0,1:T(8,128)}, f32[2,2,400,400]{3,2,0,1:T(8,128)S(1)}, u32[]{:S(2)}) %copy-start.1) | copy-done | bytes 2560024
  19.5 0.9 %all_to_all.24 = bf16[8,2,12928]{2,1,0:T(2,128)(2,1)} reshape(bf16[16,12928]{1,0:T(8,128)(2,1)S(1)} %convolution_convert_fusion) | data formatting | bytes 827392 | tf_op jit(solution)/shard_map/all_to_all | solution.py:180
  21.9 3.0 %negate_convert_fusion = bf16[1,400,400]{2,1,0:T(8,128)(2,1)S(1)} fusion(f32[]{:T(128)S(6)} %mul.154, s32[400]{0:T(512)S(1)} %fusion.112), kind=kLoop, calls=%fused_computation.62 | loop fusion | flops 960000 | bytes 321604 | tf_op jit(solution)/shard_map/convert_element_type | solution.py:61
  25.4 5.4 %all-to-all-start.2 = ((bf16[8,2,12928]{2,1,0:T(2,128)(2,1)}), bf16[8,2,12928]{2,1,0:T(2,128)(2,1)S(1)}, u32[]{:S(2)}, u32[]{:S(2)}) async-start(bf16[8,2,12928]{2,1,0:T(2,128)(2,1)} %all_to_all.24), calls=%async_computation.2 | async-start | bytes 827392 | tf_op jit(solution)/shard_map/all_to_all | solution.py:180
  31.5 2.5 %fusion.20 = f32[1,1,400,400]{3,2,1,0:T(8,128)} fusion(f32[2,2,400,400]{3,2,0,1:T(8,128)} %copy-done.1), kind=kLoop, calls=%fused_computation.43 | loop fusion | flops 160000 | bytes 1920000 | tf_op jit(solution)/shard_map/sub | solution.py:31
  34.0 2.5 %fusion.75 = f32[1,1,400,400]{3,2,1,0:T(8,128)} fusion(f32[2,2,400,400]{3,2,0,1:T(8,128)} %copy-done.1), kind=kLoop, calls=%fused_computation.122 | loop fusion | flops 320000 | bytes 1920000 | tf_op jit(solution)/shard_map/neg | solution.py:32
  36.6 6.6 %all-to-all-done.2 = bf16[8,2,12928]{2,1,0:T(2,128)(2,1)S(1)} async-done(((bf16[8,2,12928]{2,1,0:T(2,128)(2,1)}), bf16[8,2,12928]{2,1,0:T(2,128)(2,1)S(1)}, u32[]{:S(2)}, u32[]{:S(2)}) %all-to-all-start.2) | async-done | bytes 413728 | tf_op jit(solution)/shard_map/all_to_all | solution.py:180
  43.2 0.9 %broadcast_in_dim.30 = f32[32,1,2525]{2,1,0:T(1,128)} broadcast(f32[2525]{0:T(1024)S(1)} %reduce_sum.46), dimensions={2} | broadcast | bytes 333300 | tf_op jit(solution)/shard_map/broadcast_in_dim | solution.py:83
  44.1 4.0 %all-to-all-start.1 = ((f32[32,1,2525]{2,1,0:T(1,128)}), f32[32,1,2525]{2,1,0:T(1,128)}, u32[]{:S(2)}, u32[]{:S(2)}) async-start(f32[32,1,2525]{2,1,0:T(1,128)} %broadcast_in_dim.30), calls=%async_computation.1 | async-start | bytes 655360 | tf_op jit(solution)/shard_map/all_to_all | solution.py:84
  48.7 0.9 %slice_convert_fusion.1 = f32[16,12800]{1,0:T(8,128)} fusion(bf16[16,12928]{1,0:T(8,128)(2,1)S(1)} %all_to_all.26), kind=kLoop, calls=%fused_computation.89 | loop fusion | flops 204800 | bytes 1228800 | tf_op jit(solution)/shard_map/convert_element_type | solution.py:219
  51.6 2.7 %reshape.478 = f32[16,16,800]{2,1,0:T(8,128)} reshape(f32[16,12800]{1,0:T(8,128)} %slice_convert_fusion.1) | data formatting | bytes 1638400 | tf_op jit(solution)/shard_map/convert_element_type | solution.py:219
  54.3 2.7 %negate_convert_fusion.1 = (bf16[16,16,400]{2,0,1:T(8,128)(2,1)}, f32[16,16,400]{2,0,1:T(8,128)S(1)}) fusion(f32[16]{0:T(128)S(1)} %get-tuple-element.27, s32[400]{0:T(512)S(1)} %fusion.112, s32[16,16]{0,1:T(8,128)S(1)} %fusion.91), kind=kLoop, calls=%fused_computation.80 | loop fusion | flops 819200 | bytes 617088 | tf_op jit(solution)/shard_map/convert_element_type | solution.py:61
  57.0 1.2 %fusion.11 = bf16[16,2,16,400]{3,0,2,1:T(8,128)(2,1)S(1)} fusion(f32[16,2,16,1]{3,0,2,1:T(8,128)} %slice.244, f32[16,2,16,399]{3,0,2,1:T(8,128)S(1)} %slice.243, f32[16,2,16,400]{3,0,2,1:T(8,128)S(1)} %fusion.47, f32[16]{0:T(128)S(1)} %get-tuple-element.7, f32[16]{0:T(128)S(1)} %get-tuple-element.6, f32[16]{0:T(128)S(1)} %get-tuple-element.28), kind=kLoop, calls=%fused_computation.26 | loop fusion | flops 1228800 | bytes 2048192 | tf_op jit(solution)/shard_map/convert_element_type | solution.py:198
  58.3 1.1 %copy.133 = bf16[16,2,16,400]{3,2,1,0:T(8,128)(2,1)} copy(bf16[16,2,16,400]{3,0,2,1:T(8,128)(2,1)S(1)} %fusion.11) | data formatting | bytes 819200 | tf_op jit(solution)/shard_map/convert_element_type | solution.py:198
  59.4 2.1 %fusion.45 = f32[16,16,400]{2,0,1:T(8,128)S(1)} fusion(f32[16,16,399]{2,0,1:T(8,128)S(1)} %bitcast.158, f32[16,16,1]{2,0,1:T(8,128)S(1)} %slice.261, f32[16]{0:T(128)S(1)} %get-tuple-element.6, f32[16]{0:T(128)S(1)} %get-tuple-element.28, f32[16]{0:T(128)S(1)} %get-tuple-element.27, s32[400]{0:T(512)S(1)} %fusion.112, s32[16,16]{0,1:T(8,128)S(1)} %fusion.91), kind=kLoop, calls=%fused_computation.75 | loop fusion | flops 1228800 | bytes 822016 | tf_op jit(solution)/shard_map/add | solution.py:223
  61.5 5.6 %all-to-all-start.3 = ((bf16[16,2,16,400]{3,2,1,0:T(8,128)(2,1)}), bf16[16,2,16,400]{3,2,1,0:T(8,128)(2,1)S(1)}, u32[]{:S(2)}, u32[]{:S(2)}) async-start(bf16[16,2,16,400]{3,2,1,0:T(8,128)(2,1)} %copy.133), calls=%async_computation.3 | async-start | bytes 1048576 | tf_op jit(solution)/shard_map/all_to_all | solution.py:205
  67.1 1.8 %reduce.3 = f32[32,2525]{1,0:T(8,128)S(1)} reduce(f32[32,1,2525]{2,1,0:T(1,128)} %all-to-all-done.1, f32[]{:T(128)} %constant.132), dimensions={1}, to_apply=%all_to_all.23.reduce_sub_computation | reduce | bytes 646404 | tf_op jit(solution)/shard_map/all_to_all | solution.py:84
  69.8 1.0 %fusion.37 = f32[202,400]{0,1:T(8,128)S(1)} fusion(f32[202,400]{1,0:T(8,128)S(1)} %reshape.470, s32[400]{0:T(512)S(1)} %get-tuple-element.25, s32[400]{0:T(512)S(1)} %fusion.119, s32[400]{0:T(512)S(1)} %get-tuple-element.26, pred[400]{0:T(512)(128)(4,1)S(1)} %compare_and_fusion), kind=kOutput, calls=%fused_computation.64 | convolution fusion | flops 388160000 | bytes 651600 | tf_op jit(solution)/shard_map/dot_general | solution.py:90
  72.1 0.8 convolution_divide_fusion
  73.8 0.9 convolution_convert_fusion.1
  75.0 1.6 %collective-permute-start.1 = (bf16[2,32,1200]{2,1,0:T(8,128)(2,1)S(1)}, bf16[2,32,1200]{2,1,0:T(8,128)(2,1)S(1)}, u32[]{:S(2)}, u32[]{:S(2)}) collective-permute-start(bf16[2,32,1200]{2,1,0:T(8,128)(2,1)S(1)} %get-tuple-element.18), channel_id=1, source_target_pairs={{0,16},{8,24},{16,0},{24,8},{1,17},{9,25},{17,1},{25,9},{2,18},{10... | collective-permute-start | bytes 460808 | tf_op jit(solution)/shard_map/ppermute | solution.py:112
  76.6 1.4 %collective-permute-start.2 = (bf16[2,32,1200]{2,1,0:T(8,128)(2,1)S(1)}, bf16[2,32,1200]{2,1,0:T(8,128)(2,1)S(1)}, u32[]{:S(2)}, u32[]{:S(2)}) collective-permute-start(bf16[2,32,1200]{2,1,0:T(8,128)(2,1)S(1)} %get-tuple-element.17), channel_id=1, source_target_pairs={{0,24},{8,0},{16,8},{24,16},{1,25},{9,1},{17,9},{25,17},{2,26},{10... | collective-permute-start | bytes 460808 | tf_op jit(solution)/shard_map/ppermute | solution.py:112
  79.9 0.8 slice_bitcast_fusion.7
  80.9 1.2 %collective-permute-done.1 = bf16[2,32,1200]{2,1,0:T(8,128)(2,1)S(1)} collective-permute-done((bf16[2,32,1200]{2,1,0:T(8,128)(2,1)S(1)}, bf16[2,32,1200]{2,1,0:T(8,128)(2,1)S(1)}, u32[]{:S(2)}, u32[]{:S(2)}) %collective-permute-start.1) | collective-permute-done | bytes 153632 | tf_op jit(solution)/shard_map/ppermute | solution.py:112
  82.1 1.9 %collective-permute-done.2 = bf16[2,32,1200]{2,1,0:T(8,128)(2,1)S(1)} collective-permute-done((bf16[2,32,1200]{2,1,0:T(8,128)(2,1)S(1)}, bf16[2,32,1200]{2,1,0:T(8,128)(2,1)S(1)}, u32[]{:S(2)}, u32[]{:S(2)}) %collective-permute-start.2) | collective-permute-done | bytes 153632 | tf_op jit(solution)/shard_map/ppermute | solution.py:112
  84.2 0.8 slice_divide_fusion
  87.8 1.2 %fusion.17 = bf16[1,400,400]{2,1,0:T(8,128)(2,1)} fusion(f32[2,400,400]{2,1,0:T(8,128)S(1)} %fusion.29, f32[2,400,400]{2,1,0:T(8,128)S(1)} %fusion.21), kind=kLoop, calls=%fused_computation.36 | loop fusion | flops 800000 | bytes 2880000 | tf_op jit(solution)/shard_map/convert_element_type | solution.py:268
  (116 shorter events, 17.1 us)
Async XLA Ops:
  0.6 1.0 %copy-start = (bf16[1,400,400]{2,1,0:T(8,128)(2,1)S(1)}, bf16[1,400,400]{2,1,0:T(8,128)(2,1)}, u32[]{:S(2)}) copy-start(bf16[1,400,400]{2,1,0:T(8,128)(2,1)} %param.9) | copy-start | bytes 960004
  0.6 2.9 %copy-start.2 = (bf16[2,400,400]{1,2,0:T(8,128)(2,1)S(1)}, bf16[2,400,400]{1,2,0:T(8,128)(2,1)}, u32[]{:S(2)}) copy-start(bf16[2,400,400]{1,2,0:T(8,128)(2,1)} %constant.122.clone) | copy-start | bytes 1920004
  6.0 19.4 %all-to-all-start = ((f32[32,1,2525]{2,1,0:T(1,128)}), f32[32,1,2525]{2,1,0:T(1,128)S(1)}, u32[]{:S(2)}, u32[]{:S(2)}) async-start(f32[32,1,2525]{2,1,0:T(1,128)} %all_to_all.28), calls=%async_computation | async-start | bytes 655360 | tf_op jit(solution)/shard_map/all_to_all | solution.py:179
  14.4 1.7 %copy-start.1 = (f32[2,2,400,400]{3,2,0,1:T(8,128)}, f32[2,2,400,400]{3,2,0,1:T(8,128)S(1)}, u32[]{:S(2)}) copy-start(f32[2,2,400,400]{3,2,0,1:T(8,128)S(1)} %convolution_bitcast_fusion) | copy-start | bytes 7680004
  16.2 0.9 copy-start.11
  16.2 1.8 %copy-start.12 = (s32[1,8]{1,0:T(1,128)S(1)}, s32[1,8]{1,0:T(1,128)}, u32[]{:S(2)}) copy-start(s32[1,8]{1,0:T(1,128)} %param.13) | copy-start | bytes 100
  16.2 1.9 %copy-start.13 = (s32[1,8]{1,0:T(1,128)S(1)}, s32[1,8]{1,0:T(1,128)}, u32[]{:S(2)}) copy-start(s32[1,8]{1,0:T(1,128)} %param.14) | copy-start | bytes 100
  16.2 2.0 %copy-start.14 = (s32[1,8]{1,0:T(1,128)S(1)}, s32[1,8]{1,0:T(1,128)}, u32[]{:S(2)}) copy-start(s32[1,8]{1,0:T(1,128)} %param.15) | copy-start | bytes 100
  16.2 2.1 %copy-start.15 = (f32[64]{0:T(128)S(1)}, f32[64]{0:T(128)}, u32[]{:S(2)}) copy-start(f32[64]{0:T(128)} %param.11) | copy-start | bytes 772
  16.4 4.0 %copy-start.9 = (bf16[2,128,800]{1,2,0:T(8,128)(2,1)S(1)}, bf16[2,128,800]{1,2,0:T(8,128)(2,1)}, u32[]{:S(2)}) copy-start(bf16[2,128,800]{1,2,0:T(8,128)(2,1)} %param.16) | copy-start | bytes 1228804
  25.4 17.8 %all-to-all-start.2 = ((bf16[8,2,12928]{2,1,0:T(2,128)(2,1)}), bf16[8,2,12928]{2,1,0:T(2,128)(2,1)S(1)}, u32[]{:S(2)}, u32[]{:S(2)}) async-start(bf16[8,2,12928]{2,1,0:T(2,128)(2,1)} %all_to_all.24), calls=%async_computation.2 | async-start | bytes 827392 | tf_op jit(solution)/shard_map/all_to_all | solution.py:180
  44.1 17.3 %all-to-all-start.1 = ((f32[32,1,2525]{2,1,0:T(1,128)}), f32[32,1,2525]{2,1,0:T(1,128)}, u32[]{:S(2)}, u32[]{:S(2)}) async-start(f32[32,1,2525]{2,1,0:T(1,128)} %broadcast_in_dim.30), calls=%async_computation.1 | async-start | bytes 655360 | tf_op jit(solution)/shard_map/all_to_all | solution.py:84
  61.5 23.5 %all-to-all-start.3 = ((bf16[16,2,16,400]{3,2,1,0:T(8,128)(2,1)}), bf16[16,2,16,400]{3,2,1,0:T(8,128)(2,1)S(1)}, u32[]{:S(2)}, u32[]{:S(2)}) async-start(bf16[16,2,16,400]{3,2,1,0:T(8,128)(2,1)} %copy.133), calls=%async_computation.3 | async-start | bytes 1048576 | tf_op jit(solution)/shard_map/all_to_all | solution.py:205
  70.9 1.2 %copy-start.8 = (f32[16,16,800]{2,1,0:T(8,128)S(1)}, f32[16,16,800]{2,1,0:T(8,128)}, u32[]{:S(2)}) copy-start(f32[16,16,800]{2,1,0:T(8,128)} %reshape.478) | copy-start | bytes 2457604
  70.9 1.2 %copy-start.10 = (bf16[16,16,400]{2,0,1:T(8,128)(2,1)S(1)}, bf16[16,16,400]{2,0,1:T(8,128)(2,1)}, u32[]{:S(2)}) copy-start(bf16[16,16,400]{2,0,1:T(8,128)(2,1)} %get-tuple-element.23) | copy-start | bytes 614404
  74.7 3.3 %copy-start.3 = (f32[1,1,400,400]{3,2,1,0:T(8,128)S(1)}, f32[1,1,400,400]{3,2,1,0:T(8,128)}, u32[]{:S(2)}) copy-start(f32[1,1,400,400]{3,2,1,0:T(8,128)} %fusion.20) | copy-start | bytes 1920004
  74.7 3.3 %copy-start.4 = (f32[1,1,400,400]{3,2,1,0:T(8,128)S(1)}, f32[1,1,400,400]{3,2,1,0:T(8,128)}, u32[]{:S(2)}) copy-start(f32[1,1,400,400]{3,2,1,0:T(8,128)} %fusion.75) | copy-start | bytes 1920004
  74.9 5.9 %collective-permute-start = (bf16[2,32,1200]{2,1,0:T(8,128)(2,1)S(1)}, bf16[2,32,1200]{2,1,0:T(8,128)(2,1)S(1)}, u32[]{:S(2)}, u32[]{:S(2)}) collective-permute-start(bf16[2,32,1200]{2,1,0:T(8,128)(2,1)S(1)} %get-tuple-element.16), channel_id=1, source_target_pairs={{0,8},{8,16},{16,24},{24,0},{1,9},{9,17},{17,25},{25,1},{2,10},{10... | collective-permute-start | bytes 460808 | tf_op jit(solution)/shard_map/ppermute | solution.py:112
  75.0 7.1 %collective-permute-start.1 = (bf16[2,32,1200]{2,1,0:T(8,128)(2,1)S(1)}, bf16[2,32,1200]{2,1,0:T(8,128)(2,1)S(1)}, u32[]{:S(2)}, u32[]{:S(2)}) collective-permute-start(bf16[2,32,1200]{2,1,0:T(8,128)(2,1)S(1)} %get-tuple-element.18), channel_id=1, source_target_pairs={{0,16},{8,24},{16,0},{24,8},{1,17},{9,25},{17,1},{25,9},{2,18},{10... | collective-permute-start | bytes 460808 | tf_op jit(solution)/shard_map/ppermute | solution.py:112
  76.6 7.5 %collective-permute-start.2 = (bf16[2,32,1200]{2,1,0:T(8,128)(2,1)S(1)}, bf16[2,32,1200]{2,1,0:T(8,128)(2,1)S(1)}, u32[]{:S(2)}, u32[]{:S(2)}) collective-permute-start(bf16[2,32,1200]{2,1,0:T(8,128)(2,1)S(1)} %get-tuple-element.17), channel_id=1, source_target_pairs={{0,24},{8,0},{16,8},{24,16},{1,25},{9,1},{17,9},{25,17},{2,26},{10... | collective-permute-start | bytes 460808 | tf_op jit(solution)/shard_map/ppermute | solution.py:112
  85.0 1.0 %copy-start.5 = (f32[128,400]{1,0:T(8,128)S(1)}, f32[128,400]{1,0:T(8,128)}, u32[]{:S(2)}) copy-start(f32[128,400]{1,0:T(8,128)} %maximum_convert_fusion.1) | copy-start | bytes 614404
  85.0 1.0 %copy-start.6 = (f32[2,64,400]{2,1,0:T(8,128)S(1)}, f32[2,64,400]{2,1,0:T(8,128)}, u32[]{:S(2)}) copy-start(f32[2,64,400]{2,1,0:T(8,128)} %get-tuple-element.10) | copy-start | bytes 614404
  85.0 1.1 %copy-start.7 = (f32[2,64,400]{2,1,0:T(8,128)S(1)}, f32[2,64,400]{2,1,0:T(8,128)}, u32[]{:S(2)}) copy-start(f32[2,64,400]{2,1,0:T(8,128)} %get-tuple-element.11) | copy-start | bytes 614404

commit v14 on v13

--- a/solution.py
+++ b/solution.py
@@ -80,7 +80,7 @@
 
 
 def power_gather(total, device_count, rows, box_size):
-    spread = jnp.broadcast_to(total, (device_count, total.shape[1]))
+    spread = jnp.broadcast_to(total, (device_count,) + total.shape[1:])
     back = lax.all_to_all(spread, ("img", "slab"), 0, 0, tiled=True)
     half = back.reshape(rows, box_size)
     zero = lax.optimization_barrier(jnp.zeros((), jnp.int32))
@@ -114,10 +114,14 @@
 
 
 def half_rows(box_size, device_count):
-    rows = box_size // 2 + 1
+    need = box_size // 2 + 1
+    per = -(-(-(-need // device_count)) // 8) * 8
+    if per * device_count <= box_size:
+        return per * device_count, per
+    rows = need
     while (rows * box_size) % device_count:
         rows += 1
-    return rows
+    return rows, 0
 
 
 def body(images, micrograph, defocus, target_slab, target_plane, target_rows, shift_index, volume):
@@ -171,11 +175,14 @@
     send = jnp.einsum(
         "rs,rx->sx", seat_pick, payload, preferred_element_type=jnp.float32
     ).astype(jnp.bfloat16)
-    rows_half = half_rows(box_size, device_count)
+    rows_half, rows_each = half_rows(box_size, device_count)
     top_rows = -(-rows_half // RB) * RB
     low_half = jnp.stack([transform(r, tables[:, :top_rows]) for r in rowwise])[:, :, :rows_half]
     power_half = jnp.sum(low_half * low_half, axis=(0, 1))
-    pieces = power_half.reshape(device_count, rows_half * box_size // device_count)
+    if rows_each:
+        pieces = power_half.reshape(device_count, rows_each, box_size)
+    else:
+        pieces = power_half.reshape(device_count, rows_half * box_size // device_count)
     gathered = lax.all_to_all(pieces, ("img", "slab"), 0, 0, tiled=True)
     got = lax.all_to_all(send, "slab", 0, 0, tiled=True)
     got_blocks = got[:, : RB * 2 * box_size].reshape(seat_count, RB, 2 * box_size)

time: 90 us -> 115 us (1.28)
  waiting for transfers between devices: 10.3 us -> 31.9 us
  local copies, waits for them, and re-layouts: 15.9 us -> 20.4 us
  starting transfers between devices: 25.2 us -> 22.6 us
  matrix products: 11.7 us -> 12.9 us
    all_to_all x1, waiting for transfers between devices: 0.01 us -> 12.1 us  [body(): returned_rows = lax.all_to_all(projected, 'slab', 0, 0, tiled=True)]
    all_to_all x1, waiting for transfers between devices: 0.44 us -> 11.6 us  [body(): gathered = lax.all_to_all(pieces, ('img', 'slab'), 0, 0, tiled=True)]
    all_to_all x1, waiting for transfers between devices: 0.01 us -> 8.21 us  [power_gather(): back = lax.all_to_all(spread, ('img', 'slab'), 0, 0, tiled=True)]
    all_to_all x1, waiting for transfers between devices: 6.59 us -> 0.01 us  [body(): got = lax.all_to_all(send, 'slab', 0, 0, tiled=True)]
    ppermute x3, waiting for transfers between devices: 3.27 us -> 0.01 us  [reduce_over_img(): total = total + lax.ppermute(piece, 'img', pairs).astype(jnp.float32)]
    unnamed x33 -> x49, local copies, waits for them, and re-layouts: 3.32 us -> 5.83 us
    all_to_all x1, starting transfers between devices: 5.59 us -> 3.49 us  [body(): returned_rows = lax.all_to_all(projected, 'slab', 0, 0, tiled=True)]
    all_to_all x1, starting transfers between devices: 5.39 us -> 7.25 us  [body(): got = lax.all_to_all(send, 'slab', 0, 0, tiled=True)]
  transfers between devices with their start and end apart: 7 -> 7, of which waited for: 5 -> 3; matrix products, arithmetic and copies ran while one was open for 43% -> 30% of each run, Pallas kernels for 0% -> 0%
where the time goes in v14:
time: 115 us; the launch traced here: 114 us
  waiting for transfers between devices  31.9 us (28%)
  other arithmetic  24.1 us (21%)
  starting transfers between devices  22.6 us (20%)
  local copies, waits for them, and re-layouts  20.4 us (18%)
  matrix products  12.9 us (11%)
  between operations  2.57 us (2%)
    all_to_all x1, waiting for transfers between devices, body(): returned_rows = lax.all_to_all(projected, 'slab', 0, 0, tiled=True)  12.1 us
    all_to_all x1, waiting for transfers between devices, body(): gathered = lax.all_to_all(pieces, ('img', 'slab'), 0, 0, tiled=True)  11.6 us
    all_to_all x1, waiting for transfers between devices, power_gather(): back = lax.all_to_all(spread, ('img', 'slab'), 0, 0, tiled=True)  8.21 us
    all_to_all x1, starting transfers between devices, body(): got = lax.all_to_all(send, 'slab', 0, 0, tiled=True)  7.25 us
    all_to_all x1, starting transfers between devices, body(): gathered = lax.all_to_all(pieces, ('img', 'slab'), 0, 0, tiled=True)  6.04 us
    unnamed x49, local copies, waits for them, and re-layouts  5.83 us
    convert_element_type x2, other arithmetic, contrast_curve(): (-jnp.sin(defocus_of[:, None, None] * radius + 0.1)).astype(jnp.bfloat16)  4.94 us
    all_to_all x1, starting transfers between devices, power_gather(): back = lax.all_to_all(spread, ('img', 'slab'), 0, 0, tiled=True)  3.8 us
  transfers between devices with their start and end apart: 7, of which 3 were waited for; matrix products, arithmetic and copies ran while one was open for 30% of the time, Pallas kernels for 0%

profile of v14, /device:TPU:0, one launch (start us, length us, event | category | flops | bytes accessed | tf_op | source)
XLA Modules:
  0.0 114.5 jit_solution(13419197167266288202)
XLA Ops:
  0.7 1.0 copy-done
  1.6 1.9 %fusion.2 = bf16[2,400,400,1]{1,2,3,0:T(8,128)(2,1)S(1)} fusion(bf16[2,400,400]{1,2,0:T(8,128)(2,1)} %constant.122.clone, bf16[1,400,400]{2,1,0:T(8,128)(2,1)S(1)} %copy-done), kind=kOutput, calls=%fused_computation.12 | convolution fusion | flops 256320000 | bytes 1600000 | tf_op jit(solution)/shard_map/yx,hmx->hym/dot_general | solution.py:24
  3.6 1.1 convolution_bitcast_fusion
  5.0 1.3 %copy-done.1 = f32[2,2,400,400]{3,2,0,1:T(8,128)} copy-done((f32[2,2,400,400]{3,2,0,1:T(8,128)}, f32[2,2,400,400]{3,2,0,1:T(8,128)S(1)}, u32[]{:S(2)}) %copy-start.1) | copy-done | bytes 2560024
  9.0 0.9 all_to_all.19
  9.9 7.3 %all-to-all-start.2 = ((bf16[8,2,12928]{2,1,0:T(2,128)(2,1)}), bf16[8,2,12928]{2,1,0:T(2,128)(2,1)S(1)}, u32[]{:S(2)}, u32[]{:S(2)}) async-start(bf16[8,2,12928]{2,1,0:T(2,128)(2,1)} %all_to_all.19), calls=%async_computation.2 | async-start | bytes 827392 | tf_op jit(solution)/shard_map/all_to_all | solution.py:187
  17.2 1.7 %convolution_bitcast_fusion.2 = f32[2,2,256,400]{2,3,0,1:T(8,128)S(1)} fusion(bf16[2,400,400,1]{1,2,3,0:T(8,128)(2,1)} %copy-done.3, bf16[2,400,400]{1,2,0:T(8,128)(2,1)S(1)} %copy-done.2), kind=kOutput, calls=%fused_computation.6 | convolution fusion | flops 327680000 | bytes 2688000 | tf_op jit(solution)/shard_map/gky,hym->ghkm/dot_general | solution.py:30
  19.7 1.0 copy.137
  22.8 3.0 %negate_convert_fusion = bf16[1,400,400]{2,1,0:T(8,128)(2,1)S(1)} fusion(f32[]{:T(128)S(6)} %mul.162, s32[400]{0:T(512)S(1)} %fusion.111), kind=kLoop, calls=%fused_computation.61 | loop fusion | flops 960000 | bytes 321604 | tf_op jit(solution)/shard_map/convert_element_type | solution.py:61
  27.2 1.5 %fusion.19 = f32[1,1,400,400]{3,2,1,0:T(8,128)S(1)} fusion(f32[2,2,400,400]{3,2,0,1:T(8,128)} %copy-done.1), kind=kLoop, calls=%fused_computation.41 | loop fusion | flops 160000 | bytes 1920000 | tf_op jit(solution)/shard_map/sub | solution.py:31
  28.7 2.5 %fusion.74 = f32[1,1,400,400]{3,2,1,0:T(8,128)} fusion(f32[2,2,400,400]{3,2,0,1:T(8,128)} %copy-done.1), kind=kLoop, calls=%fused_computation.119 | loop fusion | flops 320000 | bytes 1920000 | tf_op jit(solution)/shard_map/neg | solution.py:32
  31.2 6.0 %all-to-all-start = ((f32[32,8,400]{2,1,0:T(8,128)}), f32[32,8,400]{2,1,0:T(8,128)S(1)}, u32[]{:S(2)}, u32[]{:S(2)}) async-start(f32[32,8,400]{2,1,0:T(8,128)} %bitcast.11), calls=%async_computation | async-start | bytes 1048576 | tf_op jit(solution)/shard_map/all_to_all | solution.py:186
  37.3 0.9 all_to_all.21
  40.9 1.1 copy.147
  42.0 11.6 %all-to-all-done = f32[32,8,400]{2,1,0:T(8,128)S(1)} async-done(((f32[32,8,400]{2,1,0:T(8,128)}), f32[32,8,400]{2,1,0:T(8,128)S(1)}, u32[]{:S(2)}, u32[]{:S(2)}) %all-to-all-start) | async-done | bytes 409632 | tf_op jit(solution)/shard_map/all_to_all | solution.py:186
  54.4 3.5 %all-to-all-start.3 = ((bf16[16,2,16,400]{3,2,1,0:T(8,128)(2,1)}), bf16[16,2,16,400]{3,2,1,0:T(8,128)(2,1)S(1)}, u32[]{:S(2)}, u32[]{:S(2)}) async-start(bf16[16,2,16,400]{3,2,1,0:T(8,128)(2,1)} %copy.147), calls=%async_computation.3 | async-start | bytes 1048576 | tf_op jit(solution)/shard_map/all_to_all | solution.py:212
  57.9 1.1 slice_convert_fusion.1
  59.0 1.1 reduce_sum.46
  60.1 12.1 %all-to-all-done.3 = bf16[16,2,16,400]{3,2,1,0:T(8,128)(2,1)S(1)} async-done(((bf16[16,2,16,400]{3,2,1,0:T(8,128)(2,1)}), bf16[16,2,16,400]{3,2,1,0:T(8,128)(2,1)S(1)}, u32[]{:S(2)}, u32[]{:S(2)}) %all-to-all-start.3) | async-done | bytes 409632 | tf_op jit(solution)/shard_map/all_to_all | solution.py:212
  72.2 1.0 broadcast_in_dim.30
  73.2 3.8 %all-to-all-start.1 = ((f32[32,8,400]{2,1,0:T(8,128)}), f32[32,8,400]{2,1,0:T(8,128)S(1)}, u32[]{:S(2)}, u32[]{:S(2)}) async-start(f32[32,8,400]{2,1,0:T(8,128)} %broadcast_in_dim.30), calls=%async_computation.1 | async-start | bytes 1048576 | tf_op jit(solution)/shard_map/all_to_all | solution.py:84
  77.0 1.5 %reshape.471 = f32[16,16,800]{2,1,0:T(8,128)} reshape(f32[16,12800]{1,0:T(8,128)S(1)} %slice_convert_fusion.1) | data formatting | bytes 1638400 | tf_op jit(solution)/shard_map/convert_element_type | solution.py:226
  78.5 1.9 %negate_convert_fusion.1 = (bf16[16,16,400]{2,0,1:T(8,128)(2,1)S(1)}, f32[16,16,400]{2,0,1:T(8,128)S(1)}) fusion(f32[16]{0:T(128)S(1)} %get-tuple-element.33, s32[400]{0:T(512)S(1)} %fusion.111, s32[16,16]{0,1:T(8,128)S(1)} %fusion.90), kind=kLoop, calls=%fused_computation.82 | loop fusion | flops 819200 | bytes 617088 | tf_op jit(solution)/shard_map/convert_element_type | solution.py:61
  80.5 2.9 %fusion.45 = f32[16,16,400]{2,0,1:T(8,128)} fusion(f32[16,16,399]{2,0,1:T(8,128)S(1)} %bitcast.146, f32[16,16,1]{2,0,1:T(8,128)S(1)} %slice.256, f32[16]{0:T(128)S(1)} %get-tuple-element.6, f32[16]{0:T(128)S(1)} %get-tuple-element.34, f32[16]{0:T(128)S(1)} %get-tuple-element.33, s32[400]{0:T(512)S(1)} %fusion.111, s32[16,16]{0,1:T(8,128)S(1)} %fusion.90), kind=kLoop, calls=%fused_computation.74 | loop fusion | flops 1228800 | bytes 822016 | tf_op jit(solution)/shard_map/add | solution.py:230
  83.8 1.1 copy.149
  84.9 8.2 %all-to-all-done.1 = f32[32,8,400]{2,1,0:T(8,128)S(1)} async-done(((f32[32,8,400]{2,1,0:T(8,128)}), f32[32,8,400]{2,1,0:T(8,128)S(1)}, u32[]{:S(2)}, u32[]{:S(2)}) %all-to-all-start.1) | async-done | bytes 409632 | tf_op jit(solution)/shard_map/all_to_all | solution.py:84
  93.7 1.0 fusion.37
  102.8 1.1 collective-permute-start.2
  105.4 1.7 %copy.152 = bf16[2,64,400]{2,1,0:T(8,128)(2,1)} copy(bf16[2,64,400]{1,2,0:T(8,128)(2,1)} %get-tuple-element.23) | data formatting | bytes 204800 | tf_op jit(solution)/shard_map/slice | solution.py:272
  107.1 1.7 %copy.153 = bf16[2,64,400]{2,1,0:T(8,128)(2,1)} copy(bf16[2,64,400]{1,2,0:T(8,128)(2,1)} %get-tuple-element.24) | data formatting | bytes 204800 | tf_op jit(solution)/shard_map/slice | solution.py:272
  111.1 1.1 %fusion.17 = bf16[1,400,400]{2,1,0:T(8,128)(2,1)} fusion(f32[2,400,400]{2,1,0:T(8,128)S(1)} %fusion.29, f32[2,400,400]{2,1,0:T(8,128)S(1)} %fusion.21), kind=kLoop, calls=%fused_computation.36 | loop fusion | flops 800000 | bytes 2880000 | tf_op jit(solution)/shard_map/convert_element_type | solution.py:275
  112.3 1.2 %fusion.67 = f32[2,32,1200]{2,1,0:T(8,128)S(1)} fusion(bf16[2,32,1200]{2,1,0:T(8,128)(2,1)} %collective-permute-done.2, bf16[2,32,1200]{2,1,0:T(8,128)(2,1)} %collective-permute-done.1, bf16[2,32,1200]{2,1,0:T(8,128)(2,1)} %collective-permute-done, bf16[2,4,32,1200]{3,2,1,0:T(8,128)(2,1)} %bitcast.148, s32[]{:T(128)S(6)} %select_n.93), kind=kLoop, calls=%fused_computation.108 | loop fusion | flops 537600 | bytes 921604 | tf_op jit(solution)/shard_map/add | solution.py:112
  (125 shorter events, 22.9 us)
Async XLA Ops:
  0.6 1.0 copy-start
  0.6 2.9 %copy-start.2 = (bf16[2,400,400]{1,2,0:T(8,128)(2,1)S(1)}, bf16[2,400,400]{1,2,0:T(8,128)(2,1)}, u32[]{:S(2)}) copy-start(bf16[2,400,400]{1,2,0:T(8,128)(2,1)} %constant.122.clone) | copy-start | bytes 1920004
  3.6 1.1 copy-start.3
  4.7 1.7 %copy-start.1 = (f32[2,2,400,400]{3,2,0,1:T(8,128)}, f32[2,2,400,400]{3,2,0,1:T(8,128)S(1)}, u32[]{:S(2)}) copy-start(f32[2,2,400,400]{3,2,0,1:T(8,128)S(1)} %convolution_bitcast_fusion) | copy-start | bytes 7680004
  6.4 0.8 copy-start.16
  6.4 1.8 %copy-start.19 = (s32[1,8]{1,0:T(1,128)S(1)}, s32[1,8]{1,0:T(1,128)}, u32[]{:S(2)}) copy-start(s32[1,8]{1,0:T(1,128)} %param.13) | copy-start | bytes 100
  6.4 1.9 %copy-start.20 = (s32[1,8]{1,0:T(1,128)S(1)}, s32[1,8]{1,0:T(1,128)}, u32[]{:S(2)}) copy-start(s32[1,8]{1,0:T(1,128)} %param.14) | copy-start | bytes 100
  6.4 2.0 %copy-start.21 = (s32[1,8]{1,0:T(1,128)S(1)}, s32[1,8]{1,0:T(1,128)}, u32[]{:S(2)}) copy-start(s32[1,8]{1,0:T(1,128)} %param.15) | copy-start | bytes 100
  9.9 21.3 %all-to-all-start.2 = ((bf16[8,2,12928]{2,1,0:T(2,128)(2,1)}), bf16[8,2,12928]{2,1,0:T(2,128)(2,1)S(1)}, u32[]{:S(2)}, u32[]{:S(2)}) async-start(bf16[8,2,12928]{2,1,0:T(2,128)(2,1)} %all_to_all.19), calls=%async_computation.2 | async-start | bytes 827392 | tf_op jit(solution)/shard_map/all_to_all | solution.py:187
  19.6 1.1 copy-start.13
  19.7 1.8 %copy-start.22 = (f32[64]{0:T(128)S(1)}, f32[64]{0:T(128)}, u32[]{:S(2)}) copy-start(f32[64]{0:T(128)} %param.11) | copy-start | bytes 772
  31.2 22.4 %all-to-all-start = ((f32[32,8,400]{2,1,0:T(8,128)}), f32[32,8,400]{2,1,0:T(8,128)S(1)}, u32[]{:S(2)}, u32[]{:S(2)}) async-start(f32[32,8,400]{2,1,0:T(8,128)} %bitcast.11), calls=%async_computation | async-start | bytes 1048576 | tf_op jit(solution)/shard_map/all_to_all | solution.py:186
  39.8 0.7 copy-start.23
  53.6 0.8 copy-start.7
  54.4 17.7 %all-to-all-start.3 = ((bf16[16,2,16,400]{3,2,1,0:T(8,128)(2,1)}), bf16[16,2,16,400]{3,2,1,0:T(8,128)(2,1)S(1)}, u32[]{:S(2)}, u32[]{:S(2)}) async-start(bf16[16,2,16,400]{3,2,1,0:T(8,128)(2,1)} %copy.147), calls=%async_computation.3 | async-start | bytes 1048576 | tf_op jit(solution)/shard_map/all_to_all | solution.py:212
  72.2 1.0 copy-start.8
  73.2 20.0 %all-to-all-start.1 = ((f32[32,8,400]{2,1,0:T(8,128)}), f32[32,8,400]{2,1,0:T(8,128)S(1)}, u32[]{:S(2)}, u32[]{:S(2)}) async-start(f32[32,8,400]{2,1,0:T(8,128)} %broadcast_in_dim.30), calls=%async_computation.1 | async-start | bytes 1048576 | tf_op jit(solution)/shard_map/all_to_all | solution.py:84
  78.5 4.9 %copy-start.9 = (bf16[16,2,16,400]{3,2,1,0:T(8,128)(2,1)S(1)}, bf16[16,2,16,400]{3,2,1,0:T(8,128)(2,1)}, u32[]{:S(2)}) copy-start(bf16[16,2,16,400]{3,2,1,0:T(8,128)(2,1)} %copy-done.8) | copy-start | bytes 1228804
  83.4 10.3 %copy-start.17 = (pred[400]{0:T(512)(128)(4,1)S(1)}, pred[400]{0:T(512)(128)(4,1)}, u32[]{:S(2)}) copy-start(pred[400]{0:T(512)(128)(4,1)} %compare_and_fusion) | copy-start | bytes 1204
  83.8 10.9 %copy-start.18 = (pred[400]{0:T(512)(128)(4,1)S(1)}, pred[400]{0:T(512)(128)(4,1)}, u32[]{:S(2)}) copy-start(pred[400]{0:T(512)(128)(4,1)} %get-tuple-element.29) | copy-start | bytes 1204
  94.8 1.2 %copy-start.12 = (f32[16,16,800]{2,1,0:T(8,128)S(1)}, f32[16,16,800]{2,1,0:T(8,128)}, u32[]{:S(2)}) copy-start(f32[16,16,800]{2,1,0:T(8,128)} %reshape.471) | copy-start | bytes 2457604
  96.8 1.1 %copy-start.4 = (f32[1,1,400,400]{3,2,1,0:T(8,128)S(1)}, f32[1,1,400,400]{3,2,1,0:T(8,128)}, u32[]{:S(2)}) copy-start(f32[1,1,400,400]{3,2,1,0:T(8,128)} %fusion.74) | copy-start | bytes 1920004
  99.0 1.0 copy-start.6
  100.9 3.0 %copy-start.10 = (f32[1,2,8,16,400]{4,3,2,1,0:T(8,128)S(1)}, f32[1,2,8,16,400]{4,3,2,1,0:T(8,128)}, u32[]{:S(2)}) copy-start(f32[1,2,8,16,400]{4,3,2,1,0:T(8,128)} %copy.149) | copy-start | bytes 1228804
  100.9 3.0 %copy-start.11 = (f32[128,400]{1,0:T(8,128)S(1)}, f32[128,400]{1,0:T(8,128)}, u32[]{:S(2)}) copy-start(f32[128,400]{1,0:T(8,128)} %maximum_convert_fusion.1) | copy-start | bytes 614404
  101.2 2.8 %copy-start.5 = (bf16[16,16,1200]{2,1,0:T(8,128)(2,1)}, bf16[16,16,1200]{2,1,0:T(8,128)(2,1)S(1)}, u32[]{:S(2)}) copy-start(bf16[16,16,1200]{2,1,0:T(8,128)(2,1)S(1)} %copy.157) | copy-start | bytes 1843204
  102.0 10.3 %collective-permute-start = (bf16[2,32,1200]{2,1,0:T(8,128)(2,1)}, bf16[2,32,1200]{2,1,0:T(8,128)(2,1)}, u32[]{:S(2)}, u32[]{:S(2)}) collective-permute-start(bf16[2,32,1200]{2,1,0:T(8,128)(2,1)} %get-tuple-element.18), channel_id=1, source_target_pairs={{0,8},{8,16},{16,24},{24,0},{1,9},{9,17},{17,25},{25,1},{2,10},{10... | collective-permute-start | bytes 460808 | tf_op jit(solution)/shard_map/ppermute | solution.py:112
  102.0 10.3 %collective-permute-start.1 = (bf16[2,32,1200]{2,1,0:T(8,128)(2,1)}, bf16[2,32,1200]{2,1,0:T(8,128)(2,1)}, u32[]{:S(2)}, u32[]{:S(2)}) collective-permute-start(bf16[2,32,1200]{2,1,0:T(8,128)(2,1)} %get-tuple-element.20), channel_id=1, source_target_pairs={{0,16},{8,24},{16,0},{24,8},{1,17},{9,25},{17,1},{25,9},{2,18},{10... | collective-permute-start | bytes 460808 | tf_op jit(solution)/shard_map/ppermute | solution.py:112
  102.8 9.5 %collective-permute-start.2 = (bf16[2,32,1200]{2,1,0:T(8,128)(2,1)}, bf16[2,32,1200]{2,1,0:T(8,128)(2,1)}, u32[]{:S(2)}, u32[]{:S(2)}) collective-permute-start(bf16[2,32,1200]{2,1,0:T(8,128)(2,1)} %get-tuple-element.19), channel_id=1, source_target_pairs={{0,24},{8,0},{16,8},{24,16},{1,25},{9,1},{17,9},{25,17},{2,26},{10... | collective-permute-start | bytes 460808 | tf_op jit(solution)/shard_map/ppermute | solution.py:112
  108.8 0.9 copy-start.14
  108.8 1.0 copy-start.15

commit v15 on v13

--- a/solution.py
+++ b/solution.py
@@ -202,7 +202,9 @@
     noise_level = jnp.sqrt(power / (particles * device_count) + 1e-06)
     level_both = jnp.concatenate([noise_level, noise_level], axis=1)
 
-    returned_rows = lax.all_to_all(projected, "slab", 0, 0, tiled=True)
+    returned_rows = lax.all_to_all(
+        projected.reshape(seat_count, 2 * RB * box_size), "slab", 0, 0, tiled=True
+    ).reshape(projected.shape)
 
     got_rows = low_row_ids(got_info[:, 4], box_size)
     got_contrast = contrast_curve(lookup_defocus(got_info[:, 5], defocus), got_rows, box_size)

time: 90 us -> 94.1 us (1.046)
  local copies, waits for them, and re-layouts: 15.9 us -> 20 us
    reshape x0 -> x1, local copies, waits for them, and re-layouts: none -> 2.24 us  [body(): returned_rows = lax.all_to_all(projected.reshape(seat_count, 2 * RB * box...]
    all_to_all x0 -> x1, local copies, waits for them, and re-layouts: none -> 1.74 us  [body(): lax.all_to_all(projected.reshape(seat_count, 2 * RB * box_size), 'slab',...]
    unnamed x33 -> x37, local copies, waits for them, and re-layouts: 3.32 us -> 4.11 us
  transfers between devices with their start and end apart: 7 -> 7, of which waited for: 5 -> 5; matrix products, arithmetic and copies ran while one was open for 43% -> 40% of each run, Pallas kernels for 0% -> 0%
where the time goes in v15:
time: 94.1 us; the launch traced here: 93 us
  starting transfers between devices  25.3 us (27%)
  other arithmetic  23.2 us (25%)
  local copies, waits for them, and re-layouts  20 us (21%)
  matrix products  11.7 us (12%)
  waiting for transfers between devices  10.3 us (11%)
  between operations  2.6 us (3%)
    all_to_all x1, starting transfers between devices, body(): gathered = lax.all_to_all(pieces, ('img', 'slab'), 0, 0, tiled=True)  7.3 us
    all_to_all x1, waiting for transfers between devices, body(): got = lax.all_to_all(send, 'slab', 0, 0, tiled=True)  6.59 us
    convert_element_type x2, other arithmetic, contrast_curve(): (-jnp.sin(defocus_of[:, None, None] * radius + 0.1)).astype(jnp.bfloat16)  5.68 us
    all_to_all x1, starting transfers between devices, body(): lax.all_to_all(projected.reshape(seat_count, 2 * RB * box_size), 'slab',...  5.59 us
    all_to_all x1, starting transfers between devices, body(): got = lax.all_to_all(send, 'slab', 0, 0, tiled=True)  5.4 us
    unnamed x37, local copies, waits for them, and re-layouts  4.11 us
    all_to_all x1, starting transfers between devices, power_gather(): back = lax.all_to_all(spread, ('img', 'slab'), 0, 0, tiled=True)  3.95 us
    ppermute x3, waiting for transfers between devices, reduce_over_img(): total = total + lax.ppermute(piece, 'img', pairs).astype(jnp.float32)  3.25 us
  transfers between devices with their start and end apart: 7, of which 5 were waited for; matrix products, arithmetic and copies ran while one was open for 40% of the time, Pallas kernels for 0%

profile of v15, /device:TPU:0, one launch (start us, length us, event | category | flops | bytes accessed | tf_op | source)
XLA Modules:
  0.0 93.0 jit_solution(12094231202809856047)
XLA Ops:
  0.7 1.0 %copy-done = bf16[1,400,400]{2,1,0:T(8,128)(2,1)S(1)} copy-done((bf16[1,400,400]{2,1,0:T(8,128)(2,1)S(1)}, bf16[1,400,400]{2,1,0:T(8,128)(2,1)}, u32[]{:S(2)}) %copy-start) | copy-done | bytes 320024
  1.6 1.9 %fusion.2 = bf16[2,400,400,1]{1,2,3,0:T(8,128)(2,1)S(1)} fusion(bf16[2,400,400]{1,2,0:T(8,128)(2,1)} %constant.122.clone, bf16[1,400,400]{2,1,0:T(8,128)(2,1)S(1)} %copy-done), kind=kOutput, calls=%fused_computation.12 | convolution fusion | flops 256320000 | bytes 1600000 | tf_op jit(solution)/shard_map/yx,hmx->hym/dot_general | solution.py:24
  4.6 1.4 %all_to_all.32 = f32[32,1,2525]{2,1,0:T(1,128)} reshape(f32[202,400]{1,0:T(8,128)S(1)} %copy.126) | data formatting | bytes 646400 | tf_op jit(solution)/shard_map/all_to_all | solution.py:179
  6.0 7.3 %all-to-all-start = ((f32[32,1,2525]{2,1,0:T(1,128)}), f32[32,1,2525]{2,1,0:T(1,128)S(1)}, u32[]{:S(2)}, u32[]{:S(2)}) async-start(f32[32,1,2525]{2,1,0:T(1,128)} %all_to_all.32), calls=%async_computation | async-start | bytes 655360 | tf_op jit(solution)/shard_map/all_to_all | solution.py:179
  13.3 1.1 %convolution_bitcast_fusion = f32[2,2,400,400]{3,2,0,1:T(8,128)S(1)} fusion(bf16[2,400,400,1]{1,2,3,0:T(8,128)(2,1)S(1)} %fusion.2, bf16[2,400,400]{1,2,0:T(8,128)(2,1)S(1)} %copy-done.2), kind=kOutput, calls=%fused_computation.2 | convolution fusion | flops 512000000 | bytes 3840000 | tf_op jit(solution)/shard_map/gky,hym->ghkm/dot_general | solution.py:30
  14.7 1.4 %copy-done.1 = f32[2,2,400,400]{3,2,0,1:T(8,128)} copy-done((f32[2,2,400,400]{3,2,0,1:T(8,128)}, f32[2,2,400,400]{3,2,0,1:T(8,128)S(1)}, u32[]{:S(2)}) %copy-start.1) | copy-done | bytes 2560024
  19.5 0.9 all_to_all.27
  21.9 3.0 %negate_convert_fusion = bf16[1,400,400]{2,1,0:T(8,128)(2,1)S(1)} fusion(f32[]{:T(128)S(6)} %mul.154, s32[400]{0:T(512)S(1)} %fusion.112), kind=kLoop, calls=%fused_computation.62 | loop fusion | flops 960000 | bytes 321604 | tf_op jit(solution)/shard_map/convert_element_type | solution.py:61
  25.4 5.4 %all-to-all-start.2 = ((bf16[8,2,12928]{2,1,0:T(2,128)(2,1)}), bf16[8,2,12928]{2,1,0:T(2,128)(2,1)S(1)}, u32[]{:S(2)}, u32[]{:S(2)}) async-start(bf16[8,2,12928]{2,1,0:T(2,128)(2,1)} %all_to_all.27), calls=%async_computation.2 | async-start | bytes 827392 | tf_op jit(solution)/shard_map/all_to_all | solution.py:180
  31.5 2.5 %fusion.20 = f32[1,1,400,400]{3,2,1,0:T(8,128)} fusion(f32[2,2,400,400]{3,2,0,1:T(8,128)} %copy-done.1), kind=kLoop, calls=%fused_computation.43 | loop fusion | flops 160000 | bytes 1920000 | tf_op jit(solution)/shard_map/sub | solution.py:31
  34.0 2.4 %fusion.75 = f32[1,1,400,400]{3,2,1,0:T(8,128)} fusion(f32[2,2,400,400]{3,2,0,1:T(8,128)} %copy-done.1), kind=kLoop, calls=%fused_computation.122 | loop fusion | flops 320000 | bytes 1920000 | tf_op jit(solution)/shard_map/neg | solution.py:32
  36.6 6.6 %all-to-all-done.2 = bf16[8,2,12928]{2,1,0:T(2,128)(2,1)S(1)} async-done(((bf16[8,2,12928]{2,1,0:T(2,128)(2,1)}), bf16[8,2,12928]{2,1,0:T(2,128)(2,1)S(1)}, u32[]{:S(2)}, u32[]{:S(2)}) %all-to-all-start.2) | async-done | bytes 413728 | tf_op jit(solution)/shard_map/all_to_all | solution.py:180
  43.2 0.9 broadcast_in_dim.30
  44.1 4.0 %all-to-all-start.1 = ((f32[32,1,2525]{2,1,0:T(1,128)}), f32[32,1,2525]{2,1,0:T(1,128)}, u32[]{:S(2)}, u32[]{:S(2)}) async-start(f32[32,1,2525]{2,1,0:T(1,128)} %broadcast_in_dim.30), calls=%async_computation.1 | async-start | bytes 655360 | tf_op jit(solution)/shard_map/all_to_all | solution.py:84
  48.7 1.0 %slice_convert_fusion.1 = f32[16,12800]{1,0:T(8,128)} fusion(bf16[16,12928]{1,0:T(8,128)(2,1)S(1)} %all_to_all.29), kind=kLoop, calls=%fused_computation.89 | loop fusion | flops 204800 | bytes 1228800 | tf_op jit(solution)/shard_map/convert_element_type | solution.py:221
  51.6 2.7 %reshape.487 = f32[16,16,800]{2,1,0:T(8,128)} reshape(f32[16,12800]{1,0:T(8,128)} %slice_convert_fusion.1) | data formatting | bytes 1638400 | tf_op jit(solution)/shard_map/convert_element_type | solution.py:221
  54.3 2.7 %negate_convert_fusion.1 = (bf16[16,16,400]{2,0,1:T(8,128)(2,1)}, f32[16,16,400]{2,0,1:T(8,128)S(1)}) fusion(f32[16]{0:T(128)S(1)} %get-tuple-element.27, s32[400]{0:T(512)S(1)} %fusion.112, s32[16,16]{0,1:T(8,128)S(1)} %fusion.91), kind=kLoop, calls=%fused_computation.80 | loop fusion | flops 819200 | bytes 617088 | tf_op jit(solution)/shard_map/convert_element_type | solution.py:61
  57.9 1.2 %fusion.11 = bf16[16,2,16,400]{3,0,2,1:T(8,128)(2,1)S(1)} fusion(f32[16,2,16,1]{3,0,2,1:T(8,128)} %slice.244, f32[16,2,16,399]{3,0,2,1:T(8,128)S(1)} %slice.243, f32[16,2,16,400]{3,0,2,1:T(8,128)S(1)} %fusion.47, f32[16]{0:T(128)S(1)} %get-tuple-element.7, f32[16]{0:T(128)S(1)} %get-tuple-element.6, f32[16]{0:T(128)S(1)} %get-tuple-element.28), kind=kLoop, calls=%fused_computation.26 | loop fusion | flops 1228800 | bytes 2048192 | tf_op jit(solution)/shard_map/convert_element_type | solution.py:198
  59.4 1.7 %all_to_all.30 = bf16[8,2,12800]{2,1,0:T(2,128)(2,1)} reshape(bf16[16,2,16,400]{3,2,1,0:T(8,128)(2,1)S(1)} %copy.137) | data formatting | bytes 819200 | tf_op jit(solution)/shard_map/all_to_all | solution.py:205
  61.2 2.1 %fusion.45 = f32[16,16,400]{2,0,1:T(8,128)S(1)} fusion(f32[16,16,399]{2,0,1:T(8,128)S(1)} %bitcast.160, f32[16,16,1]{2,0,1:T(8,128)S(1)} %slice.261, f32[16]{0:T(128)S(1)} %get-tuple-element.6, f32[16]{0:T(128)S(1)} %get-tuple-element.28, f32[16]{0:T(128)S(1)} %get-tuple-element.27, s32[400]{0:T(512)S(1)} %fusion.112, s32[16,16]{0,1:T(8,128)S(1)} %fusion.91), kind=kLoop, calls=%fused_computation.75 | loop fusion | flops 1228800 | bytes 822016 | tf_op jit(solution)/shard_map/add | solution.py:225
  63.3 5.6 %all-to-all-start.3 = ((bf16[8,2,12800]{2,1,0:T(2,128)(2,1)}), bf16[8,2,12800]{2,1,0:T(2,128)(2,1)}, u32[]{:S(2)}, u32[]{:S(2)}) async-start(bf16[8,2,12800]{2,1,0:T(2,128)(2,1)} %all_to_all.30), calls=%async_computation.3 | async-start | bytes 819200 | tf_op jit(solution)/shard_map/all_to_all | solution.py:205
  68.9 1.8 %reduce.3 = f32[32,2525]{1,0:T(8,128)S(1)} reduce(f32[32,1,2525]{2,1,0:T(1,128)} %all-to-all-done.1, f32[]{:T(128)} %constant.132), dimensions={1}, to_apply=%all_to_all.26.reduce_sub_computation | reduce | bytes 646404 | tf_op jit(solution)/shard_map/all_to_all | solution.py:84
  71.6 1.0 %fusion.37 = f32[202,400]{0,1:T(8,128)S(1)} fusion(f32[202,400]{1,0:T(8,128)S(1)} %reshape.478, s32[400]{0:T(512)S(1)} %get-tuple-element.25, s32[400]{0:T(512)S(1)} %fusion.119, s32[400]{0:T(512)S(1)} %get-tuple-element.26, pred[400]{0:T(512)(128)(4,1)S(1)} %compare_and_fusion), kind=kOutput, calls=%fused_computation.64 | convolution fusion | flops 388160000 | bytes 651600 | tf_op jit(solution)/shard_map/dot_general | solution.py:90
  73.9 0.8 convolution_divide_fusion
  75.6 0.9 convolution_convert_fusion.1
  76.8 1.6 %collective-permute-start.1 = (bf16[2,32,1200]{2,1,0:T(8,128)(2,1)S(1)}, bf16[2,32,1200]{2,1,0:T(8,128)(2,1)S(1)}, u32[]{:S(2)}, u32[]{:S(2)}) collective-permute-start(bf16[2,32,1200]{2,1,0:T(8,128)(2,1)S(1)} %get-tuple-element.18), channel_id=1, source_target_pairs={{0,16},{8,24},{16,0},{24,8},{1,17},{9,25},{17,1},{25,9},{2,18},{10... | collective-permute-start | bytes 460808 | tf_op jit(solution)/shard_map/ppermute | solution.py:112
  78.4 1.4 %collective-permute-start.2 = (bf16[2,32,1200]{2,1,0:T(8,128)(2,1)S(1)}, bf16[2,32,1200]{2,1,0:T(8,128)(2,1)S(1)}, u32[]{:S(2)}, u32[]{:S(2)}) collective-permute-start(bf16[2,32,1200]{2,1,0:T(8,128)(2,1)S(1)} %get-tuple-element.17), channel_id=1, source_target_pairs={{0,24},{8,0},{16,8},{24,16},{1,25},{9,1},{17,9},{25,17},{2,26},{10... | collective-permute-start | bytes 460808 | tf_op jit(solution)/shard_map/ppermute | solution.py:112
  81.7 0.8 slice_bitcast_fusion.7
  82.7 1.2 %collective-permute-done.1 = bf16[2,32,1200]{2,1,0:T(8,128)(2,1)S(1)} collective-permute-done((bf16[2,32,1200]{2,1,0:T(8,128)(2,1)S(1)}, bf16[2,32,1200]{2,1,0:T(8,128)(2,1)S(1)}, u32[]{:S(2)}, u32[]{:S(2)}) %collective-permute-start.1) | collective-permute-done | bytes 153632 | tf_op jit(solution)/shard_map/ppermute | solution.py:112
  83.9 1.9 %collective-permute-done.2 = bf16[2,32,1200]{2,1,0:T(8,128)(2,1)S(1)} collective-permute-done((bf16[2,32,1200]{2,1,0:T(8,128)(2,1)S(1)}, bf16[2,32,1200]{2,1,0:T(8,128)(2,1)S(1)}, u32[]{:S(2)}, u32[]{:S(2)}) %collective-permute-start.2) | collective-permute-done | bytes 153632 | tf_op jit(solution)/shard_map/ppermute | solution.py:112
  86.8 2.2 %reshape.483 = bf16[16,2,16,400]{3,2,1,0:T(8,128)(2,1)S(1)} reshape(bf16[8,2,12800]{2,1,0:T(2,128)(2,1)} %all-to-all-done.3) | data formatting | bytes 819200 | tf_op jit(solution)/shard_map/reshape | solution.py:207
  91.9 1.2 %fusion.17 = bf16[1,400,400]{2,1,0:T(8,128)(2,1)} fusion(f32[2,400,400]{2,1,0:T(8,128)S(1)} %fusion.29, f32[2,400,400]{2,1,0:T(8,128)S(1)} %fusion.21), kind=kLoop, calls=%fused_computation.36 | loop fusion | flops 800000 | bytes 2880000 | tf_op jit(solution)/shard_map/convert_element_type | solution.py:270
  (122 shorter events, 19.0 us)
Async XLA Ops:
  0.6 1.0 %copy-start = (bf16[1,400,400]{2,1,0:T(8,128)(2,1)S(1)}, bf16[1,400,400]{2,1,0:T(8,128)(2,1)}, u32[]{:S(2)}) copy-start(bf16[1,400,400]{2,1,0:T(8,128)(2,1)} %param.9) | copy-start | bytes 960004
  0.6 2.9 %copy-start.2 = (bf16[2,400,400]{1,2,0:T(8,128)(2,1)S(1)}, bf16[2,400,400]{1,2,0:T(8,128)(2,1)}, u32[]{:S(2)}) copy-start(bf16[2,400,400]{1,2,0:T(8,128)(2,1)} %constant.122.clone) | copy-start | bytes 1920004
  6.0 19.4 %all-to-all-start = ((f32[32,1,2525]{2,1,0:T(1,128)}), f32[32,1,2525]{2,1,0:T(1,128)S(1)}, u32[]{:S(2)}, u32[]{:S(2)}) async-start(f32[32,1,2525]{2,1,0:T(1,128)} %all_to_all.32), calls=%async_computation | async-start | bytes 655360 | tf_op jit(solution)/shard_map/all_to_all | solution.py:179
  14.4 1.7 %copy-start.1 = (f32[2,2,400,400]{3,2,0,1:T(8,128)}, f32[2,2,400,400]{3,2,0,1:T(8,128)S(1)}, u32[]{:S(2)}) copy-start(f32[2,2,400,400]{3,2,0,1:T(8,128)S(1)} %convolution_bitcast_fusion) | copy-start | bytes 7680004
  16.2 0.9 copy-start.13
  16.2 1.8 %copy-start.14 = (s32[1,8]{1,0:T(1,128)S(1)}, s32[1,8]{1,0:T(1,128)}, u32[]{:S(2)}) copy-start(s32[1,8]{1,0:T(1,128)} %param.13) | copy-start | bytes 100
  16.2 1.9 %copy-start.15 = (s32[1,8]{1,0:T(1,128)S(1)}, s32[1,8]{1,0:T(1,128)}, u32[]{:S(2)}) copy-start(s32[1,8]{1,0:T(1,128)} %param.14) | copy-start | bytes 100
  16.2 2.0 %copy-start.16 = (s32[1,8]{1,0:T(1,128)S(1)}, s32[1,8]{1,0:T(1,128)}, u32[]{:S(2)}) copy-start(s32[1,8]{1,0:T(1,128)} %param.15) | copy-start | bytes 100
  16.2 2.1 %copy-start.17 = (f32[64]{0:T(128)S(1)}, f32[64]{0:T(128)}, u32[]{:S(2)}) copy-start(f32[64]{0:T(128)} %param.11) | copy-start | bytes 772
  16.4 4.1 %copy-start.11 = (bf16[2,128,800]{1,2,0:T(8,128)(2,1)S(1)}, bf16[2,128,800]{1,2,0:T(8,128)(2,1)}, u32[]{:S(2)}) copy-start(bf16[2,128,800]{1,2,0:T(8,128)(2,1)} %param.16) | copy-start | bytes 1228804
  25.4 17.8 %all-to-all-start.2 = ((bf16[8,2,12928]{2,1,0:T(2,128)(2,1)}), bf16[8,2,12928]{2,1,0:T(2,128)(2,1)S(1)}, u32[]{:S(2)}, u32[]{:S(2)}) async-start(bf16[8,2,12928]{2,1,0:T(2,128)(2,1)} %all_to_all.27), calls=%async_computation.2 | async-start | bytes 827392 | tf_op jit(solution)/shard_map/all_to_all | solution.py:180
  44.1 19.1 %all-to-all-start.1 = ((f32[32,1,2525]{2,1,0:T(1,128)}), f32[32,1,2525]{2,1,0:T(1,128)}, u32[]{:S(2)}, u32[]{:S(2)}) async-start(f32[32,1,2525]{2,1,0:T(1,128)} %broadcast_in_dim.30), calls=%async_computation.1 | async-start | bytes 655360 | tf_op jit(solution)/shard_map/all_to_all | solution.py:84
  57.0 0.8 copy-start.5
  59.1 2.1 %copy-start.6 = (f32[16,16,400]{2,0,1:T(8,128)S(1)}, f32[16,16,400]{2,0,1:T(8,128)}, u32[]{:S(2)}) copy-start(f32[16,16,400]{2,0,1:T(8,128)} %copy-done.5) | copy-start | bytes 1228804
  63.3 23.5 %all-to-all-start.3 = ((bf16[8,2,12800]{2,1,0:T(2,128)(2,1)}), bf16[8,2,12800]{2,1,0:T(2,128)(2,1)}, u32[]{:S(2)}, u32[]{:S(2)}) async-start(bf16[8,2,12800]{2,1,0:T(2,128)(2,1)} %all_to_all.30), calls=%async_computation.3 | async-start | bytes 819200 | tf_op jit(solution)/shard_map/all_to_all | solution.py:205
  72.7 1.2 %copy-start.10 = (f32[16,16,800]{2,1,0:T(8,128)S(1)}, f32[16,16,800]{2,1,0:T(8,128)}, u32[]{:S(2)}) copy-start(f32[16,16,800]{2,1,0:T(8,128)} %reshape.487) | copy-start | bytes 2457604
  72.7 1.2 %copy-start.12 = (bf16[16,16,400]{2,0,1:T(8,128)(2,1)S(1)}, bf16[16,16,400]{2,0,1:T(8,128)(2,1)}, u32[]{:S(2)}) copy-start(bf16[16,16,400]{2,0,1:T(8,128)(2,1)} %get-tuple-element.23) | copy-start | bytes 614404
  76.5 3.3 %copy-start.3 = (f32[1,1,400,400]{3,2,1,0:T(8,128)S(1)}, f32[1,1,400,400]{3,2,1,0:T(8,128)}, u32[]{:S(2)}) copy-start(f32[1,1,400,400]{3,2,1,0:T(8,128)} %fusion.20) | copy-start | bytes 1920004
  76.5 3.3 %copy-start.4 = (f32[1,1,400,400]{3,2,1,0:T(8,128)S(1)}, f32[1,1,400,400]{3,2,1,0:T(8,128)}, u32[]{:S(2)}) copy-start(f32[1,1,400,400]{3,2,1,0:T(8,128)} %fusion.75) | copy-start | bytes 1920004
  76.7 5.9 %collective-permute-start = (bf16[2,32,1200]{2,1,0:T(8,128)(2,1)S(1)}, bf16[2,32,1200]{2,1,0:T(8,128)(2,1)S(1)}, u32[]{:S(2)}, u32[]{:S(2)}) collective-permute-start(bf16[2,32,1200]{2,1,0:T(8,128)(2,1)S(1)} %get-tuple-element.16), channel_id=1, source_target_pairs={{0,8},{8,16},{16,24},{24,0},{1,9},{9,17},{17,25},{25,1},{2,10},{10... | collective-permute-start | bytes 460808 | tf_op jit(solution)/shard_map/ppermute | solution.py:112
  76.8 7.1 %collective-permute-start.1 = (bf16[2,32,1200]{2,1,0:T(8,128)(2,1)S(1)}, bf16[2,32,1200]{2,1,0:T(8,128)(2,1)S(1)}, u32[]{:S(2)}, u32[]{:S(2)}) collective-permute-start(bf16[2,32,1200]{2,1,0:T(8,128)(2,1)S(1)} %get-tuple-element.18), channel_id=1, source_target_pairs={{0,16},{8,24},{16,0},{24,8},{1,17},{9,25},{17,1},{25,9},{2,18},{10... | collective-permute-start | bytes 460808 | tf_op jit(solution)/shard_map/ppermute | solution.py:112
  78.4 7.5 %collective-permute-start.2 = (bf16[2,32,1200]{2,1,0:T(8,128)(2,1)S(1)}, bf16[2,32,1200]{2,1,0:T(8,128)(2,1)S(1)}, u32[]{:S(2)}, u32[]{:S(2)}) collective-permute-start(bf16[2,32,1200]{2,1,0:T(8,128)(2,1)S(1)} %get-tuple-element.17), channel_id=1, source_target_pairs={{0,24},{8,0},{16,8},{24,16},{1,25},{9,1},{17,9},{25,17},{2,26},{10... | collective-permute-start | bytes 460808 | tf_op jit(solution)/shard_map/ppermute | solution.py:112
  89.0 1.0 %copy-start.7 = (f32[128,400]{1,0:T(8,128)S(1)}, f32[128,400]{1,0:T(8,128)}, u32[]{:S(2)}) copy-start(f32[128,400]{1,0:T(8,128)} %maximum_convert_fusion.1) | copy-start | bytes 614404
  89.1 1.0 %copy-start.8 = (f32[2,64,400]{2,1,0:T(8,128)S(1)}, f32[2,64,400]{2,1,0:T(8,128)}, u32[]{:S(2)}) copy-start(f32[2,64,400]{2,1,0:T(8,128)} %get-tuple-element.10) | copy-start | bytes 614404
  89.1 1.1 %copy-start.9 = (f32[2,64,400]{2,1,0:T(8,128)S(1)}, f32[2,64,400]{2,1,0:T(8,128)}, u32[]{:S(2)}) copy-start(f32[2,64,400]{2,1,0:T(8,128)} %get-tuple-element.11) | copy-start | bytes 614404

commit v16 on v13

--- a/solution.py
+++ b/solution.py
@@ -245,6 +245,9 @@
     own_rows = jnp.moveaxis(own_rows, 2, 1).reshape(particles, 2, 2 * low_rows, box_size)
     inner = box_size - 2 * low_rows
     inner_rows = whitened[:, :, low_rows : box_size - low_rows].astype(jnp.bfloat16)
+    routed_tables = jnp.concatenate(
+        [tables[:, :, :low_rows], tables[:, :, box_size - low_rows :]], axis=2
+    )
     residual = []
     for n in range(particles):
         inner_back = back_rows_of(inner_rows[n], tables)
@@ -260,11 +263,7 @@
             routed_white - routed_contrast[None] * own_rows[n].astype(jnp.float32)
         ).astype(jnp.bfloat16)
         routed_back = back_rows_of(routed_difference, tables)
-        middle = jnp.zeros((2, inner, box_size), jnp.bfloat16)
-        routed_part = picture_of(
-            jnp.concatenate([routed_back[:, :low_rows], middle, routed_back[:, low_rows:]], axis=1),
-            tables,
-        )
+        routed_part = picture_of(routed_back, routed_tables)
         residual.append(((inner_part + routed_part) / box_size).astype(jnp.bfloat16))
     residual = jnp.stack(residual)
     return (residual, reconstruction)

time: 90 us -> 91.8 us (1.020)
  other arithmetic: 23.2 us -> 24.2 us
    unnamed x33 -> x37, local copies, waits for them, and re-layouts: 3.32 us -> 3.33 us
  transfers between devices with their start and end apart: 7 -> 7, of which waited for: 5 -> 4; matrix products, arithmetic and copies ran while one was open for 43% -> 45% of each run, Pallas kernels for 0% -> 0%
where the time goes in v16:
time: 91.8 us; the launch traced here: 90.7 us
  starting transfers between devices  25.7 us (28%)
  other arithmetic  24.2 us (26%)
  local copies, waits for them, and re-layouts  16.3 us (18%)
  matrix products  12.2 us (13%)
  waiting for transfers between devices  9.93 us (11%)
  between operations  2.47 us (3%)
    all_to_all x1, starting transfers between devices, body(): gathered = lax.all_to_all(pieces, ('img', 'slab'), 0, 0, tiled=True)  7.3 us
    all_to_all x1, waiting for transfers between devices, body(): got = lax.all_to_all(send, 'slab', 0, 0, tiled=True)  6.66 us
    all_to_all x1, starting transfers between devices, body(): got = lax.all_to_all(send, 'slab', 0, 0, tiled=True)  5.82 us
    convert_element_type x2, other arithmetic, contrast_curve(): (-jnp.sin(defocus_of[:, None, None] * radius + 0.1)).astype(jnp.bfloat16)  5.7 us
    all_to_all x1, starting transfers between devices, body(): returned_rows = lax.all_to_all(projected, 'slab', 0, 0, tiled=True)  5.59 us
    all_to_all x1, starting transfers between devices, power_gather(): back = lax.all_to_all(spread, ('img', 'slab'), 0, 0, tiled=True)  3.95 us
    unnamed x37, local copies, waits for them, and re-layouts  3.33 us
    ppermute x3, waiting for transfers between devices, reduce_over_img(): total = total + lax.ppermute(piece, 'img', pairs).astype(jnp.float32)  3.27 us
  transfers between devices with their start and end apart: 7, of which 4 were waited for; matrix products, arithmetic and copies ran while one was open for 45% of the time, Pallas kernels for 0%

profile of v16, /device:TPU:0, one launch (start us, length us, event | category | flops | bytes accessed | tf_op | source)
XLA Modules:
  0.0 90.7 jit_solution(17067119422927583312)
XLA Ops:
  0.7 1.0 %copy-done = bf16[1,400,400]{2,1,0:T(8,128)(2,1)S(1)} copy-done((bf16[1,400,400]{2,1,0:T(8,128)(2,1)S(1)}, bf16[1,400,400]{2,1,0:T(8,128)(2,1)}, u32[]{:S(2)}) %copy-start) | copy-done | bytes 320024
  1.6 1.9 %fusion.2 = bf16[2,400,400,1]{1,2,3,0:T(8,128)(2,1)S(1)} fusion(bf16[2,400,400]{1,2,0:T(8,128)(2,1)} %constant.121.clone, bf16[1,400,400]{2,1,0:T(8,128)(2,1)S(1)} %copy-done), kind=kOutput, calls=%fused_computation.12 | convolution fusion | flops 256320000 | bytes 1600000 | tf_op jit(solution)/shard_map/yx,hmx->hym/dot_general | solution.py:24
  4.6 1.4 %all_to_all.28 = f32[32,1,2525]{2,1,0:T(1,128)} reshape(f32[202,400]{1,0:T(8,128)S(1)} %copy.114) | data formatting | bytes 646400 | tf_op jit(solution)/shard_map/all_to_all | solution.py:179
  6.0 7.3 %all-to-all-start = ((f32[32,1,2525]{2,1,0:T(1,128)}), f32[32,1,2525]{2,1,0:T(1,128)S(1)}, u32[]{:S(2)}, u32[]{:S(2)}) async-start(f32[32,1,2525]{2,1,0:T(1,128)} %all_to_all.28), calls=%async_computation | async-start | bytes 655360 | tf_op jit(solution)/shard_map/all_to_all | solution.py:179
  13.3 1.1 %convolution_bitcast_fusion = f32[2,2,400,400]{3,2,0,1:T(8,128)S(1)} fusion(bf16[2,400,400,1]{1,2,3,0:T(8,128)(2,1)S(1)} %fusion.2, bf16[2,400,400]{1,2,0:T(8,128)(2,1)S(1)} %copy-done.2), kind=kOutput, calls=%fused_computation.2 | convolution fusion | flops 512000000 | bytes 3840000 | tf_op jit(solution)/shard_map/gky,hym->ghkm/dot_general | solution.py:30
  14.7 1.3 %copy-done.1 = f32[2,2,400,400]{3,2,0,1:T(8,128)} copy-done((f32[2,2,400,400]{3,2,0,1:T(8,128)}, f32[2,2,400,400]{3,2,0,1:T(8,128)S(1)}, u32[]{:S(2)}) %copy-start.1) | copy-done | bytes 2560024
  20.5 0.9 all_to_all.24
  22.7 3.0 %negate_convert_fusion = bf16[1,400,400]{2,1,0:T(8,128)(2,1)S(1)} fusion(f32[]{:T(128)S(6)} %mul.154, s32[400]{0:T(512)S(1)} %fusion.113), kind=kLoop, calls=%fused_computation.57 | loop fusion | flops 960000 | bytes 321604 | tf_op jit(solution)/shard_map/convert_element_type | solution.py:61
  26.5 5.8 %all-to-all-start.2 = ((bf16[8,2,12928]{2,1,0:T(2,128)(2,1)}), bf16[8,2,12928]{2,1,0:T(2,128)(2,1)S(1)}, u32[]{:S(2)}, u32[]{:S(2)}) async-start(bf16[8,2,12928]{2,1,0:T(2,128)(2,1)} %all_to_all.24), calls=%async_computation.2 | async-start | bytes 827392 | tf_op jit(solution)/shard_map/all_to_all | solution.py:180
  33.0 2.4 %fusion.20 = f32[1,1,400,400]{3,2,1,0:T(8,128)} fusion(f32[2,2,400,400]{3,2,0,1:T(8,128)} %copy-done.1), kind=kLoop, calls=%fused_computation.43 | loop fusion | flops 160000 | bytes 1920000 | tf_op jit(solution)/shard_map/sub | solution.py:31
  35.5 2.5 %fusion.73 = f32[1,1,400,400]{3,2,1,0:T(8,128)} fusion(f32[2,2,400,400]{3,2,0,1:T(8,128)} %copy-done.1), kind=kLoop, calls=%fused_computation.120 | loop fusion | flops 320000 | bytes 1920000 | tf_op jit(solution)/shard_map/neg | solution.py:32
  38.1 6.7 %all-to-all-done.2 = bf16[8,2,12928]{2,1,0:T(2,128)(2,1)S(1)} async-done(((bf16[8,2,12928]{2,1,0:T(2,128)(2,1)}), bf16[8,2,12928]{2,1,0:T(2,128)(2,1)S(1)}, u32[]{:S(2)}, u32[]{:S(2)}) %all-to-all-start.2) | async-done | bytes 413728 | tf_op jit(solution)/shard_map/all_to_all | solution.py:180
  44.8 0.9 broadcast_in_dim.24
  45.7 4.0 %all-to-all-start.1 = ((f32[32,1,2525]{2,1,0:T(1,128)}), f32[32,1,2525]{2,1,0:T(1,128)}, u32[]{:S(2)}, u32[]{:S(2)}) async-start(f32[32,1,2525]{2,1,0:T(1,128)} %broadcast_in_dim.24), calls=%async_computation.1 | async-start | bytes 655360 | tf_op jit(solution)/shard_map/all_to_all | solution.py:84
  50.2 1.0 %slice_convert_fusion.1 = f32[16,12800]{1,0:T(8,128)} fusion(bf16[16,12928]{1,0:T(8,128)(2,1)S(1)} %all_to_all.26), kind=kLoop, calls=%fused_computation.84 | loop fusion | flops 204800 | bytes 1228800 | tf_op jit(solution)/shard_map/convert_element_type | solution.py:219
  53.2 2.7 %reshape.478 = f32[16,16,800]{2,1,0:T(8,128)} reshape(f32[16,12800]{1,0:T(8,128)} %slice_convert_fusion.1) | data formatting | bytes 1638400 | tf_op jit(solution)/shard_map/convert_element_type | solution.py:219
  55.9 2.7 %negate_convert_fusion.1 = (bf16[16,16,400]{2,0,1:T(8,128)(2,1)}, f32[16,16,400]{2,0,1:T(8,128)S(1)}) fusion(f32[16]{0:T(128)S(1)} %get-tuple-element.27, s32[400]{0:T(512)S(1)} %fusion.113, s32[16,16]{0,1:T(8,128)S(1)} %fusion.92), kind=kLoop, calls=%fused_computation.75 | loop fusion | flops 819200 | bytes 617088 | tf_op jit(solution)/shard_map/convert_element_type | solution.py:61
  58.7 1.2 %fusion.11 = bf16[16,2,16,400]{3,0,2,1:T(8,128)(2,1)S(1)} fusion(f32[16,2,16,1]{3,0,2,1:T(8,128)} %slice.246, f32[16,2,16,399]{3,0,2,1:T(8,128)S(1)} %slice.245, f32[16,2,16,400]{3,0,2,1:T(8,128)S(1)} %fusion.42, f32[16]{0:T(128)S(1)} %get-tuple-element.7, f32[16]{0:T(128)S(1)} %get-tuple-element.6, f32[16]{0:T(128)S(1)} %get-tuple-element.28), kind=kLoop, calls=%fused_computation.26 | loop fusion | flops 1228800 | bytes 2048192 | tf_op jit(solution)/shard_map/convert_element_type | solution.py:198
  59.9 1.1 %copy.125 = bf16[16,2,16,400]{3,2,1,0:T(8,128)(2,1)} copy(bf16[16,2,16,400]{3,0,2,1:T(8,128)(2,1)S(1)} %fusion.11) | data formatting | bytes 819200 | tf_op jit(solution)/shard_map/convert_element_type | solution.py:198
  61.0 2.1 %fusion.40 = f32[16,16,400]{2,0,1:T(8,128)S(1)} fusion(f32[16,16,399]{2,0,1:T(8,128)S(1)} %bitcast.157, f32[16,16,1]{2,0,1:T(8,128)S(1)} %slice.261, f32[16]{0:T(128)S(1)} %get-tuple-element.6, f32[16]{0:T(128)S(1)} %get-tuple-element.28, f32[16]{0:T(128)S(1)} %get-tuple-element.27, s32[400]{0:T(512)S(1)} %fusion.113, s32[16,16]{0,1:T(8,128)S(1)} %fusion.92), kind=kLoop, calls=%fused_computation.70 | loop fusion | flops 1228800 | bytes 822016 | tf_op jit(solution)/shard_map/add | solution.py:223
  63.1 5.6 %all-to-all-start.3 = ((bf16[16,2,16,400]{3,2,1,0:T(8,128)(2,1)}), bf16[16,2,16,400]{3,2,1,0:T(8,128)(2,1)S(1)}, u32[]{:S(2)}, u32[]{:S(2)}) async-start(bf16[16,2,16,400]{3,2,1,0:T(8,128)(2,1)} %copy.125), calls=%async_computation.3 | async-start | bytes 1048576 | tf_op jit(solution)/shard_map/all_to_all | solution.py:205
  68.7 1.8 %reduce.3 = f32[32,2525]{1,0:T(8,128)S(1)} reduce(f32[32,1,2525]{2,1,0:T(1,128)} %all-to-all-done.1, f32[]{:T(128)} %constant.131), dimensions={1}, to_apply=%all_to_all.23.reduce_sub_computation | reduce | bytes 646404 | tf_op jit(solution)/shard_map/all_to_all | solution.py:84
  71.5 1.0 %fusion.32 = f32[202,400]{0,1:T(8,128)S(1)} fusion(f32[202,400]{1,0:T(8,128)S(1)} %reshape.470, s32[400]{0:T(512)S(1)} %get-tuple-element.25, s32[400]{0:T(512)S(1)} %fusion.120, s32[400]{0:T(512)S(1)} %get-tuple-element.26, pred[400]{0:T(512)(128)(4,1)S(1)} %copy-done.17), kind=kOutput, calls=%fused_computation.59 | convolution fusion | flops 388160000 | bytes 651600 | tf_op jit(solution)/shard_map/dot_general | solution.py:90
  72.5 1.5 %fusion.5 = f32[400,400]{1,0:T(8,128)S(1)} fusion(f32[400,400]{1,0:T(8,128)S(1)} %fusion.56, f32[202,400]{0,1:T(8,128)S(1)} %fusion.32, s32[400]{0:T(512)S(1)} %fusion.118, pred[400]{0:T(512)(128)(4,1)} %fusion.117), kind=kOutput, calls=%fused_computation.17 | convolution fusion | flops 388481600 | bytes 1605200 | tf_op jit(solution)/shard_map/dot_general | solution.py:95
  74.2 0.8 convolution_divide_fusion
  75.9 0.9 convolution_convert_fusion.1
  77.1 1.6 %collective-permute-start.1 = (bf16[2,32,1200]{2,1,0:T(8,128)(2,1)S(1)}, bf16[2,32,1200]{2,1,0:T(8,128)(2,1)S(1)}, u32[]{:S(2)}, u32[]{:S(2)}) collective-permute-start(bf16[2,32,1200]{2,1,0:T(8,128)(2,1)S(1)} %get-tuple-element.20), channel_id=1, source_target_pairs={{0,16},{8,24},{16,0},{24,8},{1,17},{9,25},{17,1},{25,9},{2,18},{10... | collective-permute-start | bytes 460808 | tf_op jit(solution)/shard_map/ppermute | solution.py:112
  78.7 1.4 %collective-permute-start.2 = (bf16[2,32,1200]{2,1,0:T(8,128)(2,1)S(1)}, bf16[2,32,1200]{2,1,0:T(8,128)(2,1)S(1)}, u32[]{:S(2)}, u32[]{:S(2)}) collective-permute-start(bf16[2,32,1200]{2,1,0:T(8,128)(2,1)S(1)} %get-tuple-element.19), channel_id=1, source_target_pairs={{0,24},{8,0},{16,8},{24,16},{1,25},{9,1},{17,9},{25,17},{2,26},{10... | collective-permute-start | bytes 460808 | tf_op jit(solution)/shard_map/ppermute | solution.py:112
  82.1 0.8 slice_bitcast_fusion.7
  83.0 1.2 %collective-permute-done.1 = bf16[2,32,1200]{2,1,0:T(8,128)(2,1)S(1)} collective-permute-done((bf16[2,32,1200]{2,1,0:T(8,128)(2,1)S(1)}, bf16[2,32,1200]{2,1,0:T(8,128)(2,1)S(1)}, u32[]{:S(2)}, u32[]{:S(2)}) %collective-permute-start.1) | collective-permute-done | bytes 153632 | tf_op jit(solution)/shard_map/ppermute | solution.py:112
  84.2 1.9 %collective-permute-done.2 = bf16[2,32,1200]{2,1,0:T(8,128)(2,1)S(1)} collective-permute-done((bf16[2,32,1200]{2,1,0:T(8,128)(2,1)S(1)}, bf16[2,32,1200]{2,1,0:T(8,128)(2,1)S(1)}, u32[]{:S(2)}, u32[]{:S(2)}) %collective-permute-start.2) | collective-permute-done | bytes 153632 | tf_op jit(solution)/shard_map/ppermute | solution.py:112
  89.6 1.2 %fusion.17 = bf16[1,400,400]{2,1,0:T(8,128)(2,1)} fusion(f32[2,400,400]{2,1,0:T(8,128)S(1)} %fusion.67, f32[2,400,400]{2,1,0:T(8,128)S(1)} %fusion.21), kind=kLoop, calls=%fused_computation.36 | loop fusion | flops 800000 | bytes 2880000 | tf_op jit(solution)/shard_map/convert_element_type | solution.py:267
  (116 shorter events, 17.8 us)
Async XLA Ops:
  0.6 1.0 %copy-start = (bf16[1,400,400]{2,1,0:T(8,128)(2,1)S(1)}, bf16[1,400,400]{2,1,0:T(8,128)(2,1)}, u32[]{:S(2)}) copy-start(bf16[1,400,400]{2,1,0:T(8,128)(2,1)} %param.9) | copy-start | bytes 960004
  0.6 2.9 %copy-start.2 = (bf16[2,400,400]{1,2,0:T(8,128)(2,1)S(1)}, bf16[2,400,400]{1,2,0:T(8,128)(2,1)}, u32[]{:S(2)}) copy-start(bf16[2,400,400]{1,2,0:T(8,128)(2,1)} %constant.121.clone) | copy-start | bytes 1920004
  6.0 20.6 %all-to-all-start = ((f32[32,1,2525]{2,1,0:T(1,128)}), f32[32,1,2525]{2,1,0:T(1,128)S(1)}, u32[]{:S(2)}, u32[]{:S(2)}) async-start(f32[32,1,2525]{2,1,0:T(1,128)} %all_to_all.28), calls=%async_computation | async-start | bytes 655360 | tf_op jit(solution)/shard_map/all_to_all | solution.py:179
  14.4 1.7 %copy-start.1 = (f32[2,2,400,400]{3,2,0,1:T(8,128)}, f32[2,2,400,400]{3,2,0,1:T(8,128)S(1)}, u32[]{:S(2)}) copy-start(f32[2,2,400,400]{3,2,0,1:T(8,128)S(1)} %convolution_bitcast_fusion) | copy-start | bytes 7680004
  16.7 0.9 copy-start.12
  16.7 1.8 %copy-start.13 = (s32[1,8]{1,0:T(1,128)S(1)}, s32[1,8]{1,0:T(1,128)}, u32[]{:S(2)}) copy-start(s32[1,8]{1,0:T(1,128)} %param.13) | copy-start | bytes 100
  16.7 1.9 %copy-start.14 = (s32[1,8]{1,0:T(1,128)S(1)}, s32[1,8]{1,0:T(1,128)}, u32[]{:S(2)}) copy-start(s32[1,8]{1,0:T(1,128)} %param.14) | copy-start | bytes 100
  16.7 2.0 %copy-start.15 = (s32[1,8]{1,0:T(1,128)S(1)}, s32[1,8]{1,0:T(1,128)}, u32[]{:S(2)}) copy-start(s32[1,8]{1,0:T(1,128)} %param.15) | copy-start | bytes 100
  16.7 2.1 %copy-start.16 = (f32[64]{0:T(128)S(1)}, f32[64]{0:T(128)}, u32[]{:S(2)}) copy-start(f32[64]{0:T(128)} %param.11) | copy-start | bytes 772
  16.9 4.5 %copy-start.10 = (bf16[2,128,800]{1,2,0:T(8,128)(2,1)S(1)}, bf16[2,128,800]{1,2,0:T(8,128)(2,1)}, u32[]{:S(2)}) copy-start(bf16[2,128,800]{1,2,0:T(8,128)(2,1)} %param.16) | copy-start | bytes 1228804
  26.5 18.2 %all-to-all-start.2 = ((bf16[8,2,12928]{2,1,0:T(2,128)(2,1)}), bf16[8,2,12928]{2,1,0:T(2,128)(2,1)S(1)}, u32[]{:S(2)}, u32[]{:S(2)}) async-start(bf16[8,2,12928]{2,1,0:T(2,128)(2,1)} %all_to_all.24), calls=%async_computation.2 | async-start | bytes 827392 | tf_op jit(solution)/shard_map/all_to_all | solution.py:180
  45.7 17.4 %all-to-all-start.1 = ((f32[32,1,2525]{2,1,0:T(1,128)}), f32[32,1,2525]{2,1,0:T(1,128)}, u32[]{:S(2)}, u32[]{:S(2)}) async-start(f32[32,1,2525]{2,1,0:T(1,128)} %broadcast_in_dim.24), calls=%async_computation.1 | async-start | bytes 655360 | tf_op jit(solution)/shard_map/all_to_all | solution.py:84
  63.1 8.4 %copy-start.17 = (pred[400]{0:T(512)(128)(4,1)S(1)}, pred[400]{0:T(512)(128)(4,1)}, u32[]{:S(2)}) copy-start(pred[400]{0:T(512)(128)(4,1)} %compare_and_fusion) | copy-start | bytes 1204
  63.1 24.0 %all-to-all-start.3 = ((bf16[16,2,16,400]{3,2,1,0:T(8,128)(2,1)}), bf16[16,2,16,400]{3,2,1,0:T(8,128)(2,1)S(1)}, u32[]{:S(2)}, u32[]{:S(2)}) async-start(bf16[16,2,16,400]{3,2,1,0:T(8,128)(2,1)} %copy.125), calls=%async_computation.3 | async-start | bytes 1048576 | tf_op jit(solution)/shard_map/all_to_all | solution.py:205
  72.5 1.7 %copy-start.8 = (f32[16,16,800]{2,1,0:T(8,128)S(1)}, f32[16,16,800]{2,1,0:T(8,128)}, u32[]{:S(2)}) copy-start(f32[16,16,800]{2,1,0:T(8,128)} %reshape.478) | copy-start | bytes 2457604
  72.5 1.7 %copy-start.11 = (bf16[16,16,400]{2,0,1:T(8,128)(2,1)S(1)}, bf16[16,16,400]{2,0,1:T(8,128)(2,1)}, u32[]{:S(2)}) copy-start(bf16[16,16,400]{2,0,1:T(8,128)(2,1)} %get-tuple-element.23) | copy-start | bytes 614404
  76.8 3.3 %copy-start.3 = (f32[1,1,400,400]{3,2,1,0:T(8,128)S(1)}, f32[1,1,400,400]{3,2,1,0:T(8,128)}, u32[]{:S(2)}) copy-start(f32[1,1,400,400]{3,2,1,0:T(8,128)} %fusion.20) | copy-start | bytes 1920004
  76.8 3.3 %copy-start.4 = (f32[1,1,400,400]{3,2,1,0:T(8,128)S(1)}, f32[1,1,400,400]{3,2,1,0:T(8,128)}, u32[]{:S(2)}) copy-start(f32[1,1,400,400]{3,2,1,0:T(8,128)} %fusion.73) | copy-start | bytes 1920004
  77.1 5.9 %collective-permute-start = (bf16[2,32,1200]{2,1,0:T(8,128)(2,1)S(1)}, bf16[2,32,1200]{2,1,0:T(8,128)(2,1)S(1)}, u32[]{:S(2)}, u32[]{:S(2)}) collective-permute-start(bf16[2,32,1200]{2,1,0:T(8,128)(2,1)S(1)} %get-tuple-element.18), channel_id=1, source_target_pairs={{0,8},{8,16},{16,24},{24,0},{1,9},{9,17},{17,25},{25,1},{2,10},{10... | collective-permute-start | bytes 460808 | tf_op jit(solution)/shard_map/ppermute | solution.py:112
  77.1 7.1 %collective-permute-start.1 = (bf16[2,32,1200]{2,1,0:T(8,128)(2,1)S(1)}, bf16[2,32,1200]{2,1,0:T(8,128)(2,1)S(1)}, u32[]{:S(2)}, u32[]{:S(2)}) collective-permute-start(bf16[2,32,1200]{2,1,0:T(8,128)(2,1)S(1)} %get-tuple-element.20), channel_id=1, source_target_pairs={{0,16},{8,24},{16,0},{24,8},{1,17},{9,25},{17,1},{25,9},{2,18},{10... | collective-permute-start | bytes 460808 | tf_op jit(solution)/shard_map/ppermute | solution.py:112
  78.7 7.5 %collective-permute-start.2 = (bf16[2,32,1200]{2,1,0:T(8,128)(2,1)S(1)}, bf16[2,32,1200]{2,1,0:T(8,128)(2,1)S(1)}, u32[]{:S(2)}, u32[]{:S(2)}) collective-permute-start(bf16[2,32,1200]{2,1,0:T(8,128)(2,1)S(1)} %get-tuple-element.19), channel_id=1, source_target_pairs={{0,24},{8,0},{16,8},{24,16},{1,25},{9,1},{17,9},{25,17},{2,26},{10... | collective-permute-start | bytes 460808 | tf_op jit(solution)/shard_map/ppermute | solution.py:112
  87.1 1.0 %copy-start.5 = (f32[128,400]{1,0:T(8,128)S(1)}, f32[128,400]{1,0:T(8,128)}, u32[]{:S(2)}) copy-start(f32[128,400]{1,0:T(8,128)} %maximum_convert_fusion.1) | copy-start | bytes 614404
  87.1 1.0 %copy-start.6 = (f32[2,64,400]{2,1,0:T(8,128)S(1)}, f32[2,64,400]{2,1,0:T(8,128)}, u32[]{:S(2)}) copy-start(f32[2,64,400]{2,1,0:T(8,128)} %get-tuple-element.10) | copy-start | bytes 614404
  87.1 1.1 %copy-start.7 = (f32[2,64,400]{2,1,0:T(8,128)S(1)}, f32[2,64,400]{2,1,0:T(8,128)}, u32[]{:S(2)}) copy-start(f32[2,64,400]{2,1,0:T(8,128)} %get-tuple-element.11) | copy-start | bytes 614404
  88.2 0.9 copy-start.9

commit v17 on v13

--- a/solution.py
+++ b/solution.py
@@ -229,6 +229,7 @@
     share = vrows // img_count
     numerator = numerator.reshape(planes, img_count, share, 3 * box_size).astype(jnp.bfloat16)
     numerator = jnp.swapaxes(numerator, 0, 1)
+    numerator, returned_rows = lax.optimization_barrier((numerator, returned_rows))
     volume_part = reduce_over_img(numerator, img_count)
     weight_sum = volume_part[..., 2 * box_size :]
     reconstruction = volume_part[..., : 2 * box_size] / (

time: 90 us -> 99 us (1.10)
  waiting for transfers between devices: 10.3 us -> 14.6 us
  matrix products: 11.7 us -> 14 us
  local copies, waits for them, and re-layouts: 15.9 us -> 17.9 us
  other arithmetic: 23.2 us -> 24.8 us
    ppermute x3, waiting for transfers between devices: 3.27 us -> 5.9 us  [reduce_over_img(): total = total + lax.ppermute(piece, 'img', pairs).astype(jnp.float32)]
    all_to_all x1, waiting for transfers between devices: 0.01 us -> 2.62 us  [body(): returned_rows = lax.all_to_all(projected, 'slab', 0, 0, tiled=True)]
    unnamed x33 -> x53, local copies, waits for them, and re-layouts: 3.32 us -> 4.81 us
    ppermute x3, starting transfers between devices: 3 us -> 1.79 us  [reduce_over_img(): total = total + lax.ppermute(piece, 'img', pairs).astype(jnp.float32)]
    dot_general x2, matrix products: 1.36 us -> 2.57 us  [picture_of(): jnp.einsum('hxk,hkm->hxm', tables, back_rows, preferred_element_type=jnp....]
    convert_element_type x1, local copies, waits for them, and re-layouts: 2.7 us -> 1.55 us  [body(): received = got_contrast_both * got_blocks.astype(jnp.float32) / got_level]
    dot_general x1, matrix products: 0.68 us -> 1.72 us  [body(): jnp.einsum('sq,qhix->shix', slot_pick, volume_slots, preferred_element_ty...]
  transfers between devices with their start and end apart: 7 -> 7, of which waited for: 5 -> 4; matrix products, arithmetic and copies ran while one was open for 43% -> 44% of each run, Pallas kernels for 0% -> 0%
where the time goes in v17:
time: 99 us; the launch traced here: 98.2 us
  other arithmetic  24.8 us (25%)
  starting transfers between devices  24.4 us (25%)
  local copies, waits for them, and re-layouts  17.9 us (18%)
  waiting for transfers between devices  14.6 us (15%)
  matrix products  14 us (14%)
  between operations  2.56 us (3%)
    all_to_all x1, starting transfers between devices, body(): gathered = lax.all_to_all(pieces, ('img', 'slab'), 0, 0, tiled=True)  7.3 us
    all_to_all x1, waiting for transfers between devices, body(): got = lax.all_to_all(send, 'slab', 0, 0, tiled=True)  6.02 us
    ppermute x3, waiting for transfers between devices, reduce_over_img(): total = total + lax.ppermute(piece, 'img', pairs).astype(jnp.float32)  5.9 us
    all_to_all x1, starting transfers between devices, body(): got = lax.all_to_all(send, 'slab', 0, 0, tiled=True)  5.82 us
    convert_element_type x2, other arithmetic, contrast_curve(): (-jnp.sin(defocus_of[:, None, None] * radius + 0.1)).astype(jnp.bfloat16)  5.7 us
    all_to_all x1, starting transfers between devices, body(): returned_rows = lax.all_to_all(projected, 'slab', 0, 0, tiled=True)  5.59 us
    unnamed x53, local copies, waits for them, and re-layouts  4.81 us
    all_to_all x1, starting transfers between devices, power_gather(): back = lax.all_to_all(spread, ('img', 'slab'), 0, 0, tiled=True)  3.95 us
  transfers between devices with their start and end apart: 7, of which 4 were waited for; matrix products, arithmetic and copies ran while one was open for 44% of the time, Pallas kernels for 0%

profile of v17, /device:TPU:0, one launch (start us, length us, event | category | flops | bytes accessed | tf_op | source)
XLA Modules:
  0.0 98.2 jit_solution(14110678308135308806)
XLA Ops:
  0.7 1.0 copy-done
  1.6 1.9 %fusion.2 = bf16[2,400,400,1]{1,2,3,0:T(8,128)(2,1)S(1)} fusion(bf16[2,400,400]{1,2,0:T(8,128)(2,1)} %constant.122.clone, bf16[1,400,400]{2,1,0:T(8,128)(2,1)S(1)} %copy-done), kind=kOutput, calls=%fused_computation.12 | convolution fusion | flops 256320000 | bytes 1600000 | tf_op jit(solution)/shard_map/yx,hmx->hym/dot_general | solution.py:24
  4.6 1.4 %all_to_all.28 = f32[32,1,2525]{2,1,0:T(1,128)} reshape(f32[202,400]{1,0:T(8,128)S(1)} %copy.122) | data formatting | bytes 646400 | tf_op jit(solution)/shard_map/all_to_all | solution.py:179
  6.0 7.3 %all-to-all-start = ((f32[32,1,2525]{2,1,0:T(1,128)}), f32[32,1,2525]{2,1,0:T(1,128)S(1)}, u32[]{:S(2)}, u32[]{:S(2)}) async-start(f32[32,1,2525]{2,1,0:T(1,128)} %all_to_all.28), calls=%async_computation | async-start | bytes 655360 | tf_op jit(solution)/shard_map/all_to_all | solution.py:179
  13.3 1.1 %convolution_bitcast_fusion = f32[2,2,400,400]{3,2,0,1:T(8,128)S(1)} fusion(bf16[2,400,400,1]{1,2,3,0:T(8,128)(2,1)S(1)} %fusion.2, bf16[2,400,400]{1,2,0:T(8,128)(2,1)S(1)} %copy-done.4), kind=kOutput, calls=%fused_computation.2 | convolution fusion | flops 512000000 | bytes 3840000 | tf_op jit(solution)/shard_map/gky,hym->ghkm/dot_general | solution.py:30
  14.8 1.3 %copy-done.1 = f32[2,2,400,400]{3,2,0,1:T(8,128)} copy-done((f32[2,2,400,400]{3,2,0,1:T(8,128)}, f32[2,2,400,400]{3,2,0,1:T(8,128)S(1)}, u32[]{:S(2)}) %copy-start.1) | copy-done | bytes 2560024
  20.4 0.9 all_to_all.24
  21.6 1.3 %reshape.466 = bf16[2,8,16,2,400]{4,3,2,1,0:T(2,128)(2,1)} reshape(bf16[2,128,800]{2,1,0:T(8,128)(2,1)S(1)} %copy.134) | data formatting | bytes 819200 | tf_op jit(solution)/shard_map/reshape | solution.py:190
  24.2 3.0 %negate_convert_fusion = bf16[1,400,400]{2,1,0:T(8,128)(2,1)S(1)} fusion(f32[]{:T(128)S(6)} %mul.154, s32[400]{0:T(512)S(1)} %fusion.112), kind=kLoop, calls=%fused_computation.62 | loop fusion | flops 960000 | bytes 321604 | tf_op jit(solution)/shard_map/convert_element_type | solution.py:61
  27.3 5.8 %all-to-all-start.2 = ((bf16[8,2,12928]{2,1,0:T(2,128)(2,1)}), bf16[8,2,12928]{2,1,0:T(2,128)(2,1)S(1)}, u32[]{:S(2)}, u32[]{:S(2)}) async-start(bf16[8,2,12928]{2,1,0:T(2,128)(2,1)} %all_to_all.24), calls=%async_computation.2 | async-start | bytes 827392 | tf_op jit(solution)/shard_map/all_to_all | solution.py:180
  34.4 2.5 %fusion.75 = f32[1,1,400,400]{3,2,1,0:T(8,128)} fusion(f32[2,2,400,400]{3,2,0,1:T(8,128)} %copy-done.1), kind=kLoop, calls=%fused_computation.122 | loop fusion | flops 320000 | bytes 1920000 | tf_op jit(solution)/shard_map/neg | solution.py:32
  36.9 2.4 %fusion.20 = f32[1,1,400,400]{3,2,1,0:T(8,128)} fusion(f32[2,2,400,400]{3,2,0,1:T(8,128)} %copy-done.1), kind=kLoop, calls=%fused_computation.43 | loop fusion | flops 160000 | bytes 1920000 | tf_op jit(solution)/shard_map/sub | solution.py:31
  39.5 6.0 %all-to-all-done.2 = bf16[8,2,12928]{2,1,0:T(2,128)(2,1)S(1)} async-done(((bf16[8,2,12928]{2,1,0:T(2,128)(2,1)}), bf16[8,2,12928]{2,1,0:T(2,128)(2,1)S(1)}, u32[]{:S(2)}, u32[]{:S(2)}) %all-to-all-start.2) | async-done | bytes 413728 | tf_op jit(solution)/shard_map/all_to_all | solution.py:180
  45.5 0.9 broadcast_in_dim.30
  46.4 4.0 %all-to-all-start.1 = ((f32[32,1,2525]{2,1,0:T(1,128)}), f32[32,1,2525]{2,1,0:T(1,128)}, u32[]{:S(2)}, u32[]{:S(2)}) async-start(f32[32,1,2525]{2,1,0:T(1,128)} %broadcast_in_dim.30), calls=%async_computation.1 | async-start | bytes 655360 | tf_op jit(solution)/shard_map/all_to_all | solution.py:84
  51.5 1.7 %fusion.47 = f32[16,2,16,400]{3,0,2,1:T(8,128)S(1)} fusion(bf16[16,2,16,400]{3,1,2,0:T(2,128)(2,1)} %bitcast.165, s32[16]{0:T(128)S(1)} %get-tuple-element.6), kind=kOutput, calls=%fused_computation.77 | convolution fusion | flops 6553856 | bytes 1228864 | tf_op jit(solution)/shard_map/sq,qhix->shix/dot_general | solution.py:192
  53.2 1.3 %slice.253 = f32[16,2,16,399]{3,0,2,1:T(8,128)} slice(f32[16,2,16,400]{3,0,2,1:T(8,128)S(1)} %fusion.47), slice={[0:16], [0:2], [0:16], [1:400]} | slice | bytes 1634304 | tf_op jit(solution)/shard_map/jit(_roll_static)/slice | solution.py:197
  54.8 2.7 %negate_convert_fusion.1 = (bf16[16,16,400]{2,0,1:T(8,128)(2,1)}, f32[16,16,400]{2,0,1:T(8,128)S(1)}) fusion(f32[16]{0:T(128)S(1)} %get-tuple-element.29, s32[400]{0:T(512)S(1)} %fusion.112, s32[16,16]{0,1:T(8,128)S(1)} %fusion.91), kind=kLoop, calls=%fused_computation.80 | loop fusion | flops 819200 | bytes 617088 | tf_op jit(solution)/shard_map/convert_element_type | solution.py:61
  58.3 1.6 %reshape.469 = f32[16,16,800]{2,1,0:T(8,128)} reshape(f32[16,12800]{1,0:T(8,128)S(1)} %slice_convert_fusion.1) | data formatting | bytes 1638400 | tf_op jit(solution)/shard_map/convert_element_type | solution.py:219
  59.9 1.6 %fusion.11 = bf16[16,2,16,400]{3,0,2,1:T(8,128)(2,1)S(1)} fusion(f32[16,2,16,1]{3,0,2,1:T(8,128)S(1)} %slice-done, f32[16,2,16,399]{3,0,2,1:T(8,128)} %slice.253, f32[16,2,16,400]{3,0,2,1:T(8,128)S(1)} %copy-done.3, f32[16]{0:T(128)S(1)} %get-tuple-element.10, f32[16]{0:T(128)S(1)} %get-tuple-element.11, f32[16]{0:T(128)S(1)} %get-tuple-element.30), kind=kLoop, calls=%fused_computation.26 | loop fusion | flops 1228800 | bytes 2048192 | tf_op jit(solution)/shard_map/convert_element_type | solution.py:198
  61.5 1.1 %copy.136 = bf16[16,2,16,400]{3,2,1,0:T(8,128)(2,1)} copy(bf16[16,2,16,400]{3,0,2,1:T(8,128)(2,1)S(1)} %fusion.11) | data formatting | bytes 819200 | tf_op jit(solution)/shard_map/convert_element_type | solution.py:198
  62.6 2.1 %fusion.45 = f32[16,16,400]{2,0,1:T(8,128)S(1)} fusion(f32[16,16,399]{2,0,1:T(8,128)S(1)} %bitcast.162, f32[16,16,1]{2,0,1:T(8,128)S(1)} %slice.250, f32[16]{0:T(128)S(1)} %get-tuple-element.11, f32[16]{0:T(128)S(1)} %get-tuple-element.30, f32[16]{0:T(128)S(1)} %get-tuple-element.29, s32[400]{0:T(512)S(1)} %fusion.112, s32[16,16]{0,1:T(8,128)S(1)} %fusion.91), kind=kLoop, calls=%fused_computation.75 | loop fusion | flops 1228800 | bytes 822016 | tf_op jit(solution)/shard_map/add | solution.py:223
  64.7 5.6 %all-to-all-start.3 = ((bf16[16,2,16,400]{3,2,1,0:T(8,128)(2,1)}), bf16[16,2,16,400]{3,2,1,0:T(8,128)(2,1)S(1)}, u32[]{:S(2)}, u32[]{:S(2)}) async-start(bf16[16,2,16,400]{3,2,1,0:T(8,128)(2,1)} %copy.136), calls=%async_computation.3 | async-start | bytes 1048576 | tf_op jit(solution)/shard_map/all_to_all | solution.py:205
  70.3 1.8 %reduce.3 = f32[32,2525]{1,0:T(8,128)S(1)} reduce(f32[32,1,2525]{2,1,0:T(1,128)} %all-to-all-done.1, f32[]{:T(128)} %constant.132), dimensions={1}, to_apply=%all_to_all.23.reduce_sub_computation | reduce | bytes 646404 | tf_op jit(solution)/shard_map/all_to_all | solution.py:84
  73.1 1.0 %fusion.37 = f32[202,400]{0,1:T(8,128)S(1)} fusion(f32[202,400]{1,0:T(8,128)S(1)} %reshape.462, s32[400]{0:T(512)S(1)} %get-tuple-element.31, s32[400]{0:T(512)S(1)} %fusion.119, s32[400]{0:T(512)S(1)} %get-tuple-element.32, pred[400]{0:T(512)(128)(4,1)S(1)} %copy-done.25), kind=kOutput, calls=%fused_computation.64 | convolution fusion | flops 388160000 | bytes 651600 | tf_op jit(solution)/shard_map/dot_general | solution.py:90
  75.4 0.8 convolution_divide_fusion
  77.1 0.9 convolution_convert_fusion.1
  80.6 1.8 %fusion.21 = f32[2,400,400]{2,1,0:T(8,128)} fusion(bf16[2,400,400]{1,2,0:T(8,128)(2,1)S(1)} %copy-done.4, bf16[2,64,400]{2,1,0:T(8,128)(2,1)S(1)} %broadcast_in_dim.25, bf16[1,272,400]{2,1,0:T(8,128)(2,1)S(1)} %get-tuple-element.13, bf16[1,272,400]{2,1,0:T(8,128)(2,1)S(1)} %get-tuple-element.12), kind=kOutput, calls=%fused_computation.46 | convolution fusion | flops 258560000 | bytes 2457600 | tf_op jit(solution)/shard_map/hxk,hkm->hxm/dot_general | solution.py:46
  82.5 2.6 %all-to-all-done.3 = bf16[16,2,16,400]{3,2,1,0:T(8,128)(2,1)S(1)} async-done(((bf16[16,2,16,400]{3,2,1,0:T(8,128)(2,1)}), bf16[16,2,16,400]{3,2,1,0:T(8,128)(2,1)S(1)}, u32[]{:S(2)}, u32[]{:S(2)}) %all-to-all-start.3) | async-done | bytes 409632 | tf_op jit(solution)/shard_map/all_to_all | solution.py:205
  87.2 1.6 %collective-permute-start.1 = (bf16[2,32,1200]{2,1,0:T(8,128)(2,1)S(1)}, bf16[2,32,1200]{2,1,0:T(8,128)(2,1)S(1)}, u32[]{:S(2)}, u32[]{:S(2)}) collective-permute-start(bf16[2,32,1200]{2,1,0:T(8,128)(2,1)S(1)} %get-tuple-element.22), channel_id=1, source_target_pairs={{0,16},{8,24},{16,0},{24,8},{1,17},{9,25},{17,1},{25,9},{2,18},{10... | collective-permute-start | bytes 460808 | tf_op jit(solution)/shard_map/ppermute | solution.py:112
  90.2 1.1 %fusion.17 = bf16[1,400,400]{2,1,0:T(8,128)(2,1)} fusion(f32[2,400,400]{2,1,0:T(8,128)S(1)} %fusion.29, f32[2,400,400]{2,1,0:T(8,128)S(1)} %copy-done.9), kind=kLoop, calls=%fused_computation.36 | loop fusion | flops 800000 | bytes 2880000 | tf_op jit(solution)/shard_map/convert_element_type | solution.py:269
  91.4 5.8 %collective-permute-done.1 = bf16[2,32,1200]{2,1,0:T(8,128)(2,1)S(1)} collective-permute-done((bf16[2,32,1200]{2,1,0:T(8,128)(2,1)S(1)}, bf16[2,32,1200]{2,1,0:T(8,128)(2,1)S(1)}, u32[]{:S(2)}, u32[]{:S(2)}) %collective-permute-start.1) | collective-permute-done | bytes 153632 | tf_op jit(solution)/shard_map/ppermute | solution.py:112
  (137 shorter events, 19.8 us)
Async XLA Ops:
  0.6 1.0 %copy-start = (bf16[1,400,400]{2,1,0:T(8,128)(2,1)S(1)}, bf16[1,400,400]{2,1,0:T(8,128)(2,1)}, u32[]{:S(2)}) copy-start(bf16[1,400,400]{2,1,0:T(8,128)(2,1)} %param.9) | copy-start | bytes 960004
  0.6 2.9 %copy-start.4 = (bf16[2,400,400]{1,2,0:T(8,128)(2,1)S(1)}, bf16[2,400,400]{1,2,0:T(8,128)(2,1)}, u32[]{:S(2)}) copy-start(bf16[2,400,400]{1,2,0:T(8,128)(2,1)} %constant.122.clone) | copy-start | bytes 1920004
  6.0 21.3 %all-to-all-start = ((f32[32,1,2525]{2,1,0:T(1,128)}), f32[32,1,2525]{2,1,0:T(1,128)S(1)}, u32[]{:S(2)}, u32[]{:S(2)}) async-start(f32[32,1,2525]{2,1,0:T(1,128)} %all_to_all.28), calls=%async_computation | async-start | bytes 655360 | tf_op jit(solution)/shard_map/all_to_all | solution.py:179
  14.4 1.7 %copy-start.1 = (f32[2,2,400,400]{3,2,0,1:T(8,128)}, f32[2,2,400,400]{3,2,0,1:T(8,128)S(1)}, u32[]{:S(2)}) copy-start(f32[2,2,400,400]{3,2,0,1:T(8,128)S(1)} %convolution_bitcast_fusion) | copy-start | bytes 7680004
  14.6 2.1 %copy-start.21 = (s32[1,8]{1,0:T(1,128)S(1)}, s32[1,8]{1,0:T(1,128)}, u32[]{:S(2)}) copy-start(s32[1,8]{1,0:T(1,128)} %param.13) | copy-start | bytes 100
  14.6 2.2 %copy-start.22 = (s32[1,8]{1,0:T(1,128)S(1)}, s32[1,8]{1,0:T(1,128)}, u32[]{:S(2)}) copy-start(s32[1,8]{1,0:T(1,128)} %param.14) | copy-start | bytes 100
  14.6 2.3 %copy-start.23 = (s32[1,8]{1,0:T(1,128)S(1)}, s32[1,8]{1,0:T(1,128)}, u32[]{:S(2)}) copy-start(s32[1,8]{1,0:T(1,128)} %param.15) | copy-start | bytes 100
  17.7 1.1 %copy-start.24 = (f32[64]{0:T(128)S(1)}, f32[64]{0:T(128)}, u32[]{:S(2)}) copy-start(f32[64]{0:T(128)} %param.11) | copy-start | bytes 772
  17.8 3.5 %copy-start.14 = (bf16[2,128,800]{1,2,0:T(8,128)(2,1)S(1)}, bf16[2,128,800]{1,2,0:T(8,128)(2,1)}, u32[]{:S(2)}) copy-start(bf16[2,128,800]{1,2,0:T(8,128)(2,1)} %param.16) | copy-start | bytes 1228804
  27.3 18.3 %all-to-all-start.2 = ((bf16[8,2,12928]{2,1,0:T(2,128)(2,1)}), bf16[8,2,12928]{2,1,0:T(2,128)(2,1)S(1)}, u32[]{:S(2)}, u32[]{:S(2)}) async-start(bf16[8,2,12928]{2,1,0:T(2,128)(2,1)} %all_to_all.24), calls=%async_computation.2 | async-start | bytes 827392 | tf_op jit(solution)/shard_map/all_to_all | solution.py:180
  46.4 18.3 %all-to-all-start.1 = ((f32[32,1,2525]{2,1,0:T(1,128)}), f32[32,1,2525]{2,1,0:T(1,128)}, u32[]{:S(2)}, u32[]{:S(2)}) async-start(f32[32,1,2525]{2,1,0:T(1,128)} %broadcast_in_dim.30), calls=%async_computation.1 | async-start | bytes 655360 | tf_op jit(solution)/shard_map/all_to_all | solution.py:84
  53.2 4.2 %copy-start.2 = (f32[16,2,16,400]{3,0,2,1:T(8,128)}, f32[16,2,16,400]{3,0,2,1:T(8,128)S(1)}, u32[]{:S(2)}) copy-start(f32[16,2,16,400]{3,0,2,1:T(8,128)S(1)} %fusion.47) | copy-start | bytes 2457604
  58.2 1.7 %copy-start.3 = (f32[16,2,16,400]{3,0,2,1:T(8,128)S(1)}, f32[16,2,16,400]{3,0,2,1:T(8,128)}, u32[]{:S(2)}) copy-start(f32[16,2,16,400]{3,0,2,1:T(8,128)} %copy-done.2) | copy-start | bytes 2457604
  58.2 1.7 %slice-start = ((f32[16,2,16,400]{3,0,2,1:T(8,128)}), f32[16,2,16,1]{3,0,2,1:T(8,128)S(1)}, s32[]{:S(2)}) async-start(f32[16,2,16,400]{3,0,2,1:T(8,128)} %copy-done.2), calls=%async_computation.4 | async-start | bytes 524288 | tf_op jit(solution)/shard_map/jit(_roll_static)/slice | solution.py:197
  59.9 2.7 %copy-start.8 = (f32[16,16,400]{2,0,1:T(8,128)S(1)}, f32[16,16,400]{2,0,1:T(8,128)}, u32[]{:S(2)}) copy-start(f32[16,16,400]{2,0,1:T(8,128)} %copy-done.7) | copy-start | bytes 1228804
  62.6 9.9 %copy-start.18 = (pred[400]{0:T(512)(128)(4,1)S(1)}, pred[400]{0:T(512)(128)(4,1)}, u32[]{:S(2)}) copy-start(pred[400]{0:T(512)(128)(4,1)} %fusion.118) | copy-start | bytes 1204
  64.7 8.4 %copy-start.25 = (pred[400]{0:T(512)(128)(4,1)S(1)}, pred[400]{0:T(512)(128)(4,1)}, u32[]{:S(2)}) copy-start(pred[400]{0:T(512)(128)(4,1)} %compare_and_fusion) | copy-start | bytes 1204
  64.7 20.4 %all-to-all-start.3 = ((bf16[16,2,16,400]{3,2,1,0:T(8,128)(2,1)}), bf16[16,2,16,400]{3,2,1,0:T(8,128)(2,1)S(1)}, u32[]{:S(2)}, u32[]{:S(2)}) async-start(bf16[16,2,16,400]{3,2,1,0:T(8,128)(2,1)} %copy.136), calls=%async_computation.3 | async-start | bytes 1048576 | tf_op jit(solution)/shard_map/all_to_all | solution.py:205
  70.3 3.8 %copy-start.20 = (pred[400]{0:T(512)(128)(4,1)S(1)}, pred[400]{0:T(512)(128)(4,1)}, u32[]{:S(2)}) copy-start(pred[400]{0:T(512)(128)(4,1)} %fusion.116) | copy-start | bytes 1204
  74.1 1.2 %copy-start.13 = (f32[16,16,800]{2,1,0:T(8,128)S(1)}, f32[16,16,800]{2,1,0:T(8,128)}, u32[]{:S(2)}) copy-start(f32[16,16,800]{2,1,0:T(8,128)} %reshape.469) | copy-start | bytes 2457604
  74.1 1.2 %copy-start.15 = (bf16[16,16,400]{2,0,1:T(8,128)(2,1)S(1)}, bf16[16,16,400]{2,0,1:T(8,128)(2,1)}, u32[]{:S(2)}) copy-start(bf16[16,16,400]{2,0,1:T(8,128)(2,1)} %get-tuple-element.27) | copy-start | bytes 614404
  74.1 1.2 %copy-start.19 = (s32[16]{0:T(128)S(1)}, s32[16]{0:T(128)}, u32[]{:S(2)}) copy-start(s32[16]{0:T(128)} %get-tuple-element.7) | copy-start | bytes 196
  77.1 1.1 %copy-start.5 = (f32[1,1,400,400]{3,2,1,0:T(8,128)S(1)}, f32[1,1,400,400]{3,2,1,0:T(8,128)}, u32[]{:S(2)}) copy-start(f32[1,1,400,400]{3,2,1,0:T(8,128)} %fusion.75) | copy-start | bytes 1920004
  77.1 1.4 %copy-start.6 = (f32[1,1,400,400]{3,2,1,0:T(8,128)S(1)}, f32[1,1,400,400]{3,2,1,0:T(8,128)}, u32[]{:S(2)}) copy-start(f32[1,1,400,400]{3,2,1,0:T(8,128)} %fusion.20) | copy-start | bytes 1920004
  82.5 3.4 %copy-start.10 = (f32[128,400]{1,0:T(8,128)S(1)}, f32[128,400]{1,0:T(8,128)}, u32[]{:S(2)}) copy-start(f32[128,400]{1,0:T(8,128)} %maximum_convert_fusion.1) | copy-start | bytes 614404
  85.1 1.0 copy-start.11
  85.1 1.0 %copy-start.12 = (f32[2,64,400]{2,1,0:T(8,128)S(1)}, f32[2,64,400]{2,1,0:T(8,128)}, u32[]{:S(2)}) copy-start(f32[2,64,400]{2,1,0:T(8,128)} %get-tuple-element.15) | copy-start | bytes 614404
  86.6 2.3 %copy-start.17 = (bf16[400]{0:T(512)(128)(2,1)S(1)}, bf16[400]{0:T(512)(128)(2,1)}, u32[]{:S(2)}) copy-start(bf16[400]{0:T(512)(128)(2,1)} %pad.8.clone) | copy-start | bytes 2404
  87.1 4.2 %collective-permute-start.2 = (bf16[2,32,1200]{2,1,0:T(8,128)(2,1)S(1)}, bf16[2,32,1200]{2,1,0:T(8,128)(2,1)S(1)}, u32[]{:S(2)}, u32[]{:S(2)}) collective-permute-start(bf16[2,32,1200]{2,1,0:T(8,128)(2,1)S(1)} %get-tuple-element.21), channel_id=1, source_target_pairs={{0,24},{8,0},{16,8},{24,16},{1,25},{9,1},{17,9},{25,17},{2,26},{10... | collective-permute-start | bytes 460808 | tf_op jit(solution)/shard_map/ppermute | solution.py:112
  87.2 10.0 %collective-permute-start.1 = (bf16[2,32,1200]{2,1,0:T(8,128)(2,1)S(1)}, bf16[2,32,1200]{2,1,0:T(8,128)(2,1)S(1)}, u32[]{:S(2)}, u32[]{:S(2)}) collective-permute-start(bf16[2,32,1200]{2,1,0:T(8,128)(2,1)S(1)} %get-tuple-element.22), channel_id=1, source_target_pairs={{0,16},{8,24},{16,0},{24,8},{1,17},{9,25},{17,1},{25,9},{2,18},{10... | collective-permute-start | bytes 460808 | tf_op jit(solution)/shard_map/ppermute | solution.py:112
  88.8 1.4 %copy-start.9 = (f32[2,400,400]{2,1,0:T(8,128)S(1)}, f32[2,400,400]{2,1,0:T(8,128)}, u32[]{:S(2)}) copy-start(f32[2,400,400]{2,1,0:T(8,128)} %fusion.21) | copy-start | bytes 3840004
  88.8 8.5 %collective-permute-start = (bf16[2,32,1200]{2,1,0:T(8,128)(2,1)S(1)}, bf16[2,32,1200]{2,1,0:T(8,128)(2,1)S(1)}, u32[]{:S(2)}, u32[]{:S(2)}) collective-permute-start(bf16[2,32,1200]{2,1,0:T(8,128)(2,1)S(1)} %get-tuple-element.20), channel_id=1, source_target_pairs={{0,8},{8,16},{16,24},{24,0},{1,9},{9,17},{17,25},{25,1},{2,10},{10... | collective-permute-start | bytes 460808 | tf_op jit(solution)/shard_map/ppermute | solution.py:112
  (2 other events, 1.6 us)

commit v18 on v13

--- a/solution.py
+++ b/solution.py
@@ -82,7 +82,7 @@
 def power_gather(total, device_count, rows, box_size):
     spread = jnp.broadcast_to(total, (device_count, total.shape[1]))
     back = lax.all_to_all(spread, ("img", "slab"), 0, 0, tiled=True)
-    half = back.reshape(rows, box_size)
+    half = back.reshape(rows, box_size).astype(jnp.float32)
     zero = lax.optimization_barrier(jnp.zeros((), jnp.int32))
     n = lax.broadcasted_iota(jnp.int32, (box_size, box_size), 0) + zero
     m = lax.broadcasted_iota(jnp.int32, (box_size, box_size), 1)
@@ -176,7 +176,7 @@
     low_half = jnp.stack([transform(r, tables[:, :top_rows]) for r in rowwise])[:, :, :rows_half]
     power_half = jnp.sum(low_half * low_half, axis=(0, 1))
     pieces = power_half.reshape(device_count, rows_half * box_size // device_count)
-    gathered = lax.all_to_all(pieces, ("img", "slab"), 0, 0, tiled=True)
+    gathered = lax.all_to_all(pieces.astype(jnp.bfloat16), ("img", "slab"), 0, 0, tiled=True)
     got = lax.all_to_all(send, "slab", 0, 0, tiled=True)
     got_blocks = got[:, : RB * 2 * box_size].reshape(seat_count, RB, 2 * box_size)
     got_info = got[:, RB * 2 * box_size : RB * 2 * box_size + 6].astype(jnp.int32)
@@ -197,7 +197,7 @@
         ((1.0 - blend_4) * nearby + blend_4 * jnp.roll(nearby, -1, axis=-1)) * live[..., None]
     ).astype(jnp.bfloat16)
 
-    total = jnp.sum(gathered, axis=0, keepdims=True)
+    total = jnp.sum(gathered.astype(jnp.float32), axis=0, keepdims=True).astype(jnp.bfloat16)
     power = power_gather(total, device_count, rows_half, box_size)
     noise_level = jnp.sqrt(power / (particles * device_count) + 1e-06)
     level_both = jnp.concatenate([noise_level, noise_level], axis=1)

time: 90 us -> 106 us (1.18)
  waiting for transfers between devices: 10.3 us -> 21.4 us
  matrix products: 11.7 us -> 15.2 us
  other arithmetic: 23.2 us -> 24.6 us
    all_to_all x1, waiting for transfers between devices: 0.01 us -> 13.5 us  [body(): returned_rows = lax.all_to_all(projected, 'slab', 0, 0, tiled=True)]
    all_to_all x1, waiting for transfers between devices: 0.01 us -> 7.71 us  [power_gather(): back = lax.all_to_all(spread, ('img', 'slab'), 0, 0, tiled=True)]
    all_to_all x1, waiting for transfers between devices: 6.59 us -> 0.23 us  [body(): got = lax.all_to_all(send, 'slab', 0, 0, tiled=True)]
    ppermute x3, waiting for transfers between devices: 3.27 us -> 0.01 us  [reduce_over_img(): total = total + lax.ppermute(piece, 'img', pairs).astype(jnp.float32)]
    all_to_all x1, starting transfers between devices: 3.96 us -> 5.95 us  [power_gather(): back = lax.all_to_all(spread, ('img', 'slab'), 0, 0, tiled=True)]
    all_to_all x1 -> x0, local copies, waits for them, and re-layouts: 1.36 us -> none  [body(): gathered = lax.all_to_all(pieces, ('img', 'slab'), 0, 0, tiled=True)]
    convert_element_type x0 -> x2, local copies, waits for them, and re-layouts: none -> 1.27 us  [body(): pieces.astype(jnp.bfloat16)]
    dot_general x2, matrix products: 1.36 us -> 2.55 us  [picture_of(): jnp.einsum('hxk,hkm->hxm', tables, back_rows, preferred_element_type=jnp....]
  transfers between devices with their start and end apart: 7 -> 7, of which waited for: 5 -> 3; matrix products, arithmetic and copies ran while one was open for 43% -> 29% of each run, Pallas kernels for 0% -> 0%
where the time goes in v18:
time: 106 us; the launch traced here: 105 us
  starting transfers between devices  25.2 us (24%)
  other arithmetic  24.6 us (23%)
  waiting for transfers between devices  21.4 us (20%)
  local copies, waits for them, and re-layouts  16.4 us (15%)
  matrix products  15.2 us (14%)
  between operations  2.68 us (3%)
    all_to_all x1, waiting for transfers between devices, body(): returned_rows = lax.all_to_all(projected, 'slab', 0, 0, tiled=True)  13.5 us
    all_to_all x1, waiting for transfers between devices, power_gather(): back = lax.all_to_all(spread, ('img', 'slab'), 0, 0, tiled=True)  7.71 us
    all_to_all x1, starting transfers between devices, body(): lax.all_to_all(pieces.astype(jnp.bfloat16), ('img', 'slab'), 0, 0, tiled=...  7.3 us
    all_to_all x1, starting transfers between devices, power_gather(): back = lax.all_to_all(spread, ('img', 'slab'), 0, 0, tiled=True)  5.95 us
    convert_element_type x2, other arithmetic, contrast_curve(): (-jnp.sin(defocus_of[:, None, None] * radius + 0.1)).astype(jnp.bfloat16)  4.94 us
    all_to_all x1, starting transfers between devices, body(): returned_rows = lax.all_to_all(projected, 'slab', 0, 0, tiled=True)  4.73 us
    all_to_all x1, starting transfers between devices, body(): got = lax.all_to_all(send, 'slab', 0, 0, tiled=True)  4.27 us
    unnamed x55, local copies, waits for them, and re-layouts  3.59 us
  transfers between devices with their start and end apart: 7, of which 3 were waited for; matrix products, arithmetic and copies ran while one was open for 29% of the time, Pallas kernels for 0%

profile of v18, /device:TPU:0, one launch (start us, length us, event | category | flops | bytes accessed | tf_op | source)
XLA Modules:
  0.0 105.5 jit_solution(17361877263819868853)
XLA Ops:
  0.7 1.0 copy-done
  1.6 1.9 %fusion.2 = bf16[2,400,400,1]{1,2,3,0:T(8,128)(2,1)S(1)} fusion(bf16[2,400,400]{1,2,0:T(8,128)(2,1)} %constant.123.clone, bf16[1,400,400]{2,1,0:T(8,128)(2,1)S(1)} %copy-done), kind=kOutput, calls=%fused_computation.12 | convolution fusion | flops 256320000 | bytes 1600000 | tf_op jit(solution)/shard_map/yx,hmx->hym/dot_general | solution.py:24
  4.5 1.1 %convert_element_type.222 = bf16[32,1,2525]{2,1,0:T(2,128)(2,1)} reshape(bf16[202,400]{1,0:T(8,128)(2,1)S(1)} %copy.122) | data formatting | bytes 323200 | tf_op jit(solution)/shard_map/convert_element_type | solution.py:179
  5.7 7.3 %all-to-all-start = ((bf16[32,1,2525]{2,1,0:T(2,128)(2,1)}), bf16[32,1,2525]{2,1,0:T(2,128)(2,1)S(1)}, u32[]{:S(2)}, u32[]{:S(2)}) async-start(bf16[32,1,2525]{2,1,0:T(2,128)(2,1)} %convert_element_type.222), calls=%async_computation | async-start | bytes 655360 | tf_op jit(solution)/shard_map/all_to_all | solution.py:179
  13.0 1.1 %convolution_bitcast_fusion = f32[2,2,400,400]{3,2,0,1:T(8,128)S(1)} fusion(bf16[2,400,400,1]{1,2,3,0:T(8,128)(2,1)S(1)} %fusion.2, bf16[2,400,400]{1,2,0:T(8,128)(2,1)S(1)} %copy-done.4), kind=kOutput, calls=%fused_computation.2 | convolution fusion | flops 512000000 | bytes 3840000 | tf_op jit(solution)/shard_map/gky,hym->ghkm/dot_general | solution.py:30
  14.5 1.3 %copy-done.1 = f32[2,2,400,400]{3,2,0,1:T(8,128)} copy-done((f32[2,2,400,400]{3,2,0,1:T(8,128)}, f32[2,2,400,400]{3,2,0,1:T(8,128)S(1)}, u32[]{:S(2)}) %copy-start.1) | copy-done | bytes 2560024
  22.7 3.0 %negate_convert_fusion = bf16[1,400,400]{2,1,0:T(8,128)(2,1)S(1)} fusion(f32[]{:T(128)S(6)} %mul.154, s32[400]{0:T(512)S(1)} %fusion.112), kind=kLoop, calls=%fused_computation.62 | loop fusion | flops 960000 | bytes 321604 | tf_op jit(solution)/shard_map/convert_element_type | solution.py:61
  27.5 1.5 %fusion.20 = f32[1,1,400,400]{3,2,1,0:T(8,128)S(1)} fusion(f32[2,2,400,400]{3,2,0,1:T(8,128)} %copy-done.1), kind=kLoop, calls=%fused_computation.43 | loop fusion | flops 160000 | bytes 1920000 | tf_op jit(solution)/shard_map/sub | solution.py:31
  29.4 0.9 broadcast_in_dim.30
  30.3 5.9 %all-to-all-start.1 = ((bf16[32,1,2525]{2,1,0:T(2,128)(2,1)}), bf16[32,1,2525]{2,1,0:T(2,128)(2,1)}, u32[]{:S(2)}, u32[]{:S(2)}) async-start(bf16[32,1,2525]{2,1,0:T(2,128)(2,1)} %broadcast_in_dim.30), calls=%async_computation.1 | async-start | bytes 655360 | tf_op jit(solution)/shard_map/all_to_all | solution.py:84
  36.7 0.9 all_to_all.21
  39.1 1.6 %fusion.75 = f32[1,1,400,400]{3,2,1,0:T(8,128)S(1)} fusion(f32[2,2,400,400]{3,2,0,1:T(8,128)} %copy-done.1), kind=kLoop, calls=%fused_computation.122 | loop fusion | flops 320000 | bytes 1920000 | tf_op jit(solution)/shard_map/neg | solution.py:32
  40.7 7.7 %all-to-all-done.1 = bf16[32,1,2525]{2,1,0:T(2,128)(2,1)} async-done(((bf16[32,1,2525]{2,1,0:T(2,128)(2,1)}), bf16[32,1,2525]{2,1,0:T(2,128)(2,1)}, u32[]{:S(2)}, u32[]{:S(2)}) %all-to-all-start.1) | async-done | bytes 161632 | tf_op jit(solution)/shard_map/all_to_all | solution.py:84
  48.4 4.3 %all-to-all-start.2 = ((bf16[8,2,12928]{2,1,0:T(2,128)(2,1)}), bf16[8,2,12928]{2,1,0:T(2,128)(2,1)}, u32[]{:S(2)}, u32[]{:S(2)}) async-start(bf16[8,2,12928]{2,1,0:T(2,128)(2,1)} %all_to_all.21), calls=%async_computation.2 | async-start | bytes 827392 | tf_op jit(solution)/shard_map/all_to_all | solution.py:180
  52.6 1.9 %reduce.4 = bf16[32,2525]{1,0:T(8,128)(2,1)S(1)} reduce(bf16[32,1,2525]{2,1,0:T(2,128)(2,1)} %all-to-all-done.1, bf16[]{:T(256)} %constant.133), dimensions={1}, to_apply=%all_to_all.20.reduce_sub_computation | reduce | bytes 323202 | tf_op jit(solution)/shard_map/all_to_all | solution.py:84
  54.6 1.2 %reshape.484 = bf16[202,400]{1,0:T(8,128)(2,1)} reshape(bf16[32,2525]{1,0:T(8,128)(2,1)S(1)} %reduce.4) | data formatting | bytes 323200 | tf_op jit(solution)/shard_map/reshape | solution.py:85
  55.8 1.3 %fusion.62 = f32[400,400]{1,0:T(8,128)S(1)} fusion(bf16[202,400]{1,0:T(8,128)(2,1)} %reshape.484, s32[400]{0:T(512)} %get-tuple-element.26, pred[400]{0:T(512)(128)(4,1)} %fusion.118), kind=kOutput, calls=%fused_computation.106 | convolution fusion | flops 64801600 | bytes 803600 | tf_op jit(solution)/shard_map/dot_general | solution.py:95
  57.0 1.4 %fusion.37 = f32[202,400]{0,1:T(8,128)S(1)} fusion(bf16[202,400]{1,0:T(8,128)(2,1)} %reshape.484, s32[400]{0:T(512)} %get-tuple-element.25, s32[400]{0:T(512)} %fusion.119, s32[400]{0:T(512)} %get-tuple-element.26, pred[400]{0:T(512)(128)(4,1)} %compare_and_fusion), kind=kOutput, calls=%fused_computation.64 | convolution fusion | flops 64960000 | bytes 490000 | tf_op jit(solution)/shard_map/dot_general | solution.py:90
  59.3 0.9 fusion.49
  62.4 1.8 %fusion.21 = f32[2,400,400]{2,1,0:T(8,128)} fusion(bf16[2,400,400]{1,2,0:T(8,128)(2,1)S(1)} %copy-done.4, bf16[2,64,400]{2,1,0:T(8,128)(2,1)S(1)} %broadcast_in_dim.25, bf16[1,272,400]{2,1,0:T(8,128)(2,1)S(1)} %get-tuple-element.9, bf16[1,272,400]{2,1,0:T(8,128)(2,1)S(1)} %get-tuple-element.8), kind=kOutput, calls=%fused_computation.46 | convolution fusion | flops 258560000 | bytes 2457600 | tf_op jit(solution)/shard_map/hxk,hkm->hxm/dot_general | solution.py:46
  64.4 1.2 %all_to_all.23 = bf16[16,12928]{1,0:T(8,128)(2,1)S(1)} reshape(bf16[8,2,12928]{2,1,0:T(2,128)(2,1)} %all-to-all-done.2) | data formatting | bytes 827392 | tf_op jit(solution)/shard_map/all_to_all | solution.py:180
  66.3 1.5 %reshape.492 = f32[16,16,800]{2,1,0:T(8,128)} reshape(f32[16,12800]{1,0:T(8,128)S(1)} %slice_convert_fusion.1) | data formatting | bytes 1638400 | tf_op jit(solution)/shard_map/convert_element_type | solution.py:219
  67.9 1.9 %negate_convert_fusion.1 = (bf16[16,16,400]{2,0,1:T(8,128)(2,1)S(1)}, f32[16,16,400]{2,0,1:T(8,128)S(1)}) fusion(f32[16]{0:T(128)S(1)} %get-tuple-element.27, s32[400]{0:T(512)S(1)} %copy-done.12, s32[16,16]{0,1:T(8,128)S(1)} %fusion.91), kind=kLoop, calls=%fused_computation.80 | loop fusion | flops 819200 | bytes 617088 | tf_op jit(solution)/shard_map/convert_element_type | solution.py:61
  69.8 2.0 %convolution_divide_fusion = f32[16,16,800]{2,0,1:T(8,128)S(1)} fusion(f32[16,16,800]{2,1,0:T(8,128)} %reshape.492, bf16[16,16,400]{2,0,1:T(8,128)(2,1)S(1)} %get-tuple-element.23, f32[8,16,800]{2,1,0:T(8,128)S(1)} %bitcast.163, s32[16]{0:T(128)S(1)} %get-tuple-element.2), kind=kOutput, calls=%fused_computation.8 | convolution fusion | flops 20889728 | bytes 2252864 | tf_op jit(solution)/shard_map/sj,jix->six/dot_general | solution.py:215
  73.3 2.3 %fusion.45 = f32[16,16,400]{2,0,1:T(8,128)S(1)} fusion(f32[16,16,399]{2,0,1:T(8,128)S(1)} %bitcast.158, f32[16,16,1]{2,0,1:T(8,128)S(1)} %slice.261, f32[16]{0:T(128)S(1)} %get-tuple-element.6, f32[16]{0:T(128)S(1)} %get-tuple-element.28, f32[16]{0:T(128)S(1)} %get-tuple-element.27, s32[400]{0:T(512)S(1)} %copy-done.12, s32[16,16]{0,1:T(8,128)S(1)} %fusion.91), kind=kLoop, calls=%fused_computation.75 | loop fusion | flops 1228800 | bytes 822016 | tf_op jit(solution)/shard_map/add | solution.py:223
  76.2 0.9 convolution_convert_fusion.1
  77.4 1.5 %collective-permute-start.1 = (bf16[2,32,1200]{2,1,0:T(8,128)(2,1)S(1)}, bf16[2,32,1200]{2,1,0:T(8,128)(2,1)S(1)}, u32[]{:S(2)}, u32[]{:S(2)}) collective-permute-start(bf16[2,32,1200]{2,1,0:T(8,128)(2,1)S(1)} %get-tuple-element.18), channel_id=1, source_target_pairs={{0,16},{8,24},{16,0},{24,8},{1,17},{9,25},{17,1},{25,9},{2,18},{10... | collective-permute-start | bytes 460808 | tf_op jit(solution)/shard_map/ppermute | solution.py:112
  78.9 1.4 %collective-permute-start.2 = (bf16[2,32,1200]{2,1,0:T(8,128)(2,1)S(1)}, bf16[2,32,1200]{2,1,0:T(8,128)(2,1)S(1)}, u32[]{:S(2)}, u32[]{:S(2)}) collective-permute-start(bf16[2,32,1200]{2,1,0:T(8,128)(2,1)S(1)} %get-tuple-element.17), channel_id=1, source_target_pairs={{0,24},{8,0},{16,8},{24,16},{1,25},{9,1},{17,9},{25,17},{2,26},{10... | collective-permute-start | bytes 460808 | tf_op jit(solution)/shard_map/ppermute | solution.py:112
  80.6 1.1 %copy.133 = bf16[16,2,16,400]{3,2,1,0:T(8,128)(2,1)} copy(bf16[16,2,16,400]{3,0,2,1:T(8,128)(2,1)S(1)} %fusion.11) | data formatting | bytes 819200 | tf_op jit(solution)/shard_map/convert_element_type | solution.py:198
  81.7 4.7 %all-to-all-start.3 = ((bf16[16,2,16,400]{3,2,1,0:T(8,128)(2,1)}), bf16[16,2,16,400]{3,2,1,0:T(8,128)(2,1)S(1)}, u32[]{:S(2)}, u32[]{:S(2)}) async-start(bf16[16,2,16,400]{3,2,1,0:T(8,128)(2,1)} %copy.133), calls=%async_computation.3 | async-start | bytes 1048576 | tf_op jit(solution)/shard_map/all_to_all | solution.py:205
  87.5 13.5 %all-to-all-done.3 = bf16[16,2,16,400]{3,2,1,0:T(8,128)(2,1)S(1)} async-done(((bf16[16,2,16,400]{3,2,1,0:T(8,128)(2,1)}), bf16[16,2,16,400]{3,2,1,0:T(8,128)(2,1)S(1)}, u32[]{:S(2)}, u32[]{:S(2)}) %all-to-all-start.3) | async-done | bytes 409632 | tf_op jit(solution)/shard_map/all_to_all | solution.py:205
  104.3 1.1 %fusion.17 = bf16[1,400,400]{2,1,0:T(8,128)(2,1)} fusion(f32[2,400,400]{2,1,0:T(8,128)S(1)} %fusion.29, f32[2,400,400]{2,1,0:T(8,128)S(1)} %copy-done.5), kind=kLoop, calls=%fused_computation.36 | loop fusion | flops 800000 | bytes 2880000 | tf_op jit(solution)/shard_map/convert_element_type | solution.py:268
  (139 shorter events, 21.5 us)
Async XLA Ops:
  0.6 2.9 %copy-start.4 = (bf16[2,400,400]{1,2,0:T(8,128)(2,1)S(1)}, bf16[2,400,400]{1,2,0:T(8,128)(2,1)}, u32[]{:S(2)}) copy-start(bf16[2,400,400]{1,2,0:T(8,128)(2,1)} %constant.123.clone) | copy-start | bytes 1920004
  5.7 23.4 %all-to-all-start = ((bf16[32,1,2525]{2,1,0:T(2,128)(2,1)}), bf16[32,1,2525]{2,1,0:T(2,128)(2,1)S(1)}, u32[]{:S(2)}, u32[]{:S(2)}) async-start(bf16[32,1,2525]{2,1,0:T(2,128)(2,1)} %convert_element_type.222), calls=%async_computation | async-start | bytes 655360 | tf_op jit(solution)/shard_map/all_to_all | solution.py:179
  14.1 1.7 %copy-start.1 = (f32[2,2,400,400]{3,2,0,1:T(8,128)}, f32[2,2,400,400]{3,2,0,1:T(8,128)S(1)}, u32[]{:S(2)}) copy-start(f32[2,2,400,400]{3,2,0,1:T(8,128)S(1)} %convolution_bitcast_fusion) | copy-start | bytes 7680004
  15.8 6.8 %copy-start.11 = (s32[400]{0:T(512)}, s32[400]{0:T(512)S(1)}, u32[]{:S(2)}) copy-start(s32[400]{0:T(512)S(1)} %fusion.112) | copy-start | bytes 4804
  19.3 1.8 %copy-start.22 = (s32[1,8]{1,0:T(1,128)S(1)}, s32[1,8]{1,0:T(1,128)}, u32[]{:S(2)}) copy-start(s32[1,8]{1,0:T(1,128)} %param.13) | copy-start | bytes 100
  19.3 1.9 %copy-start.23 = (s32[1,8]{1,0:T(1,128)S(1)}, s32[1,8]{1,0:T(1,128)}, u32[]{:S(2)}) copy-start(s32[1,8]{1,0:T(1,128)} %param.14) | copy-start | bytes 100
  19.3 2.0 %copy-start.24 = (s32[1,8]{1,0:T(1,128)S(1)}, s32[1,8]{1,0:T(1,128)}, u32[]{:S(2)}) copy-start(s32[1,8]{1,0:T(1,128)} %param.15) | copy-start | bytes 100
  19.3 2.1 %copy-start.25 = (f32[64]{0:T(128)S(1)}, f32[64]{0:T(128)}, u32[]{:S(2)}) copy-start(f32[64]{0:T(128)} %param.11) | copy-start | bytes 772
  20.4 6.5 %copy-start.17 = (s32[8]{0:T(128)}, s32[8]{0:T(128)S(1)}, u32[]{:S(2)}) copy-start(s32[8]{0:T(128)S(1)} %multiply_add_fusion) | copy-start | bytes 100
  29.1 8.6 %copy-start.10 = (bf16[2,128,800]{1,2,0:T(8,128)(2,1)S(1)}, bf16[2,128,800]{1,2,0:T(8,128)(2,1)}, u32[]{:S(2)}) copy-start(bf16[2,128,800]{1,2,0:T(8,128)(2,1)} %param.16) | copy-start | bytes 1228804
  30.3 18.1 %all-to-all-start.1 = ((bf16[32,1,2525]{2,1,0:T(2,128)(2,1)}), bf16[32,1,2525]{2,1,0:T(2,128)(2,1)}, u32[]{:S(2)}, u32[]{:S(2)}) async-start(bf16[32,1,2525]{2,1,0:T(2,128)(2,1)} %broadcast_in_dim.30), calls=%async_computation.1 | async-start | bytes 655360 | tf_op jit(solution)/shard_map/all_to_all | solution.py:84
  48.4 16.1 %all-to-all-start.2 = ((bf16[8,2,12928]{2,1,0:T(2,128)(2,1)}), bf16[8,2,12928]{2,1,0:T(2,128)(2,1)}, u32[]{:S(2)}, u32[]{:S(2)}) async-start(bf16[8,2,12928]{2,1,0:T(2,128)(2,1)} %all_to_all.21), calls=%async_computation.2 | async-start | bytes 827392 | tf_op jit(solution)/shard_map/all_to_all | solution.py:180
  55.8 2.7 %copy-start.15 = (s32[400]{0:T(512)S(1)}, s32[400]{0:T(512)}, u32[]{:S(2)}) copy-start(s32[400]{0:T(512)} %fusion.117) | copy-start | bytes 4804
  55.8 2.7 %copy-start.21 = (pred[400]{0:T(512)(128)(4,1)S(1)}, pred[400]{0:T(512)(128)(4,1)}, u32[]{:S(2)}) copy-start(pred[400]{0:T(512)(128)(4,1)} %fusion.116) | copy-start | bytes 1204
  64.2 1.9 %copy-start.26 = (f32[64]{0:T(128)S(1)}, f32[64]{0:T(128)}, u32[]{:S(2)}) copy-start(f32[64]{0:T(128)} %param.11) | copy-start | bytes 772
  65.6 2.3 %copy-start.12 = (s32[400]{0:T(512)S(1)}, s32[400]{0:T(512)}, u32[]{:S(2)}) copy-start(s32[400]{0:T(512)} %copy-done.11) | copy-start | bytes 4804
  66.1 3.7 %copy-start.9 = (f32[128,800]{1,0:T(8,128)S(1)}, f32[128,800]{1,0:T(8,128)}, u32[]{:S(2)}) copy-start(f32[128,800]{1,0:T(8,128)} %fusion.49) | copy-start | bytes 1228804
  72.9 2.8 %copy-start.2 = (f32[16,2,16,400]{3,0,2,1:T(8,128)}, f32[16,2,16,400]{3,0,2,1:T(8,128)S(1)}, u32[]{:S(2)}) copy-start(f32[16,2,16,400]{3,0,2,1:T(8,128)S(1)} %fusion.47) | copy-start | bytes 2457604
  72.9 2.8 %copy-start.13 = (s32[800]{0:T(1024)S(1)}, s32[800]{0:T(1024)}, u32[]{:S(2)}) copy-start(s32[800]{0:T(1024)} %get-tuple-element.29) | copy-start | bytes 9604
  72.9 2.8 %copy-start.14 = (s32[800]{0:T(1024)S(1)}, s32[800]{0:T(1024)}, u32[]{:S(2)}) copy-start(s32[800]{0:T(1024)} %get-tuple-element.30) | copy-start | bytes 9604
  72.9 2.8 %copy-start.19 = (pred[800]{0:T(1024)(128)(4,1)S(1)}, pred[800]{0:T(1024)(128)(4,1)}, u32[]{:S(2)}) copy-start(pred[800]{0:T(1024)(128)(4,1)} %fusion.111) | copy-start | bytes 2404
  77.0 3.2 %copy-start.3 = (f32[16,2,16,400]{3,0,2,1:T(8,128)S(1)}, f32[16,2,16,400]{3,0,2,1:T(8,128)}, u32[]{:S(2)}) copy-start(f32[16,2,16,400]{3,0,2,1:T(8,128)} %copy-done.2) | copy-start | bytes 2457604
  77.1 3.2 %slice-start = ((f32[16,2,16,400]{3,0,2,1:T(8,128)}), f32[16,2,16,1]{3,0,2,1:T(8,128)S(1)}, s32[]{:S(2)}) async-start(f32[16,2,16,400]{3,0,2,1:T(8,128)} %copy-done.2), calls=%async_computation.4 | async-start | bytes 524288 | tf_op jit(solution)/shard_map/jit(_roll_static)/slice | solution.py:197
  77.3 9.1 %collective-permute-start = (bf16[2,32,1200]{2,1,0:T(8,128)(2,1)S(1)}, bf16[2,32,1200]{2,1,0:T(8,128)(2,1)S(1)}, u32[]{:S(2)}, u32[]{:S(2)}) collective-permute-start(bf16[2,32,1200]{2,1,0:T(8,128)(2,1)S(1)} %get-tuple-element.16), channel_id=1, source_target_pairs={{0,8},{8,16},{16,24},{24,0},{1,9},{9,17},{17,25},{25,1},{2,10},{10... | collective-permute-start | bytes 460808 | tf_op jit(solution)/shard_map/ppermute | solution.py:112
  77.4 9.1 %collective-permute-start.1 = (bf16[2,32,1200]{2,1,0:T(8,128)(2,1)S(1)}, bf16[2,32,1200]{2,1,0:T(8,128)(2,1)S(1)}, u32[]{:S(2)}, u32[]{:S(2)}) collective-permute-start(bf16[2,32,1200]{2,1,0:T(8,128)(2,1)S(1)} %get-tuple-element.18), channel_id=1, source_target_pairs={{0,16},{8,24},{16,0},{24,8},{1,17},{9,25},{17,1},{25,9},{2,18},{10... | collective-permute-start | bytes 460808 | tf_op jit(solution)/shard_map/ppermute | solution.py:112
  78.9 7.6 %collective-permute-start.2 = (bf16[2,32,1200]{2,1,0:T(8,128)(2,1)S(1)}, bf16[2,32,1200]{2,1,0:T(8,128)(2,1)S(1)}, u32[]{:S(2)}, u32[]{:S(2)}) collective-permute-start(bf16[2,32,1200]{2,1,0:T(8,128)(2,1)S(1)} %get-tuple-element.17), channel_id=1, source_target_pairs={{0,24},{8,0},{16,8},{24,16},{1,25},{9,1},{17,9},{25,17},{2,26},{10... | collective-permute-start | bytes 460808 | tf_op jit(solution)/shard_map/ppermute | solution.py:112
  81.7 19.3 %copy-start.18 = (s32[8]{0:T(128)S(1)}, s32[8]{0:T(128)}, u32[]{:S(2)}) copy-start(s32[8]{0:T(128)} %copy-done.17) | copy-start | bytes 100
  81.7 19.2 %all-to-all-start.3 = ((bf16[16,2,16,400]{3,2,1,0:T(8,128)(2,1)}), bf16[16,2,16,400]{3,2,1,0:T(8,128)(2,1)S(1)}, u32[]{:S(2)}, u32[]{:S(2)}) async-start(bf16[16,2,16,400]{3,2,1,0:T(8,128)(2,1)} %copy.133), calls=%async_computation.3 | async-start | bytes 1048576 | tf_op jit(solution)/shard_map/all_to_all | solution.py:205
  86.6 15.1 %copy-start.6 = (f32[128,400]{1,0:T(8,128)S(1)}, f32[128,400]{1,0:T(8,128)}, u32[]{:S(2)}) copy-start(f32[128,400]{1,0:T(8,128)} %maximum_convert_fusion.1) | copy-start | bytes 614404
  86.6 15.1 %copy-start.7 = (f32[2,64,400]{2,1,0:T(8,128)S(1)}, f32[2,64,400]{2,1,0:T(8,128)}, u32[]{:S(2)}) copy-start(f32[2,64,400]{2,1,0:T(8,128)} %get-tuple-element.10) | copy-start | bytes 614404
  86.6 15.1 %copy-start.8 = (f32[2,64,400]{2,1,0:T(8,128)S(1)}, f32[2,64,400]{2,1,0:T(8,128)}, u32[]{:S(2)}) copy-start(f32[2,64,400]{2,1,0:T(8,128)} %get-tuple-element.11) | copy-start | bytes 614404
  102.9 1.4 %copy-start.5 = (f32[2,400,400]{2,1,0:T(8,128)S(1)}, f32[2,400,400]{2,1,0:T(8,128)}, u32[]{:S(2)}) copy-start(f32[2,400,400]{2,1,0:T(8,128)} %fusion.21) | copy-start | bytes 3840004
  (3 other events, 2.5 us)
